TPU v7x, 128 devices: a whole 4x4x4 slice. The times are simulated.
128 devices in a mesh: seg: 8 (over x, core), leaf: 16 (over z, y).
Axes of the slice: x: 4, y: 4, z: 4, core: 2. Of those that a mesh axis runs over, the one named last changes fastest.
Arguments:
- queries: bfloat16 [32, 512, 5120], P('seg', 'leaf'), may hold values from -160 to 160
- leaf_keys: bfloat16 [32, 512, 1024], P('seg', 'leaf'), may hold values from -5 to 5
- leaf_values: bfloat16 [32, 512, 1024], P('seg', 'leaf'), may hold values from -6 to 6
- inner_keys: bfloat16 [16, 512, 1024], P('seg', 'leaf'), may hold values from -6 to 6
- inner_values: bfloat16 [16, 512, 1024], P('seg', 'leaf'), may hold values from -6 to 6
- out_grad: bfloat16 [32, 512, 5120], P('seg', 'leaf'), may hold values from -6 to 6
- ancestors: int32 [32, 4], replicated, may hold values from 0 to 15, as said below
- depths: int32 [32], replicated, may hold values from 3 to 4, as said below
Outputs:
- attention: bfloat16 [32, 512, 5120], P('seg', 'leaf')
- query_grad: bfloat16 [32, 512, 5120], P('seg', 'leaf')
- leaf_key_grad: bfloat16 [32, 512, 1024], P('seg', 'leaf')
- leaf_value_grad: bfloat16 [32, 512, 1024], P('seg', 'leaf')
- inner_key_grad: bfloat16 [16, 512, 1024], P('seg', 'leaf')
- inner_value_grad: bfloat16 [16, 512, 1024], P('seg', 'leaf')
Inputs may be any that keep to these rules, and one draw needn't show every extreme that they name: `ancestors`: leaves l and m with l // 4 == m // 4 have the same row. Entry k of a row is the leaf's ancestor at tree level k, entry 0 the prompt's segment; entries at or past the leaf's depth are 0. The live entries of one row have different values of i // 2. `depths`: equal within each aligned block of 4 leaves; some leaf has 4.
All inputs are finite; a program needn't handle non-finite values.
Results may differ from a plain program's by a relative error of at most 0.03.
Values may be sent and summed in bfloat16 or wider, within the bound.
No kernel may reach another device: no remote copies, remote signals or barrier semaphores. Data moves between devices by JAX's collectives and lax.ppermute only.
A program may use at most 128 MiB of HBM per device.

v0:
```python
import math

import jax
import jax.numpy as jnp
from jax import lax
from jax.sharding import PartitionSpec as P

HD = 128


NEG_FILL = -1e30


def head_major(packed, kv_heads, head_size):
    block_count, rows_here = (packed.shape[0], packed.shape[1])
    shaped = packed.reshape(block_count, rows_here, 2, kv_heads, head_size)
    return shaped.transpose(3, 0, 1, 2, 4).reshape(kv_heads, block_count, rows_here, 2 * head_size)


def column_major(stacked, kv_heads, head_size):
    block_count, rows_here = (stacked.shape[1], stacked.shape[2])
    shaped = stacked.reshape(kv_heads, block_count, rows_here, 2, head_size)
    return shaped.transpose(1, 2, 3, 0, 4).reshape(block_count, rows_here, 2 * kv_heads * head_size)


def attend_block(
    query_row_set,
    gradient_row_set,
    key_anc,
    value_anc,
    private_keys,
    private_values,
    anc_visible,
    own_visible,
):
    logit_scale = 1.0 / math.sqrt(query_row_set.shape[-1])
    score_anc = (
        jnp.einsum("bmd,ad->bma", query_row_set, key_anc, preferred_element_type=jnp.float32)
        * logit_scale
    )
    score_own = (
        jnp.einsum("flh,feh->fle", query_row_set, private_keys, preferred_element_type=jnp.float32)
        * logit_scale
    )
    score_anc = jnp.where(anc_visible[None, None, :], score_anc, NEG_FILL)
    score_own = jnp.where(own_visible[None], score_own, NEG_FILL)
    highest = jnp.maximum(
        jnp.max(score_anc, axis=-1, keepdims=True), jnp.max(score_own, axis=-1, keepdims=True)
    )
    weight_anc = jnp.exp(score_anc - highest)
    weight_own = jnp.exp(score_own - highest)
    denom_sum = jnp.sum(weight_anc, axis=-1, keepdims=True) + jnp.sum(
        weight_own, axis=-1, keepdims=True
    )
    prob_anc = weight_anc / denom_sum
    prob_own = weight_own / denom_sum
    round_anc = prob_anc.astype(jnp.bfloat16)
    private_round = prob_own.astype(jnp.bfloat16)
    attention_result = jnp.einsum(
        "bma,ad->bmd", round_anc, value_anc, preferred_element_type=jnp.float32
    ) + jnp.einsum(
        "oiz,ozv->oiv", private_round, private_values, preferred_element_type=jnp.float32
    )
    result_round = attention_result.astype(jnp.bfloat16)
    delta_rows = jnp.sum(
        gradient_row_set.astype(jnp.float32) * result_round.astype(jnp.float32),
        axis=-1,
        keepdims=True,
    )
    dprob_anc = jnp.einsum(
        "bmd,ad->bma", gradient_row_set, value_anc, preferred_element_type=jnp.float32
    )
    own_probability_grad = jnp.einsum(
        "flh,feh->fle", gradient_row_set, private_values, preferred_element_type=jnp.float32
    )
    dscore_anc = (prob_anc * (dprob_anc - delta_rows)).astype(jnp.bfloat16)
    own_score_grad = (prob_own * (own_probability_grad - delta_rows)).astype(jnp.bfloat16)
    query_portion = (
        jnp.einsum("bma,ad->bmd", dscore_anc, key_anc, preferred_element_type=jnp.float32)
        + jnp.einsum(
            "oiz,ozv->oiv", own_score_grad, private_keys, preferred_element_type=jnp.float32
        )
    ) * logit_scale
    dkey_anc = (
        jnp.einsum("bma,bmd->ad", dscore_anc, query_row_set, preferred_element_type=jnp.float32)
        * logit_scale
    )
    dvalue_anc = jnp.einsum(
        "bma,bmd->ad", round_anc, gradient_row_set, preferred_element_type=jnp.float32
    )
    dkey_own = (
        jnp.einsum(
            "ers,erc->esc", own_score_grad, query_row_set, preferred_element_type=jnp.float32
        )
        * logit_scale
    )
    dvalue_own = jnp.einsum(
        "ers,erc->esc", private_round, gradient_row_set, preferred_element_type=jnp.float32
    )
    return (result_round, query_portion, dkey_anc, dvalue_anc, dkey_own, dvalue_own)


def on_device(
    queries, leaf_keys, leaf_values, inner_keys, inner_values, out_grad, ancestors, depths
):
    seg_count = lax.axis_size("seg")
    leaf_count = lax.axis_size("leaf")
    seg_here = lax.axis_index("seg")
    leaf_here = lax.axis_index("leaf")
    leaf_dev, rows_here, query_width = queries.shape
    slot_count = inner_keys.shape[0]
    key_width = leaf_keys.shape[2]
    kv_heads = key_width // HD
    group_heads = query_width // key_width
    seg_len = rows_here * leaf_count
    levels = ancestors.shape[1]
    group_lists = ancestors[::leaf_dev]
    group_depth = depths[::leaf_dev]
    owners = group_lists // slot_count
    slot_of = group_lists % slot_count
    level_ids = jnp.arange(levels, dtype=jnp.int32)
    alive_levels = level_ids[None, :] < group_depth[:, None]
    served = alive_levels & (owners == seg_here)
    slot_ids = jnp.arange(slot_count, dtype=jnp.int32)
    serve_pick = jnp.sum(
        (served[:, :, None] & (slot_of[:, :, None] == slot_ids[None, None, :])).astype(jnp.float32),
        axis=1,
    ).astype(jnp.bfloat16)
    stored = jnp.concatenate([inner_keys, inner_values], axis=2)
    outgoing = jnp.einsum(
        "gs,src->grc", serve_pick, stored, preferred_element_type=jnp.float32
    ).astype(jnp.bfloat16)
    arrived = lax.all_to_all(outgoing, "seg", split_axis=0, concat_axis=0, tiled=True)
    my_owners = jnp.take(owners, seg_here, axis=0)
    my_alive = jnp.take(alive_levels, seg_here, axis=0)
    ancestor_rows = jnp.where(
        my_alive[:, None, None], jnp.take(arrived, my_owners, axis=0), jnp.zeros((), jnp.bfloat16)
    )
    own_rows = jnp.concatenate([leaf_keys, leaf_values], axis=2)
    anc_visible = jnp.repeat(my_alive, seg_len)
    blocks = jnp.concatenate([ancestor_rows, own_rows], axis=0)
    by_head = head_major(blocks, kv_heads, HD)
    query_heads = queries.reshape(leaf_dev, rows_here, kv_heads, group_heads * HD).transpose(
        2, 0, 1, 3
    )
    grad_heads = out_grad.reshape(leaf_dev, rows_here, kv_heads, group_heads * HD).transpose(
        2, 0, 1, 3
    )
    row_ids = leaf_here * rows_here + jnp.arange(rows_here, dtype=jnp.int32)
    causal = jnp.arange(seg_len, dtype=jnp.int32)[None, :] <= row_ids[:, None]
    own_visible = jnp.repeat(causal, group_heads, axis=0)

    def head_step(operands):
        query_head, grad_head, packed_head = operands
        whole_rows = lax.all_gather(packed_head, "leaf", axis=1, tiled=True)
        key_anc = whole_rows[:levels, :, :HD].reshape(levels * seg_len, HD)
        value_anc = whole_rows[:levels, :, HD:].reshape(levels * seg_len, HD)
        private_keys = whole_rows[levels:, :, :HD]
        private_values = whole_rows[levels:, :, HD:]
        query_row_set = query_head.reshape(leaf_dev, rows_here * group_heads, HD)
        gradient_row_set = grad_head.reshape(leaf_dev, rows_here * group_heads, HD)
        result_round, query_portion, dkey_anc, dvalue_anc, dkey_own, dvalue_own = attend_block(
            query_row_set,
            gradient_row_set,
            key_anc,
            value_anc,
            private_keys,
            private_values,
            anc_visible,
            own_visible,
        )
        key_grads = jnp.concatenate([dkey_anc.reshape(levels, seg_len, HD), dkey_own], axis=0)
        value_grads = jnp.concatenate([dvalue_anc.reshape(levels, seg_len, HD), dvalue_own], axis=0)
        reduced = lax.psum_scatter(
            jnp.concatenate([key_grads, value_grads], axis=2),
            "leaf",
            scatter_dimension=1,
            tiled=True,
        )
        return (
            result_round.reshape(leaf_dev, rows_here, group_heads * HD),
            query_portion.astype(jnp.bfloat16).reshape(leaf_dev, rows_here, group_heads * HD),
            reduced,
        )

    result_heads, dquery_heads, reduced_heads = lax.map(
        head_step, (query_heads, grad_heads, by_head)
    )
    attention = result_heads.transpose(1, 2, 0, 3).reshape(leaf_dev, rows_here, query_width)
    query_grad = dquery_heads.transpose(1, 2, 0, 3).reshape(leaf_dev, rows_here, query_width)
    summed = column_major(reduced_heads, kv_heads, HD)
    anc_part = summed[:levels]
    own_grads = summed[levels:].astype(jnp.bfloat16)
    leaf_key_grad = own_grads[:, :, :key_width]
    leaf_value_grad = own_grads[:, :, key_width:]
    part_round = anc_part.astype(jnp.bfloat16)
    seg_ids = jnp.arange(seg_count, dtype=jnp.int32)
    homeward_pick = ((my_owners[None, :] == seg_ids[:, None]) & my_alive[None, :]).astype(
        jnp.bfloat16
    )
    homeward = jnp.einsum(
        "ok,krc->orc", homeward_pick, part_round, preferred_element_type=jnp.float32
    ).astype(jnp.bfloat16)
    returned = lax.all_to_all(homeward, "seg", split_axis=0, concat_axis=0, tiled=True)
    collected = jnp.einsum(
        "gs,grc->src", serve_pick, returned, preferred_element_type=jnp.float32
    ).astype(jnp.bfloat16)
    return (
        attention,
        query_grad,
        leaf_key_grad,
        leaf_value_grad,
        collected[:, :, :key_width],
        collected[:, :, key_width:],
    )


def solution(mesh):
    return jax.shard_map(
        on_device,
        mesh=mesh,
        in_specs=(
            P("seg", "leaf", None),
            P("seg", "leaf", None),
            P("seg", "leaf", None),
            P("seg", "leaf", None),
            P("seg", "leaf", None),
            P("seg", "leaf", None),
            P(),
            P(),
        ),
        out_specs=(
            P("seg", "leaf", None),
            P("seg", "leaf", None),
            P("seg", "leaf", None),
            P("seg", "leaf", None),
            P("seg", "leaf", None),
            P("seg", "leaf", None),
        ),
        check_vma=False,
    )
```

profile of v0, /device:TPU:0, one launch (start us, length us, event | category | flops | bytes accessed | tf_op | source)
XLA Modules:
  0.0 1322.7 jit_solution(9653723527980471428)
XLA Ops:
  13.4 4.4 all-to-all-start
  24.1 9.7 all-to-all-done
  38.7 1249.6 %while.17 = (s32[]{:T(128)}, bf16[8,4,32,640]{3,2,1,0:T(8,128)(2,1)}, bf16[8,4,32,640]{3,2,1,0:T(8,128)(2,1)}, bf16[8,8,32,256]{3,1,2,0:T(8,128)(2,1)}, bf16[8,4...) while((s32[]{:T(128)}, ...), condition=%wide.region_8.9_spmd.clone, body=%wide.region_1.8_spmd.clone.sunk | while | flops 2550151168 | bytes 133755288 | solution.py:186
  43.5 44.3 %all-gather.6.cloned.1.call-done = bf16[1,8,512,256]{3,2,1,0:T(8,128)(2,1)} async-done(((bf16[1,8,32,256]{3,2,1,0:T(8,128)(2,1)}), bf16[1,8,512,256]{3,2,1,0:T(8,128)(2,1)}) %all-gather.6.cloned.1.call-update) | async-done | bytes 2097168 | tf_op jit(solution)/shard_map/while/body/eval_jaxpr/all_gather | solution.py:155
  111.1 5.5 copy.107
  116.7 2.7 fusion.139
  121.7 72.9 %reduce-scatter.2.cloned.1.call-done = f32[8,32,256]{2,0,1:T(8,128)} async-done(((f32[8,512,256]{2,0,1:T(8,128)}), f32[8,32,256]{2,0,1:T(8,128)}) %reduce-scatter.2.cloned.1.call-update) | async-done | bytes 262160 | tf_op jit(solution)/shard_map/while/body/eval_jaxpr/reduce_scatter | solution.py:174
  201.1 42.8 %all-gather.6.cloned.1.call-done = bf16[1,8,512,256]{3,2,1,0:T(8,128)(2,1)} async-done(((bf16[1,8,32,256]{3,2,1,0:T(8,128)(2,1)}), bf16[1,8,512,256]{3,2,1,0:T(8,128)(2,1)}) %all-gather.6.cloned.1.call-update) | async-done | bytes 2097168 | tf_op jit(solution)/shard_map/while/body/eval_jaxpr/all_gather | solution.py:155
  267.2 5.5 copy.107
  272.7 2.7 fusion.139
  277.8 72.9 %reduce-scatter.2.cloned.1.call-done = f32[8,32,256]{2,0,1:T(8,128)} async-done(((f32[8,512,256]{2,0,1:T(8,128)}), f32[8,32,256]{2,0,1:T(8,128)}) %reduce-scatter.2.cloned.1.call-update) | async-done | bytes 262160 | tf_op jit(solution)/shard_map/while/body/eval_jaxpr/reduce_scatter | solution.py:174
  357.2 42.5 %all-gather.6.cloned.1.call-done = bf16[1,8,512,256]{3,2,1,0:T(8,128)(2,1)} async-done(((bf16[1,8,32,256]{3,2,1,0:T(8,128)(2,1)}), bf16[1,8,512,256]{3,2,1,0:T(8,128)(2,1)}) %all-gather.6.cloned.1.call-update) | async-done | bytes 2097168 | tf_op jit(solution)/shard_map/while/body/eval_jaxpr/all_gather | solution.py:155
  423.0 5.5 copy.107
  433.6 72.9 %reduce-scatter.2.cloned.1.call-done = f32[8,32,256]{2,0,1:T(8,128)} async-done(((f32[8,512,256]{2,0,1:T(8,128)}), f32[8,32,256]{2,0,1:T(8,128)}) %reduce-scatter.2.cloned.1.call-update) | async-done | bytes 262160 | tf_op jit(solution)/shard_map/while/body/eval_jaxpr/reduce_scatter | solution.py:174
  512.9 42.8 %all-gather.6.cloned.1.call-done = bf16[1,8,512,256]{3,2,1,0:T(8,128)(2,1)} async-done(((bf16[1,8,32,256]{3,2,1,0:T(8,128)(2,1)}), bf16[1,8,512,256]{3,2,1,0:T(8,128)(2,1)}) %all-gather.6.cloned.1.call-update) | async-done | bytes 2097168 | tf_op jit(solution)/shard_map/while/body/eval_jaxpr/all_gather | solution.py:155
  579.1 5.5 copy.107
  589.7 72.9 %reduce-scatter.2.cloned.1.call-done = f32[8,32,256]{2,0,1:T(8,128)} async-done(((f32[8,512,256]{2,0,1:T(8,128)}), f32[8,32,256]{2,0,1:T(8,128)}) %reduce-scatter.2.cloned.1.call-update) | async-done | bytes 262160 | tf_op jit(solution)/shard_map/while/body/eval_jaxpr/reduce_scatter | solution.py:174
  669.1 42.8 %all-gather.6.cloned.1.call-done = bf16[1,8,512,256]{3,2,1,0:T(8,128)(2,1)} async-done(((bf16[1,8,32,256]{3,2,1,0:T(8,128)(2,1)}), bf16[1,8,512,256]{3,2,1,0:T(8,128)(2,1)}) %all-gather.6.cloned.1.call-update) | async-done | bytes 2097168 | tf_op jit(solution)/shard_map/while/body/eval_jaxpr/all_gather | solution.py:155
  735.2 5.5 copy.107
  745.8 72.9 %reduce-scatter.2.cloned.1.call-done = f32[8,32,256]{2,0,1:T(8,128)} async-done(((f32[8,512,256]{2,0,1:T(8,128)}), f32[8,32,256]{2,0,1:T(8,128)}) %reduce-scatter.2.cloned.1.call-update) | async-done | bytes 262160 | tf_op jit(solution)/shard_map/while/body/eval_jaxpr/reduce_scatter | solution.py:174
  825.2 42.8 %all-gather.6.cloned.1.call-done = bf16[1,8,512,256]{3,2,1,0:T(8,128)(2,1)} async-done(((bf16[1,8,32,256]{3,2,1,0:T(8,128)(2,1)}), bf16[1,8,512,256]{3,2,1,0:T(8,128)(2,1)}) %all-gather.6.cloned.1.call-update) | async-done | bytes 2097168 | tf_op jit(solution)/shard_map/while/body/eval_jaxpr/all_gather | solution.py:155
  891.3 5.5 copy.107
  901.9 72.9 %reduce-scatter.2.cloned.1.call-done = f32[8,32,256]{2,0,1:T(8,128)} async-done(((f32[8,512,256]{2,0,1:T(8,128)}), f32[8,32,256]{2,0,1:T(8,128)}) %reduce-scatter.2.cloned.1.call-update) | async-done | bytes 262160 | tf_op jit(solution)/shard_map/while/body/eval_jaxpr/reduce_scatter | solution.py:174
  981.3 42.8 %all-gather.6.cloned.1.call-done = bf16[1,8,512,256]{3,2,1,0:T(8,128)(2,1)} async-done(((bf16[1,8,32,256]{3,2,1,0:T(8,128)(2,1)}), bf16[1,8,512,256]{3,2,1,0:T(8,128)(2,1)}) %all-gather.6.cloned.1.call-update) | async-done | bytes 2097168 | tf_op jit(solution)/shard_map/while/body/eval_jaxpr/all_gather | solution.py:155
  1047.5 5.5 copy.107
  1058.1 72.9 %reduce-scatter.2.cloned.1.call-done = f32[8,32,256]{2,0,1:T(8,128)} async-done(((f32[8,512,256]{2,0,1:T(8,128)}), f32[8,32,256]{2,0,1:T(8,128)}) %reduce-scatter.2.cloned.1.call-update) | async-done | bytes 262160 | tf_op jit(solution)/shard_map/while/body/eval_jaxpr/reduce_scatter | solution.py:174
  1137.4 42.5 %all-gather.6.cloned.1.call-done = bf16[1,8,512,256]{3,2,1,0:T(8,128)(2,1)} async-done(((bf16[1,8,32,256]{3,2,1,0:T(8,128)(2,1)}), bf16[1,8,512,256]{3,2,1,0:T(8,128)(2,1)}) %all-gather.6.cloned.1.call-update) | async-done | bytes 2097168 | tf_op jit(solution)/shard_map/while/body/eval_jaxpr/all_gather | solution.py:155
  1203.2 5.5 copy.107
  1208.7 2.7 fusion.139
  1213.8 72.9 %reduce-scatter.2.cloned.1.call-done = f32[8,32,256]{2,0,1:T(8,128)} async-done(((f32[8,512,256]{2,0,1:T(8,128)}), f32[8,32,256]{2,0,1:T(8,128)}) %reduce-scatter.2.cloned.1.call-update) | async-done | bytes 262160 | tf_op jit(solution)/shard_map/while/body/eval_jaxpr/reduce_scatter | solution.py:174
  1293.6 4.3 all-to-all-start.1
  1302.2 11.5 all-to-all-done.1
  (491 shorter events, 298.7 us)
Async XLA Ops:
  11.8 6.0 copy-start.8
  13.4 20.4 %all-to-all-start = ((bf16[8,32,2048]{2,1,0:T(8,128)(2,1)}), bf16[8,32,2048]{2,1,0:T(8,128)(2,1)}, u32[]{:S(2)}, u32[]{:S(2)}) async-start(bf16[8,32,2048]{2,1,0:T(8,128)(2,1)} %copy.66), calls=%async_computation.1 | async-start | bytes 2097152 | tf_op jit(solution)/shard_map/all_to_all | solution.py:133
  23.6 12.3 copy-start.7
  23.8 12.2 copy-start.14
  38.7 49.1 %all-gather.6.cloned.1.call-start = ((), (), s32[]{:S(2)}) async-start(), calls=%async_computation.3 | async-start | bytes 2228224 | tf_op jit(solution)/shard_map/while/body/eval_jaxpr/all_gather | solution.py:155
  40.3 154.4 %reduce-scatter.2.cloned.1.call-start = ((), (), s32[]{:S(2)}) async-start(), calls=%async_computation.4 | async-start | bytes 4456448 | tf_op jit(solution)/shard_map/while/body/eval_jaxpr/reduce_scatter | solution.py:174
  116.6 4.2 copy-start.5
  196.2 47.7 %all-gather.6.cloned.1.call-start = ((), (), s32[]{:S(2)}) async-start(), calls=%async_computation.3 | async-start | bytes 2228224 | tf_op jit(solution)/shard_map/while/body/eval_jaxpr/all_gather | solution.py:155
  197.8 152.9 %reduce-scatter.2.cloned.1.call-start = ((), (), s32[]{:S(2)}) async-start(), calls=%async_computation.4 | async-start | bytes 4456448 | tf_op jit(solution)/shard_map/while/body/eval_jaxpr/reduce_scatter | solution.py:174
  272.7 4.2 copy-start.5
  352.4 47.4 %all-gather.6.cloned.1.call-start = ((), (), s32[]{:S(2)}) async-start(), calls=%async_computation.3 | async-start | bytes 2228224 | tf_op jit(solution)/shard_map/while/body/eval_jaxpr/all_gather | solution.py:155
  353.9 152.5 %reduce-scatter.2.cloned.1.call-start = ((), (), s32[]{:S(2)}) async-start(), calls=%async_computation.4 | async-start | bytes 4456448 | tf_op jit(solution)/shard_map/while/body/eval_jaxpr/reduce_scatter | solution.py:174
  415.0 4.0 copy-start.6
  428.5 4.2 copy-start.5
  508.1 47.7 %all-gather.6.cloned.1.call-start = ((), (), s32[]{:S(2)}) async-start(), calls=%async_computation.3 | async-start | bytes 2228224 | tf_op jit(solution)/shard_map/while/body/eval_jaxpr/all_gather | solution.py:155
  509.7 152.9 %reduce-scatter.2.cloned.1.call-start = ((), (), s32[]{:S(2)}) async-start(), calls=%async_computation.4 | async-start | bytes 4456448 | tf_op jit(solution)/shard_map/while/body/eval_jaxpr/reduce_scatter | solution.py:174
  571.0 4.0 copy-start.6
  584.6 4.2 copy-start.5
  664.2 47.7 %all-gather.6.cloned.1.call-start = ((), (), s32[]{:S(2)}) async-start(), calls=%async_computation.3 | async-start | bytes 2228224 | tf_op jit(solution)/shard_map/while/body/eval_jaxpr/all_gather | solution.py:155
  665.8 152.9 %reduce-scatter.2.cloned.1.call-start = ((), (), s32[]{:S(2)}) async-start(), calls=%async_computation.4 | async-start | bytes 4456448 | tf_op jit(solution)/shard_map/while/body/eval_jaxpr/reduce_scatter | solution.py:174
  740.7 4.2 copy-start.5
  820.3 47.7 %all-gather.6.cloned.1.call-start = ((), (), s32[]{:S(2)}) async-start(), calls=%async_computation.3 | async-start | bytes 2228224 | tf_op jit(solution)/shard_map/while/body/eval_jaxpr/all_gather | solution.py:155
  821.9 152.9 %reduce-scatter.2.cloned.1.call-start = ((), (), s32[]{:S(2)}) async-start(), calls=%async_computation.4 | async-start | bytes 4456448 | tf_op jit(solution)/shard_map/while/body/eval_jaxpr/reduce_scatter | solution.py:174
  896.8 4.2 copy-start.5
  976.5 47.7 %all-gather.6.cloned.1.call-start = ((), (), s32[]{:S(2)}) async-start(), calls=%async_computation.3 | async-start | bytes 2228224 | tf_op jit(solution)/shard_map/while/body/eval_jaxpr/all_gather | solution.py:155
  978.1 152.8 %reduce-scatter.2.cloned.1.call-start = ((), (), s32[]{:S(2)}) async-start(), calls=%async_computation.4 | async-start | bytes 4456448 | tf_op jit(solution)/shard_map/while/body/eval_jaxpr/reduce_scatter | solution.py:174
  1053.0 4.2 copy-start.5
  1132.5 47.4 %all-gather.6.cloned.1.call-start = ((), (), s32[]{:S(2)}) async-start(), calls=%async_computation.3 | async-start | bytes 2228224 | tf_op jit(solution)/shard_map/while/body/eval_jaxpr/all_gather | solution.py:155
  1134.1 152.6 %reduce-scatter.2.cloned.1.call-start = ((), (), s32[]{:S(2)}) async-start(), calls=%async_computation.4 | async-start | bytes 4456448 | tf_op jit(solution)/shard_map/while/body/eval_jaxpr/reduce_scatter | solution.py:174
  1208.7 4.2 copy-start.5
  1293.6 20.2 %all-to-all-start.1 = ((bf16[8,32,2048]{2,1,0:T(8,128)(2,1)}), bf16[8,32,2048]{2,1,0:T(8,128)(2,1)S(1)}, u32[]{:S(2)}, u32[]{:S(2)}) async-start(bf16[8,32,2048]{2,1,0:T(8,128)(2,1)} %copy.74), calls=%async_computation.2 | async-start | bytes 2097152 | tf_op jit(solution)/shard_map/all_to_all | solution.py:204
  1299.7 14.0 %copy-start.17 = (bf16[8,2]{0,1:T(2,128)(2,1)S(1)}, bf16[8,2]{0,1:T(2,128)(2,1)}, u32[]{:S(2)}) copy-start(bf16[8,2]{0,1:T(2,128)(2,1)} %copy-done.16) | copy-start | bytes 100
  (53 other events, 115.8 us)
Sparse Core Ops, SparseCore 0:
  42.2 45.5 all-gather.5
  116.8 77.8 reduce-scatter.1
  199.8 44.1 all-gather.5
  272.8 77.8 reduce-scatter.1
  355.6 44.1 all-gather.5
  428.6 77.7 reduce-scatter.1
  511.6 44.1 all-gather.5
  584.7 77.8 reduce-scatter.1
  667.7 44.1 all-gather.5
  740.8 77.8 reduce-scatter.1
  823.9 44.1 all-gather.5
  897.0 77.8 reduce-scatter.1
  980.0 44.1 all-gather.5
  1053.1 77.7 reduce-scatter.1
  1135.7 44.1 all-gather.5
  1208.8 77.8 reduce-scatter.1
where the time goes:
time: 1330 us; the launch traced here: 1320 us
  waiting for transfers between devices  948 us (71%)
  local copies, waits for them, and re-layouts  172 us (13%)
  matrix products  130 us (10%)
  other arithmetic  47.1 us (4%)
  between operations  14 us (1%)
    reduce_scatter x8, waiting for transfers between devices, head_step(): lax.psum_scatter(jnp.concatenate([key_grads, value_grads], axis=2), 'leaf...  583 us
    all_gather x8, waiting for transfers between devices, head_step(): whole_rows = lax.all_gather(packed_head, 'leaf', axis=1, tiled=True)  343 us
    concatenate x8, local copies, waits for them, and re-layouts, head_step(): jnp.concatenate([key_grads, value_grads], axis=2)  43.7 us
    dynamic_slice x24, local copies, waits for them, and re-layouts, on_device(): lax.map(head_step, (query_heads, grad_heads, by_head))  27.5 us
  transfers between devices with their start and end apart: 18, of which 18 were waited for; matrix products, arithmetic and copies ran while one was open for 6% of the time, Pallas kernels for 0%

commit v1 on v0

v1 whole, which is shorter than its diff:
```python
import math

import jax
import jax.numpy as jnp
from jax import lax
from jax.sharding import PartitionSpec as P

HD = 128


NEG_FILL = -1e30


def attend_leaf(query_rows, grad_rows, key_anc, value_anc, own_keys, own_values, anc_visible, own_visible):
    logit_scale = 1.0 / math.sqrt(query_rows.shape[-1])
    score_anc = jnp.einsum("md,ad->ma", query_rows, key_anc, preferred_element_type=jnp.float32) * logit_scale
    score_own = jnp.einsum("md,sd->ms", query_rows, own_keys, preferred_element_type=jnp.float32) * logit_scale
    score_anc = jnp.where(anc_visible[None, :], score_anc, NEG_FILL)
    score_own = jnp.where(own_visible, score_own, NEG_FILL)
    highest = jnp.maximum(jnp.max(score_anc, axis=-1, keepdims=True), jnp.max(score_own, axis=-1, keepdims=True))
    weight_anc = jnp.exp(score_anc - highest)
    weight_own = jnp.exp(score_own - highest)
    denom_sum = jnp.sum(weight_anc, axis=-1, keepdims=True) + jnp.sum(weight_own, axis=-1, keepdims=True)
    prob_anc = weight_anc / denom_sum
    prob_own = weight_own / denom_sum
    round_anc = prob_anc.astype(jnp.bfloat16)
    round_own = prob_own.astype(jnp.bfloat16)
    result = jnp.einsum("ma,ad->md", round_anc, value_anc, preferred_element_type=jnp.float32) + jnp.einsum(
        "ms,sd->md", round_own, own_values, preferred_element_type=jnp.float32
    )
    result_round = result.astype(jnp.bfloat16)
    delta_rows = jnp.sum(grad_rows.astype(jnp.float32) * result_round.astype(jnp.float32), axis=-1, keepdims=True)
    dprob_anc = jnp.einsum("md,ad->ma", grad_rows, value_anc, preferred_element_type=jnp.float32)
    dprob_own = jnp.einsum("md,sd->ms", grad_rows, own_values, preferred_element_type=jnp.float32)
    dscore_anc = (prob_anc * (dprob_anc - delta_rows)).astype(jnp.bfloat16)
    dscore_own = (prob_own * (dprob_own - delta_rows)).astype(jnp.bfloat16)
    query_portion = (
        jnp.einsum("ma,ad->md", dscore_anc, key_anc, preferred_element_type=jnp.float32)
        + jnp.einsum("ms,sd->md", dscore_own, own_keys, preferred_element_type=jnp.float32)
    ) * logit_scale
    dkey_anc = jnp.einsum("ma,md->ad", dscore_anc, query_rows, preferred_element_type=jnp.float32) * logit_scale
    dvalue_anc = jnp.einsum("ma,md->ad", round_anc, grad_rows, preferred_element_type=jnp.float32)
    dkey_own = jnp.einsum("ms,md->sd", dscore_own, query_rows, preferred_element_type=jnp.float32) * logit_scale
    dvalue_own = jnp.einsum("ms,md->sd", round_own, grad_rows, preferred_element_type=jnp.float32)
    return result_round, query_portion.astype(jnp.bfloat16), dkey_anc, dvalue_anc, dkey_own, dvalue_own


def on_device(queries, leaf_keys, leaf_values, inner_keys, inner_values, out_grad, ancestors, depths):
    seg_count = lax.axis_size("seg")
    leaf_count = lax.axis_size("leaf")
    seg_here = lax.axis_index("seg")
    leaf_here = lax.axis_index("leaf")
    leaf_dev, rows_here, query_width = queries.shape
    slot_count = inner_keys.shape[0]
    key_width = leaf_keys.shape[2]
    kv_heads = key_width // HD
    group_heads = query_width // key_width
    head_width = group_heads * HD
    seg_len = rows_here * leaf_count
    levels = ancestors.shape[1]
    pair_count = leaf_count // kv_heads
    pair_leaves = leaf_dev // pair_count
    my_pair = leaf_here % pair_count

    group_lists = ancestors[::leaf_dev]
    group_depth = depths[::leaf_dev]
    owners = group_lists // slot_count
    slot_of = group_lists % slot_count
    level_ids = jnp.arange(levels, dtype=jnp.int32)
    alive_levels = level_ids[None, :] < group_depth[:, None]
    served = alive_levels & (owners == seg_here)
    slot_ids = jnp.arange(slot_count, dtype=jnp.int32)
    serve_pick = jnp.sum(
        (served[:, :, None] & (slot_of[:, :, None] == slot_ids[None, None, :])).astype(jnp.float32),
        axis=1,
    ).astype(jnp.bfloat16)
    stored = jnp.concatenate([inner_keys, inner_values], axis=2)
    outgoing = jnp.einsum("gs,src->grc", serve_pick, stored, preferred_element_type=jnp.float32).astype(
        jnp.bfloat16
    )
    arrived = lax.all_to_all(outgoing, "seg", split_axis=0, concat_axis=0, tiled=True)
    my_owners = jnp.take(owners, seg_here, axis=0)
    my_alive = jnp.take(alive_levels, seg_here, axis=0)
    ancestor_rows = jnp.where(
        my_alive[:, None, None], jnp.take(arrived, my_owners, axis=0), jnp.zeros((), jnp.bfloat16)
    )

    def to_heads(x, width):
        shaped = x.reshape(pair_count, pair_leaves, rows_here, kv_heads, width)
        return shaped.transpose(3, 0, 1, 2, 4).reshape(leaf_count, pair_leaves, rows_here, width)

    packed = jnp.concatenate(
        [to_heads(queries, head_width), to_heads(out_grad, head_width), to_heads(leaf_keys, HD), to_heads(leaf_values, HD)],
        axis=3,
    )
    got = lax.all_to_all(packed, "leaf", split_axis=0, concat_axis=0, tiled=True)
    got = got.transpose(1, 0, 2, 3).reshape(pair_leaves, seg_len, packed.shape[3])
    q_here = got[:, :, :head_width]
    g_here = got[:, :, head_width : 2 * head_width]
    k_own = got[:, :, 2 * head_width : 2 * head_width + HD]
    v_own = got[:, :, 2 * head_width + HD :]

    anc_k = ancestor_rows[:, :, :key_width].reshape(levels, rows_here, kv_heads, HD)
    anc_v = ancestor_rows[:, :, key_width:].reshape(levels, rows_here, kv_heads, HD)
    anc_heads = jnp.concatenate([anc_k, anc_v], axis=3).transpose(2, 0, 1, 3)
    anc_send = jnp.broadcast_to(anc_heads[:, None], (kv_heads, pair_count) + anc_heads.shape[1:]).reshape(
        (leaf_count,) + anc_heads.shape[1:]
    )
    anc_got = lax.all_to_all(anc_send, "leaf", split_axis=0, concat_axis=0, tiled=True)
    anc_got = anc_got.transpose(1, 0, 2, 3).reshape(levels * seg_len, 2 * HD)
    key_anc = anc_got[:, :HD]
    value_anc = anc_got[:, HD:]
    anc_visible = jnp.repeat(my_alive, seg_len)
    positions = jnp.arange(seg_len, dtype=jnp.int32)
    own_visible = jnp.tile(positions[None, :] <= positions[:, None], (group_heads, 1))

    def leaf_step(operands):
        q_leaf, g_leaf, k_leaf, v_leaf = operands
        q_rows = q_leaf.reshape(seg_len, group_heads, HD).transpose(1, 0, 2).reshape(group_heads * seg_len, HD)
        g_rows = g_leaf.reshape(seg_len, group_heads, HD).transpose(1, 0, 2).reshape(group_heads * seg_len, HD)
        res, dq, dka, dva, dko, dvo = attend_leaf(q_rows, g_rows, key_anc, value_anc, k_leaf, v_leaf, anc_visible, own_visible)
        res = res.reshape(group_heads, seg_len, HD).transpose(1, 0, 2).reshape(seg_len, head_width)
        dq = dq.reshape(group_heads, seg_len, HD).transpose(1, 0, 2).reshape(seg_len, head_width)
        return res, dq, dka, dva, dko, dvo

    res, dq, dka, dva, dko, dvo = lax.map(leaf_step, (q_here, g_here, k_own, v_own))
    anc_partial = jnp.concatenate([jnp.sum(dka, axis=0), jnp.sum(dva, axis=0)], axis=1)

    back = jnp.concatenate([res, dq, dko.astype(jnp.bfloat16), dvo.astype(jnp.bfloat16)], axis=2)
    back = back.reshape(pair_leaves, leaf_count, rows_here, back.shape[2]).transpose(1, 0, 2, 3)
    home = lax.all_to_all(back, "leaf", split_axis=0, concat_axis=0, tiled=True)
    home = home.reshape(kv_heads, pair_count, pair_leaves, rows_here, home.shape[3])

    def to_rows(x):
        width = x.shape[-1]
        return x.transpose(1, 2, 3, 0, 4).reshape(leaf_dev, rows_here, kv_heads * width)

    attention = to_rows(home[..., :head_width])
    query_grad = to_rows(home[..., head_width : 2 * head_width])
    leaf_key_grad = to_rows(home[..., 2 * head_width : 2 * head_width + HD])
    leaf_value_grad = to_rows(home[..., 2 * head_width + HD :])

    anc_back = anc_partial.astype(jnp.bfloat16).reshape(levels, leaf_count, rows_here, 2 * HD).transpose(1, 0, 2, 3)
    anc_home = lax.all_to_all(anc_back, "leaf", split_axis=0, concat_axis=0, tiled=True)
    anc_home = anc_home.astype(jnp.float32).reshape(kv_heads, pair_count, levels, rows_here, 2 * HD).sum(axis=1)
    part_keys = anc_home[..., :HD].transpose(1, 2, 0, 3).reshape(levels, rows_here, key_width)
    part_values = anc_home[..., HD:].transpose(1, 2, 0, 3).reshape(levels, rows_here, key_width)
    part_round = jnp.concatenate([part_keys, part_values], axis=2).astype(jnp.bfloat16)

    seg_ids = jnp.arange(seg_count, dtype=jnp.int32)
    homeward_pick = ((my_owners[None, :] == seg_ids[:, None]) & my_alive[None, :]).astype(jnp.bfloat16)
    homeward = jnp.einsum("ok,krc->orc", homeward_pick, part_round, preferred_element_type=jnp.float32).astype(
        jnp.bfloat16
    )
    returned = lax.all_to_all(homeward, "seg", split_axis=0, concat_axis=0, tiled=True)
    collected = jnp.einsum("gs,grc->src", serve_pick, returned, preferred_element_type=jnp.float32).astype(
        jnp.bfloat16
    )
    return (
        attention,
        query_grad,
        leaf_key_grad,
        leaf_value_grad,
        collected[:, :, :key_width],
        collected[:, :, key_width:],
    )


def solution(mesh):
    spec = P("seg", "leaf", None)
    return jax.shard_map(
        on_device,
        mesh=mesh,
        in_specs=(spec, spec, spec, spec, spec, spec, P(), P()),
        out_specs=(spec, spec, spec, spec, spec, spec),
        check_vma=False,
    )
```

time: 1330 us -> 393 us (0.30)
  waiting for transfers between devices: 948 us -> 126 us
  local copies, waits for them, and re-layouts: 172 us -> 60.1 us
  blocking collectives: 0 us -> 20.1 us
  starting transfers between devices: 9.02 us -> 24.2 us
    reduce_scatter x8 -> x0, waiting for transfers between devices: 583 us -> none  [head_step(): lax.psum_scatter(jnp.concatenate([key_grads, value_grads], axis=2), 'leaf...]
    all_gather x8 -> x0, waiting for transfers between devices: 343 us -> none  [head_step(): whole_rows = lax.all_gather(packed_head, 'leaf', axis=1, tiled=True)]
    all_to_all x0 -> x3, waiting for transfers between devices: none -> 98.3 us  [the longest x1 43.9 us: on_device(): home = lax.all_to_all(back, 'leaf', split_axis=0, concat_axis=0, tiled=True)]
    concatenate x8 -> x0, local copies, waits for them, and re-layouts: 43.7 us -> none  [head_step(): jnp.concatenate([key_grads, value_grads], axis=2)]
    reshape x35 -> x16, local copies, waits for them, and re-layouts: 33.2 us -> 8.25 us  [the longest x4 4.57 us: to_rows(): x.transpose(1, 2, 3, 0, 4).reshape(leaf_dev, rows_here, kv_heads * width)]
    dynamic_slice x24 -> x8, local copies, waits for them, and re-layouts: 27.5 us -> 3.64 us  [on_device(): lax.map(leaf_step, (q_here, g_here, k_own, v_own))]
    all_to_all x0 -> x1, blocking collectives: none -> 20.1 us  [on_device(): lax.all_to_all(anc_back, 'leaf', split_axis=0, concat_axis=0, tiled=True)]
    div x0 -> x2, other arithmetic: none -> 18.9 us  [attend_leaf(): prob_anc = weight_anc / denom_sum]
  transfers between devices with their start and end apart: 18 -> 5, of which waited for: 18 -> 5; matrix products, arithmetic and copies ran while one was open for 6% -> 3% of each run, Pallas kernels for 0% -> 0%
where the time goes in v1:
time: 393 us; the launch traced here: 392 us
  waiting for transfers between devices  126 us (32%)
  matrix products  119 us (30%)
  local copies, waits for them, and re-layouts  60.1 us (15%)
  other arithmetic  41.2 us (10%)
  starting transfers between devices  24.2 us (6%)
  blocking collectives  20.1 us (5%)
    all_to_all x1, waiting for transfers between devices, on_device(): home = lax.all_to_all(back, 'leaf', split_axis=0, concat_axis=0, tiled=True)  43.9 us
    all_to_all x1, waiting for transfers between devices, on_device(): lax.all_to_all(packed, 'leaf', split_axis=0, concat_axis=0, tiled=True)  40.8 us
    dot_general x2, matrix products, attend_leaf(): jnp.einsum('md,ad->ma', grad_rows, value_anc, preferred_element_type=jnp....  24 us
    all_to_all x1, blocking collectives, on_device(): lax.all_to_all(anc_back, 'leaf', split_axis=0, concat_axis=0, tiled=True)  20.1 us
    div x2, other arithmetic, attend_leaf(): prob_anc = weight_anc / denom_sum  18.9 us
    dot_general x2, matrix products, attend_leaf(): jnp.einsum('ma,ad->md', round_anc, value_anc, preferred_element_type=jnp....  17.4 us
    dot_general x2, matrix products, attend_leaf(): jnp.einsum('ma,md->ad', round_anc, grad_rows, preferred_element_type=jnp....  17.3 us
    dot_general x2, matrix products, attend_leaf(): jnp.einsum('ma,md->ad', dscore_anc, query_rows, preferred_element_type=jn...  16 us
  transfers between devices with their start and end apart: 5, of which 5 were waited for; matrix products, arithmetic and copies ran while one was open for 3% of the time, Pallas kernels for 0%

profile of v1, /device:TPU:0, one launch (start us, length us, event | category | flops | bytes accessed | tf_op | source)
XLA Modules:
  0.0 392.1 jit_solution(17369631153189427376)
XLA Ops:
  6.4 4.4 %all-to-all-start.1 = ((bf16[8,32,2048]{2,1,0:T(8,128)(2,1)}), bf16[8,32,2048]{2,1,0:T(8,128)(2,1)S(1)}, u32[]{:S(2)}, u32[]{:S(2)}) async-start(bf16[8,32,2048]{2,1,0:T(8,128)(2,1)} %copy.201), calls=%async_computation.1 | async-start | bytes 2097152 | tf_op jit(solution)/shard_map/all_to_all | solution.py:81
  11.5 15.2 %all-to-all-done.1 = bf16[8,32,2048]{2,1,0:T(8,128)(2,1)S(1)} async-done(((bf16[8,32,2048]{2,1,0:T(8,128)(2,1)}), bf16[8,32,2048]{2,1,0:T(8,128)(2,1)S(1)}, u32[]{:S(2)}, u32[]{:S(2)}) %all-to-all-start.1) | async-done | bytes 1048608 | tf_op jit(solution)/shard_map/all_to_all | solution.py:81
  28.9 8.0 %all-to-all-start.2 = ((bf16[16,4,32,256]{3,2,1,0:T(8,128)(2,1)}), bf16[16,4,32,256]{3,2,1,0:T(8,128)(2,1)S(1)}, u32[]{:S(2)}, u32[]{:S(2)}) async-start(bf16[16,4,32,256]{3,2,1,0:T(8,128)(2,1)} %bitcast.13), calls=%async_computation.2 | async-start | bytes 2097152 | tf_op jit(solution)/shard_map/all_to_all | solution.py:109
  40.7 13.6 %all-to-all-done.2 = bf16[16,4,32,256]{3,2,1,0:T(8,128)(2,1)S(1)} async-done(((bf16[16,4,32,256]{3,2,1,0:T(8,128)(2,1)}), bf16[16,4,32,256]{3,2,1,0:T(8,128)(2,1)S(1)}, u32[]{:S(2)}, u32[]{:S(2)}) %all-to-all-start.2) | async-done | bytes 1048608 | tf_op jit(solution)/shard_map/all_to_all | solution.py:109
  54.3 4.5 %all-to-all-start = ((bf16[16,2,32,1536]{3,2,1,0:T(8,128)(2,1)}), bf16[16,2,32,1536]{3,2,1,0:T(8,128)(2,1)}, u32[]{:S(2)}, u32[]{:S(2)}) async-start(bf16[16,2,32,1536]{3,2,1,0:T(8,128)(2,1)} %pad_maximum_fusion), calls=%async_computation | async-start | bytes 6291456 | tf_op jit(solution)/shard_map/all_to_all | solution.py:96
  59.9 40.8 %all-to-all-done = bf16[16,2,32,1536]{3,2,1,0:T(8,128)(2,1)} async-done(((bf16[16,2,32,1536]{3,2,1,0:T(8,128)(2,1)}), bf16[16,2,32,1536]{3,2,1,0:T(8,128)(2,1)}, u32[]{:S(2)}, u32[]{:S(2)}) %all-to-all-start) | async-done | bytes 3145760 | tf_op jit(solution)/shard_map/all_to_all | solution.py:96
  105.5 180.6 %while.23 = (s32[]{:T(128)}, bf16[2,512,640]{2,1,0:T(8,128)(2,1)}, bf16[2,512,640]{2,1,0:T(8,128)(2,1)}, f32[2,2048,128]{2,1,0:T(8,128)}, f32[2,2048,128]{2,1,0:...) while((s32[]{:T(128)}, bf16[2,512,640]{2,1,0:T(8,128)(2,1)}, ...), condition=%wide.region_7.8_spmd.clone, body=%wide.region_1.7_spmd.clone.sunk | while | flops 10170523648 | bytes 365392704 | solution.py:126
  107.4 3.9 fusion.143
  116.1 6.0 %fusion.145 = f32[2560]{0:T(1024)S(1)} fusion(f32[2560,2048]{0,1:T(8,128)S(1)} %get-tuple-element.439, f32[2560]{0:T(1024)S(1)} %max.10, pred[2048]{0:T(1024)(128)(4,1)S(1)} %bitcast.270), kind=kLoop, calls=%fused_computation.8.clone.1 | loop fusion | flops 20968960 | bytes 20994048 | tf_op jit(solution)/shard_map/while/body/eval_jaxpr/reduce_sum | solution.py:23
  122.8 9.5 %fusion.147 = f32[2560,2048]{0,1:T(8,128)} fusion(f32[2560,2048]{0,1:T(8,128)S(1)} %get-tuple-element.439, f32[2560]{0:T(1024)S(1)} %add.80, f32[2560]{0:T(1024)S(1)} %max.10, pred[2048]{0:T(1024)(128)(4,1)S(1)} %bitcast.271), kind=kLoop, calls=%fused_computation.7.clone.1 | loop fusion | flops 20971520 | bytes 41965568 | tf_op jit(solution)/shard_map/while/body/eval_jaxpr/div | solution.py:24
  133.0 8.7 %fusion.148 = f32[2560,128]{1,0:T(8,128)S(1)} fusion(bf16[2048,128]{1,0:T(8,128)(2,1)S(1)} %get-tuple-element.489, f32[2560,2048]{0,1:T(8,128)} %fusion.147), kind=kOutput, calls=%fused_computation.12.clone.1 | convolution fusion | flops 1347420160 | bytes 22806528 | tf_op jit(solution)/shard_map/while/body/eval_jaxpr/ma,ad->md/dot_general | solution.py:28
  145.2 12.0 %multiply_convert_fusion.4 = bf16[2560,2048]{0,1:T(8,128)(2,1)} fusion(f32[2560,2048]{0,1:T(8,128)} %fusion.147, bf16[2560,128]{1,0:T(8,128)(2,1)S(1)} %bitcast.242, bf16[2048,128]{1,0:T(8,128)(2,1)S(1)} %get-tuple-element.489, f32[2560]{0:T(1024)S(1)} %get-tuple-element.443), kind=kOutput, calls=%fused_computation.3.clone.1 | convolution fusion | flops 1357905920 | bytes 32647168 | tf_op jit(solution)/shard_map/while/body/eval_jaxpr/md,ad->ma/dot_general | solution.py:33
  157.2 5.8 %fusion.150 = f32[2560,128]{1,0:T(8,128)S(1)} fusion(bf16[2560,2048]{0,1:T(8,128)(2,1)} %multiply_convert_fusion.4, bf16[2048,128]{1,0:T(8,128)(2,1)} %copy-done.5), kind=kOutput, calls=%fused_computation.112.clone.1 | convolution fusion | flops 1342177280 | bytes 12320768 | tf_op jit(solution)/shard_map/while/body/eval_jaxpr/ma,ad->md/dot_general | solution.py:38
  163.0 3.8 multiply_convert_fusion.5
  172.6 2.3 constant_dynamic-update-slice_fusion.3
  174.9 8.0 %fusion.152 = f32[2,2048,128]{2,1,0:T(8,128)} fusion(f32[2,2048,128]{2,1,0:T(8,128)} %get-tuple-element.466, s32[]{:T(128)S(6)} %copy.277, bf16[2560,2048]{0,1:T(8,128)(2,1)} %multiply_convert_fusion.4, bf16[2560,128]{1,0:T(8,128)(2,1)S(1)} %bitcast.248), kind=kOutput, calls=%fused_computation.27.clone.1 | convolution fusion | flops 1342439424 | bytes 12189700 | tf_op jit(solution)/shard_map/while/body/eval_jaxpr/ma,md->ad/dot_general | solution.py:41
  182.9 8.6 %fusion.153 = f32[2,2048,128]{2,1,0:T(8,128)S(1)} fusion(f32[2,2048,128]{2,1,0:T(8,128)S(1)} %copy-done.16, s32[]{:T(128)S(6)} %copy.277, bf16[2560,128]{1,0:T(8,128)(2,1)S(1)} %bitcast.244, f32[2560,2048]{0,1:T(8,128)} %fusion.147), kind=kOutput, calls=%fused_computation.24.clone.1 | convolution fusion | flops 1347420160 | bytes 22675460 | tf_op jit(solution)/shard_map/while/body/eval_jaxpr/ma,md->ad/dot_general | solution.py:42
  197.7 3.9 fusion.143
  206.4 6.0 %fusion.145 = f32[2560]{0:T(1024)S(1)} fusion(f32[2560,2048]{0,1:T(8,128)S(1)} %get-tuple-element.439, f32[2560]{0:T(1024)S(1)} %max.10, pred[2048]{0:T(1024)(128)(4,1)S(1)} %bitcast.270), kind=kLoop, calls=%fused_computation.8.clone.1 | loop fusion | flops 20968960 | bytes 20994048 | tf_op jit(solution)/shard_map/while/body/eval_jaxpr/reduce_sum | solution.py:23
  213.2 9.5 %fusion.147 = f32[2560,2048]{0,1:T(8,128)} fusion(f32[2560,2048]{0,1:T(8,128)S(1)} %get-tuple-element.439, f32[2560]{0:T(1024)S(1)} %add.80, f32[2560]{0:T(1024)S(1)} %max.10, pred[2048]{0:T(1024)(128)(4,1)S(1)} %bitcast.271), kind=kLoop, calls=%fused_computation.7.clone.1 | loop fusion | flops 20971520 | bytes 41965568 | tf_op jit(solution)/shard_map/while/body/eval_jaxpr/div | solution.py:24
  223.3 8.7 %fusion.148 = f32[2560,128]{1,0:T(8,128)S(1)} fusion(bf16[2048,128]{1,0:T(8,128)(2,1)S(1)} %get-tuple-element.489, f32[2560,2048]{0,1:T(8,128)} %fusion.147), kind=kOutput, calls=%fused_computation.12.clone.1 | convolution fusion | flops 1347420160 | bytes 22806528 | tf_op jit(solution)/shard_map/while/body/eval_jaxpr/ma,ad->md/dot_general | solution.py:28
  235.5 12.0 %multiply_convert_fusion.4 = bf16[2560,2048]{0,1:T(8,128)(2,1)} fusion(f32[2560,2048]{0,1:T(8,128)} %fusion.147, bf16[2560,128]{1,0:T(8,128)(2,1)S(1)} %bitcast.242, bf16[2048,128]{1,0:T(8,128)(2,1)S(1)} %get-tuple-element.489, f32[2560]{0:T(1024)S(1)} %get-tuple-element.443), kind=kOutput, calls=%fused_computation.3.clone.1 | convolution fusion | flops 1357905920 | bytes 32647168 | tf_op jit(solution)/shard_map/while/body/eval_jaxpr/md,ad->ma/dot_general | solution.py:33
  247.5 5.8 %fusion.150 = f32[2560,128]{1,0:T(8,128)S(1)} fusion(bf16[2560,2048]{0,1:T(8,128)(2,1)} %multiply_convert_fusion.4, bf16[2048,128]{1,0:T(8,128)(2,1)} %copy-done.5), kind=kOutput, calls=%fused_computation.112.clone.1 | convolution fusion | flops 1342177280 | bytes 12320768 | tf_op jit(solution)/shard_map/while/body/eval_jaxpr/ma,ad->md/dot_general | solution.py:38
  253.4 3.8 multiply_convert_fusion.5
  263.0 2.3 constant_dynamic-update-slice_fusion.3
  265.2 8.0 %fusion.152 = f32[2,2048,128]{2,1,0:T(8,128)} fusion(f32[2,2048,128]{2,1,0:T(8,128)} %get-tuple-element.466, s32[]{:T(128)S(6)} %copy.277, bf16[2560,2048]{0,1:T(8,128)(2,1)} %multiply_convert_fusion.4, bf16[2560,128]{1,0:T(8,128)(2,1)S(1)} %bitcast.248), kind=kOutput, calls=%fused_computation.27.clone.1 | convolution fusion | flops 1342439424 | bytes 12189700 | tf_op jit(solution)/shard_map/while/body/eval_jaxpr/ma,md->ad/dot_general | solution.py:41
  273.2 8.6 %fusion.153 = f32[2,2048,128]{2,1,0:T(8,128)S(1)} fusion(f32[2,2048,128]{2,1,0:T(8,128)S(1)} %copy-done.16, s32[]{:T(128)S(6)} %copy.277, bf16[2560,128]{1,0:T(8,128)(2,1)S(1)} %bitcast.244, f32[2560,2048]{0,1:T(8,128)} %fusion.147), kind=kOutput, calls=%fused_computation.24.clone.1 | convolution fusion | flops 1347420160 | bytes 22675460 | tf_op jit(solution)/shard_map/while/body/eval_jaxpr/ma,md->ad/dot_general | solution.py:42
  288.7 20.1 %all_to_all.30 = bf16[16,4,32,256]{3,2,1,0:T(8,128)(2,1)S(1)} all-to-all(bf16[16,4,32,256]{3,2,1,0:T(8,128)(2,1)S(1)} %copy.213), channel_id=1, replica_groups=mesh['seg'=8,'leaf'=16] {'leaf'}, dimensions={0} | all-to-all | bytes 2097152 | tf_op jit(solution)/shard_map/all_to_all | solution.py:144
  311.8 3.6 all-to-all-start.5
  318.8 12.4 %all-to-all-done.5 = bf16[8,32,2048]{2,1,0:T(8,128)(2,1)S(1)} async-done(((bf16[8,32,2048]{2,1,0:T(8,128)(2,1)}), bf16[8,32,2048]{2,1,0:T(8,128)(2,1)S(1)}, u32[]{:S(2)}, u32[]{:S(2)}) %all-to-all-start.5) | async-done | bytes 1048608 | tf_op jit(solution)/shard_map/all_to_all | solution.py:155
  332.2 3.7 all-to-all-start.3
  339.6 43.9 %all-to-all-done.3 = bf16[16,2,32,1536]{3,2,1,0:T(8,128)(2,1)S(1)} async-done(((bf16[16,2,32,1536]{3,2,1,0:T(8,128)(2,1)}), bf16[16,2,32,1536]{3,2,1,0:T(8,128)(2,1)S(1)}, u32[]{:S(2)}, u32[]{:S(2)}) %all-to-all-start.3) | async-done | bytes 3145760 | tf_op jit(solution)/shard_map/all_to_all | solution.py:131
  (233 shorter events, 82.9 us)
Async XLA Ops:
  6.4 20.3 %all-to-all-start.1 = ((bf16[8,32,2048]{2,1,0:T(8,128)(2,1)}), bf16[8,32,2048]{2,1,0:T(8,128)(2,1)S(1)}, u32[]{:S(2)}, u32[]{:S(2)}) async-start(bf16[8,32,2048]{2,1,0:T(8,128)(2,1)} %copy.201), calls=%async_computation.1 | async-start | bytes 2097152 | tf_op jit(solution)/shard_map/all_to_all | solution.py:81
  27.5 9.4 %copy-start.28 = (bf16[4,32,1024]{2,1,0:T(8,128)(2,1)S(1)}, bf16[4,32,1024]{2,1,0:T(8,128)(2,1)}, u32[]{:S(2)}) copy-start(bf16[4,32,1024]{2,1,0:T(8,128)(2,1)} %param.12) | copy-start | bytes 786436
  27.7 9.4 %copy-start.29 = (bf16[4,32,1024]{2,1,0:T(8,128)(2,1)S(1)}, bf16[4,32,1024]{2,1,0:T(8,128)(2,1)}, u32[]{:S(2)}) copy-start(bf16[4,32,1024]{2,1,0:T(8,128)(2,1)} %param.11) | copy-start | bytes 786436
  27.8 9.4 %copy-start.18 = (bf16[4,32,5120]{2,1,0:T(8,128)(2,1)S(1)}, bf16[4,32,5120]{2,1,0:T(8,128)(2,1)}, u32[]{:S(2)}) copy-start(bf16[4,32,5120]{2,1,0:T(8,128)(2,1)} %param.15) | copy-start | bytes 3932164
  28.9 25.4 %all-to-all-start.2 = ((bf16[16,4,32,256]{3,2,1,0:T(8,128)(2,1)}), bf16[16,4,32,256]{3,2,1,0:T(8,128)(2,1)S(1)}, u32[]{:S(2)}, u32[]{:S(2)}) async-start(bf16[16,4,32,256]{3,2,1,0:T(8,128)(2,1)} %bitcast.13), calls=%async_computation.2 | async-start | bytes 2097152 | tf_op jit(solution)/shard_map/all_to_all | solution.py:109
  54.3 46.3 %all-to-all-start = ((bf16[16,2,32,1536]{3,2,1,0:T(8,128)(2,1)}), bf16[16,2,32,1536]{3,2,1,0:T(8,128)(2,1)}, u32[]{:S(2)}, u32[]{:S(2)}) async-start(bf16[16,2,32,1536]{3,2,1,0:T(8,128)(2,1)} %pad_maximum_fusion), calls=%async_computation | async-start | bytes 6291456 | tf_op jit(solution)/shard_map/all_to_all | solution.py:96
  116.0 6.0 %copy-start = (f32[2560,512]{0,1:T(8,128)}, f32[2560,512]{0,1:T(8,128)S(1)}, u32[]{:S(2)}) copy-start(f32[2560,512]{0,1:T(8,128)S(1)} %get-tuple-element.442) | copy-start | bytes 15728644 | tf_op jit(solution)/shard_map/while
  122.8 9.5 %copy-start.12 = (f32[2560]{0:T(1024)}, f32[2560]{0:T(1024)S(1)}, u32[]{:S(2)}) copy-start(f32[2560]{0:T(1024)S(1)} %add.80) | copy-start | bytes 30724 | tf_op jit(solution)/shard_map/while
  122.8 9.5 %copy-start.7 = (bf16[2,512,640]{2,1,0:T(8,128)(2,1)S(1)}, bf16[2,512,640]{2,1,0:T(8,128)(2,1)}, u32[]{:S(2)}) copy-start(bf16[2,512,640]{2,1,0:T(8,128)(2,1)} %get-tuple-element.491) | copy-start | bytes 3932164 | tf_op jit(solution)/shard_map/while
  132.6 9.1 %slice-start = ((s8[5242880]{0:T(1024)(128)(4,1)}), s8[1048576]{0:T(1024)(128)(4,1)S(1)}, s32[]{:S(2)}) async-start(s8[5242880]{0:T(1024)(128)(4,1)} %bitcast.240), calls=%async_computation.6 | async-start | bytes 2097152 | tf_op jit(solution)/shard_map/while
  133.0 8.7 %slice-start.1 = ((s8[5242880]{0:T(1024)(128)(4,1)}), s8[4194304]{0:T(1024)(128)(4,1)S(1)}, s32[]{:S(2)}) async-start(s8[5242880]{0:T(1024)(128)(4,1)} %bitcast.240), calls=%async_computation.7 | async-start | bytes 8388608 | tf_op jit(solution)/shard_map/while
  133.0 8.7 %copy-start.13 = (f32[2560]{0:T(1024)S(1)}, f32[2560]{0:T(1024)}, u32[]{:S(2)}) copy-start(f32[2560]{0:T(1024)} %copy-done.12) | copy-start | bytes 30724 | tf_op jit(solution)/shard_map/while
  157.2 5.8 %copy-start.11 = (bf16[2,512,128]{2,1,0:T(8,128)(2,1)S(1)}, bf16[2,512,128]{2,1,0:T(8,128)(2,1)}, u32[]{:S(2)}) copy-start(bf16[2,512,128]{2,1,0:T(8,128)(2,1)} %get-tuple-element.490) | copy-start | bytes 786436 | tf_op jit(solution)/shard_map/while
  157.2 5.9 %copy-start.14 = (f32[2560]{0:T(1024)S(1)}, f32[2560]{0:T(1024)}, u32[]{:S(2)}) copy-start(f32[2560]{0:T(1024)} %copy-done.12) | copy-start | bytes 30724 | tf_op jit(solution)/shard_map/while
  174.9 8.0 %copy-start.16 = (f32[2,2048,128]{2,1,0:T(8,128)S(1)}, f32[2,2048,128]{2,1,0:T(8,128)}, u32[]{:S(2)}) copy-start(f32[2,2048,128]{2,1,0:T(8,128)} %get-tuple-element.467) | copy-start | bytes 6291460 | tf_op jit(solution)/shard_map/while
  182.9 8.7 %copy-start.4 = (bf16[2560,512]{0,1:T(8,128)(2,1)S(1)}, bf16[2560,512]{0,1:T(8,128)(2,1)}, u32[]{:S(2)}) copy-start(bf16[2560,512]{0,1:T(8,128)(2,1)} %copy-done.3) | copy-start | bytes 7864324 | tf_op jit(solution)/shard_map/while
  182.9 8.7 %copy-start.22 = (bf16[2,512,128]{2,1,0:T(8,128)(2,1)S(1)}, bf16[2,512,128]{2,1,0:T(8,128)(2,1)}, u32[]{:S(2)}) copy-start(bf16[2,512,128]{2,1,0:T(8,128)(2,1)} %get-tuple-element.468) | copy-start | bytes 786436 | tf_op jit(solution)/shard_map/while
  206.4 6.0 %copy-start = (f32[2560,512]{0,1:T(8,128)}, f32[2560,512]{0,1:T(8,128)S(1)}, u32[]{:S(2)}) copy-start(f32[2560,512]{0,1:T(8,128)S(1)} %get-tuple-element.442) | copy-start | bytes 15728644 | tf_op jit(solution)/shard_map/while
  213.1 9.5 %copy-start.12 = (f32[2560]{0:T(1024)}, f32[2560]{0:T(1024)S(1)}, u32[]{:S(2)}) copy-start(f32[2560]{0:T(1024)S(1)} %add.80) | copy-start | bytes 30724 | tf_op jit(solution)/shard_map/while
  213.2 9.5 %copy-start.7 = (bf16[2,512,640]{2,1,0:T(8,128)(2,1)S(1)}, bf16[2,512,640]{2,1,0:T(8,128)(2,1)}, u32[]{:S(2)}) copy-start(bf16[2,512,640]{2,1,0:T(8,128)(2,1)} %get-tuple-element.491) | copy-start | bytes 3932164 | tf_op jit(solution)/shard_map/while
  223.0 9.1 %slice-start = ((s8[5242880]{0:T(1024)(128)(4,1)}), s8[1048576]{0:T(1024)(128)(4,1)S(1)}, s32[]{:S(2)}) async-start(s8[5242880]{0:T(1024)(128)(4,1)} %bitcast.240), calls=%async_computation.6 | async-start | bytes 2097152 | tf_op jit(solution)/shard_map/while
  223.3 8.7 %slice-start.1 = ((s8[5242880]{0:T(1024)(128)(4,1)}), s8[4194304]{0:T(1024)(128)(4,1)S(1)}, s32[]{:S(2)}) async-start(s8[5242880]{0:T(1024)(128)(4,1)} %bitcast.240), calls=%async_computation.7 | async-start | bytes 8388608 | tf_op jit(solution)/shard_map/while
  223.3 8.7 %copy-start.13 = (f32[2560]{0:T(1024)S(1)}, f32[2560]{0:T(1024)}, u32[]{:S(2)}) copy-start(f32[2560]{0:T(1024)} %copy-done.12) | copy-start | bytes 30724 | tf_op jit(solution)/shard_map/while
  247.5 5.8 %copy-start.11 = (bf16[2,512,128]{2,1,0:T(8,128)(2,1)S(1)}, bf16[2,512,128]{2,1,0:T(8,128)(2,1)}, u32[]{:S(2)}) copy-start(bf16[2,512,128]{2,1,0:T(8,128)(2,1)} %get-tuple-element.490) | copy-start | bytes 786436 | tf_op jit(solution)/shard_map/while
  247.5 5.9 %copy-start.14 = (f32[2560]{0:T(1024)S(1)}, f32[2560]{0:T(1024)}, u32[]{:S(2)}) copy-start(f32[2560]{0:T(1024)} %copy-done.12) | copy-start | bytes 30724 | tf_op jit(solution)/shard_map/while
  265.2 8.0 %copy-start.16 = (f32[2,2048,128]{2,1,0:T(8,128)S(1)}, f32[2,2048,128]{2,1,0:T(8,128)}, u32[]{:S(2)}) copy-start(f32[2,2048,128]{2,1,0:T(8,128)} %get-tuple-element.467) | copy-start | bytes 6291460 | tf_op jit(solution)/shard_map/while
  273.2 8.7 %copy-start.4 = (bf16[2560,512]{0,1:T(8,128)(2,1)S(1)}, bf16[2560,512]{0,1:T(8,128)(2,1)}, u32[]{:S(2)}) copy-start(bf16[2560,512]{0,1:T(8,128)(2,1)} %copy-done.3) | copy-start | bytes 7864324 | tf_op jit(solution)/shard_map/while
  273.2 8.7 %copy-start.22 = (bf16[2,512,128]{2,1,0:T(8,128)(2,1)S(1)}, bf16[2,512,128]{2,1,0:T(8,128)(2,1)}, u32[]{:S(2)}) copy-start(bf16[2,512,128]{2,1,0:T(8,128)(2,1)} %get-tuple-element.468) | copy-start | bytes 786436 | tf_op jit(solution)/shard_map/while
  288.7 20.9 %copy-start.33 = (s32[4]{0:T(128)S(1)}, s32[4]{0:T(128)}, u32[]{:S(2)}) copy-start(s32[4]{0:T(128)} %copy-done.32) | copy-start | bytes 52
  311.8 19.5 %all-to-all-start.5 = ((bf16[8,32,2048]{2,1,0:T(8,128)(2,1)}), bf16[8,32,2048]{2,1,0:T(8,128)(2,1)S(1)}, u32[]{:S(2)}, u32[]{:S(2)}) async-start(bf16[8,32,2048]{2,1,0:T(8,128)(2,1)} %copy.218), calls=%async_computation.5 | async-start | bytes 2097152 | tf_op jit(solution)/shard_map/all_to_all | solution.py:155
  318.8 17.2 %copy-start.31 = (bf16[8,2]{0,1:T(2,128)(2,1)S(1)}, bf16[8,2]{0,1:T(2,128)(2,1)}, u32[]{:S(2)}) copy-start(bf16[8,2]{0,1:T(2,128)(2,1)} %copy-done.30) | copy-start | bytes 100
  332.2 51.3 %all-to-all-start.3 = ((bf16[16,2,32,1536]{3,2,1,0:T(8,128)(2,1)}), bf16[16,2,32,1536]{3,2,1,0:T(8,128)(2,1)S(1)}, u32[]{:S(2)}, u32[]{:S(2)}) async-start(bf16[16,2,32,1536]{3,2,1,0:T(8,128)(2,1)} %copy.208), calls=%async_computation.3 | async-start | bytes 6291456 | tf_op jit(solution)/shard_map/all_to_all | solution.py:131
  (30 other events, 82.5 us)

commit v2 on v1

--- a/solution.py
+++ b/solution.py
@@ -3,6 +3,8 @@
 import jax
 import jax.numpy as jnp
 from jax import lax
+from jax.experimental import pallas as pl
+from jax.experimental.pallas import tpu as pltpu
 from jax.sharding import PartitionSpec as P
 
 HD = 128
@@ -11,38 +13,100 @@
 NEG_FILL = -1e30
 
 
-def attend_leaf(query_rows, grad_rows, key_anc, value_anc, own_keys, own_values, anc_visible, own_visible):
-    logit_scale = 1.0 / math.sqrt(query_rows.shape[-1])
-    score_anc = jnp.einsum("md,ad->ma", query_rows, key_anc, preferred_element_type=jnp.float32) * logit_scale
-    score_own = jnp.einsum("md,sd->ms", query_rows, own_keys, preferred_element_type=jnp.float32) * logit_scale
-    score_anc = jnp.where(anc_visible[None, :], score_anc, NEG_FILL)
-    score_own = jnp.where(own_visible, score_own, NEG_FILL)
-    highest = jnp.maximum(jnp.max(score_anc, axis=-1, keepdims=True), jnp.max(score_own, axis=-1, keepdims=True))
-    weight_anc = jnp.exp(score_anc - highest)
-    weight_own = jnp.exp(score_own - highest)
-    denom_sum = jnp.sum(weight_anc, axis=-1, keepdims=True) + jnp.sum(weight_own, axis=-1, keepdims=True)
-    prob_anc = weight_anc / denom_sum
-    prob_own = weight_own / denom_sum
-    round_anc = prob_anc.astype(jnp.bfloat16)
-    round_own = prob_own.astype(jnp.bfloat16)
-    result = jnp.einsum("ma,ad->md", round_anc, value_anc, preferred_element_type=jnp.float32) + jnp.einsum(
-        "ms,sd->md", round_own, own_values, preferred_element_type=jnp.float32
-    )
-    result_round = result.astype(jnp.bfloat16)
-    delta_rows = jnp.sum(grad_rows.astype(jnp.float32) * result_round.astype(jnp.float32), axis=-1, keepdims=True)
-    dprob_anc = jnp.einsum("md,ad->ma", grad_rows, value_anc, preferred_element_type=jnp.float32)
-    dprob_own = jnp.einsum("md,sd->ms", grad_rows, own_values, preferred_element_type=jnp.float32)
-    dscore_anc = (prob_anc * (dprob_anc - delta_rows)).astype(jnp.bfloat16)
-    dscore_own = (prob_own * (dprob_own - delta_rows)).astype(jnp.bfloat16)
-    query_portion = (
-        jnp.einsum("ma,ad->md", dscore_anc, key_anc, preferred_element_type=jnp.float32)
-        + jnp.einsum("ms,sd->md", dscore_own, own_keys, preferred_element_type=jnp.float32)
-    ) * logit_scale
-    dkey_anc = jnp.einsum("ma,md->ad", dscore_anc, query_rows, preferred_element_type=jnp.float32) * logit_scale
-    dvalue_anc = jnp.einsum("ma,md->ad", round_anc, grad_rows, preferred_element_type=jnp.float32)
-    dkey_own = jnp.einsum("ms,md->sd", dscore_own, query_rows, preferred_element_type=jnp.float32) * logit_scale
-    dvalue_own = jnp.einsum("ms,md->sd", round_own, grad_rows, preferred_element_type=jnp.float32)
-    return result_round, query_portion.astype(jnp.bfloat16), dkey_anc, dvalue_anc, dkey_own, dvalue_own
+def attend_kernel(mask_ref, q_ref, g_ref, ko_ref, vo_ref, ka_ref, va_ref,
+                  o_ref, dq_ref, dko_ref, dvo_ref, dka_ref, dva_ref, dko_acc, dvo_acc):
+    leaf_i = pl.program_id(0)
+    head_i = pl.program_id(1)
+    row_i = pl.program_id(2)
+    head_count = pl.num_programs(1)
+    row_count = pl.num_programs(2)
+    block_rows = q_ref.shape[0]
+    seg_len = ko_ref.shape[0]
+    scale = 1.0 / math.sqrt(q_ref.shape[-1])
+
+    @pl.when((leaf_i == 0) & (head_i == 0) & (row_i == 0))
+    def _():
+        dka_ref[...] = jnp.zeros_like(dka_ref)
+        dva_ref[...] = jnp.zeros_like(dva_ref)
+
+    @pl.when((head_i == 0) & (row_i == 0))
+    def _():
+        dko_acc[...] = jnp.zeros_like(dko_acc)
+        dvo_acc[...] = jnp.zeros_like(dvo_acc)
+
+    nt = (((1,), (1,)), ((), ()))
+    tn = (((0,), (0,)), ((), ()))
+    q = q_ref[...]
+    g = g_ref[...]
+    ka = ka_ref[...]
+    va = va_ref[...]
+    ko = ko_ref[...]
+    vo = vo_ref[...]
+    s_a = lax.dot_general(q, ka, nt, preferred_element_type=jnp.float32) * scale
+    s_o = lax.dot_general(q, ko, nt, preferred_element_type=jnp.float32) * scale
+    s_a = jnp.where(mask_ref[...] > 0.5, s_a, NEG_FILL)
+    rows = row_i * block_rows + lax.broadcasted_iota(jnp.int32, (block_rows, seg_len), 0)
+    cols = lax.broadcasted_iota(jnp.int32, (block_rows, seg_len), 1)
+    s_o = jnp.where(cols <= rows, s_o, NEG_FILL)
+    m = jnp.maximum(jnp.max(s_a, axis=1, keepdims=True), jnp.max(s_o, axis=1, keepdims=True))
+    w_a = jnp.exp(s_a - m)
+    w_o = jnp.exp(s_o - m)
+    total = jnp.sum(w_a, axis=1, keepdims=True) + jnp.sum(w_o, axis=1, keepdims=True)
+    inv = 1.0 / total
+    p_a = w_a * inv
+    p_o = w_o * inv
+    pb_a = p_a.astype(jnp.bfloat16)
+    pb_o = p_o.astype(jnp.bfloat16)
+    o = jnp.dot(pb_a, va, preferred_element_type=jnp.float32) + jnp.dot(pb_o, vo, preferred_element_type=jnp.float32)
+    o_b = o.astype(jnp.bfloat16)
+    o_ref[...] = o_b
+    delta = jnp.sum(g.astype(jnp.float32) * o_b.astype(jnp.float32), axis=1, keepdims=True)
+    dp_a = lax.dot_general(g, va, nt, preferred_element_type=jnp.float32)
+    dp_o = lax.dot_general(g, vo, nt, preferred_element_type=jnp.float32)
+    ds_a = (p_a * (dp_a - delta)).astype(jnp.bfloat16)
+    ds_o = (p_o * (dp_o - delta)).astype(jnp.bfloat16)
+    dq = (jnp.dot(ds_a, ka, preferred_element_type=jnp.float32) + jnp.dot(ds_o, ko, preferred_element_type=jnp.float32)) * scale
+    dq_ref[...] = dq.astype(jnp.bfloat16)
+    dka_ref[...] += lax.dot_general(ds_a, q, tn, preferred_element_type=jnp.float32)
+    dva_ref[...] += lax.dot_general(pb_a, g, tn, preferred_element_type=jnp.float32)
+    dko_acc[...] += lax.dot_general(ds_o, q, tn, preferred_element_type=jnp.float32)
+    dvo_acc[...] += lax.dot_general(pb_o, g, tn, preferred_element_type=jnp.float32)
+
+    @pl.when((head_i == head_count - 1) & (row_i == row_count - 1))
+    def _():
+        dko_ref[...] = dko_acc[...] * scale
+        dvo_ref[...] = dvo_acc[...]
+
+    @pl.when((leaf_i == pl.num_programs(0) - 1) & (head_i == head_count - 1) & (row_i == row_count - 1))
+    def _():
+        dka_ref[...] = dka_ref[...] * scale
+
+
+def attend_all(anc_mask, packed, anc_rows, heads, block_rows=256):
+    leaves, seg_len, _ = packed.shape
+    anc = anc_rows.shape[0]
+    grid = (leaves, heads, seg_len // block_rows)
+    qspec = pl.BlockSpec((None, block_rows, HD), lambda l, h, r: (l, r, h))
+    gspec = pl.BlockSpec((None, block_rows, HD), lambda l, h, r: (l, r, heads + h))
+    kospec = pl.BlockSpec((None, seg_len, HD), lambda l, h, r: (l, 0, 2 * heads))
+    vospec = pl.BlockSpec((None, seg_len, HD), lambda l, h, r: (l, 0, 2 * heads + 1))
+    kaspec = pl.BlockSpec((anc, HD), lambda l, h, r: (0, 0))
+    vaspec = pl.BlockSpec((anc, HD), lambda l, h, r: (0, 1))
+    maskspec = pl.BlockSpec((1, anc), lambda l, h, r: (0, 0))
+    ownspec = pl.BlockSpec((None, seg_len, HD), lambda l, h, r: (l, 0, 0))
+    ancspec = pl.BlockSpec((anc, HD), lambda l, h, r: (0, 0))
+    out_rows = jax.ShapeDtypeStruct((leaves, seg_len, heads * HD), jnp.bfloat16)
+    own_grad = jax.ShapeDtypeStruct((leaves, seg_len, HD), jnp.float32)
+    anc_grad = jax.ShapeDtypeStruct((anc, HD), jnp.float32)
+    return pl.pallas_call(
+        attend_kernel,
+        grid=grid,
+        in_specs=[maskspec, qspec, gspec, kospec, vospec, kaspec, vaspec],
+        out_specs=[qspec, qspec, ownspec, ownspec, ancspec, ancspec],
+        out_shape=[out_rows, out_rows, own_grad, own_grad, anc_grad, anc_grad],
+        scratch_shapes=[pltpu.VMEM((seg_len, HD), jnp.float32), pltpu.VMEM((seg_len, HD), jnp.float32)],
+        compiler_params=pltpu.CompilerParams(dimension_semantics=("arbitrary", "arbitrary", "arbitrary")),
+    )(anc_mask, packed, packed, packed, packed, anc_rows, anc_rows)
 
 
 def on_device(queries, leaf_keys, leaf_values, inner_keys, inner_values, out_grad, ancestors, depths):
@@ -95,10 +159,6 @@
     )
     got = lax.all_to_all(packed, "leaf", split_axis=0, concat_axis=0, tiled=True)
     got = got.transpose(1, 0, 2, 3).reshape(pair_leaves, seg_len, packed.shape[3])
-    q_here = got[:, :, :head_width]
-    g_here = got[:, :, head_width : 2 * head_width]
-    k_own = got[:, :, 2 * head_width : 2 * head_width + HD]
-    v_own = got[:, :, 2 * head_width + HD :]
 
     anc_k = ancestor_rows[:, :, :key_width].reshape(levels, rows_here, kv_heads, HD)
     anc_v = ancestor_rows[:, :, key_width:].reshape(levels, rows_here, kv_heads, HD)
@@ -108,23 +168,10 @@
     )
     anc_got = lax.all_to_all(anc_send, "leaf", split_axis=0, concat_axis=0, tiled=True)
     anc_got = anc_got.transpose(1, 0, 2, 3).reshape(levels * seg_len, 2 * HD)
-    key_anc = anc_got[:, :HD]
-    value_anc = anc_got[:, HD:]
-    anc_visible = jnp.repeat(my_alive, seg_len)
-    positions = jnp.arange(seg_len, dtype=jnp.int32)
-    own_visible = jnp.tile(positions[None, :] <= positions[:, None], (group_heads, 1))
-
-    def leaf_step(operands):
-        q_leaf, g_leaf, k_leaf, v_leaf = operands
-        q_rows = q_leaf.reshape(seg_len, group_heads, HD).transpose(1, 0, 2).reshape(group_heads * seg_len, HD)
-        g_rows = g_leaf.reshape(seg_len, group_heads, HD).transpose(1, 0, 2).reshape(group_heads * seg_len, HD)
-        res, dq, dka, dva, dko, dvo = attend_leaf(q_rows, g_rows, key_anc, value_anc, k_leaf, v_leaf, anc_visible, own_visible)
-        res = res.reshape(group_heads, seg_len, HD).transpose(1, 0, 2).reshape(seg_len, head_width)
-        dq = dq.reshape(group_heads, seg_len, HD).transpose(1, 0, 2).reshape(seg_len, head_width)
-        return res, dq, dka, dva, dko, dvo
-
-    res, dq, dka, dva, dko, dvo = lax.map(leaf_step, (q_here, g_here, k_own, v_own))
-    anc_partial = jnp.concatenate([jnp.sum(dka, axis=0), jnp.sum(dva, axis=0)], axis=1)
+    anc_mask = jnp.repeat(my_alive, seg_len).astype(jnp.float32)[None, :]
+
+    res, dq, dko, dvo, dka, dva = attend_all(anc_mask, got, anc_got, group_heads)
+    anc_partial = jnp.concatenate([dka, dva], axis=1)
 
     back = jnp.concatenate([res, dq, dko.astype(jnp.bfloat16), dvo.astype(jnp.bfloat16)], axis=2)
     back = back.reshape(pair_leaves, leaf_count, rows_here, back.shape[2]).transpose(1, 0, 2, 3)

time: 393 us -> 277 us (0.70)
  matrix products: 119 us -> 3.14 us
  Pallas kernels: 0 us -> 65.5 us
  other arithmetic: 41.2 us -> 6.96 us
  local copies, waits for them, and re-layouts: 60.1 us -> 30 us
    dot_general x24 -> x0, matrix products: 116 us -> none  [the longest x2 24 us: attend_leaf(): jnp.einsum('md,ad->ma', grad_rows, value_anc, preferred_element_type=jnp....]
    pallas_call x0 -> x1, Pallas kernels: none -> 65.5 us  [attend_all(): pl.pallas_call(attend_kernel, grid=grid, in_specs=[maskspec, qspec, gspec...]
    div x2 -> x0, other arithmetic: 18.9 us -> none  [attend_leaf(): prob_anc = weight_anc / denom_sum]
    reduce_sum x6 -> x0, other arithmetic: 15.5 us -> none  [the longest x2 11.9 us: attend_leaf(): jnp.sum(weight_anc, axis=-1, keepdims=True)]
    dynamic_update_slice x6 -> x0, local copies, waits for them, and re-layouts: 9.42 us -> none  [on_device(): lax.map(leaf_step, (q_here, g_here, k_own, v_own))]
    while x88 -> x0, local copies, waits for them, and re-layouts: 7.87 us -> none
    another operation x4 -> x0, local copies, waits for them, and re-layouts: 5.43 us -> none  [on_device(): jnp.tile(positions[None, :] <= positions[:, None], (group_heads, 1))]
  transfers between devices with their start and end apart: 5 -> 5, of which waited for: 5 -> 5; matrix products, arithmetic and copies ran while one was open for 3% -> 5% of each run, Pallas kernels for 0% -> 0%
where the time goes in v2:
time: 277 us; the launch traced here: 276 us
  waiting for transfers between devices  126 us (45%)
  Pallas kernels  65.5 us (24%)
  local copies, waits for them, and re-layouts  30 us (11%)
  starting transfers between devices  23.7 us (9%)
  blocking collectives  19.9 us (7%)
  other arithmetic  6.96 us (3%)
  matrix products  3.14 us (1%)
    pallas_call x1, Pallas kernels, attend_all(): pl.pallas_call(attend_kernel, grid=grid, in_specs=[maskspec, qspec, gspec...  65.5 us
    all_to_all x1, waiting for transfers between devices, on_device(): home = lax.all_to_all(back, 'leaf', split_axis=0, concat_axis=0, tiled=True)  43.8 us
    all_to_all x1, waiting for transfers between devices, on_device(): lax.all_to_all(packed, 'leaf', split_axis=0, concat_axis=0, tiled=True)  40.3 us
    all_to_all x1, blocking collectives, on_device(): lax.all_to_all(anc_back, 'leaf', split_axis=0, concat_axis=0, tiled=True)  19.9 us
    all_to_all x1, waiting for transfers between devices, on_device(): lax.all_to_all(outgoing, 'seg', split_axis=0, concat_axis=0, tiled=True)  15.5 us
    all_to_all x1, waiting for transfers between devices, on_device(): lax.all_to_all(anc_send, 'leaf', split_axis=0, concat_axis=0, tiled=True)  13.6 us
    all_to_all x1, waiting for transfers between devices, on_device(): lax.all_to_all(homeward, 'seg', split_axis=0, concat_axis=0, tiled=True)  12.3 us
    all_to_all x1, starting transfers between devices, on_device(): lax.all_to_all(anc_send, 'leaf', split_axis=0, concat_axis=0, tiled=True)  8.05 us
  transfers between devices with their start and end apart: 5, of which 5 were waited for; matrix products, arithmetic and copies ran while one was open for 5% of the time, Pallas kernels for 0%

profile of v2, /device:TPU:0, one launch (start us, length us, event | category | flops | bytes accessed | tf_op | source)
XLA Modules:
  0.0 275.7 jit_solution(12484219947223983463)
XLA Ops:
  2.2 1.0 copy.78
  3.2 1.0 copy.79
  4.8 1.5 copy.80
  6.4 4.4 %all-to-all-start.1 = ((bf16[8,32,2048]{2,1,0:T(8,128)(2,1)}), bf16[8,32,2048]{2,1,0:T(8,128)(2,1)S(1)}, u32[]{:S(2)}, u32[]{:S(2)}) async-start(bf16[8,32,2048]{2,1,0:T(8,128)(2,1)} %copy.80), calls=%async_computation.1 | async-start | bytes 2097152 | tf_op jit(solution)/shard_map/all_to_all | solution.py:145
  11.2 15.5 %all-to-all-done.1 = bf16[8,32,2048]{2,1,0:T(8,128)(2,1)S(1)} async-done(((bf16[8,32,2048]{2,1,0:T(8,128)(2,1)}), bf16[8,32,2048]{2,1,0:T(8,128)(2,1)S(1)}, u32[]{:S(2)}, u32[]{:S(2)}) %all-to-all-start.1) | async-done | bytes 1048608 | tf_op jit(solution)/shard_map/all_to_all | solution.py:145
  27.8 1.1 broadcast_in_dim.60
  28.9 8.0 %all-to-all-start.2 = ((bf16[16,4,32,256]{3,2,1,0:T(8,128)(2,1)}), bf16[16,4,32,256]{3,2,1,0:T(8,128)(2,1)S(1)}, u32[]{:S(2)}, u32[]{:S(2)}) async-start(bf16[16,4,32,256]{3,2,1,0:T(8,128)(2,1)} %bitcast.13), calls=%async_computation.2 | async-start | bytes 2097152 | tf_op jit(solution)/shard_map/all_to_all | solution.py:169
  38.8 1.9 pad_maximum_fusion
  40.7 13.6 %all-to-all-done.2 = bf16[16,4,32,256]{3,2,1,0:T(8,128)(2,1)S(1)} async-done(((bf16[16,4,32,256]{3,2,1,0:T(8,128)(2,1)}), bf16[16,4,32,256]{3,2,1,0:T(8,128)(2,1)S(1)}, u32[]{:S(2)}, u32[]{:S(2)}) %all-to-all-start.2) | async-done | bytes 1048608 | tf_op jit(solution)/shard_map/all_to_all | solution.py:169
  54.3 1.0 copy-done.1
  55.3 3.7 %all-to-all-start = ((bf16[16,2,32,1536]{3,2,1,0:T(8,128)(2,1)}), bf16[16,2,32,1536]{3,2,1,0:T(8,128)(2,1)S(1)}, u32[]{:S(2)}, u32[]{:S(2)}) async-start(bf16[16,2,32,1536]{3,2,1,0:T(8,128)(2,1)} %pad_maximum_fusion), calls=%async_computation | async-start | bytes 6291456 | tf_op jit(solution)/shard_map/all_to_all | solution.py:160
  59.8 2.3 copy.82
  62.1 40.3 %all-to-all-done = bf16[16,2,32,1536]{3,2,1,0:T(8,128)(2,1)S(1)} async-done(((bf16[16,2,32,1536]{3,2,1,0:T(8,128)(2,1)}), bf16[16,2,32,1536]{3,2,1,0:T(8,128)(2,1)S(1)}, u32[]{:S(2)}, u32[]{:S(2)}) %all-to-all-start) | async-done | bytes 3145760 | tf_op jit(solution)/shard_map/all_to_all | solution.py:160
  102.4 1.9 copy.77
  104.3 65.5 %shard_map.127 = (bf16[2,512,640]{2,1,0:T(8,128)(2,1)}, bf16[2,512,640]{2,1,0:T(8,128)(2,1)}, f32[2,512,128]{2,1,0:T(8,128)}, f32[2,512,128]{2,1,0:T(8,128)}, f32[2048,128]{1,0:T(8,128)}, /*index=5*/f32[2048,128]{1,0:T(8,128)}) custom-call(f32[1,2048]{1,0:T(1,128)} %bitcast.130, bf16[2,512,1536]{2,1,0:T(8,128)(2,1)} %bitcast.100, ...), custom_call_target="tpu_custom_call" | custom-call | tf_op jit(solution)/shard_map/pallas_call | solution.py:101
  169.8 1.3 convert.19
  171.1 1.3 convert.20
  172.5 19.9 %all_to_all.30 = bf16[16,4,32,256]{3,2,1,0:T(8,128)(2,1)S(1)} all-to-all(bf16[16,4,32,256]{3,2,1,0:T(8,128)(2,1)S(1)} %copy_bitcast_fusion.1), channel_id=1, replica_groups=mesh['seg'=8,'leaf'=16] {'leaf'}, dimensions={0} | all-to-all | bytes 2097152 | tf_op jit(solution)/shard_map/all_to_all | solution.py:191
  193.8 1.6 copy.95
  195.4 3.6 %all-to-all-start.5 = ((bf16[8,32,2048]{2,1,0:T(8,128)(2,1)}), bf16[8,32,2048]{2,1,0:T(8,128)(2,1)S(1)}, u32[]{:S(2)}, u32[]{:S(2)}) async-start(bf16[8,32,2048]{2,1,0:T(8,128)(2,1)} %copy.95), calls=%async_computation.5 | async-start | bytes 2097152 | tf_op jit(solution)/shard_map/all_to_all | solution.py:202
  199.1 1.5 pad_maximum_fusion.1
  200.6 2.0 copy.120
  202.6 12.3 %all-to-all-done.5 = bf16[8,32,2048]{2,1,0:T(8,128)(2,1)S(1)} async-done(((bf16[8,32,2048]{2,1,0:T(8,128)(2,1)}), bf16[8,32,2048]{2,1,0:T(8,128)(2,1)S(1)}, u32[]{:S(2)}, u32[]{:S(2)}) %all-to-all-start.5) | async-done | bytes 1048608 | tf_op jit(solution)/shard_map/all_to_all | solution.py:202
  214.9 1.0 copy-done.2
  215.8 3.9 %all-to-all-start.3 = ((bf16[16,2,32,1536]{3,2,1,0:T(8,128)(2,1)}), bf16[16,2,32,1536]{3,2,1,0:T(8,128)(2,1)S(1)}, u32[]{:S(2)}, u32[]{:S(2)}) async-start(bf16[16,2,32,1536]{3,2,1,0:T(8,128)(2,1)} %bitcast.106), calls=%async_computation.3 | async-start | bytes 6291456 | tf_op jit(solution)/shard_map/all_to_all | solution.py:178
  219.8 2.1 convolution_convert_fusion.2
  223.4 43.8 %all-to-all-done.3 = bf16[16,2,32,1536]{3,2,1,0:T(8,128)(2,1)S(1)} async-done(((bf16[16,2,32,1536]{3,2,1,0:T(8,128)(2,1)}), bf16[16,2,32,1536]{3,2,1,0:T(8,128)(2,1)S(1)}, u32[]{:S(2)}, u32[]{:S(2)}) %all-to-all-start.3) | async-done | bytes 3145760 | tf_op jit(solution)/shard_map/all_to_all | solution.py:178
  267.1 0.8 slice_bitcast_fusion.4
  268.0 1.3 slice_bitcast_fusion
  270.1 1.5 reshape.154
  271.7 0.8 reshape.156
  274.3 1.5 reshape.153
  (67 shorter events, 11.8 us)
Async XLA Ops:
  6.4 20.3 %all-to-all-start.1 = ((bf16[8,32,2048]{2,1,0:T(8,128)(2,1)}), bf16[8,32,2048]{2,1,0:T(8,128)(2,1)S(1)}, u32[]{:S(2)}, u32[]{:S(2)}) async-start(bf16[8,32,2048]{2,1,0:T(8,128)(2,1)} %copy.80), calls=%async_computation.1 | async-start | bytes 2097152 | tf_op jit(solution)/shard_map/all_to_all | solution.py:145
  27.5 9.4 %copy-start.9 = (bf16[4,32,1024]{2,1,0:T(8,128)(2,1)S(1)}, bf16[4,32,1024]{2,1,0:T(8,128)(2,1)}, u32[]{:S(2)}) copy-start(bf16[4,32,1024]{2,1,0:T(8,128)(2,1)} %param.9) | copy-start | bytes 786436
  27.7 9.4 %copy-start.10 = (bf16[4,32,1024]{2,1,0:T(8,128)(2,1)S(1)}, bf16[4,32,1024]{2,1,0:T(8,128)(2,1)}, u32[]{:S(2)}) copy-start(bf16[4,32,1024]{2,1,0:T(8,128)(2,1)} %param.10) | copy-start | bytes 786436
  27.8 9.4 %copy-start.3 = (bf16[4,32,5120]{2,1,0:T(8,128)(2,1)S(1)}, bf16[4,32,5120]{2,1,0:T(8,128)(2,1)}, u32[]{:S(2)}) copy-start(bf16[4,32,5120]{2,1,0:T(8,128)(2,1)} %param.8) | copy-start | bytes 3932164
  28.9 25.4 %all-to-all-start.2 = ((bf16[16,4,32,256]{3,2,1,0:T(8,128)(2,1)}), bf16[16,4,32,256]{3,2,1,0:T(8,128)(2,1)S(1)}, u32[]{:S(2)}, u32[]{:S(2)}) async-start(bf16[16,4,32,256]{3,2,1,0:T(8,128)(2,1)} %bitcast.13), calls=%async_computation.2 | async-start | bytes 2097152 | tf_op jit(solution)/shard_map/all_to_all | solution.py:169
  37.1 1.3 copy-start.4
  54.3 1.0 copy-start.1
  55.3 47.1 %all-to-all-start = ((bf16[16,2,32,1536]{3,2,1,0:T(8,128)(2,1)}), bf16[16,2,32,1536]{3,2,1,0:T(8,128)(2,1)S(1)}, u32[]{:S(2)}, u32[]{:S(2)}) async-start(bf16[16,2,32,1536]{3,2,1,0:T(8,128)(2,1)} %pad_maximum_fusion), calls=%async_computation | async-start | bytes 6291456 | tf_op jit(solution)/shard_map/all_to_all | solution.py:160
  193.1 5.8 %copy-start.8 = (f32[2,512,128]{2,1,0:T(8,128)S(1)}, f32[2,512,128]{2,1,0:T(8,128)}, u32[]{:S(2)}) copy-start(f32[2,512,128]{2,1,0:T(8,128)} %get-tuple-element.14) | copy-start | bytes 1572868
  193.2 5.8 %copy-start.7 = (f32[2,512,128]{2,1,0:T(8,128)S(1)}, f32[2,512,128]{2,1,0:T(8,128)}, u32[]{:S(2)}) copy-start(f32[2,512,128]{2,1,0:T(8,128)} %get-tuple-element.15) | copy-start | bytes 1572868
  193.8 5.3 %copy-start.5 = (bf16[2,512,640]{2,1,0:T(8,128)(2,1)S(1)}, bf16[2,512,640]{2,1,0:T(8,128)(2,1)}, u32[]{:S(2)}) copy-start(bf16[2,512,640]{2,1,0:T(8,128)(2,1)} %get-tuple-element.12) | copy-start | bytes 3932164
  195.4 19.4 %all-to-all-start.5 = ((bf16[8,32,2048]{2,1,0:T(8,128)(2,1)}), bf16[8,32,2048]{2,1,0:T(8,128)(2,1)S(1)}, u32[]{:S(2)}, u32[]{:S(2)}) async-start(bf16[8,32,2048]{2,1,0:T(8,128)(2,1)} %copy.95), calls=%async_computation.5 | async-start | bytes 2097152 | tf_op jit(solution)/shard_map/all_to_all | solution.py:202
  214.9 1.0 copy-start.2
  215.8 51.3 %all-to-all-start.3 = ((bf16[16,2,32,1536]{3,2,1,0:T(8,128)(2,1)}), bf16[16,2,32,1536]{3,2,1,0:T(8,128)(2,1)S(1)}, u32[]{:S(2)}, u32[]{:S(2)}) async-start(bf16[16,2,32,1536]{3,2,1,0:T(8,128)(2,1)} %bitcast.106), calls=%async_computation.3 | async-start | bytes 6291456 | tf_op jit(solution)/shard_map/all_to_all | solution.py:178
  269.3 2.2 copy-start.6
  269.3 4.2 %copy-start = (bf16[2,2,32,8,640]{4,2,1,0,3:T(8,128)(2,1)S(1)}, bf16[2,2,32,8,640]{4,2,1,0,3:T(8,128)(2,1)}, u32[]{:S(2)}) copy-start(bf16[2,2,32,8,640]{4,2,1,0,3:T(8,128)(2,1)} %get-tuple-element.69) | copy-start | bytes 3932164

commit v3 on v2

--- a/solution.py
+++ b/solution.py
@@ -157,9 +157,6 @@
         [to_heads(queries, head_width), to_heads(out_grad, head_width), to_heads(leaf_keys, HD), to_heads(leaf_values, HD)],
         axis=3,
     )
-    got = lax.all_to_all(packed, "leaf", split_axis=0, concat_axis=0, tiled=True)
-    got = got.transpose(1, 0, 2, 3).reshape(pair_leaves, seg_len, packed.shape[3])
-
     anc_k = ancestor_rows[:, :, :key_width].reshape(levels, rows_here, kv_heads, HD)
     anc_v = ancestor_rows[:, :, key_width:].reshape(levels, rows_here, kv_heads, HD)
     anc_heads = jnp.concatenate([anc_k, anc_v], axis=3).transpose(2, 0, 1, 3)
@@ -170,12 +167,18 @@
     anc_got = anc_got.transpose(1, 0, 2, 3).reshape(levels * seg_len, 2 * HD)
     anc_mask = jnp.repeat(my_alive, seg_len).astype(jnp.float32)[None, :]
 
-    res, dq, dko, dvo, dka, dva = attend_all(anc_mask, got, anc_got, group_heads)
-    anc_partial = jnp.concatenate([dka, dva], axis=1)
-
-    back = jnp.concatenate([res, dq, dko.astype(jnp.bfloat16), dvo.astype(jnp.bfloat16)], axis=2)
-    back = back.reshape(pair_leaves, leaf_count, rows_here, back.shape[2]).transpose(1, 0, 2, 3)
-    home = lax.all_to_all(back, "leaf", split_axis=0, concat_axis=0, tiled=True)
+    homes = []
+    anc_partial = None
+    for chunk in range(pair_leaves):
+        got = lax.all_to_all(packed[:, chunk], "leaf", split_axis=0, concat_axis=0, tiled=True)
+        got = got.reshape(1, seg_len, packed.shape[3])
+        res, dq, dko, dvo, dka, dva = attend_all(anc_mask, got, anc_got, group_heads)
+        part = jnp.concatenate([dka, dva], axis=1)
+        anc_partial = part if anc_partial is None else anc_partial + part
+        back = jnp.concatenate([res, dq, dko.astype(jnp.bfloat16), dvo.astype(jnp.bfloat16)], axis=2)
+        back = back.reshape(leaf_count, rows_here, back.shape[2])
+        homes.append(lax.all_to_all(back, "leaf", split_axis=0, concat_axis=0, tiled=True))
+    home = jnp.stack(homes, axis=1)
     home = home.reshape(kv_heads, pair_count, pair_leaves, rows_here, home.shape[3])
 
     def to_rows(x):

time: 277 us -> 257 us (0.928)
  waiting for transfers between devices: 126 us -> 85.6 us
  starting transfers between devices: 23.7 us -> 36.2 us
    all_to_all x3 -> x5, waiting for transfers between devices: 97.7 us -> 72.1 us  [the longest x2 35.1 us: on_device(): lax.all_to_all(back, 'leaf', split_axis=0, concat_axis=0, tiled=True)]
    all_to_all x3 -> x5, starting transfers between devices: 15.7 us -> 27.2 us  [the longest x2 11.9 us: on_device(): lax.all_to_all(packed[:, chunk], 'leaf', split_axis=0, concat_axis=0, til...]
    all_to_all x1, waiting for transfers between devices: 12.3 us -> 1.89 us  [on_device(): lax.all_to_all(homeward, 'seg', split_axis=0, concat_axis=0, tiled=True)]
    reshape x4, local copies, waits for them, and re-layouts: 4.57 us -> 8.97 us  [to_rows(): x.transpose(1, 2, 3, 0, 4).reshape(leaf_dev, rows_here, kv_heads * width)]
    all_to_all x1, waiting for transfers between devices: 15.5 us -> 11.6 us  [on_device(): lax.all_to_all(outgoing, 'seg', split_axis=0, concat_axis=0, tiled=True)]
    pallas_call x1 -> x2, Pallas kernels: 65.5 us -> 67.8 us  [attend_all(): pl.pallas_call(attend_kernel, grid=grid, in_specs=[maskspec, qspec, gspec...]
    unnamed x34 -> x43, local copies, waits for them, and re-layouts: 7.46 us -> 7.65 us
  transfers between devices with their start and end apart: 5 -> 7, of which waited for: 5 -> 6; matrix products, arithmetic and copies ran while one was open for 5% -> 12% of each run, Pallas kernels for 0% -> 13%
where the time goes in v3:
time: 257 us; the launch traced here: 256 us
  waiting for transfers between devices  85.6 us (33%)
  Pallas kernels  67.8 us (26%)
  starting transfers between devices  36.2 us (14%)
  local copies, waits for them, and re-layouts  32.4 us (13%)
  blocking collectives  20.1 us (8%)
  other arithmetic  9.64 us (4%)
  matrix products  3.14 us (1%)
    pallas_call x2, Pallas kernels, attend_all(): pl.pallas_call(attend_kernel, grid=grid, in_specs=[maskspec, qspec, gspec...  67.8 us
    all_to_all x2, waiting for transfers between devices, on_device(): lax.all_to_all(back, 'leaf', split_axis=0, concat_axis=0, tiled=True)  35.1 us
    all_to_all x2, waiting for transfers between devices, on_device(): lax.all_to_all(packed[:, chunk], 'leaf', split_axis=0, concat_axis=0, til...  22.6 us
    all_to_all x1, blocking collectives, on_device(): lax.all_to_all(anc_send, 'leaf', split_axis=0, concat_axis=0, tiled=True)  20.1 us
    all_to_all x1, waiting for transfers between devices, on_device(): lax.all_to_all(anc_back, 'leaf', split_axis=0, concat_axis=0, tiled=True)  14.4 us
    all_to_all x2, starting transfers between devices, on_device(): lax.all_to_all(packed[:, chunk], 'leaf', split_axis=0, concat_axis=0, til...  11.9 us
    all_to_all x1, waiting for transfers between devices, on_device(): lax.all_to_all(outgoing, 'seg', split_axis=0, concat_axis=0, tiled=True)  11.6 us
    reshape x4, local copies, waits for them, and re-layouts, to_rows(): x.transpose(1, 2, 3, 0, 4).reshape(leaf_dev, rows_here, kv_heads * width)  8.97 us
  transfers between devices with their start and end apart: 7, of which 6 were waited for; matrix products, arithmetic and copies ran while one was open for 12% of the time, Pallas kernels for 13%

profile of v3, /device:TPU:0, one launch (start us, length us, event | category | flops | bytes accessed | tf_op | source)
XLA Modules:
  0.0 255.9 jit_solution(5747176642280806842)
XLA Ops:
  2.2 1.0 copy.71
  4.8 1.5 copy.73
  6.4 4.5 %all-to-all-start.1 = ((bf16[8,32,2048]{2,1,0:T(8,128)(2,1)}), bf16[8,32,2048]{2,1,0:T(8,128)(2,1)S(1)}, u32[]{:S(2)}, u32[]{:S(2)}) async-start(bf16[8,32,2048]{2,1,0:T(8,128)(2,1)} %copy.73), calls=%async_computation.1 | async-start | bytes 2097152 | tf_op jit(solution)/shard_map/all_to_all | solution.py:145
  13.3 1.9 slice_bitcast_fusion
  15.2 11.6 %all-to-all-done.1 = bf16[8,32,2048]{2,1,0:T(8,128)(2,1)S(1)} async-done(((bf16[8,32,2048]{2,1,0:T(8,128)(2,1)}), bf16[8,32,2048]{2,1,0:T(8,128)(2,1)S(1)}, u32[]{:S(2)}, u32[]{:S(2)}) %all-to-all-start.1) | async-done | bytes 1048608 | tf_op jit(solution)/shard_map/all_to_all | solution.py:145
  26.9 8.0 %all-to-all-start = ((bf16[16,32,1536]{2,1,0:T(8,128)(2,1)}), bf16[16,32,1536]{2,1,0:T(8,128)(2,1)S(1)}, u32[]{:S(2)}, u32[]{:S(2)}) async-start(bf16[16,32,1536]{2,1,0:T(8,128)(2,1)} %get-tuple-element.83), calls=%async_computation | async-start | bytes 3145728 | tf_op jit(solution)/shard_map/all_to_all | solution.py:173
  36.4 22.6 %all-to-all-done = bf16[16,32,1536]{2,1,0:T(8,128)(2,1)S(1)} async-done(((bf16[16,32,1536]{2,1,0:T(8,128)(2,1)}), bf16[16,32,1536]{2,1,0:T(8,128)(2,1)S(1)}, u32[]{:S(2)}, u32[]{:S(2)}) %all-to-all-start) | async-done | bytes 1572896 | tf_op jit(solution)/shard_map/all_to_all | solution.py:173
  59.1 20.1 %all_to_all.40 = bf16[16,4,32,256]{3,2,1,0:T(8,128)(2,1)} all-to-all(bf16[16,4,32,256]{3,2,1,0:T(8,128)(2,1)S(1)} %bitcast.123), channel_id=1, replica_groups=mesh['seg'=8,'leaf'=16] {'leaf'}, dimensions={0} | all-to-all | bytes 2097152 | tf_op jit(solution)/shard_map/all_to_all | solution.py:166
  79.2 3.9 %all-to-all-start.4 = ((bf16[16,32,1536]{2,1,0:T(8,128)(2,1)}), bf16[16,32,1536]{2,1,0:T(8,128)(2,1)S(1)}, u32[]{:S(2)}, u32[]{:S(2)}) async-start(bf16[16,32,1536]{2,1,0:T(8,128)(2,1)} %get-tuple-element.82), calls=%async_computation.4 | async-start | bytes 3145728 | tf_op jit(solution)/shard_map/all_to_all | solution.py:173
  83.8 2.3 copy.75
  86.1 33.8 %shard_map.127 = (bf16[1,512,640]{2,1,0:T(8,128)(2,1)}, bf16[1,512,640]{2,1,0:T(8,128)(2,1)}, f32[1,512,128]{2,1,0:T(8,128)}, f32[1,512,128]{2,1,0:T(8,128)}, f32[2048,128]{1,0:T(8,128)}, /*index=5*/f32[2048,128]{1,0:T(8,128)}) custom-call(f32[1,2048]{1,0:T(1,128)} %bitcast.140, bf16[1,512,1536]{2,1,0:T(8,128)(2,1)} %bitcast.105, ...), custom_call_target="tpu_custom_call" | custom-call | tf_op jit(solution)/shard_map/pallas_call | solution.py:101
  119.9 1.1 copy-done.1
  121.1 33.9 %shard_map.128 = (bf16[1,512,640]{2,1,0:T(8,128)(2,1)}, bf16[1,512,640]{2,1,0:T(8,128)(2,1)}, f32[1,512,128]{2,1,0:T(8,128)}, f32[1,512,128]{2,1,0:T(8,128)}, f32[2048,128]{1,0:T(8,128)}, /*index=5*/f32[2048,128]{1,0:T(8,128)}) custom-call(f32[1,2048]{1,0:T(1,128)} %bitcast.141, bf16[1,512,1536]{2,1,0:T(8,128)(2,1)} %bitcast.109, ...), custom_call_target="tpu_custom_call" | custom-call | tf_op jit(solution)/shard_map/pallas_call | solution.py:101
  155.0 2.3 pad_maximum_fusion.1
  157.3 1.3 fusion.1
  158.7 7.1 %all-to-all-start.6 = ((bf16[16,4,32,256]{3,2,1,0:T(8,128)(2,1)}), bf16[16,4,32,256]{3,2,1,0:T(8,128)(2,1)S(1)}, u32[]{:S(2)}, u32[]{:S(2)}) async-start(bf16[16,4,32,256]{3,2,1,0:T(8,128)(2,1)} %fusion.1), calls=%async_computation.6 | async-start | bytes 2097152 | tf_op jit(solution)/shard_map/all_to_all | solution.py:194
  165.9 1.3 pad_maximum_fusion.3
  167.2 14.4 %all-to-all-done.6 = bf16[16,4,32,256]{3,2,1,0:T(8,128)(2,1)S(1)} async-done(((bf16[16,4,32,256]{3,2,1,0:T(8,128)(2,1)}), bf16[16,4,32,256]{3,2,1,0:T(8,128)(2,1)S(1)}, u32[]{:S(2)}, u32[]{:S(2)}) %all-to-all-start.6) | async-done | bytes 1048608 | tf_op jit(solution)/shard_map/all_to_all | solution.py:194
  181.6 3.7 %all-to-all-start.3 = ((bf16[16,32,1536]{2,1,0:T(8,128)(2,1)}), bf16[16,32,1536]{2,1,0:T(8,128)(2,1)S(1)}, u32[]{:S(2)}, u32[]{:S(2)}) async-start(bf16[16,32,1536]{2,1,0:T(8,128)(2,1)} %bitcast.16), calls=%async_computation.3 | async-start | bytes 3145728 | tf_op jit(solution)/shard_map/all_to_all | solution.py:180
  186.3 2.4 pad_maximum_fusion.4
  188.8 17.9 %all-to-all-done.3 = bf16[16,32,1536]{2,1,0:T(8,128)(2,1)S(1)} async-done(((bf16[16,32,1536]{2,1,0:T(8,128)(2,1)}), bf16[16,32,1536]{2,1,0:T(8,128)(2,1)S(1)}, u32[]{:S(2)}, u32[]{:S(2)}) %all-to-all-start.3) | async-done | bytes 1572896 | tf_op jit(solution)/shard_map/all_to_all | solution.py:180
  206.7 4.4 %all-to-all-start.5 = ((bf16[16,32,1536]{2,1,0:T(8,128)(2,1)}), bf16[16,32,1536]{2,1,0:T(8,128)(2,1)}, u32[]{:S(2)}, u32[]{:S(2)}) async-start(bf16[16,32,1536]{2,1,0:T(8,128)(2,1)} %bitcast.20), calls=%async_computation.5 | async-start | bytes 3145728 | tf_op jit(solution)/shard_map/all_to_all | solution.py:180
  212.6 1.6 copy.87
  215.0 17.1 %all-to-all-done.5 = bf16[16,32,1536]{2,1,0:T(8,128)(2,1)} async-done(((bf16[16,32,1536]{2,1,0:T(8,128)(2,1)}), bf16[16,32,1536]{2,1,0:T(8,128)(2,1)}, u32[]{:S(2)}, u32[]{:S(2)}) %all-to-all-start.5) | async-done | bytes 1572896 | tf_op jit(solution)/shard_map/all_to_all | solution.py:180
  232.1 4.5 %all-to-all-start.7 = ((bf16[8,32,2048]{2,1,0:T(8,128)(2,1)}), bf16[8,32,2048]{2,1,0:T(8,128)(2,1)}, u32[]{:S(2)}, u32[]{:S(2)}) async-start(bf16[8,32,2048]{2,1,0:T(8,128)(2,1)} %copy.87), calls=%async_computation.7 | async-start | bytes 2097152 | tf_op jit(solution)/shard_map/all_to_all | solution.py:205
  236.6 2.3 copy_dynamic-update-slice_fusion
  238.9 1.8 slice_bitcast_fusion.2
  240.7 3.2 %reshape.163 = bf16[4,32,5120]{2,1,0:T(8,128)(2,1)} reshape(bf16[2,2,32,8,640]{4,3,2,1,0:T(8,128)(2,1)} %get-tuple-element.80) | data formatting | bytes 2621440 | tf_op jit(solution)/shard_map/reshape | solution.py:186
  244.7 1.8 reshape.165
  247.2 3.2 %reshape.162 = bf16[4,32,5120]{2,1,0:T(8,128)(2,1)} reshape(bf16[2,2,32,8,640]{4,3,2,1,0:T(8,128)(2,1)} %get-tuple-element.81) | data formatting | bytes 2621440 | tf_op jit(solution)/shard_map/reshape | solution.py:186
  250.4 1.9 all-to-all-done.7
  252.3 2.1 convolution_convert_fusion.2
  (79 shorter events, 14.1 us)
Async XLA Ops:
  4.8 6.1 %copy-start.13 = (bf16[4,32,1024]{2,1,0:T(8,128)(2,1)S(1)}, bf16[4,32,1024]{2,1,0:T(8,128)(2,1)}, u32[]{:S(2)}) copy-start(bf16[4,32,1024]{2,1,0:T(8,128)(2,1)} %param.9) | copy-start | bytes 786436
  6.4 4.7 %copy-start.14 = (bf16[4,32,1024]{2,1,0:T(8,128)(2,1)S(1)}, bf16[4,32,1024]{2,1,0:T(8,128)(2,1)}, u32[]{:S(2)}) copy-start(bf16[4,32,1024]{2,1,0:T(8,128)(2,1)} %param.10) | copy-start | bytes 786436
  6.4 4.8 %copy-start.4 = (bf16[4,32,5120]{2,1,0:T(8,128)(2,1)S(1)}, bf16[4,32,5120]{2,1,0:T(8,128)(2,1)}, u32[]{:S(2)}) copy-start(bf16[4,32,5120]{2,1,0:T(8,128)(2,1)} %param.8) | copy-start | bytes 3932164
  6.4 20.5 %all-to-all-start.1 = ((bf16[8,32,2048]{2,1,0:T(8,128)(2,1)}), bf16[8,32,2048]{2,1,0:T(8,128)(2,1)S(1)}, u32[]{:S(2)}, u32[]{:S(2)}) async-start(bf16[8,32,2048]{2,1,0:T(8,128)(2,1)} %copy.73), calls=%async_computation.1 | async-start | bytes 2097152 | tf_op jit(solution)/shard_map/all_to_all | solution.py:145
  11.2 1.3 copy-start.5
  26.9 32.1 %all-to-all-start = ((bf16[16,32,1536]{2,1,0:T(8,128)(2,1)}), bf16[16,32,1536]{2,1,0:T(8,128)(2,1)S(1)}, u32[]{:S(2)}, u32[]{:S(2)}) async-start(bf16[16,32,1536]{2,1,0:T(8,128)(2,1)} %get-tuple-element.83), calls=%async_computation | async-start | bytes 3145728 | tf_op jit(solution)/shard_map/all_to_all | solution.py:173
  59.0 20.2 %copy-start = (bf16[16,32,1536]{2,1,0:T(8,128)(2,1)}, bf16[16,32,1536]{2,1,0:T(8,128)(2,1)S(1)}, u32[]{:S(2)}) copy-start(bf16[16,32,1536]{2,1,0:T(8,128)(2,1)S(1)} %all-to-all-done) | copy-start | bytes 4718596
  79.2 40.7 %all-to-all-start.4 = ((bf16[16,32,1536]{2,1,0:T(8,128)(2,1)}), bf16[16,32,1536]{2,1,0:T(8,128)(2,1)S(1)}, u32[]{:S(2)}, u32[]{:S(2)}) async-start(bf16[16,32,1536]{2,1,0:T(8,128)(2,1)} %get-tuple-element.82), calls=%async_computation.4 | async-start | bytes 3145728 | tf_op jit(solution)/shard_map/all_to_all | solution.py:173
  119.9 1.1 copy-start.1
  121.1 33.9 %copy-start.6 = (f32[2048,128]{1,0:T(8,128)S(1)}, f32[2048,128]{1,0:T(8,128)}, u32[]{:S(2)}) copy-start(f32[2048,128]{1,0:T(8,128)} %get-tuple-element.26) | copy-start | bytes 3145732
  158.7 7.1 %copy-start.12 = (f32[1,512,128]{2,1,0:T(8,128)S(1)}, f32[1,512,128]{2,1,0:T(8,128)}, u32[]{:S(2)}) copy-start(f32[1,512,128]{2,1,0:T(8,128)} %get-tuple-element.20) | copy-start | bytes 786436
  158.7 7.2 %copy-start.11 = (f32[1,512,128]{2,1,0:T(8,128)S(1)}, f32[1,512,128]{2,1,0:T(8,128)}, u32[]{:S(2)}) copy-start(f32[1,512,128]{2,1,0:T(8,128)} %get-tuple-element.21) | copy-start | bytes 786436
  158.7 7.2 %copy-start.8 = (bf16[1,512,640]{2,1,0:T(8,128)(2,1)S(1)}, bf16[1,512,640]{2,1,0:T(8,128)(2,1)}, u32[]{:S(2)}) copy-start(bf16[1,512,640]{2,1,0:T(8,128)(2,1)} %get-tuple-element.18) | copy-start | bytes 1966084
  158.7 7.2 %copy-start.9 = (bf16[1,512,640]{2,1,0:T(8,128)(2,1)S(1)}, bf16[1,512,640]{2,1,0:T(8,128)(2,1)}, u32[]{:S(2)}) copy-start(bf16[1,512,640]{2,1,0:T(8,128)(2,1)} %get-tuple-element.19) | copy-start | bytes 1966084
  158.7 22.9 %all-to-all-start.6 = ((bf16[16,4,32,256]{3,2,1,0:T(8,128)(2,1)}), bf16[16,4,32,256]{3,2,1,0:T(8,128)(2,1)S(1)}, u32[]{:S(2)}, u32[]{:S(2)}) async-start(bf16[16,4,32,256]{3,2,1,0:T(8,128)(2,1)} %fusion.1), calls=%async_computation.6 | async-start | bytes 2097152 | tf_op jit(solution)/shard_map/all_to_all | solution.py:194
  167.2 19.1 %copy-start.10 = (f32[1,512,128]{2,1,0:T(8,128)S(1)}, f32[1,512,128]{2,1,0:T(8,128)}, u32[]{:S(2)}) copy-start(f32[1,512,128]{2,1,0:T(8,128)} %get-tuple-element.25) | copy-start | bytes 786436
  167.2 19.1 %copy-start.7 = (bf16[1,512,640]{2,1,0:T(8,128)(2,1)S(1)}, bf16[1,512,640]{2,1,0:T(8,128)(2,1)}, u32[]{:S(2)}) copy-start(bf16[1,512,640]{2,1,0:T(8,128)(2,1)} %get-tuple-element.22) | copy-start | bytes 1966084
  181.6 25.1 %all-to-all-start.3 = ((bf16[16,32,1536]{2,1,0:T(8,128)(2,1)}), bf16[16,32,1536]{2,1,0:T(8,128)(2,1)S(1)}, u32[]{:S(2)}, u32[]{:S(2)}) async-start(bf16[16,32,1536]{2,1,0:T(8,128)(2,1)} %bitcast.16), calls=%async_computation.3 | async-start | bytes 3145728 | tf_op jit(solution)/shard_map/all_to_all | solution.py:180
  206.7 4.6 %copy-start.2 = (bf16[16,32,1536]{2,1,0:T(8,128)(2,1)}, bf16[16,32,1536]{2,1,0:T(8,128)(2,1)S(1)}, u32[]{:S(2)}) copy-start(bf16[16,32,1536]{2,1,0:T(8,128)(2,1)S(1)} %all-to-all-done.3) | copy-start | bytes 4718596
  206.7 25.4 %all-to-all-start.5 = ((bf16[16,32,1536]{2,1,0:T(8,128)(2,1)}), bf16[16,32,1536]{2,1,0:T(8,128)(2,1)}, u32[]{:S(2)}, u32[]{:S(2)}) async-start(bf16[16,32,1536]{2,1,0:T(8,128)(2,1)} %bitcast.20), calls=%async_computation.5 | async-start | bytes 3145728 | tf_op jit(solution)/shard_map/all_to_all | solution.py:180
  212.0 2.2 copy-start.3
  232.1 20.2 %all-to-all-start.7 = ((bf16[8,32,2048]{2,1,0:T(8,128)(2,1)}), bf16[8,32,2048]{2,1,0:T(8,128)(2,1)}, u32[]{:S(2)}, u32[]{:S(2)}) async-start(bf16[8,32,2048]{2,1,0:T(8,128)(2,1)} %copy.87), calls=%async_computation.7 | async-start | bytes 2097152 | tf_op jit(solution)/shard_map/all_to_all | solution.py:205

commit v4 on v2

v4 whole, which is shorter than its diff:
```python
import functools
import math

import jax
import jax.numpy as jnp
from jax import lax
from jax.experimental import pallas as pl
from jax.experimental.pallas import tpu as pltpu
from jax.sharding import PartitionSpec as P

HD = 128


NEG_FILL = -1e30


def attend_kernel(row_half, half_rows, mask_ref, qg_ref, ko_ref, vo_ref, ka_ref, va_ref,
                  dka_in, dva_in, dko_in, dvo_in, out_ref, dka_ref, dva_ref, dko_ref, dvo_ref):
    head_i = pl.program_id(0)
    sources = qg_ref.shape[0]
    block_rows = sources * half_rows
    seg_len = ko_ref.shape[0] * ko_ref.shape[1]
    scale = 1.0 / math.sqrt(HD)

    @pl.when(head_i == 0)
    def _():
        dka_ref[...] = dka_in[...]
        dva_ref[...] = dva_in[...]
        dko_ref[...] = dko_in[...]
        dvo_ref[...] = dvo_in[...]

    nt = (((1,), (1,)), ((), ()))
    tn = (((0,), (0,)), ((), ()))
    qg = qg_ref[...]
    q = qg[:, :, :HD].reshape(block_rows, HD)
    g = qg[:, :, HD:].reshape(block_rows, HD)
    ka = ka_ref[...]
    va = va_ref[...]
    ko = ko_ref[...].reshape(seg_len, HD)
    vo = vo_ref[...].reshape(seg_len, HD)
    s_a = lax.dot_general(q, ka, nt, preferred_element_type=jnp.float32) * scale
    s_o = lax.dot_general(q, ko, nt, preferred_element_type=jnp.float32) * scale
    s_a = jnp.where(mask_ref[...] > 0.5, s_a, NEG_FILL)
    local = lax.broadcasted_iota(jnp.int32, (block_rows, seg_len), 0)
    rows = (local // half_rows) * (2 * half_rows) + row_half * half_rows + local % half_rows
    cols = lax.broadcasted_iota(jnp.int32, (block_rows, seg_len), 1)
    s_o = jnp.where(cols <= rows, s_o, NEG_FILL)
    m = jnp.maximum(jnp.max(s_a, axis=1, keepdims=True), jnp.max(s_o, axis=1, keepdims=True))
    w_a = jnp.exp(s_a - m)
    w_o = jnp.exp(s_o - m)
    total = jnp.sum(w_a, axis=1, keepdims=True) + jnp.sum(w_o, axis=1, keepdims=True)
    inv = 1.0 / total
    p_a = w_a * inv
    p_o = w_o * inv
    pb_a = p_a.astype(jnp.bfloat16)
    pb_o = p_o.astype(jnp.bfloat16)
    o = jnp.dot(pb_a, va, preferred_element_type=jnp.float32) + jnp.dot(pb_o, vo, preferred_element_type=jnp.float32)
    o_b = o.astype(jnp.bfloat16)
    delta = jnp.sum(g.astype(jnp.float32) * o_b.astype(jnp.float32), axis=1, keepdims=True)
    dp_a = lax.dot_general(g, va, nt, preferred_element_type=jnp.float32)
    dp_o = lax.dot_general(g, vo, nt, preferred_element_type=jnp.float32)
    ds_a = (p_a * (dp_a - delta)).astype(jnp.bfloat16)
    ds_o = (p_o * (dp_o - delta)).astype(jnp.bfloat16)
    dq = (jnp.dot(ds_a, ka, preferred_element_type=jnp.float32) + jnp.dot(ds_o, ko, preferred_element_type=jnp.float32)) * scale
    out_ref[:, :, :HD] = o_b.reshape(sources, half_rows, HD)
    out_ref[:, :, HD:] = dq.astype(jnp.bfloat16).reshape(sources, half_rows, HD)
    dka_ref[...] += lax.dot_general(ds_a, q, tn, preferred_element_type=jnp.float32)
    dva_ref[...] += lax.dot_general(pb_a, g, tn, preferred_element_type=jnp.float32)
    dko_ref[...] += lax.dot_general(ds_o, q, tn, preferred_element_type=jnp.float32).reshape(dko_ref.shape)
    dvo_ref[...] += lax.dot_general(pb_o, g, tn, preferred_element_type=jnp.float32).reshape(dvo_ref.shape)


def attend_chunk(row_half, leaf, anc_mask, qg, own, anc_rows, accs):
    sources, heads, half_rows, _ = qg.shape
    rows_here = own.shape[2]
    anc = anc_rows.shape[0]
    qgspec = pl.BlockSpec((sources, None, half_rows, 2 * HD), lambda h: (0, h, 0, 0))
    kospec = pl.BlockSpec((sources, None, rows_here, HD), lambda h: (0, leaf, 0, 0))
    vospec = pl.BlockSpec((sources, None, rows_here, HD), lambda h: (0, leaf, 0, 1))
    kaspec = pl.BlockSpec((anc, HD), lambda h: (0, 0))
    vaspec = pl.BlockSpec((anc, HD), lambda h: (0, 1))
    maskspec = pl.BlockSpec((1, anc), lambda h: (0, 0))
    ownspec = pl.BlockSpec((sources, rows_here, HD), lambda h: (0, 0, 0))
    return pl.pallas_call(
        functools.partial(attend_kernel, row_half, half_rows),
        grid=(heads,),
        in_specs=[maskspec, qgspec, kospec, vospec, kaspec, vaspec, kaspec, kaspec, ownspec, ownspec],
        out_specs=[qgspec, kaspec, kaspec, ownspec, ownspec],
        out_shape=[jax.ShapeDtypeStruct(qg.shape, jnp.bfloat16)] + [jax.ShapeDtypeStruct(a.shape, jnp.float32) for a in accs],
        input_output_aliases={6: 1, 7: 2, 8: 3, 9: 4},
        compiler_params=pltpu.CompilerParams(dimension_semantics=("arbitrary",)),
    )(anc_mask, qg, own, own, anc_rows, anc_rows, *accs)


def on_device(queries, leaf_keys, leaf_values, inner_keys, inner_values, out_grad, ancestors, depths):
    seg_count = lax.axis_size("seg")
    leaf_count = lax.axis_size("leaf")
    seg_here = lax.axis_index("seg")
    leaf_dev, rows_here, query_width = queries.shape
    slot_count = inner_keys.shape[0]
    key_width = leaf_keys.shape[2]
    kv_heads = key_width // HD
    group_heads = query_width // key_width
    seg_len = rows_here * leaf_count
    levels = ancestors.shape[1]
    pair_count = leaf_count // kv_heads
    pair_leaves = leaf_dev // pair_count
    halves = 2
    half_rows = rows_here // halves

    group_lists = ancestors[::leaf_dev]
    group_depth = depths[::leaf_dev]
    owners = group_lists // slot_count
    slot_of = group_lists % slot_count
    level_ids = jnp.arange(levels, dtype=jnp.int32)
    alive_levels = level_ids[None, :] < group_depth[:, None]
    served = alive_levels & (owners == seg_here)
    slot_ids = jnp.arange(slot_count, dtype=jnp.int32)
    serve_pick = jnp.sum(
        (served[:, :, None] & (slot_of[:, :, None] == slot_ids[None, None, :])).astype(jnp.float32),
        axis=1,
    ).astype(jnp.bfloat16)
    stored = jnp.concatenate([inner_keys, inner_values], axis=2)
    outgoing = jnp.einsum("gs,src->grc", serve_pick, stored, preferred_element_type=jnp.float32).astype(
        jnp.bfloat16
    )
    arrived = lax.all_to_all(outgoing, "seg", split_axis=0, concat_axis=0, tiled=True)
    my_owners = jnp.take(owners, seg_here, axis=0)
    my_alive = jnp.take(alive_levels, seg_here, axis=0)
    ancestor_rows = jnp.where(
        my_alive[:, None, None], jnp.take(arrived, my_owners, axis=0), jnp.zeros((), jnp.bfloat16)
    )

    def exchange(x):
        return lax.all_to_all(x, "leaf", split_axis=0, concat_axis=0, tiled=True)

    own_kv = jnp.concatenate(
        [leaf_keys.reshape(leaf_dev, rows_here, kv_heads, 1, HD), leaf_values.reshape(leaf_dev, rows_here, kv_heads, 1, HD)],
        axis=3,
    ).reshape(pair_count, pair_leaves, rows_here, kv_heads, 2 * HD)
    own_send = own_kv.transpose(3, 0, 1, 2, 4).reshape(leaf_count, pair_leaves * rows_here, 2 * HD)
    anc_kv = jnp.concatenate(
        [
            ancestor_rows[:, :, :key_width].reshape(levels, rows_here, kv_heads, 1, HD),
            ancestor_rows[:, :, key_width:].reshape(levels, rows_here, kv_heads, 1, HD),
        ],
        axis=3,
    ).reshape(levels, rows_here, kv_heads, 2 * HD)
    anc_heads = anc_kv.transpose(2, 0, 1, 3)
    anc_send = jnp.broadcast_to(anc_heads[:, None], (kv_heads, pair_count) + anc_heads.shape[1:]).reshape(
        leaf_count, levels * rows_here, 2 * HD
    )
    qg_all = jnp.concatenate(
        [
            queries.reshape(pair_count, pair_leaves, halves, half_rows, kv_heads, group_heads, 1, HD),
            out_grad.reshape(pair_count, pair_leaves, halves, half_rows, kv_heads, group_heads, 1, HD),
        ],
        axis=6,
    )
    qg_send = qg_all.transpose(1, 2, 4, 0, 5, 3, 6, 7).reshape(
        pair_leaves, halves, leaf_count, group_heads * half_rows, 2 * HD
    )
    chunks = [(leaf, half) for leaf in range(pair_leaves) for half in range(halves)]
    chunk_rows = group_heads * half_rows

    own_rows_n = pair_leaves * rows_here
    anc_rows_n = levels * rows_here
    first = exchange(jnp.concatenate([own_send, anc_send, qg_send[0, 0]], axis=1))
    own_got = first[:, :own_rows_n].reshape(leaf_count, pair_leaves, rows_here, 2 * HD)
    anc_got = first[:, own_rows_n : own_rows_n + anc_rows_n].reshape(leaf_count * anc_rows_n, 2 * HD)
    inputs = {0: first[:, own_rows_n + anc_rows_n :]}
    anc_mask = jnp.broadcast_to(
        jnp.repeat(my_alive, rows_here).astype(jnp.float32)[None, :], (leaf_count, anc_rows_n)
    ).reshape(1, leaf_count * anc_rows_n)

    accs_anc = [jnp.zeros((leaf_count * anc_rows_n, HD), jnp.float32)] * 2
    accs_own = {leaf: [jnp.zeros((leaf_count, rows_here, HD), jnp.float32)] * 2 for leaf in range(pair_leaves)}
    outputs = {}
    homes = {}
    count = len(chunks)
    for t in range(count):
        leaf, half = chunks[t]
        qg = inputs.pop(t).reshape(leaf_count, group_heads, half_rows, 2 * HD)
        out, dka, dva, dko, dvo = attend_chunk(half, leaf, anc_mask, qg, own_got, anc_got, accs_anc + accs_own[leaf])
        accs_anc = [dka, dva]
        accs_own[leaf] = [dko, dvo]
        outputs[t] = out.reshape(leaf_count, chunk_rows, 2 * HD)
        nxt = t + 1
        parts = []
        if nxt < count:
            parts.append(qg_send[chunks[nxt][0], chunks[nxt][1]])
        if nxt - 2 >= 0:
            parts.append(outputs.pop(nxt - 2))
        if nxt < count:
            got = exchange(jnp.concatenate(parts, axis=1))
            inputs[nxt] = got[:, :chunk_rows]
            if nxt - 2 >= 0:
                homes[nxt - 2] = got[:, chunk_rows:]
        else:
            homes[nxt - 2] = exchange(parts[0])
    logit_scale = 1.0 / math.sqrt(HD)
    own_back = jnp.concatenate(
        [
            jnp.concatenate([accs_own[leaf][0] * logit_scale, accs_own[leaf][1]], axis=2).astype(jnp.bfloat16)
            for leaf in range(pair_leaves)
        ],
        axis=1,
    )
    anc_back = jnp.concatenate([accs_anc[0] * logit_scale, accs_anc[1]], axis=1).astype(jnp.bfloat16)
    anc_back = anc_back.reshape(leaf_count, anc_rows_n, 2 * HD)
    last = exchange(jnp.concatenate([outputs.pop(count - 1), own_back, anc_back], axis=1))
    homes[count - 1] = last[:, :chunk_rows]
    own_home = last[:, chunk_rows : chunk_rows + own_rows_n]
    anc_home = last[:, chunk_rows + own_rows_n :]

    stacked = jnp.stack([homes[t] for t in range(count)], axis=0).reshape(
        pair_leaves, halves, kv_heads, pair_count, group_heads, half_rows, 2, HD
    )

    def to_rows(x):
        return x.transpose(3, 0, 1, 5, 2, 4, 6).reshape(leaf_dev, rows_here, query_width)

    attention = to_rows(stacked[..., 0, :])
    query_grad = to_rows(stacked[..., 1, :])
    own_home = own_home.reshape(kv_heads, pair_count, pair_leaves, rows_here, 2, HD)
    leaf_key_grad = own_home[..., 0, :].transpose(1, 2, 3, 0, 4).reshape(leaf_dev, rows_here, key_width)
    leaf_value_grad = own_home[..., 1, :].transpose(1, 2, 3, 0, 4).reshape(leaf_dev, rows_here, key_width)

    anc_home = anc_home.astype(jnp.float32).reshape(kv_heads, pair_count, levels, rows_here, 2 * HD).sum(axis=1)
    part_keys = anc_home[..., :HD].transpose(1, 2, 0, 3).reshape(levels, rows_here, key_width)
    part_values = anc_home[..., HD:].transpose(1, 2, 0, 3).reshape(levels, rows_here, key_width)
    part_round = jnp.concatenate([part_keys, part_values], axis=2).astype(jnp.bfloat16)

    seg_ids = jnp.arange(seg_count, dtype=jnp.int32)
    homeward_pick = ((my_owners[None, :] == seg_ids[:, None]) & my_alive[None, :]).astype(jnp.bfloat16)
    homeward = jnp.einsum("ok,krc->orc", homeward_pick, part_round, preferred_element_type=jnp.float32).astype(
        jnp.bfloat16
    )
    returned = lax.all_to_all(homeward, "seg", split_axis=0, concat_axis=0, tiled=True)
    collected = jnp.einsum("gs,grc->src", serve_pick, returned, preferred_element_type=jnp.float32).astype(
        jnp.bfloat16
    )
    return (
        attention,
        query_grad,
        leaf_key_grad,
        leaf_value_grad,
        collected[:, :, :key_width],
        collected[:, :, key_width:],
    )


def solution(mesh):
    spec = P("seg", "leaf", None)
    return jax.shard_map(
        on_device,
        mesh=mesh,
        in_specs=(spec, spec, spec, spec, spec, spec, P(), P()),
        out_specs=(spec, spec, spec, spec, spec, spec),
        check_vma=False,
    )
```

time: 277 us -> 277 us (level)
  waiting for transfers between devices: 126 us -> 0.02 us
  blocking collectives: 19.9 us -> 73.5 us
  local copies, waits for them, and re-layouts: 30 us -> 69.9 us
  Pallas kernels: 65.5 us -> 76.8 us
  other arithmetic: 6.96 us -> 17.3 us
  starting transfers between devices: 23.7 us -> 31.7 us
    all_to_all x3 -> x4, waiting for transfers between devices: 97.7 us -> 0.01 us  [exchange(): return lax.all_to_all(x, 'leaf', split_axis=0, concat_axis=0, tiled=True)]
    all_to_all x1 -> x2, blocking collectives: 19.9 us -> 73.5 us  [exchange(): return lax.all_to_all(x, 'leaf', split_axis=0, concat_axis=0, tiled=True)]
    reshape x9, local copies, waits for them, and re-layouts: 7.06 us -> 23.6 us  [the longest x2 6.32 us: to_rows(): x.transpose(3, 0, 1, 5, 2, 4, 6).reshape(leaf_dev, rows_here, query_width)]
    all_to_all x1, waiting for transfers between devices: 15.5 us -> 0.01 us  [on_device(): lax.all_to_all(outgoing, 'seg', split_axis=0, concat_axis=0, tiled=True)]
    all_to_all x1, waiting for transfers between devices: 12.3 us -> 0.01 us  [on_device(): lax.all_to_all(homeward, 'seg', split_axis=0, concat_axis=0, tiled=True)]
    pallas_call x1 -> x4, Pallas kernels: 65.5 us -> 76.8 us  [attend_chunk(): pl.pallas_call(functools.partial(attend_kernel, row_half, half_rows), gri...]
    slice x1 -> x8, local copies, waits for them, and re-layouts: 0.04 us -> 10 us  [the longest x1 5.85 us: on_device(): query_grad = to_rows(stacked[..., 1, :])]
    all_to_all x3 -> x4, starting transfers between devices: 15.7 us -> 22.8 us  [exchange(): return lax.all_to_all(x, 'leaf', split_axis=0, concat_axis=0, tiled=True)]
  transfers between devices with their start and end apart: 5 -> 6, of which waited for: 5 -> 0; matrix products, arithmetic and copies ran while one was open for 5% -> 27% of each run, Pallas kernels for 0% -> 21%
where the time goes in v4:
time: 277 us; the launch traced here: 274 us
  Pallas kernels  76.8 us (28%)
  blocking collectives  73.5 us (27%)
  local copies, waits for them, and re-layouts  69.9 us (25%)
  starting transfers between devices  31.7 us (11%)
  other arithmetic  17.3 us (6%)
  matrix products  4.09 us (1%)
    pallas_call x4, Pallas kernels, attend_chunk(): pl.pallas_call(functools.partial(attend_kernel, row_half, half_rows), gri...  76.8 us
    all_to_all x2, blocking collectives, exchange(): return lax.all_to_all(x, 'leaf', split_axis=0, concat_axis=0, tiled=True)  73.5 us
    all_to_all x4, starting transfers between devices, exchange(): return lax.all_to_all(x, 'leaf', split_axis=0, concat_axis=0, tiled=True)  22.8 us
    transpose x1, local copies, waits for them, and re-layouts, on_device(): qg_all.transpose(1, 2, 4, 0, 5, 3, 6, 7)  6.67 us
    reshape x2, local copies, waits for them, and re-layouts, to_rows(): x.transpose(3, 0, 1, 5, 2, 4, 6).reshape(leaf_dev, rows_here, query_width)  6.32 us
    slice x1, local copies, waits for them, and re-layouts, on_device(): query_grad = to_rows(stacked[..., 1, :])  5.85 us
  transfers between devices with their start and end apart: 6, of which 0 were waited for; matrix products, arithmetic and copies ran while one was open for 27% of the time, Pallas kernels for 21%

profile of v4, /device:TPU:0, one launch (start us, length us, event | category | flops | bytes accessed | tf_op | source)
XLA Modules:
  0.0 274.5 jit_solution(9105923002236712428)
XLA Ops:
  4.8 1.5 copy.137
  6.4 4.4 %all-to-all-start = ((bf16[8,32,2048]{2,1,0:T(8,128)(2,1)}), bf16[8,32,2048]{2,1,0:T(8,128)(2,1)}, u32[]{:S(2)}, u32[]{:S(2)}) async-start(bf16[8,32,2048]{2,1,0:T(8,128)(2,1)} %copy.137), calls=%async_computation | async-start | bytes 2097152 | tf_op jit(solution)/shard_map/all_to_all | solution.py:127
  10.8 1.6 reshape.160
  12.4 4.2 %reshape.161 = bf16[2,2,2,16,8,5,1,128]{7,5,4,3,2,1,0,6:T(8,128)(2,1)} reshape(bf16[4,32,5120]{2,1,0:T(8,128)(2,1)} %param.13) | data formatting | bytes 2621440 | tf_op jit(solution)/shard_map/reshape | solution.py:156
  16.8 4.5 %maximum_bitcast_fusion = bf16[2,2,8,2,5,16,2,128]{7,4,2,5,1,0,3,6:T(8,128)(2,1)} fusion(bf16[2,2,2,16,8,5,1,128]{7,5,4,3,2,1,0,6:T(8,128)(2,1)} %reshape.161, bf16[2,2,2,16,8,5,1,128]{7,5,4,3,2,1,0,6:T(8,128)(2,1)S(1)} %reshape.160), kind=kLoop, calls=%fused_computation.1 | loop fusion | flops 1310720 | bytes 5242880 | tf_op jit(solution)/shard_map/transpose | solution.py:160
  21.3 6.7 %copy.133 = bf16[2,2,8,2,5,16,2,128]{7,6,5,4,3,2,1,0:T(2,128)(2,1)} copy(bf16[2,2,8,2,5,16,2,128]{7,4,2,5,1,0,3,6:T(8,128)(2,1)} %maximum_bitcast_fusion) | data formatting | bytes 5242880 | tf_op jit(solution)/shard_map/transpose | solution.py:160
  28.0 4.2 %reshape.162 = bf16[2,2,16,80,256]{4,3,2,1,0:T(8,128)(2,1)S(1)} reshape(bf16[2,2,8,2,5,16,2,128]{7,6,5,4,3,2,1,0:T(2,128)(2,1)} %copy.133) | data formatting | bytes 5242880 | tf_op jit(solution)/shard_map/reshape | solution.py:160
  34.8 1.8 gather_fusion
  38.2 38.4 %all_to_all.40 = bf16[16,272,256]{2,1,0:T(8,128)(2,1)S(1)} all-to-all(bf16[16,272,256]{2,1,0:T(8,128)(2,1)S(1)} %pad_maximum_fusion.1), channel_id=1, replica_groups=mesh['seg'=8,'leaf'=16] {'leaf'}, dimensions={0} | all-to-all | bytes 4456448 | tf_op jit(solution)/shard_map/all_to_all | solution.py:135
  76.6 4.4 %all-to-all-start.3 = ((bf16[16,80,256]{2,1,0:T(8,128)(2,1)}), bf16[16,80,256]{2,1,0:T(8,128)(2,1)}, u32[]{:S(2)}, u32[]{:S(2)}) async-start(bf16[16,80,256]{2,1,0:T(8,128)(2,1)} %get-tuple-element.115), calls=%async_computation.3 | async-start | bytes 1310720 | tf_op jit(solution)/shard_map/all_to_all | solution.py:135
  88.2 19.2 %shard_map.127 = (bf16[16,5,16,256]{3,2,1,0:T(8,128)(2,1)}, f32[2048,128]{1,0:T(8,128)}, f32[2048,128]{1,0:T(8,128)}, f32[16,32,128]{2,1,0:T(8,128)}, f32[16,32,128]{2,1,0:T(8,128)}) custom-call(f32[1,2048]{1,0:T(1,128)} %bitcast.150, bf16[16,5,16,256]{3,2,1,0:T(8,128)(2,1)} %bitcast.134, ...), custom_call_target="tpu_custom_call", output_to_operand_aliasing={{1}: (6, {}), {2}: (7, {}), {3}: (8, {}), {4}: (9, {})} | custom-call | tf_op jit(solution)/shard_map/pallas_call | solution.py:84
  107.4 2.3 pad_maximum_fusion.2
  109.7 6.9 %all-to-all-start.2 = ((bf16[16,160,256]{2,1,0:T(8,128)(2,1)}), bf16[16,160,256]{2,1,0:T(8,128)(2,1)S(1)}, u32[]{:S(2)}, u32[]{:S(2)}) async-start(bf16[16,160,256]{2,1,0:T(8,128)(2,1)} %pad_maximum_fusion.2), calls=%async_computation.2 | async-start | bytes 2621440 | tf_op jit(solution)/shard_map/all_to_all | solution.py:135
  116.6 19.3 %shard_map.128 = (bf16[16,5,16,256]{3,2,1,0:T(8,128)(2,1)}, f32[2048,128]{1,0:T(8,128)}, f32[2048,128]{1,0:T(8,128)}, f32[16,32,128]{2,1,0:T(8,128)}, f32[16,32,128]{2,1,0:T(8,128)}) custom-call(f32[1,2048]{1,0:T(1,128)} %bitcast.151, ...), custom_call_target="tpu_custom_call", output_to_operand_aliasing={{1}: (6, {}), {2}: (7, {}), {3}: (8, {}), {4}: (9, {})} | custom-call | tf_op jit(solution)/shard_map/pallas_call | solution.py:84
  135.9 2.3 pad_maximum_fusion.3
  138.2 7.2 %all-to-all-start.4 = ((bf16[16,160,256]{2,1,0:T(8,128)(2,1)}), bf16[16,160,256]{2,1,0:T(8,128)(2,1)S(1)}, u32[]{:S(2)}, u32[]{:S(2)}) async-start(bf16[16,160,256]{2,1,0:T(8,128)(2,1)} %pad_maximum_fusion.3), calls=%async_computation.4 | async-start | bytes 2621440 | tf_op jit(solution)/shard_map/all_to_all | solution.py:135
  148.1 19.2 %shard_map.129 = (bf16[16,5,16,256]{3,2,1,0:T(8,128)(2,1)}, f32[2048,128]{1,0:T(8,128)}, f32[2048,128]{1,0:T(8,128)}, f32[16,32,128]{2,1,0:T(8,128)}, f32[16,32,128]{2,1,0:T(8,128)}) custom-call(f32[1,2048]{1,0:T(1,128)} %bitcast.152, bf16[16,5,16,256]{3,2,1,0:T(8,128)(2,1)} %bitcast.133, ...), custom_call_target="tpu_custom_call", output_to_operand_aliasing={{1}: (6, {}), {2}: (7, {}), {3}: (8, {}), {4}: (9, {})} | custom-call | tf_op jit(solution)/shard_map/pallas_call | solution.py:84
  168.5 19.2 %shard_map.130 = (bf16[16,5,16,256]{3,2,1,0:T(8,128)(2,1)}, f32[2048,128]{1,0:T(8,128)}, f32[2048,128]{1,0:T(8,128)}, f32[16,32,128]{2,1,0:T(8,128)}, f32[16,32,128]{2,1,0:T(8,128)}) custom-call(f32[1,2048]{1,0:T(1,128)} %bitcast.153, bf16[16,5,16,256]{3,2,1,0:T(8,128)(2,1)} %bitcast.132, ...), custom_call_target="tpu_custom_call", output_to_operand_aliasing={{1}: (6, {}), {2}: (7, {}), {3}: (8, {}), {4}: (9, {})} | custom-call | tf_op jit(solution)/shard_map/pallas_call | solution.py:84
  190.7 35.0 %all_to_all.41 = bf16[16,272,256]{2,1,0:T(8,128)(2,1)S(1)} all-to-all(bf16[16,272,256]{2,1,0:T(8,128)(2,1)S(1)} %maximum_maximum_fusion), channel_id=1, replica_groups=mesh['seg'=8,'leaf'=16] {'leaf'}, dimensions={0} | all-to-all | bytes 4456448 | tf_op jit(solution)/shard_map/all_to_all | solution.py:135
  225.8 4.3 %all-to-all-start.5 = ((bf16[16,80,256]{2,1,0:T(8,128)(2,1)}), bf16[16,80,256]{2,1,0:T(8,128)(2,1)}, u32[]{:S(2)}, u32[]{:S(2)}) async-start(bf16[16,80,256]{2,1,0:T(8,128)(2,1)} %bitcast.25), calls=%async_computation.5 | async-start | bytes 1310720 | tf_op jit(solution)/shard_map/all_to_all | solution.py:135
  234.9 1.5 convolution_convert_fusion
  236.5 1.6 copy.151
  239.4 1.9 reshape.186
  241.3 1.8 reshape.187
  244.0 4.5 %all-to-all-start.7 = ((bf16[8,32,2048]{2,1,0:T(8,128)(2,1)}), bf16[8,32,2048]{2,1,0:T(8,128)(2,1)}, u32[]{:S(2)}, u32[]{:S(2)}) async-start(bf16[8,32,2048]{2,1,0:T(8,128)(2,1)} %copy.151), calls=%async_computation.7 | async-start | bytes 2097152 | tf_op jit(solution)/shard_map/all_to_all | solution.py:239
  248.5 3.1 %pad_maximum_fusion = bf16[4,16,80,256]{3,2,1,0:T(8,128)(2,1)} fusion(bf16[1,16,80,256]{3,2,1,0:T(8,128)(2,1)} %slice_bitcast_fusion, bf16[1,16,80,256]{3,2,1,0:T(8,128)(2,1)} %bitcast.26, bf16[1,16,80,256]{3,2,1,0:T(8,128)(2,1)S(1)} %copy-done.5, bf16[1,16,80,256]{3,2,1,0:T(8,128)(2,1)S(1)} %copy-done.4), kind=kLoop, calls=%fused_computation.2 | loop fusion | flops 3932160 | bytes 5242880 | tf_op jit(solution)/shard_map/stack | solution.py:216
  251.6 3.5 %reshape.182 = bf16[2,2,8,2,5,16,2,128]{7,6,5,4,3,2,1,0:T(2,128)(2,1)S(1)} reshape(bf16[4,16,80,256]{3,2,1,0:T(8,128)(2,1)} %pad_maximum_fusion) | data formatting | bytes 5242880 | tf_op jit(solution)/shard_map/reshape | solution.py:216
  255.2 5.9 %fusion.21 = (bf16[2,2,8,2,5,16,1,128]{7,6,5,4,3,2,1,0:T(2,128)(2,1)S(1)}, bf16[2,2,8,2,5,16,1,128]{7,6,5,4,3,2,1,0:T(2,128)(2,1)S(1)}) fusion(bf16[2,2,8,2,5,16,2,128]{7,6,5,4,3,2,1,0:T(2,128)(2,1)S(1)} %reshape.182), kind=kLoop, calls=%fused_computation.67 | loop fusion | bytes 5242880 | tf_op jit(solution)/shard_map/slice | solution.py:224
  261.0 3.5 %copy_bitcast_fusion = (bf16[2,2,2,16,8,5,128]{6,5,4,3,2,1,0:T(8,128)(2,1)S(1)}, bf16[2,2,2,16,8,5,128]{6,5,4,3,2,1,0:T(8,128)(2,1)}) fusion(bf16[2,2,8,2,5,16,1,128]{7,6,5,4,3,2,1,0:T(2,128)(2,1)S(1)} %get-tuple-element.112, bf16[2,2,8,2,5,16,1,128]{7,6,5,4,3,2,1,0:T(2,128)(2,1)S(1)} %get-tuple-element.113), kind=kLoop, calls=%fused_computation.8 | loop fusion | bytes 5242880 | tf_op jit(solution)/shard_map/transpose | solution.py:221
  264.5 4.0 %reshape.183 = bf16[4,32,5120]{2,1,0:T(8,128)(2,1)} reshape(bf16[2,2,2,16,8,5,128]{6,5,4,3,2,1,0:T(8,128)(2,1)} %get-tuple-element.132) | data formatting | bytes 2621440 | tf_op jit(solution)/shard_map/reshape | solution.py:221
  268.6 2.3 reshape.184
  270.9 2.1 convolution_convert_fusion.2
  (95 shorter events, 31.1 us)
Async XLA Ops:
  4.3 6.5 %copy-start.9 = (bf16[4,32,5120]{2,1,0:T(8,128)(2,1)S(1)}, bf16[4,32,5120]{2,1,0:T(8,128)(2,1)}, u32[]{:S(2)}) copy-start(bf16[4,32,5120]{2,1,0:T(8,128)(2,1)} %param.8) | copy-start | bytes 3932164
  6.4 28.5 %all-to-all-start = ((bf16[8,32,2048]{2,1,0:T(8,128)(2,1)}), bf16[8,32,2048]{2,1,0:T(8,128)(2,1)}, u32[]{:S(2)}, u32[]{:S(2)}) async-start(bf16[8,32,2048]{2,1,0:T(8,128)(2,1)} %copy.137), calls=%async_computation | async-start | bytes 2097152 | tf_op jit(solution)/shard_map/all_to_all | solution.py:127
  12.4 4.2 %copy-start.11 = (bf16[4,32,1024]{2,1,0:T(8,128)(2,1)S(1)}, bf16[4,32,1024]{2,1,0:T(8,128)(2,1)}, u32[]{:S(2)}) copy-start(bf16[4,32,1024]{2,1,0:T(8,128)(2,1)} %param.9) | copy-start | bytes 786436
  12.4 4.3 %copy-start.12 = (bf16[4,32,1024]{2,1,0:T(8,128)(2,1)S(1)}, bf16[4,32,1024]{2,1,0:T(8,128)(2,1)}, u32[]{:S(2)}) copy-start(bf16[4,32,1024]{2,1,0:T(8,128)(2,1)} %param.10) | copy-start | bytes 786436
  36.8 1.1 copy-start.7
  36.8 1.2 copy-start.8
  76.6 33.1 %all-to-all-start.3 = ((bf16[16,80,256]{2,1,0:T(8,128)(2,1)}), bf16[16,80,256]{2,1,0:T(8,128)(2,1)}, u32[]{:S(2)}, u32[]{:S(2)}) async-start(bf16[16,80,256]{2,1,0:T(8,128)(2,1)} %get-tuple-element.115), calls=%async_computation.3 | async-start | bytes 1310720 | tf_op jit(solution)/shard_map/all_to_all | solution.py:135
  109.7 28.5 %all-to-all-start.2 = ((bf16[16,160,256]{2,1,0:T(8,128)(2,1)}), bf16[16,160,256]{2,1,0:T(8,128)(2,1)S(1)}, u32[]{:S(2)}, u32[]{:S(2)}) async-start(bf16[16,160,256]{2,1,0:T(8,128)(2,1)} %pad_maximum_fusion.2), calls=%async_computation.2 | async-start | bytes 2621440 | tf_op jit(solution)/shard_map/all_to_all | solution.py:135
  116.6 19.3 %copy-start.6 = (bf16[16,80,256]{2,1,0:T(8,128)(2,1)S(1)}, bf16[16,80,256]{2,1,0:T(8,128)(2,1)}, u32[]{:S(2)}) copy-start(bf16[16,80,256]{2,1,0:T(8,128)(2,1)} %get-tuple-element.116) | copy-start | bytes 1966084
  135.9 9.6 %copy-start.3 = (f32[16,32,128]{2,1,0:T(8,128)S(1)}, f32[16,32,128]{2,1,0:T(8,128)}, u32[]{:S(2)}) copy-start(f32[16,32,128]{2,1,0:T(8,128)} %get-tuple-element.41) | copy-start | bytes 786436
  135.9 9.6 %copy-start.2 = (f32[16,32,128]{2,1,0:T(8,128)S(1)}, f32[16,32,128]{2,1,0:T(8,128)}, u32[]{:S(2)}) copy-start(f32[16,32,128]{2,1,0:T(8,128)} %get-tuple-element.40) | copy-start | bytes 786436
  138.2 29.1 %all-to-all-start.4 = ((bf16[16,160,256]{2,1,0:T(8,128)(2,1)}), bf16[16,160,256]{2,1,0:T(8,128)(2,1)S(1)}, u32[]{:S(2)}, u32[]{:S(2)}) async-start(bf16[16,160,256]{2,1,0:T(8,128)(2,1)} %pad_maximum_fusion.3), calls=%async_computation.4 | async-start | bytes 2621440 | tf_op jit(solution)/shard_map/all_to_all | solution.py:135
  187.6 2.7 copy-start.1
  187.6 2.7 %copy-start = (f32[16,32,128]{2,1,0:T(8,128)S(1)}, f32[16,32,128]{2,1,0:T(8,128)}, u32[]{:S(2)}) copy-start(f32[16,32,128]{2,1,0:T(8,128)} %get-tuple-element.42) | copy-start | bytes 786436
  187.7 2.8 %copy-start.10 = (bf16[16,5,16,256]{3,2,1,0:T(8,128)(2,1)S(1)}, bf16[16,5,16,256]{3,2,1,0:T(8,128)(2,1)}, u32[]{:S(2)}) copy-start(bf16[16,5,16,256]{3,2,1,0:T(8,128)(2,1)} %get-tuple-element.39) | copy-start | bytes 1966084
  225.8 18.2 %all-to-all-start.5 = ((bf16[16,80,256]{2,1,0:T(8,128)(2,1)}), bf16[16,80,256]{2,1,0:T(8,128)(2,1)}, u32[]{:S(2)}, u32[]{:S(2)}) async-start(bf16[16,80,256]{2,1,0:T(8,128)(2,1)} %bitcast.25), calls=%async_computation.5 | async-start | bytes 1310720 | tf_op jit(solution)/shard_map/all_to_all | solution.py:135
  239.4 9.0 %copy-start.4 = (bf16[1,16,80,256]{3,2,1,0:T(8,128)(2,1)S(1)}, bf16[1,16,80,256]{3,2,1,0:T(8,128)(2,1)}, u32[]{:S(2)}) copy-start(bf16[1,16,80,256]{3,2,1,0:T(8,128)(2,1)} %get-tuple-element.118) | copy-start | bytes 1966084
  239.4 9.0 %copy-start.5 = (bf16[1,16,80,256]{3,2,1,0:T(8,128)(2,1)S(1)}, bf16[1,16,80,256]{3,2,1,0:T(8,128)(2,1)}, u32[]{:S(2)}) copy-start(bf16[1,16,80,256]{3,2,1,0:T(8,128)(2,1)} %get-tuple-element.120) | copy-start | bytes 1966084
  244.0 26.9 %all-to-all-start.7 = ((bf16[8,32,2048]{2,1,0:T(8,128)(2,1)}), bf16[8,32,2048]{2,1,0:T(8,128)(2,1)}, u32[]{:S(2)}, u32[]{:S(2)}) async-start(bf16[8,32,2048]{2,1,0:T(8,128)(2,1)} %copy.151), calls=%async_computation.7 | async-start | bytes 2097152 | tf_op jit(solution)/shard_map/all_to_all | solution.py:239

commit v5 on v3

--- a/solution.py
+++ b/solution.py
@@ -109,6 +109,15 @@
     )(anc_mask, packed, packed, packed, packed, anc_rows, anc_rows)
 
 
+def seg_shift(blocks, seg_here, seg_count):
+    got = [jnp.take(blocks, seg_here, axis=0)]
+    for shift in range(1, seg_count):
+        piece = jnp.take(blocks, (seg_here + shift) % seg_count, axis=0)
+        pairs = [(i, (i + shift) % seg_count) for i in range(seg_count)]
+        got.append(lax.ppermute(piece, "seg", pairs))
+    return jnp.stack(got, axis=0)
+
+
 def on_device(queries, leaf_keys, leaf_values, inner_keys, inner_values, out_grad, ancestors, depths):
     seg_count = lax.axis_size("seg")
     leaf_count = lax.axis_size("leaf")
@@ -142,11 +151,13 @@
     outgoing = jnp.einsum("gs,src->grc", serve_pick, stored, preferred_element_type=jnp.float32).astype(
         jnp.bfloat16
     )
-    arrived = lax.all_to_all(outgoing, "seg", split_axis=0, concat_axis=0, tiled=True)
+    arrived_by_shift = seg_shift(outgoing, seg_here, seg_count)
     my_owners = jnp.take(owners, seg_here, axis=0)
     my_alive = jnp.take(alive_levels, seg_here, axis=0)
     ancestor_rows = jnp.where(
-        my_alive[:, None, None], jnp.take(arrived, my_owners, axis=0), jnp.zeros((), jnp.bfloat16)
+        my_alive[:, None, None],
+        jnp.take(arrived_by_shift, (seg_here - my_owners) % seg_count, axis=0),
+        jnp.zeros((), jnp.bfloat16),
     )
 
     def to_heads(x, width):
@@ -202,7 +213,8 @@
     homeward = jnp.einsum("ok,krc->orc", homeward_pick, part_round, preferred_element_type=jnp.float32).astype(
         jnp.bfloat16
     )
-    returned = lax.all_to_all(homeward, "seg", split_axis=0, concat_axis=0, tiled=True)
+    returned_by_shift = seg_shift(homeward, seg_here, seg_count)
+    returned = jnp.take(returned_by_shift, (seg_here - seg_ids) % seg_count, axis=0)
     collected = jnp.einsum("gs,grc->src", serve_pick, returned, preferred_element_type=jnp.float32).astype(
         jnp.bfloat16
     )

time: 257 us -> 259 us (level)
  waiting for transfers between devices: 85.6 us -> 56 us
  local copies, waits for them, and re-layouts: 32.4 us -> 44.5 us
  starting transfers between devices: 36.2 us -> 47 us
  blocking collectives: 20.1 us -> 25.9 us
  other arithmetic: 9.64 us -> 13.5 us
    all_to_all x2 -> x1, waiting for transfers between devices: 22.6 us -> 0.01 us  [on_device(): lax.all_to_all(packed[:, chunk], 'leaf', split_axis=0, concat_axis=0, til...]
    ppermute x0 -> x14, starting transfers between devices: none -> 16.9 us  [seg_shift(): got.append(lax.ppermute(piece, 'seg', pairs))]
    all_to_all x2, waiting for transfers between devices: 35.1 us -> 21.9 us  [on_device(): lax.all_to_all(back, 'leaf', split_axis=0, concat_axis=0, tiled=True)]
    unnamed x43 -> x77, local copies, waits for them, and re-layouts: 7.65 us -> 19.8 us
    all_to_all x2 -> x1, starting transfers between devices: 11.9 us -> 3.89 us  [on_device(): lax.all_to_all(packed[:, chunk], 'leaf', split_axis=0, concat_axis=0, til...]
    select_n x2 -> x6, other arithmetic: 0.13 us -> 6 us  [the longest x2 5.68 us: seg_shift(): piece = jnp.take(blocks, (seg_here + shift) % seg_count, axis=0)]
    all_to_all x1, blocking collectives: 20.1 us -> 25.9 us  [on_device(): lax.all_to_all(packed[:, chunk], 'leaf', split_axis=0, concat_axis=0, til...]
    ppermute x0 -> x14, waiting for transfers between devices: none -> 3.97 us  [seg_shift(): got.append(lax.ppermute(piece, 'seg', pairs))]
  transfers between devices with their start and end apart: 7 -> 19, of which waited for: 6 -> 6; matrix products, arithmetic and copies ran while one was open for 12% -> 12% of each run, Pallas kernels for 13% -> 13%
where the time goes in v5:
time: 259 us; the launch traced here: 258 us
  Pallas kernels  67.9 us (26%)
  waiting for transfers between devices  56 us (22%)
  starting transfers between devices  47 us (18%)
  local copies, waits for them, and re-layouts  44.5 us (17%)
  blocking collectives  25.9 us (10%)
  other arithmetic  13.5 us (5%)
    pallas_call x2, Pallas kernels, attend_all(): pl.pallas_call(attend_kernel, grid=grid, in_specs=[maskspec, qspec, gspec...  67.9 us
    all_to_all x1, blocking collectives, on_device(): lax.all_to_all(packed[:, chunk], 'leaf', split_axis=0, concat_axis=0, til...  25.9 us
    all_to_all x2, waiting for transfers between devices, on_device(): lax.all_to_all(back, 'leaf', split_axis=0, concat_axis=0, tiled=True)  21.9 us
    unnamed x77, local copies, waits for them, and re-layouts  19.8 us
    all_to_all x1, waiting for transfers between devices, on_device(): lax.all_to_all(anc_send, 'leaf', split_axis=0, concat_axis=0, tiled=True)  17 us
    ppermute x14, starting transfers between devices, seg_shift(): got.append(lax.ppermute(piece, 'seg', pairs))  16.9 us
    all_to_all x1, waiting for transfers between devices, on_device(): lax.all_to_all(anc_back, 'leaf', split_axis=0, concat_axis=0, tiled=True)  13.1 us
    all_to_all x2, starting transfers between devices, on_device(): lax.all_to_all(back, 'leaf', split_axis=0, concat_axis=0, tiled=True)  10.9 us
  transfers between devices with their start and end apart: 19, of which 6 were waited for; matrix products, arithmetic and copies ran while one was open for 12% of the time, Pallas kernels for 13%

profile of v5, /device:TPU:0, one launch (start us, length us, event | category | flops | bytes accessed | tf_op | source)
XLA Modules:
  0.0 258.1 jit_solution(140873947131194805)
XLA Ops:
  5.0 2.8 %broadcast_select_fusion.2 = (bf16[1,32,2048]{2,0,1:T(2,128)(2,1)S(1)}, bf16[1,32,2048]{2,0,1:T(2,128)(2,1)S(1)}, bf16[1,32,2048]{2,0,1:T(2,128)(2,1)S(1)}, bf16...) fusion(pred[]{:T(512)S(6)} %and.195, ...), kind=kLoop, calls=%fused_computation.28 | loop fusion | flops 524288 | bytes 2097192 | tf_op jit(solution)/shard_map/jit(_take)/select_n | solution.py:115
  8.1 1.7 collective-permute-start.1
  9.8 2.2 collective-permute-start.2
  12.1 2.1 collective-permute-start.3
  14.2 1.7 collective-permute-start.4
  19.9 1.5 collective-permute-start.5
  26.3 1.8 gather_fusion
  29.7 8.2 %all-to-all-start.1 = ((bf16[16,4,32,256]{3,2,1,0:T(8,128)(2,1)}), bf16[16,4,32,256]{3,2,1,0:T(8,128)(2,1)}, u32[]{:S(2)}, u32[]{:S(2)}) async-start(bf16[16,4,32,256]{3,2,1,0:T(8,128)(2,1)} %bitcast.196), calls=%async_computation.1 | async-start | bytes 2097152 | tf_op jit(solution)/shard_map/all_to_all | solution.py:177
  39.7 17.0 %all-to-all-done.1 = bf16[16,4,32,256]{3,2,1,0:T(8,128)(2,1)} async-done(((bf16[16,4,32,256]{3,2,1,0:T(8,128)(2,1)}), bf16[16,4,32,256]{3,2,1,0:T(8,128)(2,1)}, u32[]{:S(2)}, u32[]{:S(2)}) %all-to-all-start.1) | async-done | bytes 1048608 | tf_op jit(solution)/shard_map/all_to_all | solution.py:177
  56.7 25.9 %all_to_all.30 = bf16[16,32,1536]{2,1,0:T(8,128)(2,1)} all-to-all(bf16[16,32,1536]{2,1,0:T(8,128)(2,1)S(1)} %get-tuple-element.137), channel_id=1, replica_groups=mesh['seg'=8,'leaf'=16] {'leaf'}, dimensions={0} | all-to-all | bytes 3145728 | tf_op jit(solution)/shard_map/all_to_all | solution.py:184
  82.7 3.9 %all-to-all-start.3 = ((bf16[16,32,1536]{2,1,0:T(8,128)(2,1)}), bf16[16,32,1536]{2,1,0:T(8,128)(2,1)S(1)}, u32[]{:S(2)}, u32[]{:S(2)}) async-start(bf16[16,32,1536]{2,1,0:T(8,128)(2,1)} %get-tuple-element.136), calls=%async_computation.3 | async-start | bytes 3145728 | tf_op jit(solution)/shard_map/all_to_all | solution.py:184
  87.2 2.3 copy.225
  89.5 33.9 %shard_map.127 = (bf16[1,512,640]{2,1,0:T(8,128)(2,1)}, bf16[1,512,640]{2,1,0:T(8,128)(2,1)}, f32[1,512,128]{2,1,0:T(8,128)}, f32[1,512,128]{2,1,0:T(8,128)}, f32[2048,128]{1,0:T(8,128)}, /*index=5*/f32[2048,128]{1,0:T(8,128)}) custom-call(f32[1,2048]{1,0:T(1,128)} %bitcast.227, bf16[1,512,1536]{2,1,0:T(8,128)(2,1)} %bitcast.183, ...), custom_call_target="tpu_custom_call" | custom-call | tf_op jit(solution)/shard_map/pallas_call | solution.py:101
  124.6 34.0 %shard_map.128 = (bf16[1,512,640]{2,1,0:T(8,128)(2,1)}, bf16[1,512,640]{2,1,0:T(8,128)(2,1)}, f32[1,512,128]{2,1,0:T(8,128)}, f32[1,512,128]{2,1,0:T(8,128)}, f32[2048,128]{1,0:T(8,128)}, /*index=5*/f32[2048,128]{1,0:T(8,128)}) custom-call(f32[1,2048]{1,0:T(1,128)} %bitcast.228, bf16[1,512,1536]{2,1,0:T(8,128)(2,1)} %bitcast.179, ...), custom_call_target="tpu_custom_call" | custom-call | tf_op jit(solution)/shard_map/pallas_call | solution.py:101
  158.6 2.3 pad_maximum_fusion.1
  162.3 7.1 %all-to-all-start.5 = ((bf16[16,4,32,256]{3,2,1,0:T(8,128)(2,1)}), bf16[16,4,32,256]{3,2,1,0:T(8,128)(2,1)S(1)}, u32[]{:S(2)}, u32[]{:S(2)}) async-start(bf16[16,4,32,256]{3,2,1,0:T(8,128)(2,1)} %fusion.1), calls=%async_computation.5 | async-start | bytes 2097152 | tf_op jit(solution)/shard_map/all_to_all | solution.py:205
  172.3 13.1 %all-to-all-done.5 = bf16[16,4,32,256]{3,2,1,0:T(8,128)(2,1)S(1)} async-done(((bf16[16,4,32,256]{3,2,1,0:T(8,128)(2,1)}), bf16[16,4,32,256]{3,2,1,0:T(8,128)(2,1)S(1)}, u32[]{:S(2)}, u32[]{:S(2)}) %all-to-all-start.5) | async-done | bytes 1048608 | tf_op jit(solution)/shard_map/all_to_all | solution.py:205
  185.4 3.9 %all-to-all-start.2 = ((bf16[16,32,1536]{2,1,0:T(8,128)(2,1)}), bf16[16,32,1536]{2,1,0:T(8,128)(2,1)S(1)}, u32[]{:S(2)}, u32[]{:S(2)}) async-start(bf16[16,32,1536]{2,1,0:T(8,128)(2,1)} %bitcast.24), calls=%async_computation.2 | async-start | bytes 3145728 | tf_op jit(solution)/shard_map/all_to_all | solution.py:191
  190.8 2.8 %broadcast_select_fusion.1 = (bf16[1,32,2048]{2,0,1:T(2,128)(2,1)S(1)}, bf16[1,32,2048]{2,0,1:T(2,128)(2,1)S(1)}, bf16[1,32,2048]{2,0,1:T(2,128)(2,1)S(1)}, bf16...) fusion(pred[]{:T(512)S(6)} %and.195, ...), kind=kLoop, calls=%fused_computation.27 | loop fusion | flops 524288 | bytes 2097192 | tf_op jit(solution)/shard_map/jit(_take)/select_n | solution.py:115
  195.6 2.6 collective-permute-start.9
  198.2 1.7 collective-permute-start.10
  200.0 2.0 collective-permute-start.11
  204.1 1.5 collective-permute-done.9
  206.3 2.2 collective-permute-done.10
  211.2 1.8 gather_fusion.1
  213.0 7.0 %all-to-all-start.4 = ((bf16[16,32,1536]{2,1,0:T(8,128)(2,1)}), bf16[16,32,1536]{2,1,0:T(8,128)(2,1)}, u32[]{:S(2)}, u32[]{:S(2)}) async-start(bf16[16,32,1536]{2,1,0:T(8,128)(2,1)} %bitcast.28), calls=%async_computation.4 | async-start | bytes 3145728 | tf_op jit(solution)/shard_map/all_to_all | solution.py:191
  222.6 2.3 copy_dynamic-update-slice_fusion.1
  224.9 21.9 %all-to-all-done.4 = bf16[16,32,1536]{2,1,0:T(8,128)(2,1)} async-done(((bf16[16,32,1536]{2,1,0:T(8,128)(2,1)}), bf16[16,32,1536]{2,1,0:T(8,128)(2,1)}, u32[]{:S(2)}, u32[]{:S(2)}) %all-to-all-start.4) | async-done | bytes 1572896 | tf_op jit(solution)/shard_map/all_to_all | solution.py:191
  246.8 2.3 copy_dynamic-update-slice_fusion
  249.1 1.8 slice_bitcast_fusion.2
  251.7 3.3 %reshape.255 = bf16[4,32,5120]{2,1,0:T(8,128)(2,1)} reshape(bf16[2,2,32,8,640]{4,3,2,1,0:T(8,128)(2,1)} %get-tuple-element.135) | data formatting | bytes 2621440 | tf_op jit(solution)/shard_map/reshape | solution.py:197
  255.0 1.4 reshape.256
  (144 shorter events, 36.6 us)
Async XLA Ops:
  7.8 9.0 %copy-start.16 = (bf16[4,32,1024]{2,1,0:T(8,128)(2,1)S(1)}, bf16[4,32,1024]{2,1,0:T(8,128)(2,1)}, u32[]{:S(2)}) copy-start(bf16[4,32,1024]{2,1,0:T(8,128)(2,1)} %param.12) | copy-start | bytes 786436
  7.8 9.1 %copy-start.17 = (bf16[4,32,1024]{2,1,0:T(8,128)(2,1)S(1)}, bf16[4,32,1024]{2,1,0:T(8,128)(2,1)}, u32[]{:S(2)}) copy-start(bf16[4,32,1024]{2,1,0:T(8,128)(2,1)} %param.11) | copy-start | bytes 786436
  7.9 9.9 %copy-start.3 = (bf16[4,32,5120]{2,1,0:T(8,128)(2,1)S(1)}, bf16[4,32,5120]{2,1,0:T(8,128)(2,1)}, u32[]{:S(2)}) copy-start(bf16[4,32,5120]{2,1,0:T(8,128)(2,1)} %param.15) | copy-start | bytes 3932164
  7.9 12.0 %collective-permute-start = (bf16[32,2048]{1,0:T(8,128)(2,1)S(1)}, bf16[32,2048]{1,0:T(8,128)(2,1)S(1)}, u32[]{:S(2)}, u32[]{:S(2)}) collective-permute-start(bf16[32,2048]{1,0:T(8,128)(2,1)S(1)} %bitcast.217), channel_id=1, source_target_pairs={{0,16},{16,32},{32,48},{48,64},{64,80},{80,96},{96,112},{112,0},{1... | collective-permute-start | bytes 393224 | tf_op jit(solution)/shard_map/ppermute | solution.py:117
  8.1 14.0 %collective-permute-start.1 = (bf16[32,2048]{1,0:T(8,128)(2,1)S(1)}, bf16[32,2048]{1,0:T(8,128)(2,1)S(1)}, u32[]{:S(2)}, u32[]{:S(2)}) collective-permute-start(bf16[32,2048]{1,0:T(8,128)(2,1)S(1)} %bitcast.216), channel_id=1, source_target_pairs={{0,32},{16,48},{32,64},{48,80},{64,96},{80,112},{96,0},{112,16},{1... | collective-permute-start | bytes 393224 | tf_op jit(solution)/shard_map/ppermute | solution.py:117
  9.8 13.0 %collective-permute-start.2 = (bf16[32,2048]{1,0:T(8,128)(2,1)S(1)}, bf16[32,2048]{1,0:T(8,128)(2,1)S(1)}, u32[]{:S(2)}, u32[]{:S(2)}) collective-permute-start(bf16[32,2048]{1,0:T(8,128)(2,1)S(1)} %bitcast.215), channel_id=1, source_target_pairs={{0,48},{16,64},{32,80},{48,96},{64,112},{80,0},{96,16},{112,32},{1... | collective-permute-start | bytes 393224 | tf_op jit(solution)/shard_map/ppermute | solution.py:117
  12.1 11.4 %collective-permute-start.3 = (bf16[32,2048]{1,0:T(8,128)(2,1)S(1)}, bf16[32,2048]{1,0:T(8,128)(2,1)S(1)}, u32[]{:S(2)}, u32[]{:S(2)}) collective-permute-start(bf16[32,2048]{1,0:T(8,128)(2,1)S(1)} %bitcast.214), channel_id=1, source_target_pairs={{0,64},{16,80},{32,96},{48,112},{64,0},{80,16},{96,32},{112,48},{1... | collective-permute-start | bytes 393224 | tf_op jit(solution)/shard_map/ppermute | solution.py:117
  14.2 9.9 %collective-permute-start.4 = (bf16[32,2048]{1,0:T(8,128)(2,1)S(1)}, bf16[32,2048]{1,0:T(8,128)(2,1)S(1)}, u32[]{:S(2)}, u32[]{:S(2)}) collective-permute-start(bf16[32,2048]{1,0:T(8,128)(2,1)S(1)} %bitcast.213), channel_id=1, source_target_pairs={{0,80},{16,96},{32,112},{48,0},{64,16},{80,32},{96,48},{112,64},{1... | collective-permute-start | bytes 393224 | tf_op jit(solution)/shard_map/ppermute | solution.py:117
  19.9 5.0 %collective-permute-start.5 = (bf16[32,2048]{1,0:T(8,128)(2,1)S(1)}, bf16[32,2048]{1,0:T(8,128)(2,1)S(1)}, u32[]{:S(2)}, u32[]{:S(2)}) collective-permute-start(bf16[32,2048]{1,0:T(8,128)(2,1)S(1)} %bitcast.219), channel_id=1, source_target_pairs={{0,96},{16,112},{32,0},{48,16},{64,32},{80,48},{96,64},{112,80},{1... | collective-permute-start | bytes 393224 | tf_op jit(solution)/shard_map/ppermute | solution.py:117
  22.1 3.5 %collective-permute-start.6 = (bf16[32,2048]{1,0:T(8,128)(2,1)S(1)}, bf16[32,2048]{1,0:T(8,128)(2,1)S(1)}, u32[]{:S(2)}, u32[]{:S(2)}) collective-permute-start(bf16[32,2048]{1,0:T(8,128)(2,1)S(1)} %bitcast.218), channel_id=1, source_target_pairs={{0,112},{16,0},{32,16},{48,32},{64,48},{80,64},{96,80},{112,96},{1... | collective-permute-start | bytes 393224 | tf_op jit(solution)/shard_map/ppermute | solution.py:117
  28.6 9.3 %copy-start.5 = (bf16[8,2,2,32,128]{4,3,1,0,2:T(8,128)(2,1)S(1)}, bf16[8,2,2,32,128]{4,3,1,0,2:T(8,128)(2,1)}, u32[]{:S(2)}) copy-start(bf16[8,2,2,32,128]{4,3,1,0,2:T(8,128)(2,1)} %copy.220) | copy-start | bytes 786436
  29.7 27.0 %all-to-all-start.1 = ((bf16[16,4,32,256]{3,2,1,0:T(8,128)(2,1)}), bf16[16,4,32,256]{3,2,1,0:T(8,128)(2,1)}, u32[]{:S(2)}, u32[]{:S(2)}) async-start(bf16[16,4,32,256]{3,2,1,0:T(8,128)(2,1)} %bitcast.196), calls=%async_computation.1 | async-start | bytes 2097152 | tf_op jit(solution)/shard_map/all_to_all | solution.py:177
  82.7 40.7 %all-to-all-start.3 = ((bf16[16,32,1536]{2,1,0:T(8,128)(2,1)}), bf16[16,32,1536]{2,1,0:T(8,128)(2,1)S(1)}, u32[]{:S(2)}, u32[]{:S(2)}) async-start(bf16[16,32,1536]{2,1,0:T(8,128)(2,1)} %get-tuple-element.136), calls=%async_computation.3 | async-start | bytes 3145728 | tf_op jit(solution)/shard_map/all_to_all | solution.py:184
  124.6 34.0 %copy-start.7 = (f32[2048,128]{1,0:T(8,128)S(1)}, f32[2048,128]{1,0:T(8,128)}, u32[]{:S(2)}) copy-start(f32[2048,128]{1,0:T(8,128)} %get-tuple-element.27) | copy-start | bytes 3145732
  162.2 7.2 %copy-start.13 = (f32[1,512,128]{2,1,0:T(8,128)S(1)}, f32[1,512,128]{2,1,0:T(8,128)}, u32[]{:S(2)}) copy-start(f32[1,512,128]{2,1,0:T(8,128)} %get-tuple-element.22) | copy-start | bytes 786436
  162.2 7.2 %copy-start.12 = (f32[1,512,128]{2,1,0:T(8,128)S(1)}, f32[1,512,128]{2,1,0:T(8,128)}, u32[]{:S(2)}) copy-start(f32[1,512,128]{2,1,0:T(8,128)} %get-tuple-element.21) | copy-start | bytes 786436
  162.2 7.3 %copy-start.15 = (f32[1,512,128]{2,1,0:T(8,128)S(1)}, f32[1,512,128]{2,1,0:T(8,128)}, u32[]{:S(2)}) copy-start(f32[1,512,128]{2,1,0:T(8,128)} %get-tuple-element.26) | copy-start | bytes 786436
  162.2 7.3 %copy-start.14 = (f32[1,512,128]{2,1,0:T(8,128)S(1)}, f32[1,512,128]{2,1,0:T(8,128)}, u32[]{:S(2)}) copy-start(f32[1,512,128]{2,1,0:T(8,128)} %get-tuple-element.25) | copy-start | bytes 786436
  162.2 7.4 %copy-start.8 = (bf16[1,512,640]{2,1,0:T(8,128)(2,1)S(1)}, bf16[1,512,640]{2,1,0:T(8,128)(2,1)}, u32[]{:S(2)}) copy-start(bf16[1,512,640]{2,1,0:T(8,128)(2,1)} %get-tuple-element.19) | copy-start | bytes 1966084
  162.3 7.4 %copy-start.9 = (bf16[1,512,640]{2,1,0:T(8,128)(2,1)S(1)}, bf16[1,512,640]{2,1,0:T(8,128)(2,1)}, u32[]{:S(2)}) copy-start(bf16[1,512,640]{2,1,0:T(8,128)(2,1)} %get-tuple-element.20) | copy-start | bytes 1966084
  162.3 23.2 %all-to-all-start.5 = ((bf16[16,4,32,256]{3,2,1,0:T(8,128)(2,1)}), bf16[16,4,32,256]{3,2,1,0:T(8,128)(2,1)S(1)}, u32[]{:S(2)}, u32[]{:S(2)}) async-start(bf16[16,4,32,256]{3,2,1,0:T(8,128)(2,1)} %fusion.1), calls=%async_computation.5 | async-start | bytes 2097152 | tf_op jit(solution)/shard_map/all_to_all | solution.py:205
  185.4 27.6 %all-to-all-start.2 = ((bf16[16,32,1536]{2,1,0:T(8,128)(2,1)}), bf16[16,32,1536]{2,1,0:T(8,128)(2,1)S(1)}, u32[]{:S(2)}, u32[]{:S(2)}) async-start(bf16[16,32,1536]{2,1,0:T(8,128)(2,1)} %bitcast.24), calls=%async_computation.2 | async-start | bytes 3145728 | tf_op jit(solution)/shard_map/all_to_all | solution.py:191
  193.7 8.5 %collective-permute-start.7 = (bf16[32,2048]{1,0:T(8,128)(2,1)S(1)}, bf16[32,2048]{1,0:T(8,128)(2,1)S(1)}, u32[]{:S(2)}, u32[]{:S(2)}) collective-permute-start(bf16[32,2048]{1,0:T(8,128)(2,1)S(1)} %bitcast.226), channel_id=1, source_target_pairs={{0,16},{16,32},{32,48},{48,64},{64,80},{80,96},{96,112},{112,0},{1... | collective-permute-start | bytes 393224 | tf_op jit(solution)/shard_map/ppermute | solution.py:117
  194.5 8.9 %collective-permute-start.8 = (bf16[32,2048]{1,0:T(8,128)(2,1)S(1)}, bf16[32,2048]{1,0:T(8,128)(2,1)S(1)}, u32[]{:S(2)}, u32[]{:S(2)}) collective-permute-start(bf16[32,2048]{1,0:T(8,128)(2,1)S(1)} %bitcast.225), channel_id=1, source_target_pairs={{0,32},{16,48},{32,64},{48,80},{64,96},{80,112},{96,0},{112,16},{1... | collective-permute-start | bytes 393224 | tf_op jit(solution)/shard_map/ppermute | solution.py:117
  195.6 10.0 %collective-permute-start.9 = (bf16[32,2048]{1,0:T(8,128)(2,1)S(1)}, bf16[32,2048]{1,0:T(8,128)(2,1)S(1)}, u32[]{:S(2)}, u32[]{:S(2)}) collective-permute-start(bf16[32,2048]{1,0:T(8,128)(2,1)S(1)} %bitcast.224), channel_id=1, source_target_pairs={{0,48},{16,64},{32,80},{48,96},{64,112},{80,0},{96,16},{112,32},{1... | collective-permute-start | bytes 393224 | tf_op jit(solution)/shard_map/ppermute | solution.py:117
  198.2 10.3 %collective-permute-start.10 = (bf16[32,2048]{1,0:T(8,128)(2,1)S(1)}, bf16[32,2048]{1,0:T(8,128)(2,1)S(1)}, u32[]{:S(2)}, u32[]{:S(2)}) collective-permute-start(bf16[32,2048]{1,0:T(8,128)(2,1)S(1)} %bitcast.223), channel_id=1, source_target_pairs={{0,64},{16,80},{32,96},{48,112},{64,0},{80,16},{96,32},{112,48},{1... | collective-permute-start | bytes 393224 | tf_op jit(solution)/shard_map/ppermute | solution.py:117
  200.0 9.1 %collective-permute-start.11 = (bf16[32,2048]{1,0:T(8,128)(2,1)S(1)}, bf16[32,2048]{1,0:T(8,128)(2,1)S(1)}, u32[]{:S(2)}, u32[]{:S(2)}) collective-permute-start(bf16[32,2048]{1,0:T(8,128)(2,1)S(1)} %bitcast.222), channel_id=1, source_target_pairs={{0,80},{16,96},{32,112},{48,0},{64,16},{80,32},{96,48},{112,64},{1... | collective-permute-start | bytes 393224 | tf_op jit(solution)/shard_map/ppermute | solution.py:117
  202.2 7.6 %collective-permute-start.12 = (bf16[32,2048]{1,0:T(8,128)(2,1)S(1)}, bf16[32,2048]{1,0:T(8,128)(2,1)S(1)}, u32[]{:S(2)}, u32[]{:S(2)}) collective-permute-start(bf16[32,2048]{1,0:T(8,128)(2,1)S(1)} %bitcast.221), channel_id=1, source_target_pairs={{0,96},{16,112},{32,0},{48,16},{64,32},{80,48},{96,64},{112,80},{1... | collective-permute-start | bytes 393224 | tf_op jit(solution)/shard_map/ppermute | solution.py:117
  203.4 7.1 %collective-permute-start.13 = (bf16[32,2048]{1,0:T(8,128)(2,1)S(1)}, bf16[32,2048]{1,0:T(8,128)(2,1)S(1)}, u32[]{:S(2)}, u32[]{:S(2)}) collective-permute-start(bf16[32,2048]{1,0:T(8,128)(2,1)S(1)} %bitcast.220), channel_id=1, source_target_pairs={{0,112},{16,0},{32,16},{48,32},{64,48},{80,64},{96,80},{112,96},{1... | collective-permute-start | bytes 393224 | tf_op jit(solution)/shard_map/ppermute | solution.py:117
  213.0 7.2 %copy-start.1 = (bf16[16,32,1536]{2,1,0:T(8,128)(2,1)}, bf16[16,32,1536]{2,1,0:T(8,128)(2,1)S(1)}, u32[]{:S(2)}) copy-start(bf16[16,32,1536]{2,1,0:T(8,128)(2,1)S(1)} %all-to-all-done.2) | copy-start | bytes 4718596
  213.0 33.8 %all-to-all-start.4 = ((bf16[16,32,1536]{2,1,0:T(8,128)(2,1)}), bf16[16,32,1536]{2,1,0:T(8,128)(2,1)}, u32[]{:S(2)}, u32[]{:S(2)}) async-start(bf16[16,32,1536]{2,1,0:T(8,128)(2,1)} %bitcast.28), calls=%async_computation.4 | async-start | bytes 3145728 | tf_op jit(solution)/shard_map/all_to_all | solution.py:191
  251.7 4.8 %copy-start.6 = (bf16[2,2,32,8,128]{4,3,2,1,0:T(8,128)(2,1)S(1)}, bf16[2,2,32,8,128]{4,3,2,1,0:T(8,128)(2,1)}, u32[]{:S(2)}) copy-start(bf16[2,2,32,8,128]{4,3,2,1,0:T(8,128)(2,1)} %get-tuple-element.133) | copy-start | bytes 786436
  (5 other events, 8.8 us)

commit v6 on v3

--- a/solution.py
+++ b/solution.py
@@ -82,7 +82,7 @@
         dka_ref[...] = dka_ref[...] * scale
 
 
-def attend_all(anc_mask, packed, anc_rows, heads, block_rows=256):
+def attend_all(anc_mask, packed, anc_rows, heads, block_rows=512):
     leaves, seg_len, _ = packed.shape
     anc = anc_rows.shape[0]
     grid = (leaves, heads, seg_len // block_rows)
@@ -177,7 +177,19 @@
         anc_partial = part if anc_partial is None else anc_partial + part
         back = jnp.concatenate([res, dq, dko.astype(jnp.bfloat16), dvo.astype(jnp.bfloat16)], axis=2)
         back = back.reshape(leaf_count, rows_here, back.shape[2])
-        homes.append(lax.all_to_all(back, "leaf", split_axis=0, concat_axis=0, tiled=True))
+        if chunk < pair_leaves - 1:
+            homes.append(lax.all_to_all(back, "leaf", split_axis=0, concat_axis=0, tiled=True))
+    width = back.shape[2]
+    anc_back = anc_partial.astype(jnp.bfloat16).reshape(levels, leaf_count, rows_here, 2 * HD).transpose(1, 2, 0, 3)
+    tail = lax.all_to_all(
+        jnp.concatenate([back, anc_back.reshape(leaf_count, rows_here, levels * 2 * HD)], axis=2),
+        "leaf",
+        split_axis=0,
+        concat_axis=0,
+        tiled=True,
+    )
+    homes.append(tail[..., :width])
+    anc_home = tail[..., width:].reshape(leaf_count, rows_here, levels, 2 * HD).transpose(0, 2, 1, 3)
     home = jnp.stack(homes, axis=1)
     home = home.reshape(kv_heads, pair_count, pair_leaves, rows_here, home.shape[3])
 
@@ -190,8 +202,6 @@
     leaf_key_grad = to_rows(home[..., 2 * head_width : 2 * head_width + HD])
     leaf_value_grad = to_rows(home[..., 2 * head_width + HD :])
 
-    anc_back = anc_partial.astype(jnp.bfloat16).reshape(levels, leaf_count, rows_here, 2 * HD).transpose(1, 0, 2, 3)
-    anc_home = lax.all_to_all(anc_back, "leaf", split_axis=0, concat_axis=0, tiled=True)
     anc_home = anc_home.astype(jnp.float32).reshape(kv_heads, pair_count, levels, rows_here, 2 * HD).sum(axis=1)
     part_keys = anc_home[..., :HD].transpose(1, 2, 0, 3).reshape(levels, rows_here, key_width)
     part_values = anc_home[..., HD:].transpose(1, 2, 0, 3).reshape(levels, rows_here, key_width)

time: 257 us -> 252 us (0.981)
  waiting for transfers between devices: 85.6 us -> 71.2 us
  local copies, waits for them, and re-layouts: 32.4 us -> 42.9 us
  Pallas kernels: 67.8 us -> 62.8 us
  other arithmetic: 9.64 us -> 14.4 us
    all_to_all x2 -> x1, waiting for transfers between devices: 35.1 us -> 0.01 us  [on_device(): lax.all_to_all(back, 'leaf', split_axis=0, concat_axis=0, tiled=True)]
    all_to_all x1, waiting for transfers between devices: 14.4 us -> 31 us  [on_device(): lax.all_to_all(jnp.concatenate([back, anc_back.reshape(leaf_count, rows_h...]
    concatenate x0 -> x4, local copies, waits for them, and re-layouts: none -> 6.43 us  [on_device(): part = jnp.concatenate([dka, dva], axis=1)]
    unnamed x43 -> x40, local copies, waits for them, and re-layouts: 7.65 us -> 13.6 us
    pallas_call x2, Pallas kernels: 67.8 us -> 62.8 us  [attend_all(): pl.pallas_call(attend_kernel, grid=grid, in_specs=[maskspec, qspec, gspec...]
    reshape x4, local copies, waits for them, and re-layouts: 8.97 us -> 4.53 us  [to_rows(): x.transpose(1, 2, 3, 0, 4).reshape(leaf_dev, rows_here, kv_heads * width)]
    all_to_all x1, waiting for transfers between devices: 1.89 us -> 5.93 us  [on_device(): lax.all_to_all(homeward, 'seg', split_axis=0, concat_axis=0, tiled=True)]
    convert_element_type x0 -> x1, local copies, waits for them, and re-layouts: none -> 2.63 us  [on_device(): anc_home.astype(jnp.float32)]
  transfers between devices with their start and end apart: 7 -> 6, of which waited for: 6 -> 4; matrix products, arithmetic and copies ran while one was open for 12% -> 15% of each run, Pallas kernels for 13% -> 25%
where the time goes in v6:
time: 252 us; the launch traced here: 251 us
  waiting for transfers between devices  71.2 us (28%)
  Pallas kernels  62.8 us (25%)
  local copies, waits for them, and re-layouts  42.9 us (17%)
  starting transfers between devices  34.9 us (14%)
  blocking collectives  20.1 us (8%)
  other arithmetic  14.4 us (6%)
  matrix products  3.14 us (1%)
    pallas_call x2, Pallas kernels, attend_all(): pl.pallas_call(attend_kernel, grid=grid, in_specs=[maskspec, qspec, gspec...  62.8 us
    all_to_all x1, waiting for transfers between devices, on_device(): lax.all_to_all(jnp.concatenate([back, anc_back.reshape(leaf_count, rows_h...  31 us
    all_to_all x2, waiting for transfers between devices, on_device(): lax.all_to_all(packed[:, chunk], 'leaf', split_axis=0, concat_axis=0, til...  22.6 us
    all_to_all x1, blocking collectives, on_device(): lax.all_to_all(anc_send, 'leaf', split_axis=0, concat_axis=0, tiled=True)  20.1 us
    unnamed x40, local copies, waits for them, and re-layouts  13.6 us
    all_to_all x2, starting transfers between devices, on_device(): lax.all_to_all(packed[:, chunk], 'leaf', split_axis=0, concat_axis=0, til...  11.8 us
    all_to_all x1, waiting for transfers between devices, on_device(): lax.all_to_all(outgoing, 'seg', split_axis=0, concat_axis=0, tiled=True)  11.6 us
    all_to_all x1, starting transfers between devices, on_device(): lax.all_to_all(jnp.concatenate([back, anc_back.reshape(leaf_count, rows_h...  7.21 us
  transfers between devices with their start and end apart: 6, of which 4 were waited for; matrix products, arithmetic and copies ran while one was open for 15% of the time, Pallas kernels for 25%

profile of v6, /device:TPU:0, one launch (start us, length us, event | category | flops | bytes accessed | tf_op | source)
XLA Modules:
  0.0 250.5 jit_solution(17584315369972825863)
XLA Ops:
  4.8 1.5 copy.76
  6.4 4.5 %all-to-all-start.1 = ((bf16[8,32,2048]{2,1,0:T(8,128)(2,1)}), bf16[8,32,2048]{2,1,0:T(8,128)(2,1)S(1)}, u32[]{:S(2)}, u32[]{:S(2)}) async-start(bf16[8,32,2048]{2,1,0:T(8,128)(2,1)} %copy.76), calls=%async_computation.1 | async-start | bytes 2097152 | tf_op jit(solution)/shard_map/all_to_all | solution.py:145
  13.3 1.9 slice_bitcast_fusion
  15.2 11.6 %all-to-all-done.1 = bf16[8,32,2048]{2,1,0:T(8,128)(2,1)S(1)} async-done(((bf16[8,32,2048]{2,1,0:T(8,128)(2,1)}), bf16[8,32,2048]{2,1,0:T(8,128)(2,1)S(1)}, u32[]{:S(2)}, u32[]{:S(2)}) %all-to-all-start.1) | async-done | bytes 1048608 | tf_op jit(solution)/shard_map/all_to_all | solution.py:145
  26.9 8.0 %all-to-all-start = ((bf16[16,32,1536]{2,1,0:T(8,128)(2,1)}), bf16[16,32,1536]{2,1,0:T(8,128)(2,1)S(1)}, u32[]{:S(2)}, u32[]{:S(2)}) async-start(bf16[16,32,1536]{2,1,0:T(8,128)(2,1)} %get-tuple-element.83), calls=%async_computation | async-start | bytes 3145728 | tf_op jit(solution)/shard_map/all_to_all | solution.py:173
  36.4 22.6 %all-to-all-done = bf16[16,32,1536]{2,1,0:T(8,128)(2,1)S(1)} async-done(((bf16[16,32,1536]{2,1,0:T(8,128)(2,1)}), bf16[16,32,1536]{2,1,0:T(8,128)(2,1)S(1)}, u32[]{:S(2)}, u32[]{:S(2)}) %all-to-all-start) | async-done | bytes 1572896 | tf_op jit(solution)/shard_map/all_to_all | solution.py:173
  59.1 20.1 %all_to_all.35 = bf16[16,4,32,256]{3,2,1,0:T(8,128)(2,1)} all-to-all(bf16[16,4,32,256]{3,2,1,0:T(8,128)(2,1)S(1)} %bitcast.124), channel_id=1, replica_groups=mesh['seg'=8,'leaf'=16] {'leaf'}, dimensions={0} | all-to-all | bytes 2097152 | tf_op jit(solution)/shard_map/all_to_all | solution.py:166
  79.2 3.7 %all-to-all-start.4 = ((bf16[16,32,1536]{2,1,0:T(8,128)(2,1)}), bf16[16,32,1536]{2,1,0:T(8,128)(2,1)S(1)}, u32[]{:S(2)}, u32[]{:S(2)}) async-start(bf16[16,32,1536]{2,1,0:T(8,128)(2,1)} %get-tuple-element.82), calls=%async_computation.4 | async-start | bytes 3145728 | tf_op jit(solution)/shard_map/all_to_all | solution.py:173
  83.6 2.3 copy.78
  85.9 31.4 %shard_map.127 = (bf16[1,512,640]{2,1,0:T(8,128)(2,1)}, bf16[1,512,640]{2,1,0:T(8,128)(2,1)}, f32[1,512,128]{2,1,0:T(8,128)}, f32[1,512,128]{2,1,0:T(8,128)}, f32[2048,128]{1,0:T(8,128)}, /*index=5*/f32[2048,128]{1,0:T(8,128)}) custom-call(f32[1,2048]{1,0:T(1,128)} %bitcast.141, bf16[1,512,1536]{2,1,0:T(8,128)(2,1)} %bitcast.103, ...), custom_call_target="tpu_custom_call" | custom-call | tf_op jit(solution)/shard_map/pallas_call | solution.py:101
  119.2 2.6 %pad_maximum_fusion.2 = bf16[1,512,1536]{2,1,0:T(8,128)(2,1)} fusion(bf16[1,512,128]{2,1,0:T(8,128)(2,1)S(1)} %convert_element_type.60, bf16[1,512,128]{2,1,0:T(8,128)(2,1)S(1)} %convert_element_type.59, bf16[1,512,640]{2,1,0:T(8,128)(2,1)} %get-tuple-element.19, bf16[1,512,640]{2,1,0:T(8,128)(2,1)} %get-tuple-element.18), kind=kLoop, calls=%fused_computation.10 | loop fusion | flops 6291456 | bytes 3145728 | tf_op jit(solution)/shard_map/concatenate | solution.py:178
  121.8 7.2 %all-to-all-start.3 = ((bf16[16,32,1536]{2,1,0:T(8,128)(2,1)}), bf16[16,32,1536]{2,1,0:T(8,128)(2,1)S(1)}, u32[]{:S(2)}, u32[]{:S(2)}) async-start(bf16[16,32,1536]{2,1,0:T(8,128)(2,1)} %bitcast.116), calls=%async_computation.3 | async-start | bytes 3145728 | tf_op jit(solution)/shard_map/all_to_all | solution.py:181
  129.0 3.0 %copy.79 = f32[4,16,32,128]{3,0,2,1:T(4,128)} copy(f32[4,16,32,128]{3,2,1,0:T(8,128)} %bitcast.130) | data formatting | bytes 2097152 | tf_op jit(solution)/shard_map/concatenate | solution.py:176
  132.7 31.4 %shard_map.128 = (bf16[1,512,640]{2,1,0:T(8,128)(2,1)}, bf16[1,512,640]{2,1,0:T(8,128)(2,1)}, f32[1,512,128]{2,1,0:T(8,128)}, f32[1,512,128]{2,1,0:T(8,128)}, f32[2048,128]{1,0:T(8,128)}, /*index=5*/f32[2048,128]{1,0:T(8,128)}) custom-call(f32[1,2048]{1,0:T(1,128)} %bitcast.142, bf16[1,512,1536]{2,1,0:T(8,128)(2,1)} %bitcast.107, ...), custom_call_target="tpu_custom_call" | custom-call | tf_op jit(solution)/shard_map/pallas_call | solution.py:101
  166.1 2.0 copy.81
  168.9 1.8 fusion.2
  170.7 1.9 reshape.168
  172.5 1.2 pad_maximum_fusion.3
  173.8 1.7 pad_maximum_fusion.1
  176.7 7.2 %all-to-all-start.5 = ((bf16[16,32,2560]{2,1,0:T(8,128)(2,1)}), bf16[16,32,2560]{2,1,0:T(8,128)(2,1)S(1)}, u32[]{:S(2)}, u32[]{:S(2)}) async-start(bf16[16,32,2560]{2,1,0:T(8,128)(2,1)} %pad_maximum_fusion.1), calls=%async_computation.5 | async-start | bytes 5242880 | tf_op jit(solution)/shard_map/all_to_all | solution.py:184
  183.9 3.4 %copy_dynamic-update-slice_fusion.1 = bf16[8,2,2,32,1536]{4,0,3,2,1:T(8,128)(2,1)} fusion(bf16[8,2,1,32,1536]{4,3,1,0,2:T(8,128)(2,1)} %bitcast.115), kind=kLoop, calls=%fused_computation.13 | loop fusion | bytes 3145728
  187.3 31.0 %all-to-all-done.5 = bf16[16,32,2560]{2,1,0:T(8,128)(2,1)S(1)} async-done(((bf16[16,32,2560]{2,1,0:T(8,128)(2,1)}), bf16[16,32,2560]{2,1,0:T(8,128)(2,1)S(1)}, u32[]{:S(2)}, u32[]{:S(2)}) %all-to-all-start.5) | async-done | bytes 2621472 | tf_op jit(solution)/shard_map/all_to_all | solution.py:184
  219.4 2.6 %convert_element_type.64 = bf16[16,32,4,256]{3,2,1,0:T(4,128)(2,1)} reshape(bf16[16,32,1024]{2,1,0:T(8,128)(2,1)} %slice.91) | data formatting | bytes 2097152 | tf_op jit(solution)/shard_map/convert_element_type | solution.py:205
  222.0 2.1 bitcast_reduce_fusion
  225.2 1.6 copy.89
  226.7 4.2 %all-to-all-start.6 = ((bf16[8,32,2048]{2,1,0:T(8,128)(2,1)}), bf16[8,32,2048]{2,1,0:T(8,128)(2,1)}, u32[]{:S(2)}, u32[]{:S(2)}) async-start(bf16[8,32,2048]{2,1,0:T(8,128)(2,1)} %copy.89), calls=%async_computation.6 | async-start | bytes 2097152 | tf_op jit(solution)/shard_map/all_to_all | solution.py:215
  231.1 1.8 copy-done.2
  234.0 1.4 copy-done.3
  235.4 1.4 reshape.170
  239.5 1.4 reshape.169
  241.0 5.9 %all-to-all-done.6 = bf16[8,32,2048]{2,1,0:T(8,128)(2,1)} async-done(((bf16[8,32,2048]{2,1,0:T(8,128)(2,1)}), bf16[8,32,2048]{2,1,0:T(8,128)(2,1)}, u32[]{:S(2)}, u32[]{:S(2)}) %all-to-all-start.6) | async-done | bytes 1048608 | tf_op jit(solution)/shard_map/all_to_all | solution.py:215
  246.9 2.1 convolution_convert_fusion.2
  (78 shorter events, 22.8 us)
Async XLA Ops:
  4.8 6.1 %copy-start.11 = (bf16[4,32,1024]{2,1,0:T(8,128)(2,1)S(1)}, bf16[4,32,1024]{2,1,0:T(8,128)(2,1)}, u32[]{:S(2)}) copy-start(bf16[4,32,1024]{2,1,0:T(8,128)(2,1)} %param.9) | copy-start | bytes 786436
  6.4 4.7 %copy-start.12 = (bf16[4,32,1024]{2,1,0:T(8,128)(2,1)S(1)}, bf16[4,32,1024]{2,1,0:T(8,128)(2,1)}, u32[]{:S(2)}) copy-start(bf16[4,32,1024]{2,1,0:T(8,128)(2,1)} %param.10) | copy-start | bytes 786436
  6.4 4.8 %copy-start.6 = (bf16[4,32,5120]{2,1,0:T(8,128)(2,1)S(1)}, bf16[4,32,5120]{2,1,0:T(8,128)(2,1)}, u32[]{:S(2)}) copy-start(bf16[4,32,5120]{2,1,0:T(8,128)(2,1)} %param.8) | copy-start | bytes 3932164
  6.4 20.5 %all-to-all-start.1 = ((bf16[8,32,2048]{2,1,0:T(8,128)(2,1)}), bf16[8,32,2048]{2,1,0:T(8,128)(2,1)S(1)}, u32[]{:S(2)}, u32[]{:S(2)}) async-start(bf16[8,32,2048]{2,1,0:T(8,128)(2,1)} %copy.76), calls=%async_computation.1 | async-start | bytes 2097152 | tf_op jit(solution)/shard_map/all_to_all | solution.py:145
  11.2 1.3 copy-start.7
  26.9 32.1 %all-to-all-start = ((bf16[16,32,1536]{2,1,0:T(8,128)(2,1)}), bf16[16,32,1536]{2,1,0:T(8,128)(2,1)S(1)}, u32[]{:S(2)}, u32[]{:S(2)}) async-start(bf16[16,32,1536]{2,1,0:T(8,128)(2,1)} %get-tuple-element.83), calls=%async_computation | async-start | bytes 3145728 | tf_op jit(solution)/shard_map/all_to_all | solution.py:173
  59.0 20.2 %copy-start = (bf16[16,32,1536]{2,1,0:T(8,128)(2,1)}, bf16[16,32,1536]{2,1,0:T(8,128)(2,1)S(1)}, u32[]{:S(2)}) copy-start(bf16[16,32,1536]{2,1,0:T(8,128)(2,1)S(1)} %all-to-all-done) | copy-start | bytes 4718596
  79.2 42.6 %all-to-all-start.4 = ((bf16[16,32,1536]{2,1,0:T(8,128)(2,1)}), bf16[16,32,1536]{2,1,0:T(8,128)(2,1)S(1)}, u32[]{:S(2)}, u32[]{:S(2)}) async-start(bf16[16,32,1536]{2,1,0:T(8,128)(2,1)} %get-tuple-element.82), calls=%async_computation.4 | async-start | bytes 3145728 | tf_op jit(solution)/shard_map/all_to_all | solution.py:173
  121.8 10.2 %copy-start.1 = (bf16[16,32,1536]{2,1,0:T(8,128)(2,1)}, bf16[16,32,1536]{2,1,0:T(8,128)(2,1)S(1)}, u32[]{:S(2)}) copy-start(bf16[16,32,1536]{2,1,0:T(8,128)(2,1)S(1)} %all-to-all-done.4) | copy-start | bytes 4718596
  121.8 53.7 %all-to-all-start.3 = ((bf16[16,32,1536]{2,1,0:T(8,128)(2,1)}), bf16[16,32,1536]{2,1,0:T(8,128)(2,1)S(1)}, u32[]{:S(2)}, u32[]{:S(2)}) async-start(bf16[16,32,1536]{2,1,0:T(8,128)(2,1)} %bitcast.116), calls=%async_computation.3 | async-start | bytes 3145728 | tf_op jit(solution)/shard_map/all_to_all | solution.py:181
  129.0 3.0 %copy-start.8 = (f32[2048,128]{1,0:T(8,128)S(1)}, f32[2048,128]{1,0:T(8,128)}, u32[]{:S(2)}) copy-start(f32[2048,128]{1,0:T(8,128)} %get-tuple-element.27) | copy-start | bytes 3145732
  164.1 4.1 %copy-start.9 = (f32[2048,128]{1,0:T(8,128)S(1)}, f32[2048,128]{1,0:T(8,128)}, u32[]{:S(2)}) copy-start(f32[2048,128]{1,0:T(8,128)} %get-tuple-element.29) | copy-start | bytes 3145732
  166.1 2.8 %copy-start.5 = (f32[4,16,32,128]{3,0,2,1:T(4,128)S(1)}, f32[4,16,32,128]{3,0,2,1:T(4,128)}, u32[]{:S(2)}) copy-start(f32[4,16,32,128]{3,0,2,1:T(4,128)} %copy.79) | copy-start | bytes 3145732
  170.7 1.9 copy-start.10
  175.5 1.2 copy-start.4
  176.7 41.7 %all-to-all-start.5 = ((bf16[16,32,2560]{2,1,0:T(8,128)(2,1)}), bf16[16,32,2560]{2,1,0:T(8,128)(2,1)S(1)}, u32[]{:S(2)}, u32[]{:S(2)}) async-start(bf16[16,32,2560]{2,1,0:T(8,128)(2,1)} %pad_maximum_fusion.1), calls=%async_computation.5 | async-start | bytes 5242880 | tf_op jit(solution)/shard_map/all_to_all | solution.py:184
  226.7 20.2 %all-to-all-start.6 = ((bf16[8,32,2048]{2,1,0:T(8,128)(2,1)}), bf16[8,32,2048]{2,1,0:T(8,128)(2,1)}, u32[]{:S(2)}, u32[]{:S(2)}) async-start(bf16[8,32,2048]{2,1,0:T(8,128)(2,1)} %copy.89), calls=%async_computation.6 | async-start | bytes 2097152 | tf_op jit(solution)/shard_map/all_to_all | solution.py:215
  231.0 1.9 copy-start.2
  233.7 1.6 copy-start.3

commit v7 on v6

--- a/solution.py
+++ b/solution.py
@@ -153,24 +153,31 @@
         shaped = x.reshape(pair_count, pair_leaves, rows_here, kv_heads, width)
         return shaped.transpose(3, 0, 1, 2, 4).reshape(leaf_count, pair_leaves, rows_here, width)
 
-    packed = jnp.concatenate(
-        [to_heads(queries, head_width), to_heads(out_grad, head_width), to_heads(leaf_keys, HD), to_heads(leaf_values, HD)],
-        axis=3,
-    )
     anc_k = ancestor_rows[:, :, :key_width].reshape(levels, rows_here, kv_heads, HD)
     anc_v = ancestor_rows[:, :, key_width:].reshape(levels, rows_here, kv_heads, HD)
     anc_heads = jnp.concatenate([anc_k, anc_v], axis=3).transpose(2, 0, 1, 3)
     anc_send = jnp.broadcast_to(anc_heads[:, None], (kv_heads, pair_count) + anc_heads.shape[1:]).reshape(
         (leaf_count,) + anc_heads.shape[1:]
     )
-    anc_got = lax.all_to_all(anc_send, "leaf", split_axis=0, concat_axis=0, tiled=True)
-    anc_got = anc_got.transpose(1, 0, 2, 3).reshape(levels * seg_len, 2 * HD)
+    anc_cols = anc_send.transpose(0, 2, 1, 3).reshape(leaf_count, rows_here, levels * 2 * HD)
     anc_mask = jnp.repeat(my_alive, seg_len).astype(jnp.float32)[None, :]
 
+    packed = jnp.concatenate(
+        [to_heads(queries, head_width), to_heads(out_grad, head_width), to_heads(leaf_keys, HD), to_heads(leaf_values, HD)],
+        axis=3,
+    )
     homes = []
     anc_partial = None
     for chunk in range(pair_leaves):
-        got = lax.all_to_all(packed[:, chunk], "leaf", split_axis=0, concat_axis=0, tiled=True)
+        if chunk == 0:
+            first = lax.all_to_all(
+                jnp.concatenate([packed[:, 0], anc_cols], axis=2), "leaf", split_axis=0, concat_axis=0, tiled=True
+            )
+            got = first[..., : packed.shape[3]]
+            anc_got = first[..., packed.shape[3] :].reshape(leaf_count, rows_here, levels, 2 * HD)
+            anc_got = anc_got.transpose(2, 0, 1, 3).reshape(levels * seg_len, 2 * HD)
+        else:
+            got = lax.all_to_all(packed[:, chunk], "leaf", split_axis=0, concat_axis=0, tiled=True)
         got = got.reshape(1, seg_len, packed.shape[3])
         res, dq, dko, dvo, dka, dva = attend_all(anc_mask, got, anc_got, group_heads)
         part = jnp.concatenate([dka, dva], axis=1)

time: 252 us -> 249 us (0.988)
  waiting for transfers between devices: 71.2 us -> 48.8 us
  blocking collectives: 20.1 us -> 41.7 us
  starting transfers between devices: 34.9 us -> 27 us
  local copies, waits for them, and re-layouts: 42.9 us -> 47.7 us
    all_to_all x2 -> x1, waiting for transfers between devices: 22.6 us -> 0.01 us  [on_device(): lax.all_to_all(packed[:, chunk], 'leaf', split_axis=0, concat_axis=0, til...]
    all_to_all x1, blocking collectives: 20.1 us -> 41.7 us  [on_device(): lax.all_to_all(jnp.concatenate([packed[:, 0], anc_cols], axis=2), 'leaf',...]
    all_to_all x2 -> x1, starting transfers between devices: 11.8 us -> 4.02 us  [on_device(): lax.all_to_all(packed[:, chunk], 'leaf', split_axis=0, concat_axis=0, til...]
    reshape x0 -> x2, local copies, waits for them, and re-layouts: none -> 3.35 us  [the longest x1 1.79 us: on_device(): anc_send.transpose(0, 2, 1, 3)]
    slice x0 -> x3, local copies, waits for them, and re-layouts: none -> 2.72 us  [the longest x1 2.71 us: on_device(): got = first[..., :packed.shape[3]]]
    unnamed x40 -> x36, local copies, waits for them, and re-layouts: 13.6 us -> 13.6 us
  transfers between devices with their start and end apart: 6 -> 5, of which waited for: 4 -> 3; matrix products, arithmetic and copies ran while one was open for 15% -> 15% of each run, Pallas kernels for 25% -> 25%
where the time goes in v7:
time: 249 us; the launch traced here: 247 us
  Pallas kernels  62.8 us (25%)
  waiting for transfers between devices  48.8 us (20%)
  local copies, waits for them, and re-layouts  47.7 us (19%)
  blocking collectives  41.7 us (17%)
  starting transfers between devices  27 us (11%)
  other arithmetic  14.9 us (6%)
  matrix products  3.13 us (1%)
    pallas_call x2, Pallas kernels, attend_all(): pl.pallas_call(attend_kernel, grid=grid, in_specs=[maskspec, qspec, gspec...  62.8 us
    all_to_all x1, blocking collectives, on_device(): lax.all_to_all(jnp.concatenate([packed[:, 0], anc_cols], axis=2), 'leaf',...  41.7 us
    all_to_all x1, waiting for transfers between devices, on_device(): lax.all_to_all(jnp.concatenate([back, anc_back.reshape(leaf_count, rows_h...  31.1 us
    unnamed x36, local copies, waits for them, and re-layouts  13.6 us
    all_to_all x1, waiting for transfers between devices, on_device(): lax.all_to_all(outgoing, 'seg', split_axis=0, concat_axis=0, tiled=True)  11.7 us
    all_to_all x1, starting transfers between devices, on_device(): lax.all_to_all(jnp.concatenate([back, anc_back.reshape(leaf_count, rows_h...  7.22 us
    all_to_all x1, starting transfers between devices, on_device(): lax.all_to_all(back, 'leaf', split_axis=0, concat_axis=0, tiled=True)  6.98 us
    all_to_all x1, waiting for transfers between devices, on_device(): lax.all_to_all(homeward, 'seg', split_axis=0, concat_axis=0, tiled=True)  5.92 us
  transfers between devices with their start and end apart: 5, of which 3 were waited for; matrix products, arithmetic and copies ran while one was open for 15% of the time, Pallas kernels for 25%

profile of v7, /device:TPU:0, one launch (start us, length us, event | category | flops | bytes accessed | tf_op | source)
XLA Modules:
  0.0 247.0 jit_solution(2462354854845459640)
XLA Ops:
  4.8 1.5 copy.77
  6.4 4.5 %all-to-all-start = ((bf16[8,32,2048]{2,1,0:T(8,128)(2,1)}), bf16[8,32,2048]{2,1,0:T(8,128)(2,1)S(1)}, u32[]{:S(2)}, u32[]{:S(2)}) async-start(bf16[8,32,2048]{2,1,0:T(8,128)(2,1)} %copy.77), calls=%async_computation | async-start | bytes 2097152 | tf_op jit(solution)/shard_map/all_to_all | solution.py:145
  15.1 11.7 %all-to-all-done = bf16[8,32,2048]{2,1,0:T(8,128)(2,1)S(1)} async-done(((bf16[8,32,2048]{2,1,0:T(8,128)(2,1)}), bf16[8,32,2048]{2,1,0:T(8,128)(2,1)S(1)}, u32[]{:S(2)}, u32[]{:S(2)}) %all-to-all-start) | async-done | bytes 1048608 | tf_op jit(solution)/shard_map/all_to_all | solution.py:145
  28.2 1.4 broadcast_in_dim.60
  29.6 1.8 reshape.169
  31.6 41.7 %all_to_all.30 = bf16[16,32,2560]{2,1,0:T(8,128)(2,1)} all-to-all(bf16[16,32,2560]{2,1,0:T(8,128)(2,1)S(1)} %pad_maximum_fusion.1), channel_id=1, replica_groups=mesh['seg'=8,'leaf'=16] {'leaf'}, dimensions={0} | all-to-all | bytes 5242880 | tf_op jit(solution)/shard_map/all_to_all | solution.py:173
  73.3 4.0 %all-to-all-start.3 = ((bf16[16,32,1536]{2,1,0:T(8,128)(2,1)}), bf16[16,32,1536]{2,1,0:T(8,128)(2,1)S(1)}, u32[]{:S(2)}, u32[]{:S(2)}) async-start(bf16[16,32,1536]{2,1,0:T(8,128)(2,1)} %get-tuple-element.82), calls=%async_computation.3 | async-start | bytes 3145728 | tf_op jit(solution)/shard_map/all_to_all | solution.py:180
  78.0 1.6 reshape.171
  79.6 2.4 copy.79
  81.9 2.7 %slice.93 = bf16[16,32,1536]{2,1,0:T(8,128)(2,1)} slice(bf16[16,32,2560]{2,1,0:T(8,128)(2,1)} %all_to_all.30), slice={[0:16], [0:32], [0:1536]} | slice | bytes 3145728 | tf_op jit(solution)/shard_map/slice | solution.py:176
  84.7 31.4 %shard_map.127 = (bf16[1,512,640]{2,1,0:T(8,128)(2,1)}, bf16[1,512,640]{2,1,0:T(8,128)(2,1)}, f32[1,512,128]{2,1,0:T(8,128)}, f32[1,512,128]{2,1,0:T(8,128)}, f32[2048,128]{1,0:T(8,128)}, /*index=5*/f32[2048,128]{1,0:T(8,128)}) custom-call(f32[1,2048]{1,0:T(1,128)} %bitcast.143, bf16[1,512,1536]{2,1,0:T(8,128)(2,1)} %bitcast.109, ...), custom_call_target="tpu_custom_call" | custom-call | tf_op jit(solution)/shard_map/pallas_call | solution.py:101
  118.0 2.6 %pad_maximum_fusion.3 = bf16[1,512,1536]{2,1,0:T(8,128)(2,1)} fusion(bf16[1,512,128]{2,1,0:T(8,128)(2,1)S(1)} %convert_element_type.60, bf16[1,512,128]{2,1,0:T(8,128)(2,1)S(1)} %convert_element_type.59, bf16[1,512,640]{2,1,0:T(8,128)(2,1)} %get-tuple-element.19, bf16[1,512,640]{2,1,0:T(8,128)(2,1)} %get-tuple-element.18), kind=kLoop, calls=%fused_computation.11 | loop fusion | flops 6291456 | bytes 3145728 | tf_op jit(solution)/shard_map/concatenate | solution.py:185
  120.6 7.0 %all-to-all-start.2 = ((bf16[16,32,1536]{2,1,0:T(8,128)(2,1)}), bf16[16,32,1536]{2,1,0:T(8,128)(2,1)S(1)}, u32[]{:S(2)}, u32[]{:S(2)}) async-start(bf16[16,32,1536]{2,1,0:T(8,128)(2,1)} %bitcast.118), calls=%async_computation.2 | async-start | bytes 3145728 | tf_op jit(solution)/shard_map/all_to_all | solution.py:188
  127.6 31.4 %shard_map.128 = (bf16[1,512,640]{2,1,0:T(8,128)(2,1)}, bf16[1,512,640]{2,1,0:T(8,128)(2,1)}, f32[1,512,128]{2,1,0:T(8,128)}, f32[1,512,128]{2,1,0:T(8,128)}, f32[2048,128]{1,0:T(8,128)}, /*index=5*/f32[2048,128]{1,0:T(8,128)}) custom-call(f32[1,2048]{1,0:T(1,128)} %bitcast.144, bf16[1,512,1536]{2,1,0:T(8,128)(2,1)} %bitcast.105, ...), custom_call_target="tpu_custom_call" | custom-call | tf_op jit(solution)/shard_map/pallas_call | solution.py:101
  161.1 1.9 copy.82
  165.2 1.8 fusion.2
  167.0 1.8 reshape.176
  168.8 1.4 pad_maximum_fusion.4
  170.2 1.7 pad_maximum_fusion.2
  173.1 7.2 %all-to-all-start.4 = ((bf16[16,32,2560]{2,1,0:T(8,128)(2,1)}), bf16[16,32,2560]{2,1,0:T(8,128)(2,1)S(1)}, u32[]{:S(2)}, u32[]{:S(2)}) async-start(bf16[16,32,2560]{2,1,0:T(8,128)(2,1)} %pad_maximum_fusion.2), calls=%async_computation.4 | async-start | bytes 5242880 | tf_op jit(solution)/shard_map/all_to_all | solution.py:191
  180.3 3.4 %copy_dynamic-update-slice_fusion.1 = bf16[8,2,2,32,1536]{4,0,3,2,1:T(8,128)(2,1)} fusion(bf16[8,2,1,32,1536]{4,3,1,0,2:T(8,128)(2,1)} %bitcast.117), kind=kLoop, calls=%fused_computation.14 | loop fusion | bytes 3145728
  183.7 31.1 %all-to-all-done.4 = bf16[16,32,2560]{2,1,0:T(8,128)(2,1)S(1)} async-done(((bf16[16,32,2560]{2,1,0:T(8,128)(2,1)}), bf16[16,32,2560]{2,1,0:T(8,128)(2,1)S(1)}, u32[]{:S(2)}, u32[]{:S(2)}) %all-to-all-start.4) | async-done | bytes 2621472 | tf_op jit(solution)/shard_map/all_to_all | solution.py:191
  215.9 2.6 %convert_element_type.64 = bf16[16,32,4,256]{3,2,1,0:T(4,128)(2,1)} reshape(bf16[16,32,1024]{2,1,0:T(8,128)(2,1)} %slice.101) | data formatting | bytes 2097152 | tf_op jit(solution)/shard_map/convert_element_type | solution.py:212
  218.6 2.1 bitcast_reduce_fusion
  221.7 1.6 copy.90
  223.2 4.2 %all-to-all-start.5 = ((bf16[8,32,2048]{2,1,0:T(8,128)(2,1)}), bf16[8,32,2048]{2,1,0:T(8,128)(2,1)}, u32[]{:S(2)}, u32[]{:S(2)}) async-start(bf16[8,32,2048]{2,1,0:T(8,128)(2,1)} %copy.90), calls=%async_computation.5 | async-start | bytes 2097152 | tf_op jit(solution)/shard_map/all_to_all | solution.py:222
  227.6 1.8 copy-done.1
  230.5 1.4 copy-done.2
  231.9 1.4 reshape.178
  236.0 1.4 reshape.177
  237.5 5.9 %all-to-all-done.5 = bf16[8,32,2048]{2,1,0:T(8,128)(2,1)} async-done(((bf16[8,32,2048]{2,1,0:T(8,128)(2,1)}), bf16[8,32,2048]{2,1,0:T(8,128)(2,1)}, u32[]{:S(2)}, u32[]{:S(2)}) %all-to-all-start.5) | async-done | bytes 1048608 | tf_op jit(solution)/shard_map/all_to_all | solution.py:222
  243.4 2.1 convolution_convert_fusion.2
  (78 shorter events, 25.4 us)
Async XLA Ops:
  4.3 7.0 %copy-start.9 = (bf16[4,32,1024]{2,1,0:T(8,128)(2,1)S(1)}, bf16[4,32,1024]{2,1,0:T(8,128)(2,1)}, u32[]{:S(2)}) copy-start(bf16[4,32,1024]{2,1,0:T(8,128)(2,1)} %param.9) | copy-start | bytes 786436
  4.8 6.6 %copy-start.10 = (bf16[4,32,1024]{2,1,0:T(8,128)(2,1)S(1)}, bf16[4,32,1024]{2,1,0:T(8,128)(2,1)}, u32[]{:S(2)}) copy-start(bf16[4,32,1024]{2,1,0:T(8,128)(2,1)} %param.10) | copy-start | bytes 786436
  6.4 5.2 %copy-start.4 = (bf16[4,32,5120]{2,1,0:T(8,128)(2,1)S(1)}, bf16[4,32,5120]{2,1,0:T(8,128)(2,1)}, u32[]{:S(2)}) copy-start(bf16[4,32,5120]{2,1,0:T(8,128)(2,1)} %param.8) | copy-start | bytes 3932164
  6.4 20.5 %all-to-all-start = ((bf16[8,32,2048]{2,1,0:T(8,128)(2,1)}), bf16[8,32,2048]{2,1,0:T(8,128)(2,1)S(1)}, u32[]{:S(2)}, u32[]{:S(2)}) async-start(bf16[8,32,2048]{2,1,0:T(8,128)(2,1)} %copy.77), calls=%async_computation | async-start | bytes 2097152 | tf_op jit(solution)/shard_map/all_to_all | solution.py:145
  11.6 1.3 copy-start.5
  73.3 4.7 %slice-start = ((bf16[16,32,2560]{2,1,0:T(8,128)(2,1)}), bf16[16,32,1024]{2,1,0:T(8,128)(2,1)S(1)}, s32[]{:S(2)}) async-start(bf16[16,32,2560]{2,1,0:T(8,128)(2,1)} %all_to_all.30), calls=%async_computation.6 | async-start | bytes 2097152 | tf_op jit(solution)/shard_map/slice | solution.py:177
  73.3 47.3 %all-to-all-start.3 = ((bf16[16,32,1536]{2,1,0:T(8,128)(2,1)}), bf16[16,32,1536]{2,1,0:T(8,128)(2,1)S(1)}, u32[]{:S(2)}, u32[]{:S(2)}) async-start(bf16[16,32,1536]{2,1,0:T(8,128)(2,1)} %get-tuple-element.82), calls=%async_computation.3 | async-start | bytes 3145728 | tf_op jit(solution)/shard_map/all_to_all | solution.py:180
  120.6 7.0 %copy-start = (bf16[16,32,1536]{2,1,0:T(8,128)(2,1)}, bf16[16,32,1536]{2,1,0:T(8,128)(2,1)S(1)}, u32[]{:S(2)}) copy-start(bf16[16,32,1536]{2,1,0:T(8,128)(2,1)S(1)} %all-to-all-done.3) | copy-start | bytes 4718596
  120.6 51.3 %all-to-all-start.2 = ((bf16[16,32,1536]{2,1,0:T(8,128)(2,1)}), bf16[16,32,1536]{2,1,0:T(8,128)(2,1)S(1)}, u32[]{:S(2)}, u32[]{:S(2)}) async-start(bf16[16,32,1536]{2,1,0:T(8,128)(2,1)} %bitcast.118), calls=%async_computation.2 | async-start | bytes 3145728 | tf_op jit(solution)/shard_map/all_to_all | solution.py:188
  159.0 4.1 %copy-start.8 = (f32[2048,128]{1,0:T(8,128)S(1)}, f32[2048,128]{1,0:T(8,128)}, u32[]{:S(2)}) copy-start(f32[2048,128]{1,0:T(8,128)} %get-tuple-element.29) | copy-start | bytes 3145732
  159.0 4.8 %copy-start.7 = (f32[2048,128]{1,0:T(8,128)S(1)}, f32[2048,128]{1,0:T(8,128)}, u32[]{:S(2)}) copy-start(f32[2048,128]{1,0:T(8,128)} %get-tuple-element.26) | copy-start | bytes 3145732
  163.0 1.5 copy-start.6
  171.9 1.2 copy-start.3
  173.1 41.7 %all-to-all-start.4 = ((bf16[16,32,2560]{2,1,0:T(8,128)(2,1)}), bf16[16,32,2560]{2,1,0:T(8,128)(2,1)S(1)}, u32[]{:S(2)}, u32[]{:S(2)}) async-start(bf16[16,32,2560]{2,1,0:T(8,128)(2,1)} %pad_maximum_fusion.2), calls=%async_computation.4 | async-start | bytes 5242880 | tf_op jit(solution)/shard_map/all_to_all | solution.py:191
  223.2 20.2 %all-to-all-start.5 = ((bf16[8,32,2048]{2,1,0:T(8,128)(2,1)}), bf16[8,32,2048]{2,1,0:T(8,128)(2,1)}, u32[]{:S(2)}, u32[]{:S(2)}) async-start(bf16[8,32,2048]{2,1,0:T(8,128)(2,1)} %copy.90), calls=%async_computation.5 | async-start | bytes 2097152 | tf_op jit(solution)/shard_map/all_to_all | solution.py:222
  227.5 1.9 copy-start.1
  230.2 1.7 copy-start.2

commit v8 on v3

--- a/solution.py
+++ b/solution.py
@@ -82,7 +82,7 @@
         dka_ref[...] = dka_ref[...] * scale
 
 
-def attend_all(anc_mask, packed, anc_rows, heads, block_rows=256):
+def attend_all(anc_mask, packed, anc_rows, heads, block_rows=512):
     leaves, seg_len, _ = packed.shape
     anc = anc_rows.shape[0]
     grid = (leaves, heads, seg_len // block_rows)
@@ -142,12 +142,24 @@
     outgoing = jnp.einsum("gs,src->grc", serve_pick, stored, preferred_element_type=jnp.float32).astype(
         jnp.bfloat16
     )
-    arrived = lax.all_to_all(outgoing, "seg", split_axis=0, concat_axis=0, tiled=True)
     my_owners = jnp.take(owners, seg_here, axis=0)
     my_alive = jnp.take(alive_levels, seg_here, axis=0)
-    ancestor_rows = jnp.where(
-        my_alive[:, None, None], jnp.take(arrived, my_owners, axis=0), jnp.zeros((), jnp.bfloat16)
-    )
+    out_heads = jnp.concatenate(
+        [
+            outgoing[:, :, :key_width].reshape(seg_count, rows_here, kv_heads, 1, HD),
+            outgoing[:, :, key_width:].reshape(seg_count, rows_here, kv_heads, 1, HD),
+        ],
+        axis=3,
+    ).reshape(seg_count, rows_here, kv_heads, 2 * HD).transpose(0, 2, 1, 3)
+    anc_send = jnp.broadcast_to(
+        out_heads[:, :, None], (seg_count, kv_heads, pair_count, rows_here, 2 * HD)
+    ).reshape(seg_count * leaf_count, rows_here, 2 * HD)
+    anc_arrived = lax.all_to_all(anc_send, ("seg", "leaf"), split_axis=0, concat_axis=0, tiled=True)
+    anc_arrived = anc_arrived.reshape(seg_count, leaf_count * rows_here, 2 * HD)
+    anc_got = jnp.where(
+        my_alive[:, None, None], jnp.take(anc_arrived, my_owners, axis=0), jnp.zeros((), jnp.bfloat16)
+    ).reshape(levels * seg_len, 2 * HD)
+    anc_mask = jnp.repeat(my_alive, seg_len).astype(jnp.float32)[None, :]
 
     def to_heads(x, width):
         shaped = x.reshape(pair_count, pair_leaves, rows_here, kv_heads, width)
@@ -157,16 +169,6 @@
         [to_heads(queries, head_width), to_heads(out_grad, head_width), to_heads(leaf_keys, HD), to_heads(leaf_values, HD)],
         axis=3,
     )
-    anc_k = ancestor_rows[:, :, :key_width].reshape(levels, rows_here, kv_heads, HD)
-    anc_v = ancestor_rows[:, :, key_width:].reshape(levels, rows_here, kv_heads, HD)
-    anc_heads = jnp.concatenate([anc_k, anc_v], axis=3).transpose(2, 0, 1, 3)
-    anc_send = jnp.broadcast_to(anc_heads[:, None], (kv_heads, pair_count) + anc_heads.shape[1:]).reshape(
-        (leaf_count,) + anc_heads.shape[1:]
-    )
-    anc_got = lax.all_to_all(anc_send, "leaf", split_axis=0, concat_axis=0, tiled=True)
-    anc_got = anc_got.transpose(1, 0, 2, 3).reshape(levels * seg_len, 2 * HD)
-    anc_mask = jnp.repeat(my_alive, seg_len).astype(jnp.float32)[None, :]
-
     homes = []
     anc_partial = None
     for chunk in range(pair_leaves):
@@ -190,29 +192,27 @@
     leaf_key_grad = to_rows(home[..., 2 * head_width : 2 * head_width + HD])
     leaf_value_grad = to_rows(home[..., 2 * head_width + HD :])
 
-    anc_back = anc_partial.astype(jnp.bfloat16).reshape(levels, leaf_count, rows_here, 2 * HD).transpose(1, 0, 2, 3)
-    anc_home = lax.all_to_all(anc_back, "leaf", split_axis=0, concat_axis=0, tiled=True)
-    anc_home = anc_home.astype(jnp.float32).reshape(kv_heads, pair_count, levels, rows_here, 2 * HD).sum(axis=1)
-    part_keys = anc_home[..., :HD].transpose(1, 2, 0, 3).reshape(levels, rows_here, key_width)
-    part_values = anc_home[..., HD:].transpose(1, 2, 0, 3).reshape(levels, rows_here, key_width)
-    part_round = jnp.concatenate([part_keys, part_values], axis=2).astype(jnp.bfloat16)
-
     seg_ids = jnp.arange(seg_count, dtype=jnp.int32)
     homeward_pick = ((my_owners[None, :] == seg_ids[:, None]) & my_alive[None, :]).astype(jnp.bfloat16)
-    homeward = jnp.einsum("ok,krc->orc", homeward_pick, part_round, preferred_element_type=jnp.float32).astype(
+    partial_rows = anc_partial.astype(jnp.bfloat16).reshape(levels, seg_len, 2 * HD)
+    homeward = jnp.einsum("ok,krc->orc", homeward_pick, partial_rows, preferred_element_type=jnp.float32).astype(
         jnp.bfloat16
     )
-    returned = lax.all_to_all(homeward, "seg", split_axis=0, concat_axis=0, tiled=True)
-    collected = jnp.einsum("gs,grc->src", serve_pick, returned, preferred_element_type=jnp.float32).astype(
-        jnp.bfloat16
-    )
+    homeward = homeward.reshape(seg_count * leaf_count, rows_here, 2 * HD)
+    returned = lax.all_to_all(homeward, ("seg", "leaf"), split_axis=0, concat_axis=0, tiled=True)
+    returned = returned.astype(jnp.float32).reshape(seg_count, kv_heads, pair_count, rows_here, 2 * HD).sum(axis=2)
+    collected = jnp.einsum(
+        "gs,ghrc->shrc", serve_pick.astype(jnp.float32), returned, preferred_element_type=jnp.float32
+    )
+    inner_key_grad = collected[..., :HD].transpose(0, 2, 1, 3).reshape(slot_count, rows_here, key_width)
+    inner_value_grad = collected[..., HD:].transpose(0, 2, 1, 3).reshape(slot_count, rows_here, key_width)
     return (
         attention,
         query_grad,
         leaf_key_grad,
         leaf_value_grad,
-        collected[:, :, :key_width],
-        collected[:, :, key_width:],
+        inner_key_grad.astype(jnp.bfloat16),
+        inner_value_grad.astype(jnp.bfloat16),
     )
 
 

time: 257 us -> 234 us (0.911)
  blocking collectives: 20.1 us -> 0 us
  waiting for transfers between devices: 85.6 us -> 79.5 us
  Pallas kernels: 67.8 us -> 62.8 us
  other arithmetic: 9.64 us -> 13 us
  local copies, waits for them, and re-layouts: 32.4 us -> 35.7 us
    all_to_all x2, waiting for transfers between devices: 35.1 us -> 13.7 us  [on_device(): lax.all_to_all(back, 'leaf', split_axis=0, concat_axis=0, tiled=True)]
    all_to_all x1 -> x0, blocking collectives: 20.1 us -> none  [on_device(): lax.all_to_all(anc_send, 'leaf', split_axis=0, concat_axis=0, tiled=True)]
    all_to_all x3 -> x2, waiting for transfers between devices: 27.9 us -> 43 us  [the longest x1 28.9 us: on_device(): lax.all_to_all(anc_send, ('seg', 'leaf'), split_axis=0, concat_axis=0, ti...]
    all_to_all x2, starting transfers between devices: 8.11 us -> 14.4 us  [on_device(): lax.all_to_all(back, 'leaf', split_axis=0, concat_axis=0, tiled=True)]
    pallas_call x2, Pallas kernels: 67.8 us -> 62.8 us  [attend_all(): pl.pallas_call(attend_kernel, grid=grid, in_specs=[maskspec, qspec, gspec...]
    all_to_all x3 -> x2, starting transfers between devices: 16.1 us -> 11.2 us  [the longest x1 6.37 us: on_device(): lax.all_to_all(anc_send, ('seg', 'leaf'), split_axis=0, concat_axis=0, ti...]
    concatenate x0 -> x4, local copies, waits for them, and re-layouts: none -> 4.08 us  [on_device(): part = jnp.concatenate([dka, dva], axis=1)]
  transfers between devices with their start and end apart: 7 -> 6, of which waited for: 6 -> 4; matrix products, arithmetic and copies ran while one was open for 12% -> 17% of each run, Pallas kernels for 13% -> 27%
where the time goes in v8:
time: 234 us; the launch traced here: 233 us
  waiting for transfers between devices  79.5 us (34%)
  Pallas kernels  62.8 us (27%)
  starting transfers between devices  37.6 us (16%)
  local copies, waits for them, and re-layouts  35.7 us (15%)
  other arithmetic  13 us (6%)
  matrix products  3.52 us (2%)
    pallas_call x2, Pallas kernels, attend_all(): pl.pallas_call(attend_kernel, grid=grid, in_specs=[maskspec, qspec, gspec...  62.8 us
    all_to_all x1, waiting for transfers between devices, on_device(): lax.all_to_all(anc_send, ('seg', 'leaf'), split_axis=0, concat_axis=0, ti...  28.9 us
    all_to_all x2, waiting for transfers between devices, on_device(): lax.all_to_all(packed[:, chunk], 'leaf', split_axis=0, concat_axis=0, til...  22.8 us
    all_to_all x2, starting transfers between devices, on_device(): lax.all_to_all(back, 'leaf', split_axis=0, concat_axis=0, tiled=True)  14.4 us
    all_to_all x1, waiting for transfers between devices, on_device(): lax.all_to_all(homeward, ('seg', 'leaf'), split_axis=0, concat_axis=0, ti...  14.2 us
    all_to_all x2, waiting for transfers between devices, on_device(): lax.all_to_all(back, 'leaf', split_axis=0, concat_axis=0, tiled=True)  13.7 us
    all_to_all x2, starting transfers between devices, on_device(): lax.all_to_all(packed[:, chunk], 'leaf', split_axis=0, concat_axis=0, til...  12 us
    unnamed x43, local copies, waits for them, and re-layouts  8.64 us
  transfers between devices with their start and end apart: 6, of which 4 were waited for; matrix products, arithmetic and copies ran while one was open for 17% of the time, Pallas kernels for 27%

profile of v8, /device:TPU:0, one launch (start us, length us, event | category | flops | bytes accessed | tf_op | source)
XLA Modules:
  0.0 233.2 jit_solution(13366534977520161878)
XLA Ops:
  0.6 1.1 copy.93
  1.8 1.0 copy.94
  5.0 1.9 slice_bitcast_fusion
  6.9 8.3 %all-to-all-start = ((bf16[16,32,1536]{2,1,0:T(8,128)(2,1)}), bf16[16,32,1536]{2,1,0:T(8,128)(2,1)S(1)}, u32[]{:S(2)}, u32[]{:S(2)}) async-start(bf16[16,32,1536]{2,1,0:T(8,128)(2,1)} %get-tuple-element.59), calls=%async_computation | async-start | bytes 3145728 | tf_op jit(solution)/shard_map/all_to_all | solution.py:175
  17.0 22.8 %all-to-all-done = bf16[16,32,1536]{2,1,0:T(8,128)(2,1)S(1)} async-done(((bf16[16,32,1536]{2,1,0:T(8,128)(2,1)}), bf16[16,32,1536]{2,1,0:T(8,128)(2,1)S(1)}, u32[]{:S(2)}, u32[]{:S(2)}) %all-to-all-start) | async-done | bytes 1572896 | tf_op jit(solution)/shard_map/all_to_all | solution.py:175
  39.7 1.7 broadcast_in_dim.70
  41.5 6.4 %all-to-all-start.1 = ((bf16[128,32,256]{2,1,0:T(8,128)(2,1)}), bf16[128,32,256]{2,1,0:T(8,128)(2,1)}, u32[]{:S(2)}, u32[]{:S(2)}) async-start(bf16[128,32,256]{2,1,0:T(8,128)(2,1)} %bitcast.117), calls=%async_computation.1 | async-start | bytes 4194304 | tf_op jit(solution)/shard_map/all_to_all | solution.py:157
  48.4 28.9 %all-to-all-done.1 = bf16[128,32,256]{2,1,0:T(8,128)(2,1)} async-done(((bf16[128,32,256]{2,1,0:T(8,128)(2,1)}), bf16[128,32,256]{2,1,0:T(8,128)(2,1)}, u32[]{:S(2)}, u32[]{:S(2)}) %all-to-all-start.1) | async-done | bytes 2097184 | tf_op jit(solution)/shard_map/all_to_all | solution.py:157
  77.3 3.7 %all-to-all-start.3 = ((bf16[16,32,1536]{2,1,0:T(8,128)(2,1)}), bf16[16,32,1536]{2,1,0:T(8,128)(2,1)S(1)}, u32[]{:S(2)}, u32[]{:S(2)}) async-start(bf16[16,32,1536]{2,1,0:T(8,128)(2,1)} %get-tuple-element.58), calls=%async_computation.3 | async-start | bytes 3145728 | tf_op jit(solution)/shard_map/all_to_all | solution.py:175
  81.7 2.2 gather_fusion
  84.0 2.4 %fusion.6.ka_ref.va_ref = bf16[2048,256]{1,0:T(8,128)(2,1)} fusion(bf16[4,512,256]{2,1,0:T(8,128)(2,1)S(1)} %gather_fusion, pred[2048]{0:T(1024)(128)(4,1)S(1)} %bitcast.140, pred[2048]{0:T(1024)(128)(4,1)S(1)} %bitcast.141), kind=kLoop, calls=%fused_computation.20 | loop fusion | flops 1048576 | bytes 2101248 | tf_op jit(solution)/shard_map/jit(_where)/select_n | solution.py:159
  86.4 31.4 %shard_map.127 = (bf16[1,512,640]{2,1,0:T(8,128)(2,1)}, bf16[1,512,640]{2,1,0:T(8,128)(2,1)}, f32[1,512,128]{2,1,0:T(8,128)}, f32[1,512,128]{2,1,0:T(8,128)}, f32[2048,128]{1,0:T(8,128)}, /*index=5*/f32[2048,128]{1,0:T(8,128)}) custom-call(f32[1,2048]{1,0:T(1,128)} %bitcast.138, bf16[1,512,1536]{2,1,0:T(8,128)(2,1)} %bitcast.109, ...), custom_call_target="tpu_custom_call" | custom-call | tf_op jit(solution)/shard_map/pallas_call | solution.py:101
  119.7 2.6 %pad_maximum_fusion.1 = bf16[1,512,1536]{2,1,0:T(8,128)(2,1)} fusion(bf16[1,512,128]{2,1,0:T(8,128)(2,1)S(1)} %convert_element_type.65, bf16[1,512,128]{2,1,0:T(8,128)(2,1)S(1)} %convert_element_type.64, bf16[1,512,640]{2,1,0:T(8,128)(2,1)} %get-tuple-element.19, bf16[1,512,640]{2,1,0:T(8,128)(2,1)} %get-tuple-element.18), kind=kLoop, calls=%fused_computation.11 | loop fusion | flops 6291456 | bytes 3145728 | tf_op jit(solution)/shard_map/concatenate | solution.py:180
  122.3 7.2 %all-to-all-start.2 = ((bf16[16,32,1536]{2,1,0:T(8,128)(2,1)}), bf16[16,32,1536]{2,1,0:T(8,128)(2,1)S(1)}, u32[]{:S(2)}, u32[]{:S(2)}) async-start(bf16[16,32,1536]{2,1,0:T(8,128)(2,1)} %bitcast.120), calls=%async_computation.2 | async-start | bytes 3145728 | tf_op jit(solution)/shard_map/all_to_all | solution.py:182
  129.5 31.4 %shard_map.128 = (bf16[1,512,640]{2,1,0:T(8,128)(2,1)}, bf16[1,512,640]{2,1,0:T(8,128)(2,1)}, f32[1,512,128]{2,1,0:T(8,128)}, f32[1,512,128]{2,1,0:T(8,128)}, f32[2048,128]{1,0:T(8,128)}, /*index=5*/f32[2048,128]{1,0:T(8,128)}) custom-call(f32[1,2048]{1,0:T(1,128)} %bitcast.139, bf16[1,512,1536]{2,1,0:T(8,128)(2,1)} %bitcast.113, ...), custom_call_target="tpu_custom_call" | custom-call | tf_op jit(solution)/shard_map/pallas_call | solution.py:101
  160.9 1.0 convert_element_type.66
  162.8 2.6 %pad_maximum_fusion.2 = bf16[1,512,1536]{2,1,0:T(8,128)(2,1)} fusion(bf16[1,512,128]{2,1,0:T(8,128)(2,1)S(1)} %convert_element_type.67, bf16[1,512,128]{2,1,0:T(8,128)(2,1)S(1)} %convert_element_type.66, bf16[1,512,640]{2,1,0:T(8,128)(2,1)} %get-tuple-element.23, bf16[1,512,640]{2,1,0:T(8,128)(2,1)} %get-tuple-element.22), kind=kLoop, calls=%fused_computation.12 | loop fusion | flops 6291456 | bytes 3145728 | tf_op jit(solution)/shard_map/concatenate | solution.py:180
  165.4 7.2 %all-to-all-start.4 = ((bf16[16,32,1536]{2,1,0:T(8,128)(2,1)}), bf16[16,32,1536]{2,1,0:T(8,128)(2,1)S(1)}, u32[]{:S(2)}, u32[]{:S(2)}) async-start(bf16[16,32,1536]{2,1,0:T(8,128)(2,1)} %bitcast.121), calls=%async_computation.4 | async-start | bytes 3145728 | tf_op jit(solution)/shard_map/all_to_all | solution.py:182
  172.6 2.0 copy.81
  176.8 2.3 convolution_convert_fusion.1
  179.1 1.8 copy.85
  180.9 13.7 %all-to-all-done.4 = bf16[16,32,1536]{2,1,0:T(8,128)(2,1)S(1)} async-done(((bf16[16,32,1536]{2,1,0:T(8,128)(2,1)}), bf16[16,32,1536]{2,1,0:T(8,128)(2,1)S(1)}, u32[]{:S(2)}, u32[]{:S(2)}) %all-to-all-start.4) | async-done | bytes 1572896 | tf_op jit(solution)/shard_map/all_to_all | solution.py:182
  194.6 1.1 copy-done.4
  195.7 4.9 %all-to-all-start.5 = ((bf16[128,32,256]{2,1,0:T(8,128)(2,1)}), bf16[128,32,256]{2,1,0:T(8,128)(2,1)S(1)}, u32[]{:S(2)}, u32[]{:S(2)}) async-start(bf16[128,32,256]{2,1,0:T(8,128)(2,1)} %bitcast.36), calls=%async_computation.5 | async-start | bytes 4194304 | tf_op jit(solution)/shard_map/all_to_all | solution.py:202
  200.6 2.4 %copy_dynamic-update-slice_fusion.1 = bf16[8,2,2,32,1536]{4,0,3,2,1:T(8,128)(2,1)S(1)} fusion(bf16[8,2,1,32,1536]{4,3,1,0,2:T(8,128)(2,1)} %bitcast.118), kind=kLoop, calls=%fused_computation.14 | loop fusion | bytes 3145728
  203.9 1.5 slice_bitcast_fusion.2
  205.9 3.2 %reshape.170 = bf16[4,32,5120]{2,1,0:T(8,128)(2,1)} reshape(bf16[2,2,32,8,640]{4,3,2,1,0:T(8,128)(2,1)} %get-tuple-element.56) | data formatting | bytes 2621440 | tf_op jit(solution)/shard_map/reshape | solution.py:188
  209.1 1.9 slice_bitcast_fusion.6
  211.0 1.8 reshape.172
  212.8 1.8 reshape.171
  214.5 1.4 reshape.169
  216.0 14.2 %all-to-all-done.5 = bf16[128,32,256]{2,1,0:T(8,128)(2,1)S(1)} async-done(((bf16[128,32,256]{2,1,0:T(8,128)(2,1)}), bf16[128,32,256]{2,1,0:T(8,128)(2,1)S(1)}, u32[]{:S(2)}, u32[]{:S(2)}) %all-to-all-start.5) | async-done | bytes 2097184 | tf_op jit(solution)/shard_map/all_to_all | solution.py:202
  (77 shorter events, 14.6 us)
Async XLA Ops:
  0.6 2.2 copy-start.6
  2.9 1.3 copy-start.7
  6.9 8.3 %copy-start.14 = (s32[32]{0:T(128)S(1)}, s32[32]{0:T(128)}, u32[]{:S(2)}) copy-start(s32[32]{0:T(128)} %param.15) | copy-start | bytes 388
  6.9 8.4 %copy-start.13 = (s32[32,4]{0,1:T(4,128)S(1)}, s32[32,4]{0,1:T(4,128)}, u32[]{:S(2)}) copy-start(s32[32,4]{0,1:T(4,128)} %param.14) | copy-start | bytes 1540
  6.9 8.5 %copy-start.11 = (bf16[2,32,1024]{2,1,0:T(8,128)(2,1)S(1)}, bf16[2,32,1024]{2,1,0:T(8,128)(2,1)}, u32[]{:S(2)}) copy-start(bf16[2,32,1024]{2,1,0:T(8,128)(2,1)} %param.11) | copy-start | bytes 393220
  6.9 8.7 %copy-start.12 = (bf16[2,32,1024]{2,1,0:T(8,128)(2,1)S(1)}, bf16[2,32,1024]{2,1,0:T(8,128)(2,1)}, u32[]{:S(2)}) copy-start(bf16[2,32,1024]{2,1,0:T(8,128)(2,1)} %param.12) | copy-start | bytes 393220
  6.9 32.8 %all-to-all-start = ((bf16[16,32,1536]{2,1,0:T(8,128)(2,1)}), bf16[16,32,1536]{2,1,0:T(8,128)(2,1)S(1)}, u32[]{:S(2)}, u32[]{:S(2)}) async-start(bf16[16,32,1536]{2,1,0:T(8,128)(2,1)} %get-tuple-element.59), calls=%async_computation | async-start | bytes 3145728 | tf_op jit(solution)/shard_map/all_to_all | solution.py:175
  39.7 1.8 copy-start
  41.5 35.7 %all-to-all-start.1 = ((bf16[128,32,256]{2,1,0:T(8,128)(2,1)}), bf16[128,32,256]{2,1,0:T(8,128)(2,1)}, u32[]{:S(2)}, u32[]{:S(2)}) async-start(bf16[128,32,256]{2,1,0:T(8,128)(2,1)} %bitcast.117), calls=%async_computation.1 | async-start | bytes 4194304 | tf_op jit(solution)/shard_map/all_to_all | solution.py:157
  77.3 45.0 %all-to-all-start.3 = ((bf16[16,32,1536]{2,1,0:T(8,128)(2,1)}), bf16[16,32,1536]{2,1,0:T(8,128)(2,1)S(1)}, u32[]{:S(2)}, u32[]{:S(2)}) async-start(bf16[16,32,1536]{2,1,0:T(8,128)(2,1)} %get-tuple-element.58), calls=%async_computation.3 | async-start | bytes 3145728 | tf_op jit(solution)/shard_map/all_to_all | solution.py:175
  122.3 7.2 %copy-start.1 = (bf16[16,32,1536]{2,1,0:T(8,128)(2,1)}, bf16[16,32,1536]{2,1,0:T(8,128)(2,1)S(1)}, u32[]{:S(2)}) copy-start(bf16[16,32,1536]{2,1,0:T(8,128)(2,1)S(1)} %all-to-all-done.3) | copy-start | bytes 4718596
  122.3 43.1 %all-to-all-start.2 = ((bf16[16,32,1536]{2,1,0:T(8,128)(2,1)}), bf16[16,32,1536]{2,1,0:T(8,128)(2,1)S(1)}, u32[]{:S(2)}, u32[]{:S(2)}) async-start(bf16[16,32,1536]{2,1,0:T(8,128)(2,1)} %bitcast.120), calls=%async_computation.2 | async-start | bytes 3145728 | tf_op jit(solution)/shard_map/all_to_all | solution.py:182
  165.4 9.3 %copy-start.3 = (bf16[16,32,1536]{2,1,0:T(8,128)(2,1)}, bf16[16,32,1536]{2,1,0:T(8,128)(2,1)S(1)}, u32[]{:S(2)}) copy-start(bf16[16,32,1536]{2,1,0:T(8,128)(2,1)S(1)} %all-to-all-done.2) | copy-start | bytes 4718596
  165.4 29.2 %all-to-all-start.4 = ((bf16[16,32,1536]{2,1,0:T(8,128)(2,1)}), bf16[16,32,1536]{2,1,0:T(8,128)(2,1)S(1)}, u32[]{:S(2)}, u32[]{:S(2)}) async-start(bf16[16,32,1536]{2,1,0:T(8,128)(2,1)} %bitcast.121), calls=%async_computation.4 | async-start | bytes 3145728 | tf_op jit(solution)/shard_map/all_to_all | solution.py:182
  172.6 2.1 copy-start.8
  172.6 2.8 %copy-start.10 = (f32[2048,128]{1,0:T(8,128)S(1)}, f32[2048,128]{1,0:T(8,128)}, u32[]{:S(2)}) copy-start(f32[2048,128]{1,0:T(8,128)} %get-tuple-element.28) | copy-start | bytes 3145732
  174.7 1.4 copy-start.9
  194.6 1.1 copy-start.4
  195.7 34.4 %all-to-all-start.5 = ((bf16[128,32,256]{2,1,0:T(8,128)(2,1)}), bf16[128,32,256]{2,1,0:T(8,128)(2,1)S(1)}, u32[]{:S(2)}, u32[]{:S(2)}) async-start(bf16[128,32,256]{2,1,0:T(8,128)(2,1)} %bitcast.36), calls=%async_computation.5 | async-start | bytes 4194304 | tf_op jit(solution)/shard_map/all_to_all | solution.py:202
  200.6 2.4 %copy-start.5 = (bf16[16,32,1536]{2,1,0:T(8,128)(2,1)S(1)}, bf16[16,32,1536]{2,1,0:T(8,128)(2,1)}, u32[]{:S(2)}) copy-start(bf16[16,32,1536]{2,1,0:T(8,128)(2,1)} %copy-done.4) | copy-start | bytes 4718596
  203.9 2.0 copy-start.2

commit v9 on v8

--- a/solution.py
+++ b/solution.py
@@ -109,6 +109,17 @@
     )(anc_mask, packed, packed, packed, packed, anc_rows, anc_rows)
 
 
+def leaf_shift(blocks, leaf_here, leaf_count):
+    pieces = [jnp.take(blocks, leaf_here, axis=0)]
+    for shift in range(1, leaf_count):
+        piece = jnp.take(blocks, (leaf_here + shift) % leaf_count, axis=0)
+        pairs = [(i, (i + shift) % leaf_count) for i in range(leaf_count)]
+        pieces.append(lax.ppermute(piece, "leaf", pairs))
+    by_shift = jnp.stack(pieces, axis=0)
+    sources = jnp.arange(leaf_count, dtype=jnp.int32)
+    return jnp.take(by_shift, (leaf_here - sources) % leaf_count, axis=0)
+
+
 def on_device(queries, leaf_keys, leaf_values, inner_keys, inner_values, out_grad, ancestors, depths):
     seg_count = lax.axis_size("seg")
     leaf_count = lax.axis_size("leaf")
@@ -172,7 +183,10 @@
     homes = []
     anc_partial = None
     for chunk in range(pair_leaves):
-        got = lax.all_to_all(packed[:, chunk], "leaf", split_axis=0, concat_axis=0, tiled=True)
+        if chunk == 0:
+            got = leaf_shift(packed[:, chunk], leaf_here, leaf_count)
+        else:
+            got = lax.all_to_all(packed[:, chunk], "leaf", split_axis=0, concat_axis=0, tiled=True)
         got = got.reshape(1, seg_len, packed.shape[3])
         res, dq, dko, dvo, dka, dva = attend_all(anc_mask, got, anc_got, group_heads)
         part = jnp.concatenate([dka, dva], axis=1)

time: 234 us -> 294 us (1.26)
  waiting for transfers between devices: 79.5 us -> 105 us
  local copies, waits for them, and re-layouts: 35.7 us -> 51.9 us
  starting transfers between devices: 37.6 us -> 53 us
    ppermute x0 -> x15, waiting for transfers between devices: none -> 81.9 us  [leaf_shift(): pieces.append(lax.ppermute(piece, 'leaf', pairs))]
    all_to_all x1, waiting for transfers between devices: 28.9 us -> 0.01 us  [on_device(): lax.all_to_all(anc_send, ('seg', 'leaf'), split_axis=0, concat_axis=0, ti...]
    all_to_all x2 -> x1, waiting for transfers between devices: 22.8 us -> 0.01 us  [on_device(): lax.all_to_all(packed[:, chunk], 'leaf', split_axis=0, concat_axis=0, til...]
    unnamed x43 -> x51, local copies, waits for them, and re-layouts: 8.64 us -> 21.4 us
    ppermute x0 -> x15, starting transfers between devices: none -> 11.3 us  [leaf_shift(): pieces.append(lax.ppermute(piece, 'leaf', pairs))]
    all_to_all x1, starting transfers between devices: 6.37 us -> 11.7 us  [on_device(): lax.all_to_all(anc_send, ('seg', 'leaf'), split_axis=0, concat_axis=0, ti...]
    all_to_all x2, waiting for transfers between devices: 13.7 us -> 8.62 us  [on_device(): lax.all_to_all(back, 'leaf', split_axis=0, concat_axis=0, tiled=True)]
    all_to_all x2 -> x1, starting transfers between devices: 12 us -> 8.74 us  [on_device(): lax.all_to_all(packed[:, chunk], 'leaf', split_axis=0, concat_axis=0, til...]
  transfers between devices with their start and end apart: 6 -> 20, of which waited for: 4 -> 13; matrix products, arithmetic and copies ran while one was open for 17% -> 19% of each run, Pallas kernels for 27% -> 21%
where the time goes in v9:
time: 294 us; the launch traced here: 292 us
  waiting for transfers between devices  105 us (36%)
  Pallas kernels  62.8 us (21%)
  starting transfers between devices  53 us (18%)
  local copies, waits for them, and re-layouts  51.9 us (18%)
  other arithmetic  15.3 us (5%)
  matrix products  3.52 us (1%)
    ppermute x15, waiting for transfers between devices, leaf_shift(): pieces.append(lax.ppermute(piece, 'leaf', pairs))  81.9 us
    pallas_call x2, Pallas kernels, attend_all(): pl.pallas_call(attend_kernel, grid=grid, in_specs=[maskspec, qspec, gspec...  62.8 us
    unnamed x51, local copies, waits for them, and re-layouts  21.4 us
    all_to_all x2, starting transfers between devices, on_device(): lax.all_to_all(back, 'leaf', split_axis=0, concat_axis=0, tiled=True)  14.4 us
    all_to_all x1, waiting for transfers between devices, on_device(): lax.all_to_all(homeward, ('seg', 'leaf'), split_axis=0, concat_axis=0, ti...  14.1 us
    all_to_all x1, starting transfers between devices, on_device(): lax.all_to_all(anc_send, ('seg', 'leaf'), split_axis=0, concat_axis=0, ti...  11.7 us
    ppermute x15, starting transfers between devices, leaf_shift(): pieces.append(lax.ppermute(piece, 'leaf', pairs))  11.3 us
    all_to_all x1, starting transfers between devices, on_device(): lax.all_to_all(packed[:, chunk], 'leaf', split_axis=0, concat_axis=0, til...  8.74 us
  transfers between devices with their start and end apart: 20, of which 13 were waited for; matrix products, arithmetic and copies ran while one was open for 19% of the time, Pallas kernels for 21%

profile of v9, /device:TPU:0, one launch (start us, length us, event | category | flops | bytes accessed | tf_op | source)
XLA Modules:
  0.0 292.5 jit_solution(18238495557611471453)
XLA Ops:
  7.1 11.7 %all-to-all-start = ((bf16[128,32,256]{2,1,0:T(8,128)(2,1)}), bf16[128,32,256]{2,1,0:T(8,128)(2,1)}, u32[]{:S(2)}, u32[]{:S(2)}) async-start(bf16[128,32,256]{2,1,0:T(8,128)(2,1)} %bitcast.47), calls=%async_computation | async-start | bytes 4194304 | tf_op jit(solution)/shard_map/all_to_all | solution.py:168
  24.0 5.1 %collective-permute-start.14 = (bf16[32,1536]{1,0:T(8,128)(2,1)S(1)}, bf16[32,1536]{1,0:T(8,128)(2,1)S(1)}, u32[]{:S(2)}, u32[]{:S(2)}) collective-permute-start(bf16[32,1536]{1,0:T(8,128)(2,1)S(1)} %get-tuple-element.72), channel_id=1, source_target_pairs={{0,15},{1,0},{2,1},{3,2},{4,3},{5,4},{6,5},{7,6},{8,7},{9,8},{10,9... | collective-permute-start | bytes 294920 | tf_op jit(solution)/shard_map/ppermute | solution.py:117
  31.8 1.8 collective-permute-start
  35.1 17.5 %collective-permute-done = bf16[32,1536]{1,0:T(8,128)(2,1)S(1)} collective-permute-done((bf16[32,1536]{1,0:T(8,128)(2,1)S(1)}, bf16[32,1536]{1,0:T(8,128)(2,1)S(1)}, u32[]{:S(2)}, u32[]{:S(2)}) %collective-permute-start) | collective-permute-done | bytes 98336 | tf_op jit(solution)/shard_map/ppermute | solution.py:117
  53.3 7.6 %collective-permute-done.1 = bf16[32,1536]{1,0:T(8,128)(2,1)S(1)} collective-permute-done((bf16[32,1536]{1,0:T(8,128)(2,1)S(1)}, bf16[32,1536]{1,0:T(8,128)(2,1)S(1)}, u32[]{:S(2)}, u32[]{:S(2)}) %collective-permute-start.1) | collective-permute-done | bytes 98336 | tf_op jit(solution)/shard_map/ppermute | solution.py:117
  61.5 6.1 %collective-permute-done.2 = bf16[32,1536]{1,0:T(8,128)(2,1)S(1)} collective-permute-done((bf16[32,1536]{1,0:T(8,128)(2,1)S(1)}, bf16[32,1536]{1,0:T(8,128)(2,1)S(1)}, u32[]{:S(2)}, u32[]{:S(2)}) %collective-permute-start.2) | collective-permute-done | bytes 98336 | tf_op jit(solution)/shard_map/ppermute | solution.py:117
  68.2 5.2 %collective-permute-done.3 = bf16[32,1536]{1,0:T(8,128)(2,1)S(1)} collective-permute-done((bf16[32,1536]{1,0:T(8,128)(2,1)S(1)}, bf16[32,1536]{1,0:T(8,128)(2,1)S(1)}, u32[]{:S(2)}, u32[]{:S(2)}) %collective-permute-start.3) | collective-permute-done | bytes 98336 | tf_op jit(solution)/shard_map/ppermute | solution.py:117
  74.0 7.6 %collective-permute-done.4 = bf16[32,1536]{1,0:T(8,128)(2,1)S(1)} collective-permute-done((bf16[32,1536]{1,0:T(8,128)(2,1)S(1)}, bf16[32,1536]{1,0:T(8,128)(2,1)S(1)}, u32[]{:S(2)}, u32[]{:S(2)}) %collective-permute-start.4) | collective-permute-done | bytes 98336 | tf_op jit(solution)/shard_map/ppermute | solution.py:117
  82.3 8.8 %collective-permute-done.5 = bf16[32,1536]{1,0:T(8,128)(2,1)S(1)} collective-permute-done((bf16[32,1536]{1,0:T(8,128)(2,1)S(1)}, bf16[32,1536]{1,0:T(8,128)(2,1)S(1)}, u32[]{:S(2)}, u32[]{:S(2)}) %collective-permute-start.5) | collective-permute-done | bytes 98336 | tf_op jit(solution)/shard_map/ppermute | solution.py:117
  91.7 6.4 %collective-permute-done.6 = bf16[32,1536]{1,0:T(8,128)(2,1)S(1)} collective-permute-done((bf16[32,1536]{1,0:T(8,128)(2,1)S(1)}, bf16[32,1536]{1,0:T(8,128)(2,1)S(1)}, u32[]{:S(2)}, u32[]{:S(2)}) %collective-permute-start.6) | collective-permute-done | bytes 98336 | tf_op jit(solution)/shard_map/ppermute | solution.py:117
  98.7 5.5 %collective-permute-done.7 = bf16[32,1536]{1,0:T(8,128)(2,1)S(1)} collective-permute-done((bf16[32,1536]{1,0:T(8,128)(2,1)S(1)}, bf16[32,1536]{1,0:T(8,128)(2,1)S(1)}, u32[]{:S(2)}, u32[]{:S(2)}) %collective-permute-start.7) | collective-permute-done | bytes 98336 | tf_op jit(solution)/shard_map/ppermute | solution.py:117
  104.8 6.1 %collective-permute-done.8 = bf16[32,1536]{1,0:T(8,128)(2,1)S(1)} collective-permute-done((bf16[32,1536]{1,0:T(8,128)(2,1)S(1)}, bf16[32,1536]{1,0:T(8,128)(2,1)S(1)}, u32[]{:S(2)}, u32[]{:S(2)}) %collective-permute-start.8) | collective-permute-done | bytes 98336 | tf_op jit(solution)/shard_map/ppermute | solution.py:117
  112.3 5.7 %collective-permute-done.9 = bf16[32,1536]{1,0:T(8,128)(2,1)S(1)} collective-permute-done((bf16[32,1536]{1,0:T(8,128)(2,1)S(1)}, bf16[32,1536]{1,0:T(8,128)(2,1)S(1)}, u32[]{:S(2)}, u32[]{:S(2)}) %collective-permute-start.9) | collective-permute-done | bytes 98336 | tf_op jit(solution)/shard_map/ppermute | solution.py:117
  120.3 5.6 %collective-permute-done.10 = bf16[32,1536]{1,0:T(8,128)(2,1)S(1)} collective-permute-done((bf16[32,1536]{1,0:T(8,128)(2,1)S(1)}, bf16[32,1536]{1,0:T(8,128)(2,1)S(1)}, u32[]{:S(2)}, u32[]{:S(2)}) %collective-permute-start.10) | collective-permute-done | bytes 98336 | tf_op jit(solution)/shard_map/ppermute | solution.py:117
  128.4 8.7 %all-to-all-start.2 = ((bf16[16,32,1536]{2,1,0:T(8,128)(2,1)}), bf16[16,32,1536]{2,1,0:T(8,128)(2,1)S(1)}, u32[]{:S(2)}, u32[]{:S(2)}) async-start(bf16[16,32,1536]{2,1,0:T(8,128)(2,1)} %get-tuple-element.70), calls=%async_computation.2 | async-start | bytes 3145728 | tf_op jit(solution)/shard_map/all_to_all | solution.py:189
  137.8 2.1 gather_fusion
  141.3 2.2 gather_fusion.1
  143.5 2.4 fusion.6.ka_ref.va_ref
  145.9 31.4 %shard_map.127 = (bf16[1,512,640]{2,1,0:T(8,128)(2,1)}, bf16[1,512,640]{2,1,0:T(8,128)(2,1)}, f32[1,512,128]{2,1,0:T(8,128)}, f32[1,512,128]{2,1,0:T(8,128)}, f32[2048,128]{1,0:T(8,128)}, /*index=5*/f32[2048,128]{1,0:T(8,128)}) custom-call(f32[1,2048]{1,0:T(1,128)} %bitcast.199, bf16[1,512,1536]{2,1,0:T(8,128)(2,1)} %bitcast_select_fusion.q_ref.g_ref.ko_ref.vo_ref, ...), custom_call_target="tpu_custom_call" | custom-call | tf_op jit(solution)/shard_map/pallas_call | solution.py:101
  179.3 2.6 pad_maximum_fusion.1
  183.0 7.2 %all-to-all-start.1 = ((bf16[16,32,1536]{2,1,0:T(8,128)(2,1)}), bf16[16,32,1536]{2,1,0:T(8,128)(2,1)S(1)}, u32[]{:S(2)}, u32[]{:S(2)}) async-start(bf16[16,32,1536]{2,1,0:T(8,128)(2,1)} %bitcast.180), calls=%async_computation.1 | async-start | bytes 3145728 | tf_op jit(solution)/shard_map/all_to_all | solution.py:196
  190.2 31.4 %shard_map.128 = (bf16[1,512,640]{2,1,0:T(8,128)(2,1)}, bf16[1,512,640]{2,1,0:T(8,128)(2,1)}, f32[1,512,128]{2,1,0:T(8,128)}, f32[1,512,128]{2,1,0:T(8,128)}, f32[2048,128]{1,0:T(8,128)}, /*index=5*/f32[2048,128]{1,0:T(8,128)}) custom-call(f32[1,2048]{1,0:T(1,128)} %bitcast.200, bf16[1,512,1536]{2,1,0:T(8,128)(2,1)} %bitcast.174, ...), custom_call_target="tpu_custom_call" | custom-call | tf_op jit(solution)/shard_map/pallas_call | solution.py:101
  223.6 2.6 pad_maximum_fusion.2
  227.4 7.2 %all-to-all-start.3 = ((bf16[16,32,1536]{2,1,0:T(8,128)(2,1)}), bf16[16,32,1536]{2,1,0:T(8,128)(2,1)S(1)}, u32[]{:S(2)}, u32[]{:S(2)}) async-start(bf16[16,32,1536]{2,1,0:T(8,128)(2,1)} %bitcast.181), calls=%async_computation.3 | async-start | bytes 3145728 | tf_op jit(solution)/shard_map/all_to_all | solution.py:196
  234.6 2.0 copy.81
  239.3 2.3 convolution_convert_fusion.1
  243.3 8.6 %all-to-all-done.3 = bf16[16,32,1536]{2,1,0:T(8,128)(2,1)S(1)} async-done(((bf16[16,32,1536]{2,1,0:T(8,128)(2,1)}), bf16[16,32,1536]{2,1,0:T(8,128)(2,1)S(1)}, u32[]{:S(2)}, u32[]{:S(2)}) %all-to-all-start.3) | async-done | bytes 1572896 | tf_op jit(solution)/shard_map/all_to_all | solution.py:196
  253.1 6.8 %all-to-all-start.4 = ((bf16[128,32,256]{2,1,0:T(8,128)(2,1)}), bf16[128,32,256]{2,1,0:T(8,128)(2,1)S(1)}, u32[]{:S(2)}, u32[]{:S(2)}) async-start(bf16[128,32,256]{2,1,0:T(8,128)(2,1)} %bitcast.68), calls=%async_computation.4 | async-start | bytes 4194304 | tf_op jit(solution)/shard_map/all_to_all | solution.py:216
  259.9 2.4 copy_dynamic-update-slice_fusion.1
  265.2 3.2 %reshape.254 = bf16[4,32,5120]{2,1,0:T(8,128)(2,1)} reshape(bf16[2,2,32,8,640]{4,3,2,1,0:T(8,128)(2,1)} %get-tuple-element.68) | data formatting | bytes 2621440 | tf_op jit(solution)/shard_map/reshape | solution.py:202
  268.4 1.9 slice_bitcast_fusion.6
  275.3 14.1 %all-to-all-done.4 = bf16[128,32,256]{2,1,0:T(8,128)(2,1)S(1)} async-done(((bf16[128,32,256]{2,1,0:T(8,128)(2,1)}), bf16[128,32,256]{2,1,0:T(8,128)(2,1)S(1)}, u32[]{:S(2)}, u32[]{:S(2)}) %all-to-all-start.4) | async-done | bytes 2097184 | tf_op jit(solution)/shard_map/all_to_all | solution.py:216
  (123 shorter events, 51.5 us)
Async XLA Ops:
  7.1 11.9 %copy-start.10 = (bf16[4,32,1024]{2,1,0:T(8,128)(2,1)S(1)}, bf16[4,32,1024]{2,1,0:T(8,128)(2,1)}, u32[]{:S(2)}) copy-start(bf16[4,32,1024]{2,1,0:T(8,128)(2,1)} %param.11) | copy-start | bytes 786436
  7.1 12.0 %copy-start.11 = (bf16[4,32,1024]{2,1,0:T(8,128)(2,1)S(1)}, bf16[4,32,1024]{2,1,0:T(8,128)(2,1)}, u32[]{:S(2)}) copy-start(bf16[4,32,1024]{2,1,0:T(8,128)(2,1)} %param.12) | copy-start | bytes 786436
  7.1 121.3 %all-to-all-start = ((bf16[128,32,256]{2,1,0:T(8,128)(2,1)}), bf16[128,32,256]{2,1,0:T(8,128)(2,1)}, u32[]{:S(2)}, u32[]{:S(2)}) async-start(bf16[128,32,256]{2,1,0:T(8,128)(2,1)} %bitcast.47), calls=%async_computation | async-start | bytes 4194304 | tf_op jit(solution)/shard_map/all_to_all | solution.py:168
  18.8 1.3 copy-start.5
  20.3 1.3 copy-start.6
  24.0 113.2 %collective-permute-start.14 = (bf16[32,1536]{1,0:T(8,128)(2,1)S(1)}, bf16[32,1536]{1,0:T(8,128)(2,1)S(1)}, u32[]{:S(2)}, u32[]{:S(2)}) collective-permute-start(bf16[32,1536]{1,0:T(8,128)(2,1)S(1)} %get-tuple-element.72), channel_id=1, source_target_pairs={{0,15},{1,0},{2,1},{3,2},{4,3},{5,4},{6,5},{7,6},{8,7},{9,8},{10,9... | collective-permute-start | bytes 294920 | tf_op jit(solution)/shard_map/ppermute | solution.py:117
  29.1 98.7 %collective-permute-start.13 = (bf16[32,1536]{1,0:T(8,128)(2,1)S(1)}, bf16[32,1536]{1,0:T(8,128)(2,1)S(1)}, u32[]{:S(2)}, u32[]{:S(2)}) collective-permute-start(bf16[32,1536]{1,0:T(8,128)(2,1)S(1)} %get-tuple-element.73), channel_id=1, source_target_pairs={{0,14},{1,15},{2,0},{3,1},{4,2},{5,3},{6,4},{7,5},{8,6},{9,7},{10,... | collective-permute-start | bytes 294920 | tf_op jit(solution)/shard_map/ppermute | solution.py:117
  29.8 97.3 %collective-permute-start.12 = (bf16[32,1536]{1,0:T(8,128)(2,1)S(1)}, bf16[32,1536]{1,0:T(8,128)(2,1)S(1)}, u32[]{:S(2)}, u32[]{:S(2)}) collective-permute-start(bf16[32,1536]{1,0:T(8,128)(2,1)S(1)} %get-tuple-element.74), channel_id=1, source_target_pairs={{0,13},{1,14},{2,15},{3,0},{4,1},{5,2},{6,3},{7,4},{8,5},{9,6},{10... | collective-permute-start | bytes 294920 | tf_op jit(solution)/shard_map/ppermute | solution.py:117
  30.8 95.7 %collective-permute-start.11 = (bf16[32,1536]{1,0:T(8,128)(2,1)S(1)}, bf16[32,1536]{1,0:T(8,128)(2,1)S(1)}, u32[]{:S(2)}, u32[]{:S(2)}) collective-permute-start(bf16[32,1536]{1,0:T(8,128)(2,1)S(1)} %get-tuple-element.75), channel_id=1, source_target_pairs={{0,12},{1,13},{2,14},{3,15},{4,0},{5,1},{6,2},{7,3},{8,4},{9,5},{1... | collective-permute-start | bytes 294920 | tf_op jit(solution)/shard_map/ppermute | solution.py:117
  31.8 20.8 %collective-permute-start = (bf16[32,1536]{1,0:T(8,128)(2,1)S(1)}, bf16[32,1536]{1,0:T(8,128)(2,1)S(1)}, u32[]{:S(2)}, u32[]{:S(2)}) collective-permute-start(bf16[32,1536]{1,0:T(8,128)(2,1)S(1)} %get-tuple-element.86), channel_id=1, source_target_pairs={{0,1},{1,2},{2,3},{3,4},{4,5},{5,6},{6,7},{7,8},{8,9},{9,10},{10,1... | collective-permute-start | bytes 294920 | tf_op jit(solution)/shard_map/ppermute | solution.py:117
  52.6 8.2 %collective-permute-start.1 = (bf16[32,1536]{1,0:T(8,128)(2,1)S(1)}, bf16[32,1536]{1,0:T(8,128)(2,1)S(1)}, u32[]{:S(2)}, u32[]{:S(2)}) collective-permute-start(bf16[32,1536]{1,0:T(8,128)(2,1)S(1)} %get-tuple-element.85), channel_id=1, source_target_pairs={{0,2},{1,3},{2,4},{3,5},{4,6},{5,7},{6,8},{7,9},{8,10},{9,11},{10,... | collective-permute-start | bytes 294920 | tf_op jit(solution)/shard_map/ppermute | solution.py:117
  60.8 6.7 %collective-permute-start.2 = (bf16[32,1536]{1,0:T(8,128)(2,1)S(1)}, bf16[32,1536]{1,0:T(8,128)(2,1)S(1)}, u32[]{:S(2)}, u32[]{:S(2)}) collective-permute-start(bf16[32,1536]{1,0:T(8,128)(2,1)S(1)} %get-tuple-element.84), channel_id=1, source_target_pairs={{0,3},{1,4},{2,5},{3,6},{4,7},{5,8},{6,9},{7,10},{8,11},{9,12},{10... | collective-permute-start | bytes 294920 | tf_op jit(solution)/shard_map/ppermute | solution.py:117
  67.6 5.8 %collective-permute-start.3 = (bf16[32,1536]{1,0:T(8,128)(2,1)S(1)}, bf16[32,1536]{1,0:T(8,128)(2,1)S(1)}, u32[]{:S(2)}, u32[]{:S(2)}) collective-permute-start(bf16[32,1536]{1,0:T(8,128)(2,1)S(1)} %get-tuple-element.83), channel_id=1, source_target_pairs={{0,4},{1,5},{2,6},{3,7},{4,8},{5,9},{6,10},{7,11},{8,12},{9,13},{1... | collective-permute-start | bytes 294920 | tf_op jit(solution)/shard_map/ppermute | solution.py:117
  73.4 8.2 %collective-permute-start.4 = (bf16[32,1536]{1,0:T(8,128)(2,1)S(1)}, bf16[32,1536]{1,0:T(8,128)(2,1)S(1)}, u32[]{:S(2)}, u32[]{:S(2)}) collective-permute-start(bf16[32,1536]{1,0:T(8,128)(2,1)S(1)} %get-tuple-element.82), channel_id=1, source_target_pairs={{0,5},{1,6},{2,7},{3,8},{4,9},{5,10},{6,11},{7,12},{8,13},{9,14},{... | collective-permute-start | bytes 294920 | tf_op jit(solution)/shard_map/ppermute | solution.py:117
  81.6 9.4 %collective-permute-start.5 = (bf16[32,1536]{1,0:T(8,128)(2,1)S(1)}, bf16[32,1536]{1,0:T(8,128)(2,1)S(1)}, u32[]{:S(2)}, u32[]{:S(2)}) collective-permute-start(bf16[32,1536]{1,0:T(8,128)(2,1)S(1)} %get-tuple-element.81), channel_id=1, source_target_pairs={{0,6},{1,7},{2,8},{3,9},{4,10},{5,11},{6,12},{7,13},{8,14},{9,15},... | collective-permute-start | bytes 294920 | tf_op jit(solution)/shard_map/ppermute | solution.py:117
  91.1 7.0 %collective-permute-start.6 = (bf16[32,1536]{1,0:T(8,128)(2,1)S(1)}, bf16[32,1536]{1,0:T(8,128)(2,1)S(1)}, u32[]{:S(2)}, u32[]{:S(2)}) collective-permute-start(bf16[32,1536]{1,0:T(8,128)(2,1)S(1)} %get-tuple-element.80), channel_id=1, source_target_pairs={{0,7},{1,8},{2,9},{3,10},{4,11},{5,12},{6,13},{7,14},{8,15},{9,0},... | collective-permute-start | bytes 294920 | tf_op jit(solution)/shard_map/ppermute | solution.py:117
  98.1 6.1 %collective-permute-start.7 = (bf16[32,1536]{1,0:T(8,128)(2,1)S(1)}, bf16[32,1536]{1,0:T(8,128)(2,1)S(1)}, u32[]{:S(2)}, u32[]{:S(2)}) collective-permute-start(bf16[32,1536]{1,0:T(8,128)(2,1)S(1)} %get-tuple-element.79), channel_id=1, source_target_pairs={{0,8},{1,9},{2,10},{3,11},{4,12},{5,13},{6,14},{7,15},{8,0},{9,1},... | collective-permute-start | bytes 294920 | tf_op jit(solution)/shard_map/ppermute | solution.py:117
  104.2 6.7 %collective-permute-start.8 = (bf16[32,1536]{1,0:T(8,128)(2,1)S(1)}, bf16[32,1536]{1,0:T(8,128)(2,1)S(1)}, u32[]{:S(2)}, u32[]{:S(2)}) collective-permute-start(bf16[32,1536]{1,0:T(8,128)(2,1)S(1)} %get-tuple-element.78), channel_id=1, source_target_pairs={{0,9},{1,10},{2,11},{3,12},{4,13},{5,14},{6,15},{7,0},{8,1},{9,2},... | collective-permute-start | bytes 294920 | tf_op jit(solution)/shard_map/ppermute | solution.py:117
  110.9 7.0 %collective-permute-start.9 = (bf16[32,1536]{1,0:T(8,128)(2,1)S(1)}, bf16[32,1536]{1,0:T(8,128)(2,1)S(1)}, u32[]{:S(2)}, u32[]{:S(2)}) collective-permute-start(bf16[32,1536]{1,0:T(8,128)(2,1)S(1)} %get-tuple-element.77), channel_id=1, source_target_pairs={{0,10},{1,11},{2,12},{3,13},{4,14},{5,15},{6,0},{7,1},{8,2},{9,3},... | collective-permute-start | bytes 294920 | tf_op jit(solution)/shard_map/ppermute | solution.py:117
  118.0 7.9 %collective-permute-start.10 = (bf16[32,1536]{1,0:T(8,128)(2,1)S(1)}, bf16[32,1536]{1,0:T(8,128)(2,1)S(1)}, u32[]{:S(2)}, u32[]{:S(2)}) collective-permute-start(bf16[32,1536]{1,0:T(8,128)(2,1)S(1)} %get-tuple-element.76), channel_id=1, source_target_pairs={{0,11},{1,12},{2,13},{3,14},{4,15},{5,0},{6,1},{7,2},{8,3},{9,4},{... | collective-permute-start | bytes 294920 | tf_op jit(solution)/shard_map/ppermute | solution.py:117
  128.4 53.4 %all-to-all-start.2 = ((bf16[16,32,1536]{2,1,0:T(8,128)(2,1)}), bf16[16,32,1536]{2,1,0:T(8,128)(2,1)S(1)}, u32[]{:S(2)}, u32[]{:S(2)}) async-start(bf16[16,32,1536]{2,1,0:T(8,128)(2,1)} %get-tuple-element.70), calls=%async_computation.2 | async-start | bytes 3145728 | tf_op jit(solution)/shard_map/all_to_all | solution.py:189
  181.8 1.2 copy-start
  183.0 43.2 %all-to-all-start.1 = ((bf16[16,32,1536]{2,1,0:T(8,128)(2,1)}), bf16[16,32,1536]{2,1,0:T(8,128)(2,1)S(1)}, u32[]{:S(2)}, u32[]{:S(2)}) async-start(bf16[16,32,1536]{2,1,0:T(8,128)(2,1)} %bitcast.180), calls=%async_computation.1 | async-start | bytes 3145728 | tf_op jit(solution)/shard_map/all_to_all | solution.py:196
  226.2 1.2 copy-start.2
  227.4 24.5 %all-to-all-start.3 = ((bf16[16,32,1536]{2,1,0:T(8,128)(2,1)}), bf16[16,32,1536]{2,1,0:T(8,128)(2,1)S(1)}, u32[]{:S(2)}, u32[]{:S(2)}) async-start(bf16[16,32,1536]{2,1,0:T(8,128)(2,1)} %bitcast.181), calls=%async_computation.3 | async-start | bytes 3145728 | tf_op jit(solution)/shard_map/all_to_all | solution.py:196
  234.6 2.0 copy-start.7
  236.6 1.2 copy-start.9
  237.3 1.3 copy-start.8
  251.9 1.2 copy-start.3
  253.1 36.3 %all-to-all-start.4 = ((bf16[128,32,256]{2,1,0:T(8,128)(2,1)}), bf16[128,32,256]{2,1,0:T(8,128)(2,1)S(1)}, u32[]{:S(2)}, u32[]{:S(2)}) async-start(bf16[128,32,256]{2,1,0:T(8,128)(2,1)} %bitcast.68), calls=%async_computation.4 | async-start | bytes 4194304 | tf_op jit(solution)/shard_map/all_to_all | solution.py:216
  259.9 2.4 copy-start.4
  263.2 2.0 copy-start.1

commit v10 on v8

--- a/solution.py
+++ b/solution.py
@@ -151,14 +151,24 @@
         ],
         axis=3,
     ).reshape(seg_count, rows_here, kv_heads, 2 * HD).transpose(0, 2, 1, 3)
-    anc_send = jnp.broadcast_to(
-        out_heads[:, :, None], (seg_count, kv_heads, pair_count, rows_here, 2 * HD)
-    ).reshape(seg_count * leaf_count, rows_here, 2 * HD)
-    anc_arrived = lax.all_to_all(anc_send, ("seg", "leaf"), split_axis=0, concat_axis=0, tiled=True)
-    anc_arrived = anc_arrived.reshape(seg_count, leaf_count * rows_here, 2 * HD)
-    anc_got = jnp.where(
-        my_alive[:, None, None], jnp.take(anc_arrived, my_owners, axis=0), jnp.zeros((), jnp.bfloat16)
-    ).reshape(levels * seg_len, 2 * HD)
+    anc_send = out_heads.reshape(seg_count * kv_heads, rows_here, 2 * HD)
+    parity_groups = [
+        [s * leaf_count + j for s in range(seg_count) for j in range(leaf_count) if j % pair_count == q]
+        for q in range(pair_count)
+    ]
+    anc_half = lax.all_to_all(
+        anc_send, ("seg", "leaf"), split_axis=0, concat_axis=0, tiled=True, axis_index_groups=parity_groups
+    )
+    anc_half = anc_half.reshape(seg_count, leaf_count // pair_count, rows_here, 2 * HD)
+    mine = jnp.where(
+        my_alive[:, None, None, None], jnp.take(anc_half, my_owners, axis=0), jnp.zeros((), jnp.bfloat16)
+    )
+    swap = [(j, j + 1 - 2 * (j % 2)) for j in range(leaf_count)]
+    theirs = lax.ppermute(mine, "leaf", swap)
+    my_parity = leaf_here % pair_count
+    even = jnp.where(my_parity == 0, mine, theirs)
+    odd = jnp.where(my_parity == 0, theirs, mine)
+    anc_got = jnp.stack([even, odd], axis=2).reshape(levels * seg_len, 2 * HD)
     anc_mask = jnp.repeat(my_alive, seg_len).astype(jnp.float32)[None, :]
 
     def to_heads(x, width):

time: 234 us -> 251 us (1.073)
  waiting for transfers between devices: 79.5 us -> 91 us
    ppermute x0 -> x1, waiting for transfers between devices: none -> 22.7 us  [on_device(): theirs = lax.ppermute(mine, 'leaf', swap)]
    all_to_all x1, waiting for transfers between devices: 28.9 us -> 15 us  [on_device(): lax.all_to_all(anc_send, ('seg', 'leaf'), split_axis=0, concat_axis=0, ti...]
    all_to_all x1, starting transfers between devices: 6.37 us -> 11.7 us  [on_device(): lax.all_to_all(anc_send, ('seg', 'leaf'), split_axis=0, concat_axis=0, ti...]
    all_to_all x2, starting transfers between devices: 12 us -> 7.42 us  [on_device(): lax.all_to_all(packed[:, chunk], 'leaf', split_axis=0, concat_axis=0, til...]
    all_to_all x2, waiting for transfers between devices: 22.8 us -> 25.6 us  [on_device(): lax.all_to_all(packed[:, chunk], 'leaf', split_axis=0, concat_axis=0, til...]
    unnamed x43 -> x37, local copies, waits for them, and re-layouts: 8.64 us -> 8.23 us
  transfers between devices with their start and end apart: 6 -> 7, of which waited for: 4 -> 5; matrix products, arithmetic and copies ran while one was open for 17% -> 17% of each run, Pallas kernels for 27% -> 25%
where the time goes in v10:
time: 251 us; the launch traced here: 250 us
  waiting for transfers between devices  91 us (36%)
  Pallas kernels  62.8 us (25%)
  starting transfers between devices  40.1 us (16%)
  local copies, waits for them, and re-layouts  36.3 us (14%)
  other arithmetic  14.8 us (6%)
  matrix products  3.52 us (1%)
    pallas_call x2, Pallas kernels, attend_all(): pl.pallas_call(attend_kernel, grid=grid, in_specs=[maskspec, qspec, gspec...  62.8 us
    all_to_all x2, waiting for transfers between devices, on_device(): lax.all_to_all(packed[:, chunk], 'leaf', split_axis=0, concat_axis=0, til...  25.6 us
    ppermute x1, waiting for transfers between devices, on_device(): theirs = lax.ppermute(mine, 'leaf', swap)  22.7 us
    all_to_all x1, waiting for transfers between devices, on_device(): lax.all_to_all(anc_send, ('seg', 'leaf'), split_axis=0, concat_axis=0, ti...  15 us
    all_to_all x2, starting transfers between devices, on_device(): lax.all_to_all(back, 'leaf', split_axis=0, concat_axis=0, tiled=True)  14.4 us
    all_to_all x1, waiting for transfers between devices, on_device(): lax.all_to_all(homeward, ('seg', 'leaf'), split_axis=0, concat_axis=0, ti...  14.2 us
    all_to_all x2, waiting for transfers between devices, on_device(): lax.all_to_all(back, 'leaf', split_axis=0, concat_axis=0, tiled=True)  13.5 us
    all_to_all x1, starting transfers between devices, on_device(): lax.all_to_all(anc_send, ('seg', 'leaf'), split_axis=0, concat_axis=0, ti...  11.7 us
  transfers between devices with their start and end apart: 7, of which 5 were waited for; matrix products, arithmetic and copies ran while one was open for 17% of the time, Pallas kernels for 25%

profile of v10, /device:TPU:0, one launch (start us, length us, event | category | flops | bytes accessed | tf_op | source)
XLA Modules:
  0.0 249.5 jit_solution(7467157796797040668)
XLA Ops:
  5.2 1.2 copy.80
  6.5 11.7 %all-to-all-start.1 = ((bf16[64,32,256]{2,1,0:T(8,128)(2,1)}), bf16[64,32,256]{2,1,0:T(8,128)(2,1)S(1)}, u32[]{:S(2)}, u32[]{:S(2)}) async-start(bf16[64,32,256]{2,1,0:T(8,128)(2,1)} %bitcast.15), calls=%async_computation.1 | async-start | bytes 2097152 | tf_op jit(solution)/shard_map/all_to_all | solution.py:159
  20.6 1.9 slice_bitcast_fusion
  22.4 15.0 %all-to-all-done.1 = bf16[64,32,256]{2,1,0:T(8,128)(2,1)S(1)} async-done(((bf16[64,32,256]{2,1,0:T(8,128)(2,1)}), bf16[64,32,256]{2,1,0:T(8,128)(2,1)S(1)}, u32[]{:S(2)}, u32[]{:S(2)}) %all-to-all-start.1) | async-done | bytes 1048608 | tf_op jit(solution)/shard_map/all_to_all | solution.py:159
  37.4 3.7 %all-to-all-start = ((bf16[16,32,1536]{2,1,0:T(8,128)(2,1)}), bf16[16,32,1536]{2,1,0:T(8,128)(2,1)S(1)}, u32[]{:S(2)}, u32[]{:S(2)}) async-start(bf16[16,32,1536]{2,1,0:T(8,128)(2,1)} %get-tuple-element.59), calls=%async_computation | async-start | bytes 3145728 | tf_op jit(solution)/shard_map/all_to_all | solution.py:185
  41.3 25.6 %all-to-all-done = bf16[16,32,1536]{2,1,0:T(8,128)(2,1)S(1)} async-done(((bf16[16,32,1536]{2,1,0:T(8,128)(2,1)}), bf16[16,32,1536]{2,1,0:T(8,128)(2,1)S(1)}, u32[]{:S(2)}, u32[]{:S(2)}) %all-to-all-start) | async-done | bytes 1572896 | tf_op jit(solution)/shard_map/all_to_all | solution.py:185
  66.9 3.7 %all-to-all-start.3 = ((bf16[16,32,1536]{2,1,0:T(8,128)(2,1)}), bf16[16,32,1536]{2,1,0:T(8,128)(2,1)S(1)}, u32[]{:S(2)}, u32[]{:S(2)}) async-start(bf16[16,32,1536]{2,1,0:T(8,128)(2,1)} %get-tuple-element.58), calls=%async_computation.3 | async-start | bytes 3145728 | tf_op jit(solution)/shard_map/all_to_all | solution.py:185
  70.9 2.6 %gather_fusion = bf16[4,8,32,256]{3,2,1,0:T(8,128)(2,1)} fusion(bf16[8,8,32,256]{3,2,1,0:T(8,128)(2,1)} %bitcast.126, s32[1024]{0:T(1024)S(1)} %pad_clamp_fusion), kind=kCustom, calls=%fused_computation | custom fusion | bytes 1048592 | tf_op jit(solution)/shard_map/jit(_take)/gather | solution.py:164
  73.5 2.0 select_select_fusion
  75.4 1.8 collective-permute-start
  77.9 22.7 %collective-permute-done = bf16[4,8,32,256]{3,2,1,0:T(8,128)(2,1)S(1)} collective-permute-done((bf16[4,8,32,256]{3,2,1,0:T(8,128)(2,1)}, bf16[4,8,32,256]{3,2,1,0:T(8,128)(2,1)S(1)}, u32[]{:S(2)}, u32[]{:S(2)}) %collective-permute-start) | collective-permute-done | bytes 524320 | tf_op jit(solution)/shard_map/ppermute | solution.py:167
  100.7 1.2 select_bitcast_fusion.1
  102.9 31.4 %shard_map.127 = (bf16[1,512,640]{2,1,0:T(8,128)(2,1)}, bf16[1,512,640]{2,1,0:T(8,128)(2,1)}, f32[1,512,128]{2,1,0:T(8,128)}, f32[1,512,128]{2,1,0:T(8,128)}, f32[2048,128]{1,0:T(8,128)}, /*index=5*/f32[2048,128]{1,0:T(8,128)}) custom-call(f32[1,2048]{1,0:T(1,128)} %bitcast.139, bf16[1,512,1536]{2,1,0:T(8,128)(2,1)} %bitcast.106, ...), custom_call_target="tpu_custom_call" | custom-call | tf_op jit(solution)/shard_map/pallas_call | solution.py:101
  136.2 2.6 %pad_maximum_fusion.1 = bf16[1,512,1536]{2,1,0:T(8,128)(2,1)} fusion(bf16[1,512,128]{2,1,0:T(8,128)(2,1)S(1)} %convert_element_type.65, bf16[1,512,128]{2,1,0:T(8,128)(2,1)S(1)} %convert_element_type.64, bf16[1,512,640]{2,1,0:T(8,128)(2,1)} %get-tuple-element.19, bf16[1,512,640]{2,1,0:T(8,128)(2,1)} %get-tuple-element.18), kind=kLoop, calls=%fused_computation.11 | loop fusion | flops 6291456 | bytes 3145728 | tf_op jit(solution)/shard_map/concatenate | solution.py:190
  138.8 7.2 %all-to-all-start.2 = ((bf16[16,32,1536]{2,1,0:T(8,128)(2,1)}), bf16[16,32,1536]{2,1,0:T(8,128)(2,1)S(1)}, u32[]{:S(2)}, u32[]{:S(2)}) async-start(bf16[16,32,1536]{2,1,0:T(8,128)(2,1)} %bitcast.120), calls=%async_computation.2 | async-start | bytes 3145728 | tf_op jit(solution)/shard_map/all_to_all | solution.py:192
  146.0 31.4 %shard_map.128 = (bf16[1,512,640]{2,1,0:T(8,128)(2,1)}, bf16[1,512,640]{2,1,0:T(8,128)(2,1)}, f32[1,512,128]{2,1,0:T(8,128)}, f32[1,512,128]{2,1,0:T(8,128)}, f32[2048,128]{1,0:T(8,128)}, /*index=5*/f32[2048,128]{1,0:T(8,128)}) custom-call(f32[1,2048]{1,0:T(1,128)} %bitcast.140, bf16[1,512,1536]{2,1,0:T(8,128)(2,1)} %bitcast.110, ...), custom_call_target="tpu_custom_call" | custom-call | tf_op jit(solution)/shard_map/pallas_call | solution.py:101
  179.3 2.6 %pad_maximum_fusion.2 = bf16[1,512,1536]{2,1,0:T(8,128)(2,1)} fusion(bf16[1,512,128]{2,1,0:T(8,128)(2,1)S(1)} %convert_element_type.67, bf16[1,512,128]{2,1,0:T(8,128)(2,1)S(1)} %convert_element_type.66, bf16[1,512,640]{2,1,0:T(8,128)(2,1)} %get-tuple-element.23, bf16[1,512,640]{2,1,0:T(8,128)(2,1)} %get-tuple-element.22), kind=kLoop, calls=%fused_computation.12 | loop fusion | flops 6291456 | bytes 3145728 | tf_op jit(solution)/shard_map/concatenate | solution.py:190
  181.9 7.2 %all-to-all-start.4 = ((bf16[16,32,1536]{2,1,0:T(8,128)(2,1)}), bf16[16,32,1536]{2,1,0:T(8,128)(2,1)S(1)}, u32[]{:S(2)}, u32[]{:S(2)}) async-start(bf16[16,32,1536]{2,1,0:T(8,128)(2,1)} %bitcast.121), calls=%async_computation.4 | async-start | bytes 3145728 | tf_op jit(solution)/shard_map/all_to_all | solution.py:192
  189.2 2.0 copy.84
  193.3 2.3 convolution_convert_fusion.1
  195.6 1.8 copy.88
  197.4 13.5 %all-to-all-done.4 = bf16[16,32,1536]{2,1,0:T(8,128)(2,1)S(1)} async-done(((bf16[16,32,1536]{2,1,0:T(8,128)(2,1)}), bf16[16,32,1536]{2,1,0:T(8,128)(2,1)S(1)}, u32[]{:S(2)}, u32[]{:S(2)}) %all-to-all-start.4) | async-done | bytes 1572896 | tf_op jit(solution)/shard_map/all_to_all | solution.py:192
  210.9 1.1 copy-done.4
  212.0 4.9 %all-to-all-start.5 = ((bf16[128,32,256]{2,1,0:T(8,128)(2,1)}), bf16[128,32,256]{2,1,0:T(8,128)(2,1)S(1)}, u32[]{:S(2)}, u32[]{:S(2)}) async-start(bf16[128,32,256]{2,1,0:T(8,128)(2,1)} %bitcast.39), calls=%async_computation.5 | async-start | bytes 4194304 | tf_op jit(solution)/shard_map/all_to_all | solution.py:212
  216.9 2.4 copy_dynamic-update-slice_fusion.1
  220.2 1.5 slice_bitcast_fusion.2
  222.2 3.2 %reshape.169 = bf16[4,32,5120]{2,1,0:T(8,128)(2,1)} reshape(bf16[2,2,32,8,640]{4,3,2,1,0:T(8,128)(2,1)} %get-tuple-element.56) | data formatting | bytes 2621440 | tf_op jit(solution)/shard_map/reshape | solution.py:198
  225.4 1.9 slice_bitcast_fusion.6
  227.3 1.8 reshape.171
  229.1 1.8 reshape.170
  230.8 1.4 reshape.168
  232.3 14.2 %all-to-all-done.5 = bf16[128,32,256]{2,1,0:T(8,128)(2,1)S(1)} async-done(((bf16[128,32,256]{2,1,0:T(8,128)(2,1)}), bf16[128,32,256]{2,1,0:T(8,128)(2,1)S(1)}, u32[]{:S(2)}, u32[]{:S(2)}) %all-to-all-start.5) | async-done | bytes 2097184 | tf_op jit(solution)/shard_map/all_to_all | solution.py:212
  (74 shorter events, 19.3 us)
Async XLA Ops:
  5.2 12.9 %copy-start.12 = (bf16[4,32,1024]{2,1,0:T(8,128)(2,1)S(1)}, bf16[4,32,1024]{2,1,0:T(8,128)(2,1)}, u32[]{:S(2)}) copy-start(bf16[4,32,1024]{2,1,0:T(8,128)(2,1)} %param.9) | copy-start | bytes 786436
  6.5 11.8 %copy-start.13 = (bf16[4,32,1024]{2,1,0:T(8,128)(2,1)S(1)}, bf16[4,32,1024]{2,1,0:T(8,128)(2,1)}, u32[]{:S(2)}) copy-start(bf16[4,32,1024]{2,1,0:T(8,128)(2,1)} %param.10) | copy-start | bytes 786436
  6.5 11.9 %copy-start.7 = (bf16[4,32,5120]{2,1,0:T(8,128)(2,1)S(1)}, bf16[4,32,5120]{2,1,0:T(8,128)(2,1)}, u32[]{:S(2)}) copy-start(bf16[4,32,5120]{2,1,0:T(8,128)(2,1)} %param.8) | copy-start | bytes 3932164
  6.5 30.9 %all-to-all-start.1 = ((bf16[64,32,256]{2,1,0:T(8,128)(2,1)}), bf16[64,32,256]{2,1,0:T(8,128)(2,1)S(1)}, u32[]{:S(2)}, u32[]{:S(2)}) async-start(bf16[64,32,256]{2,1,0:T(8,128)(2,1)} %bitcast.15), calls=%async_computation.1 | async-start | bytes 2097152 | tf_op jit(solution)/shard_map/all_to_all | solution.py:159
  18.4 1.3 copy-start.8
  37.4 29.6 %copy-start.6 = (bf16[64,32,256]{2,1,0:T(8,128)(2,1)}, bf16[64,32,256]{2,1,0:T(8,128)(2,1)S(1)}, u32[]{:S(2)}) copy-start(bf16[64,32,256]{2,1,0:T(8,128)(2,1)S(1)} %all-to-all-done.1) | copy-start | bytes 3145732
  37.4 29.5 %all-to-all-start = ((bf16[16,32,1536]{2,1,0:T(8,128)(2,1)}), bf16[16,32,1536]{2,1,0:T(8,128)(2,1)S(1)}, u32[]{:S(2)}, u32[]{:S(2)}) async-start(bf16[16,32,1536]{2,1,0:T(8,128)(2,1)} %get-tuple-element.59), calls=%async_computation | async-start | bytes 3145728 | tf_op jit(solution)/shard_map/all_to_all | solution.py:185
  66.9 6.5 %copy-start = (bf16[16,32,1536]{2,1,0:T(8,128)(2,1)}, bf16[16,32,1536]{2,1,0:T(8,128)(2,1)S(1)}, u32[]{:S(2)}) copy-start(bf16[16,32,1536]{2,1,0:T(8,128)(2,1)S(1)} %all-to-all-done) | copy-start | bytes 4718596
  66.9 71.9 %all-to-all-start.3 = ((bf16[16,32,1536]{2,1,0:T(8,128)(2,1)}), bf16[16,32,1536]{2,1,0:T(8,128)(2,1)S(1)}, u32[]{:S(2)}, u32[]{:S(2)}) async-start(bf16[16,32,1536]{2,1,0:T(8,128)(2,1)} %get-tuple-element.58), calls=%async_computation.3 | async-start | bytes 3145728 | tf_op jit(solution)/shard_map/all_to_all | solution.py:185
  75.4 25.2 %collective-permute-start = (bf16[4,8,32,256]{3,2,1,0:T(8,128)(2,1)}, bf16[4,8,32,256]{3,2,1,0:T(8,128)(2,1)S(1)}, u32[]{:S(2)}, u32[]{:S(2)}) collective-permute-start(bf16[4,8,32,256]{3,2,1,0:T(8,128)(2,1)} %select_select_fusion), channel_id=1, source_target_pairs={{0,1},{1,0},{2,3},{3,2},{4,5},{5,4},{6,7},{7,6},{8,9},{9,8},{10,11... | collective-permute-start | bytes 1572872 | tf_op jit(solution)/shard_map/ppermute | solution.py:167
  138.8 7.2 %copy-start.1 = (bf16[16,32,1536]{2,1,0:T(8,128)(2,1)}, bf16[16,32,1536]{2,1,0:T(8,128)(2,1)S(1)}, u32[]{:S(2)}) copy-start(bf16[16,32,1536]{2,1,0:T(8,128)(2,1)S(1)} %all-to-all-done.3) | copy-start | bytes 4718596
  138.8 43.1 %all-to-all-start.2 = ((bf16[16,32,1536]{2,1,0:T(8,128)(2,1)}), bf16[16,32,1536]{2,1,0:T(8,128)(2,1)S(1)}, u32[]{:S(2)}, u32[]{:S(2)}) async-start(bf16[16,32,1536]{2,1,0:T(8,128)(2,1)} %bitcast.120), calls=%async_computation.2 | async-start | bytes 3145728 | tf_op jit(solution)/shard_map/all_to_all | solution.py:192
  181.9 9.3 %copy-start.3 = (bf16[16,32,1536]{2,1,0:T(8,128)(2,1)}, bf16[16,32,1536]{2,1,0:T(8,128)(2,1)S(1)}, u32[]{:S(2)}) copy-start(bf16[16,32,1536]{2,1,0:T(8,128)(2,1)S(1)} %all-to-all-done.2) | copy-start | bytes 4718596
  181.9 29.0 %all-to-all-start.4 = ((bf16[16,32,1536]{2,1,0:T(8,128)(2,1)}), bf16[16,32,1536]{2,1,0:T(8,128)(2,1)S(1)}, u32[]{:S(2)}, u32[]{:S(2)}) async-start(bf16[16,32,1536]{2,1,0:T(8,128)(2,1)} %bitcast.121), calls=%async_computation.4 | async-start | bytes 3145728 | tf_op jit(solution)/shard_map/all_to_all | solution.py:192
  189.1 2.1 copy-start.9
  189.2 2.8 %copy-start.11 = (f32[2048,128]{1,0:T(8,128)S(1)}, f32[2048,128]{1,0:T(8,128)}, u32[]{:S(2)}) copy-start(f32[2048,128]{1,0:T(8,128)} %get-tuple-element.28) | copy-start | bytes 3145732
  191.2 1.4 copy-start.10
  210.9 1.1 copy-start.4
  212.0 34.4 %all-to-all-start.5 = ((bf16[128,32,256]{2,1,0:T(8,128)(2,1)}), bf16[128,32,256]{2,1,0:T(8,128)(2,1)S(1)}, u32[]{:S(2)}, u32[]{:S(2)}) async-start(bf16[128,32,256]{2,1,0:T(8,128)(2,1)} %bitcast.39), calls=%async_computation.5 | async-start | bytes 4194304 | tf_op jit(solution)/shard_map/all_to_all | solution.py:212
  216.9 2.4 copy-start.5
  220.2 2.0 copy-start.2

commit v11 on v8

--- a/solution.py
+++ b/solution.py
@@ -14,7 +14,7 @@
 
 
 def attend_kernel(mask_ref, q_ref, g_ref, ko_ref, vo_ref, ka_ref, va_ref,
-                  o_ref, dq_ref, dko_ref, dvo_ref, dka_ref, dva_ref, dko_acc, dvo_acc):
+                  back_ref, dka_ref, dva_ref, dko_acc, dvo_acc):
     leaf_i = pl.program_id(0)
     head_i = pl.program_id(1)
     row_i = pl.program_id(2)
@@ -59,14 +59,15 @@
     pb_o = p_o.astype(jnp.bfloat16)
     o = jnp.dot(pb_a, va, preferred_element_type=jnp.float32) + jnp.dot(pb_o, vo, preferred_element_type=jnp.float32)
     o_b = o.astype(jnp.bfloat16)
-    o_ref[...] = o_b
+    row_span = pl.ds(pl.multiple_of(row_i * block_rows, block_rows), block_rows)
+    back_ref[row_span, pl.ds(pl.multiple_of(head_i * HD, HD), HD)] = o_b
     delta = jnp.sum(g.astype(jnp.float32) * o_b.astype(jnp.float32), axis=1, keepdims=True)
     dp_a = lax.dot_general(g, va, nt, preferred_element_type=jnp.float32)
     dp_o = lax.dot_general(g, vo, nt, preferred_element_type=jnp.float32)
     ds_a = (p_a * (dp_a - delta)).astype(jnp.bfloat16)
     ds_o = (p_o * (dp_o - delta)).astype(jnp.bfloat16)
     dq = (jnp.dot(ds_a, ka, preferred_element_type=jnp.float32) + jnp.dot(ds_o, ko, preferred_element_type=jnp.float32)) * scale
-    dq_ref[...] = dq.astype(jnp.bfloat16)
+    back_ref[row_span, pl.ds(pl.multiple_of((head_count + head_i) * HD, HD), HD)] = dq.astype(jnp.bfloat16)
     dka_ref[...] += lax.dot_general(ds_a, q, tn, preferred_element_type=jnp.float32)
     dva_ref[...] += lax.dot_general(pb_a, g, tn, preferred_element_type=jnp.float32)
     dko_acc[...] += lax.dot_general(ds_o, q, tn, preferred_element_type=jnp.float32)
@@ -74,8 +75,8 @@
 
     @pl.when((head_i == head_count - 1) & (row_i == row_count - 1))
     def _():
-        dko_ref[...] = dko_acc[...] * scale
-        dvo_ref[...] = dvo_acc[...]
+        back_ref[:, 2 * head_count * HD : (2 * head_count + 1) * HD] = (dko_acc[...] * scale).astype(jnp.bfloat16)
+        back_ref[:, (2 * head_count + 1) * HD :] = dvo_acc[...].astype(jnp.bfloat16)
 
     @pl.when((leaf_i == pl.num_programs(0) - 1) & (head_i == head_count - 1) & (row_i == row_count - 1))
     def _():
@@ -95,15 +96,15 @@
     maskspec = pl.BlockSpec((1, anc), lambda l, h, r: (0, 0))
     ownspec = pl.BlockSpec((None, seg_len, HD), lambda l, h, r: (l, 0, 0))
     ancspec = pl.BlockSpec((anc, HD), lambda l, h, r: (0, 0))
-    out_rows = jax.ShapeDtypeStruct((leaves, seg_len, heads * HD), jnp.bfloat16)
-    own_grad = jax.ShapeDtypeStruct((leaves, seg_len, HD), jnp.float32)
+    back_rows = jax.ShapeDtypeStruct((leaves, seg_len, (2 * heads + 2) * HD), jnp.bfloat16)
+    backspec = pl.BlockSpec((None, seg_len, (2 * heads + 2) * HD), lambda l, h, r: (l, 0, 0))
     anc_grad = jax.ShapeDtypeStruct((anc, HD), jnp.float32)
     return pl.pallas_call(
         attend_kernel,
         grid=grid,
         in_specs=[maskspec, qspec, gspec, kospec, vospec, kaspec, vaspec],
-        out_specs=[qspec, qspec, ownspec, ownspec, ancspec, ancspec],
-        out_shape=[out_rows, out_rows, own_grad, own_grad, anc_grad, anc_grad],
+        out_specs=[backspec, ancspec, ancspec],
+        out_shape=[back_rows, anc_grad, anc_grad],
         scratch_shapes=[pltpu.VMEM((seg_len, HD), jnp.float32), pltpu.VMEM((seg_len, HD), jnp.float32)],
         compiler_params=pltpu.CompilerParams(dimension_semantics=("arbitrary", "arbitrary", "arbitrary")),
     )(anc_mask, packed, packed, packed, packed, anc_rows, anc_rows)
@@ -174,10 +175,9 @@
     for chunk in range(pair_leaves):
         got = lax.all_to_all(packed[:, chunk], "leaf", split_axis=0, concat_axis=0, tiled=True)
         got = got.reshape(1, seg_len, packed.shape[3])
-        res, dq, dko, dvo, dka, dva = attend_all(anc_mask, got, anc_got, group_heads)
+        back, dka, dva = attend_all(anc_mask, got, anc_got, group_heads)
         part = jnp.concatenate([dka, dva], axis=1)
         anc_partial = part if anc_partial is None else anc_partial + part
-        back = jnp.concatenate([res, dq, dko.astype(jnp.bfloat16), dvo.astype(jnp.bfloat16)], axis=2)
         back = back.reshape(leaf_count, rows_here, back.shape[2])
         homes.append(lax.all_to_all(back, "leaf", split_axis=0, concat_axis=0, tiled=True))
     home = jnp.stack(homes, axis=1)

time: 234 us -> 225 us (0.962)
  other arithmetic: 13 us -> 3.96 us
    concatenate x2 -> x0, other arithmetic: 5.15 us -> none  [on_device(): jnp.concatenate([res, dq, dko.astype(jnp.bfloat16), dvo.astype(jnp.bfloat...]
    convert_element_type x4 -> x0, other arithmetic: 3.87 us -> none  [the longest x2 1.93 us: on_device(): dko.astype(jnp.bfloat16)]
  transfers between devices with their start and end apart: 6 -> 6, of which waited for: 4 -> 4; matrix products, arithmetic and copies ran while one was open for 17% -> 14% of each run, Pallas kernels for 27% -> 28%
where the time goes in v11:
time: 225 us
  waiting for transfers between devices  79.6 us (35%)
  Pallas kernels  63.2 us (28%)
  starting transfers between devices  37.6 us (17%)
  local copies, waits for them, and re-layouts  35.7 us (16%)
  other arithmetic  3.96 us (2%)
  matrix products  3.52 us (2%)
    pallas_call x2, Pallas kernels, attend_all(): pl.pallas_call(attend_kernel, grid=grid, in_specs=[maskspec, qspec, gspec...  63.2 us
    all_to_all x1, waiting for transfers between devices, on_device(): lax.all_to_all(anc_send, ('seg', 'leaf'), split_axis=0, concat_axis=0, ti...  28.9 us
    all_to_all x2, waiting for transfers between devices, on_device(): lax.all_to_all(packed[:, chunk], 'leaf', split_axis=0, concat_axis=0, til...  22.8 us
    all_to_all x2, starting transfers between devices, on_device(): lax.all_to_all(back, 'leaf', split_axis=0, concat_axis=0, tiled=True)  14.4 us
    all_to_all x1, waiting for transfers between devices, on_device(): lax.all_to_all(homeward, ('seg', 'leaf'), split_axis=0, concat_axis=0, ti...  14.2 us
    all_to_all x2, waiting for transfers between devices, on_device(): lax.all_to_all(back, 'leaf', split_axis=0, concat_axis=0, tiled=True)  13.7 us
    all_to_all x2, starting transfers between devices, on_device(): lax.all_to_all(packed[:, chunk], 'leaf', split_axis=0, concat_axis=0, til...  12 us
    unnamed x43, local copies, waits for them, and re-layouts  8.64 us
  transfers between devices with their start and end apart: 6, of which 4 were waited for; matrix products, arithmetic and copies ran while one was open for 14% of the time, Pallas kernels for 28%

profile of v11, /device:TPU:0, one launch (start us, length us, event | category | flops | bytes accessed | tf_op | source)
XLA Modules:
  0.0 224.7 jit_solution(2624036256614423479)
XLA Ops:
  0.6 1.1 copy.93
  1.8 1.0 copy.94
  3.3 0.9 copy-done.7
  5.0 1.9 slice_bitcast_fusion
  6.9 8.3 %all-to-all-start = ((bf16[16,32,1536]{2,1,0:T(8,128)(2,1)}), bf16[16,32,1536]{2,1,0:T(8,128)(2,1)S(1)}, u32[]{:S(2)}, u32[]{:S(2)}) async-start(bf16[16,32,1536]{2,1,0:T(8,128)(2,1)} %get-tuple-element.47), calls=%async_computation | async-start | bytes 3145728 | tf_op jit(solution)/shard_map/all_to_all | solution.py:176
  17.0 22.8 %all-to-all-done = bf16[16,32,1536]{2,1,0:T(8,128)(2,1)S(1)} async-done(((bf16[16,32,1536]{2,1,0:T(8,128)(2,1)}), bf16[16,32,1536]{2,1,0:T(8,128)(2,1)S(1)}, u32[]{:S(2)}, u32[]{:S(2)}) %all-to-all-start) | async-done | bytes 1572896 | tf_op jit(solution)/shard_map/all_to_all | solution.py:176
  39.7 1.7 broadcast_in_dim.70
  41.5 6.4 %all-to-all-start.1 = ((bf16[128,32,256]{2,1,0:T(8,128)(2,1)}), bf16[128,32,256]{2,1,0:T(8,128)(2,1)}, u32[]{:S(2)}, u32[]{:S(2)}) async-start(bf16[128,32,256]{2,1,0:T(8,128)(2,1)} %bitcast.117), calls=%async_computation.1 | async-start | bytes 4194304 | tf_op jit(solution)/shard_map/all_to_all | solution.py:158
  48.3 28.9 %all-to-all-done.1 = bf16[128,32,256]{2,1,0:T(8,128)(2,1)} async-done(((bf16[128,32,256]{2,1,0:T(8,128)(2,1)}), bf16[128,32,256]{2,1,0:T(8,128)(2,1)}, u32[]{:S(2)}, u32[]{:S(2)}) %all-to-all-start.1) | async-done | bytes 2097184 | tf_op jit(solution)/shard_map/all_to_all | solution.py:158
  77.3 3.7 %all-to-all-start.3 = ((bf16[16,32,1536]{2,1,0:T(8,128)(2,1)}), bf16[16,32,1536]{2,1,0:T(8,128)(2,1)S(1)}, u32[]{:S(2)}, u32[]{:S(2)}) async-start(bf16[16,32,1536]{2,1,0:T(8,128)(2,1)} %get-tuple-element.46), calls=%async_computation.3 | async-start | bytes 3145728 | tf_op jit(solution)/shard_map/all_to_all | solution.py:176
  81.8 2.2 gather_fusion
  84.0 2.4 %fusion.6.ka_ref.va_ref = bf16[2048,256]{1,0:T(8,128)(2,1)} fusion(bf16[4,512,256]{2,1,0:T(8,128)(2,1)S(1)} %gather_fusion, pred[2048]{0:T(1024)(128)(4,1)S(1)} %bitcast.140, pred[2048]{0:T(1024)(128)(4,1)S(1)} %bitcast.141), kind=kLoop, calls=%fused_computation.18 | loop fusion | flops 1048576 | bytes 2101248 | tf_op jit(solution)/shard_map/jit(_where)/select_n | solution.py:160
  86.5 31.6 %shard_map.127 = (bf16[1,512,1536]{2,1,0:T(8,128)(2,1)}, f32[2048,128]{1,0:T(8,128)}, f32[2048,128]{1,0:T(8,128)}) custom-call(f32[1,2048]{1,0:T(1,128)} %bitcast.138, bf16[1,512,1536]{2,1,0:T(8,128)(2,1)} %bitcast.109, bf16[1,512,1536]{2,1,0:T(8,128)(2,1)} %bitcast.110, bf16[1,512,1536]{2,1,0:T(8,128)(2,1)} %bitcast.111, bf16[1,512,1536]{2,1,0:T(8,128)(2,1)} %bitcast.112, ...), custom_call_target="tpu_custom_call" | custom-call | tf_op jit(solution)/shard_map/pallas_call | solution.py:102
  118.1 7.2 %all-to-all-start.2 = ((bf16[16,32,1536]{2,1,0:T(8,128)(2,1)}), bf16[16,32,1536]{2,1,0:T(8,128)(2,1)S(1)}, u32[]{:S(2)}, u32[]{:S(2)}) async-start(bf16[16,32,1536]{2,1,0:T(8,128)(2,1)} %bitcast.125), calls=%async_computation.2 | async-start | bytes 3145728 | tf_op jit(solution)/shard_map/all_to_all | solution.py:182
  125.3 31.5 %shard_map.128 = (bf16[1,512,1536]{2,1,0:T(8,128)(2,1)}, f32[2048,128]{1,0:T(8,128)}, f32[2048,128]{1,0:T(8,128)}) custom-call(f32[1,2048]{1,0:T(1,128)} %bitcast.139, bf16[1,512,1536]{2,1,0:T(8,128)(2,1)} %bitcast.113, bf16[1,512,1536]{2,1,0:T(8,128)(2,1)} %bitcast.114, bf16[1,512,1536]{2,1,0:T(8,128)(2,1)} %bitcast.115, bf16[1,512,1536]{2,1,0:T(8,128)(2,1)} %bitcast.116, ...), custom_call_target="tpu_custom_call" | custom-call | tf_op jit(solution)/shard_map/pallas_call | solution.py:102
  156.8 7.2 %all-to-all-start.4 = ((bf16[16,32,1536]{2,1,0:T(8,128)(2,1)}), bf16[16,32,1536]{2,1,0:T(8,128)(2,1)S(1)}, u32[]{:S(2)}, u32[]{:S(2)}) async-start(bf16[16,32,1536]{2,1,0:T(8,128)(2,1)} %bitcast.124), calls=%async_computation.4 | async-start | bytes 3145728 | tf_op jit(solution)/shard_map/all_to_all | solution.py:182
  164.1 2.0 copy.81
  168.2 2.3 %convolution_convert_fusion.1 = bf16[8,512,256]{2,0,1:T(8,128)(2,1)S(1)} fusion(f32[4,512,128]{2,0,1:T(4,128)S(1)} %copy.82, f32[4,512,128]{2,0,1:T(4,128)S(1)} %copy.81, f32[4,512,128]{2,0,1:T(4,128)S(1)} %copy.84, f32[4,512,128]{2,0,1:T(4,128)S(1)} %copy.83, s32[4]{0:T(128)S(1)} %select_reduce_fusion, pred[4]{0:T(512)(128)(4,1)S(1)} %select_reduce_fusion.1), kind=kOutput, calls=%fused_computation.8 | convolution fusion | flops 11534400 | bytes 6291476 | tf_op jit(solution)/shard_map/ok,krc->orc/dot_general | solution.py:198
  170.5 1.8 copy.85
  172.3 13.7 %all-to-all-done.4 = bf16[16,32,1536]{2,1,0:T(8,128)(2,1)S(1)} async-done(((bf16[16,32,1536]{2,1,0:T(8,128)(2,1)}), bf16[16,32,1536]{2,1,0:T(8,128)(2,1)S(1)}, u32[]{:S(2)}, u32[]{:S(2)}) %all-to-all-start.4) | async-done | bytes 1572896 | tf_op jit(solution)/shard_map/all_to_all | solution.py:182
  186.0 1.1 copy-done.4
  187.2 4.9 %all-to-all-start.5 = ((bf16[128,32,256]{2,1,0:T(8,128)(2,1)}), bf16[128,32,256]{2,1,0:T(8,128)(2,1)S(1)}, u32[]{:S(2)}, u32[]{:S(2)}) async-start(bf16[128,32,256]{2,1,0:T(8,128)(2,1)} %bitcast.36), calls=%async_computation.5 | async-start | bytes 4194304 | tf_op jit(solution)/shard_map/all_to_all | solution.py:202
  192.1 2.4 %copy_dynamic-update-slice_fusion.1 = bf16[8,2,2,32,1536]{4,0,3,2,1:T(8,128)(2,1)S(1)} fusion(bf16[8,2,1,32,1536]{4,3,1,0,2:T(8,128)(2,1)} %bitcast.118), kind=kLoop, calls=%fused_computation.12 | loop fusion | bytes 3145728
  194.5 0.9 copy_dynamic-update-slice_fusion
  195.3 1.5 slice_bitcast_fusion.2
  197.4 3.2 %reshape.170 = bf16[4,32,5120]{2,1,0:T(8,128)(2,1)} reshape(bf16[2,2,32,8,640]{4,3,2,1,0:T(8,128)(2,1)} %get-tuple-element.44) | data formatting | bytes 2621440 | tf_op jit(solution)/shard_map/reshape | solution.py:188
  200.6 1.9 slice_bitcast_fusion.6
  202.4 1.8 reshape.172
  204.2 1.8 reshape.171
  206.0 1.4 reshape.169
  207.4 14.2 %all-to-all-done.5 = bf16[128,32,256]{2,1,0:T(8,128)(2,1)S(1)} async-done(((bf16[128,32,256]{2,1,0:T(8,128)(2,1)}), bf16[128,32,256]{2,1,0:T(8,128)(2,1)S(1)}, u32[]{:S(2)}, u32[]{:S(2)}) %all-to-all-start.5) | async-done | bytes 2097184 | tf_op jit(solution)/shard_map/all_to_all | solution.py:202
  222.1 0.7 fusion.3
  (71 shorter events, 9.2 us)
Async XLA Ops:
  0.6 2.2 copy-start.6
  2.9 1.3 copy-start.7
  6.9 8.3 %copy-start.14 = (s32[32]{0:T(128)S(1)}, s32[32]{0:T(128)}, u32[]{:S(2)}) copy-start(s32[32]{0:T(128)} %param.15) | copy-start | bytes 388
  6.9 8.4 %copy-start.13 = (s32[32,4]{0,1:T(4,128)S(1)}, s32[32,4]{0,1:T(4,128)}, u32[]{:S(2)}) copy-start(s32[32,4]{0,1:T(4,128)} %param.14) | copy-start | bytes 1540
  6.9 8.5 %copy-start.11 = (bf16[2,32,1024]{2,1,0:T(8,128)(2,1)S(1)}, bf16[2,32,1024]{2,1,0:T(8,128)(2,1)}, u32[]{:S(2)}) copy-start(bf16[2,32,1024]{2,1,0:T(8,128)(2,1)} %param.11) | copy-start | bytes 393220
  6.9 8.7 %copy-start.12 = (bf16[2,32,1024]{2,1,0:T(8,128)(2,1)S(1)}, bf16[2,32,1024]{2,1,0:T(8,128)(2,1)}, u32[]{:S(2)}) copy-start(bf16[2,32,1024]{2,1,0:T(8,128)(2,1)} %param.12) | copy-start | bytes 393220
  6.9 32.8 %all-to-all-start = ((bf16[16,32,1536]{2,1,0:T(8,128)(2,1)}), bf16[16,32,1536]{2,1,0:T(8,128)(2,1)S(1)}, u32[]{:S(2)}, u32[]{:S(2)}) async-start(bf16[16,32,1536]{2,1,0:T(8,128)(2,1)} %get-tuple-element.47), calls=%async_computation | async-start | bytes 3145728 | tf_op jit(solution)/shard_map/all_to_all | solution.py:176
  39.7 1.8 copy-start
  41.5 35.7 %all-to-all-start.1 = ((bf16[128,32,256]{2,1,0:T(8,128)(2,1)}), bf16[128,32,256]{2,1,0:T(8,128)(2,1)}, u32[]{:S(2)}, u32[]{:S(2)}) async-start(bf16[128,32,256]{2,1,0:T(8,128)(2,1)} %bitcast.117), calls=%async_computation.1 | async-start | bytes 4194304 | tf_op jit(solution)/shard_map/all_to_all | solution.py:158
  77.3 40.9 %all-to-all-start.3 = ((bf16[16,32,1536]{2,1,0:T(8,128)(2,1)}), bf16[16,32,1536]{2,1,0:T(8,128)(2,1)S(1)}, u32[]{:S(2)}, u32[]{:S(2)}) async-start(bf16[16,32,1536]{2,1,0:T(8,128)(2,1)} %get-tuple-element.46), calls=%async_computation.3 | async-start | bytes 3145728 | tf_op jit(solution)/shard_map/all_to_all | solution.py:176
  118.1 7.2 %copy-start.1 = (bf16[16,32,1536]{2,1,0:T(8,128)(2,1)}, bf16[16,32,1536]{2,1,0:T(8,128)(2,1)S(1)}, u32[]{:S(2)}) copy-start(bf16[16,32,1536]{2,1,0:T(8,128)(2,1)S(1)} %all-to-all-done.3) | copy-start | bytes 4718596
  118.1 38.7 %all-to-all-start.2 = ((bf16[16,32,1536]{2,1,0:T(8,128)(2,1)}), bf16[16,32,1536]{2,1,0:T(8,128)(2,1)S(1)}, u32[]{:S(2)}, u32[]{:S(2)}) async-start(bf16[16,32,1536]{2,1,0:T(8,128)(2,1)} %bitcast.125), calls=%async_computation.2 | async-start | bytes 3145728 | tf_op jit(solution)/shard_map/all_to_all | solution.py:182
  156.8 9.3 %copy-start.3 = (bf16[16,32,1536]{2,1,0:T(8,128)(2,1)}, bf16[16,32,1536]{2,1,0:T(8,128)(2,1)S(1)}, u32[]{:S(2)}) copy-start(bf16[16,32,1536]{2,1,0:T(8,128)(2,1)S(1)} %all-to-all-done.2) | copy-start | bytes 4718596
  156.8 29.2 %all-to-all-start.4 = ((bf16[16,32,1536]{2,1,0:T(8,128)(2,1)}), bf16[16,32,1536]{2,1,0:T(8,128)(2,1)S(1)}, u32[]{:S(2)}, u32[]{:S(2)}) async-start(bf16[16,32,1536]{2,1,0:T(8,128)(2,1)} %bitcast.124), calls=%async_computation.4 | async-start | bytes 3145728 | tf_op jit(solution)/shard_map/all_to_all | solution.py:182
  164.1 2.1 copy-start.10
  164.1 2.8 %copy-start.9 = (f32[2048,128]{1,0:T(8,128)S(1)}, f32[2048,128]{1,0:T(8,128)}, u32[]{:S(2)}) copy-start(f32[2048,128]{1,0:T(8,128)} %get-tuple-element.17) | copy-start | bytes 3145732
  166.2 1.4 copy-start.8
  186.0 1.1 copy-start.4
  187.2 34.4 %all-to-all-start.5 = ((bf16[128,32,256]{2,1,0:T(8,128)(2,1)}), bf16[128,32,256]{2,1,0:T(8,128)(2,1)S(1)}, u32[]{:S(2)}, u32[]{:S(2)}) async-start(bf16[128,32,256]{2,1,0:T(8,128)(2,1)} %bitcast.36), calls=%async_computation.5 | async-start | bytes 4194304 | tf_op jit(solution)/shard_map/all_to_all | solution.py:202
  192.1 2.4 %copy-start.5 = (bf16[16,32,1536]{2,1,0:T(8,128)(2,1)S(1)}, bf16[16,32,1536]{2,1,0:T(8,128)(2,1)}, u32[]{:S(2)}) copy-start(bf16[16,32,1536]{2,1,0:T(8,128)(2,1)} %copy-done.4) | copy-start | bytes 4718596
  195.3 2.0 copy-start.2

commit v12 on v11

--- a/solution.py
+++ b/solution.py
@@ -13,8 +13,10 @@
 NEG_FILL = -1e30
 
 
-def attend_kernel(mask_ref, q_ref, g_ref, ko_ref, vo_ref, ka_ref, va_ref,
-                  back_ref, dka_ref, dva_ref, dko_acc, dvo_acc):
+def attend_kernel(owner_ref, mask_ref, q_ref, g_ref, ko_ref, vo_ref, *refs):
+    levels = (len(refs) - 5) // 2
+    ka_refs, va_refs = refs[:levels], refs[levels : 2 * levels]
+    back_ref, dka_ref, dva_ref, dko_acc, dvo_acc = refs[2 * levels :]
     leaf_i = pl.program_id(0)
     head_i = pl.program_id(1)
     row_i = pl.program_id(2)
@@ -38,8 +40,8 @@
     tn = (((0,), (0,)), ((), ()))
     q = q_ref[...]
     g = g_ref[...]
-    ka = ka_ref[...]
-    va = va_ref[...]
+    ka = jnp.concatenate([r[...] for r in ka_refs], axis=0)
+    va = jnp.concatenate([r[...] for r in va_refs], axis=0)
     ko = ko_ref[...]
     vo = vo_ref[...]
     s_a = lax.dot_general(q, ka, nt, preferred_element_type=jnp.float32) * scale
@@ -83,31 +85,38 @@
         dka_ref[...] = dka_ref[...] * scale
 
 
-def attend_all(anc_mask, packed, anc_rows, heads, block_rows=512):
+def attend_all(anc_mask, packed, anc_blocks, anc_owner, heads, block_rows=512):
     leaves, seg_len, _ = packed.shape
-    anc = anc_rows.shape[0]
+    levels = anc_owner.shape[0]
+    anc = levels * seg_len
     grid = (leaves, heads, seg_len // block_rows)
-    qspec = pl.BlockSpec((None, block_rows, HD), lambda l, h, r: (l, r, h))
-    gspec = pl.BlockSpec((None, block_rows, HD), lambda l, h, r: (l, r, heads + h))
-    kospec = pl.BlockSpec((None, seg_len, HD), lambda l, h, r: (l, 0, 2 * heads))
-    vospec = pl.BlockSpec((None, seg_len, HD), lambda l, h, r: (l, 0, 2 * heads + 1))
-    kaspec = pl.BlockSpec((anc, HD), lambda l, h, r: (0, 0))
-    vaspec = pl.BlockSpec((anc, HD), lambda l, h, r: (0, 1))
-    maskspec = pl.BlockSpec((1, anc), lambda l, h, r: (0, 0))
-    ownspec = pl.BlockSpec((None, seg_len, HD), lambda l, h, r: (l, 0, 0))
-    ancspec = pl.BlockSpec((anc, HD), lambda l, h, r: (0, 0))
+    qspec = pl.BlockSpec((None, block_rows, HD), lambda l, h, r, own: (l, r, h))
+    gspec = pl.BlockSpec((None, block_rows, HD), lambda l, h, r, own: (l, r, heads + h))
+    kospec = pl.BlockSpec((None, seg_len, HD), lambda l, h, r, own: (l, 0, 2 * heads))
+    vospec = pl.BlockSpec((None, seg_len, HD), lambda l, h, r, own: (l, 0, 2 * heads + 1))
+    maskspec = pl.BlockSpec((1, anc), lambda l, h, r, own: (0, 0))
+    ancspec = pl.BlockSpec((anc, HD), lambda l, h, r, own: (0, 0))
+
+    def level_spec(level, column):
+        return pl.BlockSpec((None, seg_len, HD), lambda l, h, r, own: (own[level], 0, column))
+
+    kaspecs = [level_spec(level, 0) for level in range(levels)]
+    vaspecs = [level_spec(level, 1) for level in range(levels)]
     back_rows = jax.ShapeDtypeStruct((leaves, seg_len, (2 * heads + 2) * HD), jnp.bfloat16)
-    backspec = pl.BlockSpec((None, seg_len, (2 * heads + 2) * HD), lambda l, h, r: (l, 0, 0))
+    backspec = pl.BlockSpec((None, seg_len, (2 * heads + 2) * HD), lambda l, h, r, own: (l, 0, 0))
     anc_grad = jax.ShapeDtypeStruct((anc, HD), jnp.float32)
     return pl.pallas_call(
         attend_kernel,
-        grid=grid,
-        in_specs=[maskspec, qspec, gspec, kospec, vospec, kaspec, vaspec],
-        out_specs=[backspec, ancspec, ancspec],
+        grid_spec=pltpu.PrefetchScalarGridSpec(
+            num_scalar_prefetch=1,
+            grid=grid,
+            in_specs=[maskspec, qspec, gspec, kospec, vospec] + kaspecs + vaspecs,
+            out_specs=[backspec, ancspec, ancspec],
+            scratch_shapes=[pltpu.VMEM((seg_len, HD), jnp.float32), pltpu.VMEM((seg_len, HD), jnp.float32)],
+        ),
         out_shape=[back_rows, anc_grad, anc_grad],
-        scratch_shapes=[pltpu.VMEM((seg_len, HD), jnp.float32), pltpu.VMEM((seg_len, HD), jnp.float32)],
         compiler_params=pltpu.CompilerParams(dimension_semantics=("arbitrary", "arbitrary", "arbitrary")),
-    )(anc_mask, packed, packed, packed, packed, anc_rows, anc_rows)
+    )(anc_owner, anc_mask, packed, packed, packed, packed, *([anc_blocks] * (2 * levels)))
 
 
 def on_device(queries, leaf_keys, leaf_values, inner_keys, inner_values, out_grad, ancestors, depths):
@@ -157,9 +166,6 @@
     ).reshape(seg_count * leaf_count, rows_here, 2 * HD)
     anc_arrived = lax.all_to_all(anc_send, ("seg", "leaf"), split_axis=0, concat_axis=0, tiled=True)
     anc_arrived = anc_arrived.reshape(seg_count, leaf_count * rows_here, 2 * HD)
-    anc_got = jnp.where(
-        my_alive[:, None, None], jnp.take(anc_arrived, my_owners, axis=0), jnp.zeros((), jnp.bfloat16)
-    ).reshape(levels * seg_len, 2 * HD)
     anc_mask = jnp.repeat(my_alive, seg_len).astype(jnp.float32)[None, :]
 
     def to_heads(x, width):
@@ -175,7 +181,7 @@
     for chunk in range(pair_leaves):
         got = lax.all_to_all(packed[:, chunk], "leaf", split_axis=0, concat_axis=0, tiled=True)
         got = got.reshape(1, seg_len, packed.shape[3])
-        back, dka, dva = attend_all(anc_mask, got, anc_got, group_heads)
+        back, dka, dva = attend_all(anc_mask, got, anc_arrived, my_owners.astype(jnp.int32), group_heads)
         part = jnp.concatenate([dka, dva], axis=1)
         anc_partial = part if anc_partial is None else anc_partial + part
         back = back.reshape(leaf_count, rows_here, back.shape[2])

time: 225 us -> 222 us (0.987)
  blocking collectives: 0 us -> 35.5 us
  waiting for transfers between devices: 79.6 us -> 50.6 us
  starting transfers between devices: 37.6 us -> 31.3 us
  local copies, waits for them, and re-layouts: 35.7 us -> 31.8 us
    all_to_all x0 -> x1, blocking collectives: none -> 35.5 us  [on_device(): lax.all_to_all(anc_send, ('seg', 'leaf'), split_axis=0, concat_axis=0, ti...]
    all_to_all x1 -> x0, waiting for transfers between devices: 28.9 us -> none  [on_device(): lax.all_to_all(anc_send, ('seg', 'leaf'), split_axis=0, concat_axis=0, ti...]
    all_to_all x1 -> x0, starting transfers between devices: 6.37 us -> none  [on_device(): lax.all_to_all(anc_send, ('seg', 'leaf'), split_axis=0, concat_axis=0, ti...]
    select_n x2 -> x0, other arithmetic: 2.43 us -> none  [the longest x1 2.43 us: on_device(): jnp.where(my_alive[:, None, None], jnp.take(anc_arrived, my_owners, axis=...]
    unnamed x43 -> x41, local copies, waits for them, and re-layouts: 8.64 us -> 8.41 us
  transfers between devices with their start and end apart: 6 -> 5, of which waited for: 4 -> 3; matrix products, arithmetic and copies ran while one was open for 14% -> 12% of each run, Pallas kernels for 28% -> 29%
where the time goes in v12:
time: 222 us; the launch traced here: 221 us
  Pallas kernels  65 us (29%)
  waiting for transfers between devices  50.6 us (23%)
  blocking collectives  35.5 us (16%)
  local copies, waits for them, and re-layouts  31.8 us (14%)
  starting transfers between devices  31.3 us (14%)
  matrix products  3.52 us (2%)
    pallas_call x2, Pallas kernels, attend_all(): pl.pallas_call(attend_kernel, grid_spec=pltpu.PrefetchScalarGridSpec(num_...  65 us
    all_to_all x1, blocking collectives, on_device(): lax.all_to_all(anc_send, ('seg', 'leaf'), split_axis=0, concat_axis=0, ti...  35.5 us
    all_to_all x2, waiting for transfers between devices, on_device(): lax.all_to_all(packed[:, chunk], 'leaf', split_axis=0, concat_axis=0, til...  22.8 us
    all_to_all x2, starting transfers between devices, on_device(): lax.all_to_all(back, 'leaf', split_axis=0, concat_axis=0, tiled=True)  14.4 us
    all_to_all x1, waiting for transfers between devices, on_device(): lax.all_to_all(homeward, ('seg', 'leaf'), split_axis=0, concat_axis=0, ti...  14.1 us
    all_to_all x2, waiting for transfers between devices, on_device(): lax.all_to_all(back, 'leaf', split_axis=0, concat_axis=0, tiled=True)  13.7 us
    all_to_all x2, starting transfers between devices, on_device(): lax.all_to_all(packed[:, chunk], 'leaf', split_axis=0, concat_axis=0, til...  12 us
    unnamed x41, local copies, waits for them, and re-layouts  8.41 us
  transfers between devices with their start and end apart: 5, of which 3 were waited for; matrix products, arithmetic and copies ran while one was open for 12% of the time, Pallas kernels for 29%

profile of v12, /device:TPU:0, one launch (start us, length us, event | category | flops | bytes accessed | tf_op | source)
XLA Modules:
  0.0 220.8 jit_solution(13228856110673441008)
XLA Ops:
  0.6 1.1 copy.92
  1.8 1.0 copy.93
  3.3 0.9 copy-done.7
  5.0 1.8 slice_bitcast_fusion
  6.9 8.3 %all-to-all-start = ((bf16[16,32,1536]{2,1,0:T(8,128)(2,1)}), bf16[16,32,1536]{2,1,0:T(8,128)(2,1)S(1)}, u32[]{:S(2)}, u32[]{:S(2)}) async-start(bf16[16,32,1536]{2,1,0:T(8,128)(2,1)} %get-tuple-element.47), calls=%async_computation | async-start | bytes 3145728 | tf_op jit(solution)/shard_map/all_to_all | solution.py:182
  17.0 22.8 %all-to-all-done = bf16[16,32,1536]{2,1,0:T(8,128)(2,1)S(1)} async-done(((bf16[16,32,1536]{2,1,0:T(8,128)(2,1)}), bf16[16,32,1536]{2,1,0:T(8,128)(2,1)S(1)}, u32[]{:S(2)}, u32[]{:S(2)}) %all-to-all-start) | async-done | bytes 1572896 | tf_op jit(solution)/shard_map/all_to_all | solution.py:182
  40.0 35.5 %all_to_all.30 = bf16[128,32,256]{2,1,0:T(8,128)(2,1)} all-to-all(bf16[128,32,256]{2,1,0:T(8,128)(2,1)S(1)} %bitcast.119), channel_id=1, replica_groups=mesh['seg'=8,'leaf'=16] {'seg','leaf'}, dimensions={0} | all-to-all | bytes 4194304 | tf_op jit(solution)/shard_map/all_to_all | solution.py:167
  75.5 3.7 %all-to-all-start.3 = ((bf16[16,32,1536]{2,1,0:T(8,128)(2,1)}), bf16[16,32,1536]{2,1,0:T(8,128)(2,1)S(1)}, u32[]{:S(2)}, u32[]{:S(2)}) async-start(bf16[16,32,1536]{2,1,0:T(8,128)(2,1)} %get-tuple-element.46), calls=%async_computation.3 | async-start | bytes 3145728 | tf_op jit(solution)/shard_map/all_to_all | solution.py:182
  80.1 0.7 select_reduce_fusion.owner_ref
  80.8 32.5 %shard_map.127 = (bf16[1,512,1536]{2,1,0:T(8,128)(2,1)}, f32[2048,128]{1,0:T(8,128)}, f32[2048,128]{1,0:T(8,128)}) custom-call(s32[4]{0:T(128)} %select_reduce_fusion.owner_ref, f32[1,2048]{1,0:T(1,128)} %bitcast.140, bf16[1,512,1536]{2,1,0:T(8,128)(2,1)} %bitcast.111, bf16[1,512,1536]{2,1,0:T(8,128)(2,1)} %bitcast.112, bf16[1,512,1536]{2,1,0:T(8,128)(2,1)} %bitcast.113, ...), custom_call_target="tpu_custom_call" | custom-call | tf_op jit(solution)/shard_map/pallas_call | solution.py:108
  113.3 7.2 %all-to-all-start.2 = ((bf16[16,32,1536]{2,1,0:T(8,128)(2,1)}), bf16[16,32,1536]{2,1,0:T(8,128)(2,1)S(1)}, u32[]{:S(2)}, u32[]{:S(2)}) async-start(bf16[16,32,1536]{2,1,0:T(8,128)(2,1)} %bitcast.127), calls=%async_computation.2 | async-start | bytes 3145728 | tf_op jit(solution)/shard_map/all_to_all | solution.py:188
  120.5 32.5 %shard_map.128 = (bf16[1,512,1536]{2,1,0:T(8,128)(2,1)}, f32[2048,128]{1,0:T(8,128)}, f32[2048,128]{1,0:T(8,128)}) custom-call(s32[4]{0:T(128)} %select_reduce_fusion.owner_ref, f32[1,2048]{1,0:T(1,128)} %bitcast.141, bf16[1,512,1536]{2,1,0:T(8,128)(2,1)} %bitcast.115, bf16[1,512,1536]{2,1,0:T(8,128)(2,1)} %bitcast.116, bf16[1,512,1536]{2,1,0:T(8,128)(2,1)} %bitcast.117, ...), custom_call_target="tpu_custom_call" | custom-call | tf_op jit(solution)/shard_map/pallas_call | solution.py:108
  153.0 7.2 %all-to-all-start.4 = ((bf16[16,32,1536]{2,1,0:T(8,128)(2,1)}), bf16[16,32,1536]{2,1,0:T(8,128)(2,1)S(1)}, u32[]{:S(2)}, u32[]{:S(2)}) async-start(bf16[16,32,1536]{2,1,0:T(8,128)(2,1)} %bitcast.126), calls=%async_computation.4 | async-start | bytes 3145728 | tf_op jit(solution)/shard_map/all_to_all | solution.py:188
  160.3 2.0 copy.82
  162.3 0.7 copy.80
  164.4 2.3 %convolution_convert_fusion.1 = bf16[8,512,256]{2,0,1:T(8,128)(2,1)S(1)} fusion(f32[4,512,128]{2,0,1:T(4,128)S(1)} %copy.81, f32[4,512,128]{2,0,1:T(4,128)S(1)} %copy.80, f32[4,512,128]{2,0,1:T(4,128)S(1)} %copy.83, f32[4,512,128]{2,0,1:T(4,128)S(1)} %copy.82, s32[4]{0:T(128)S(1)} %copy-done.13, pred[4]{0:T(512)(128)(4,1)S(1)} %select_reduce_fusion.1), kind=kOutput, calls=%fused_computation.7 | convolution fusion | flops 11534400 | bytes 6291476 | tf_op jit(solution)/shard_map/ok,krc->orc/dot_general | solution.py:204
  166.7 1.8 copy.84
  168.5 13.7 %all-to-all-done.4 = bf16[16,32,1536]{2,1,0:T(8,128)(2,1)S(1)} async-done(((bf16[16,32,1536]{2,1,0:T(8,128)(2,1)}), bf16[16,32,1536]{2,1,0:T(8,128)(2,1)S(1)}, u32[]{:S(2)}, u32[]{:S(2)}) %all-to-all-start.4) | async-done | bytes 1572896 | tf_op jit(solution)/shard_map/all_to_all | solution.py:188
  182.2 1.1 copy-done.4
  183.3 4.9 %all-to-all-start.5 = ((bf16[128,32,256]{2,1,0:T(8,128)(2,1)}), bf16[128,32,256]{2,1,0:T(8,128)(2,1)S(1)}, u32[]{:S(2)}, u32[]{:S(2)}) async-start(bf16[128,32,256]{2,1,0:T(8,128)(2,1)} %bitcast.34), calls=%async_computation.5 | async-start | bytes 4194304 | tf_op jit(solution)/shard_map/all_to_all | solution.py:208
  188.2 2.4 %copy_dynamic-update-slice_fusion.1 = bf16[8,2,2,32,1536]{4,0,3,2,1:T(8,128)(2,1)S(1)} fusion(bf16[8,2,1,32,1536]{4,3,1,0,2:T(8,128)(2,1)} %bitcast.120), kind=kLoop, calls=%fused_computation.11 | loop fusion | bytes 3145728
  190.6 0.9 copy_dynamic-update-slice_fusion
  191.5 1.6 slice_bitcast_fusion.2
  193.6 3.2 %reshape.139 = bf16[4,32,5120]{2,1,0:T(8,128)(2,1)} reshape(bf16[2,2,32,8,640]{4,3,2,1,0:T(8,128)(2,1)} %get-tuple-element.44) | data formatting | bytes 2621440 | tf_op jit(solution)/shard_map/reshape | solution.py:194
  196.8 1.9 slice_bitcast_fusion.6
  198.7 1.8 reshape.141
  200.4 1.8 reshape.140
  202.2 1.4 reshape.138
  203.7 14.1 %all-to-all-done.5 = bf16[128,32,256]{2,1,0:T(8,128)(2,1)S(1)} async-done(((bf16[128,32,256]{2,1,0:T(8,128)(2,1)}), bf16[128,32,256]{2,1,0:T(8,128)(2,1)S(1)}, u32[]{:S(2)}, u32[]{:S(2)}) %all-to-all-start.5) | async-done | bytes 2097184 | tf_op jit(solution)/shard_map/all_to_all | solution.py:208
  218.3 0.7 fusion.3
  219.3 0.7 convert_element_type.57
  220.1 0.7 convert_element_type.55
  (63 shorter events, 6.9 us)
Async XLA Ops:
  0.6 2.2 %copy-start.6 = (bf16[4,32,5120]{2,1,0:T(8,128)(2,1)S(1)}, bf16[4,32,5120]{2,1,0:T(8,128)(2,1)}, u32[]{:S(2)}) copy-start(bf16[4,32,5120]{2,1,0:T(8,128)(2,1)} %param.8) | copy-start | bytes 3932164
  2.9 1.3 copy-start.7
  6.9 8.3 %copy-start.15 = (s32[32]{0:T(128)S(1)}, s32[32]{0:T(128)}, u32[]{:S(2)}) copy-start(s32[32]{0:T(128)} %param.15) | copy-start | bytes 388
  6.9 8.4 %copy-start.14 = (s32[32,4]{0,1:T(4,128)S(1)}, s32[32,4]{0,1:T(4,128)}, u32[]{:S(2)}) copy-start(s32[32,4]{0,1:T(4,128)} %param.14) | copy-start | bytes 1540
  6.9 8.5 %copy-start.11 = (bf16[2,32,1024]{2,1,0:T(8,128)(2,1)S(1)}, bf16[2,32,1024]{2,1,0:T(8,128)(2,1)}, u32[]{:S(2)}) copy-start(bf16[2,32,1024]{2,1,0:T(8,128)(2,1)} %param.11) | copy-start | bytes 393220
  6.9 8.7 %copy-start.12 = (bf16[2,32,1024]{2,1,0:T(8,128)(2,1)S(1)}, bf16[2,32,1024]{2,1,0:T(8,128)(2,1)}, u32[]{:S(2)}) copy-start(bf16[2,32,1024]{2,1,0:T(8,128)(2,1)} %param.12) | copy-start | bytes 393220
  6.9 32.8 %all-to-all-start = ((bf16[16,32,1536]{2,1,0:T(8,128)(2,1)}), bf16[16,32,1536]{2,1,0:T(8,128)(2,1)S(1)}, u32[]{:S(2)}, u32[]{:S(2)}) async-start(bf16[16,32,1536]{2,1,0:T(8,128)(2,1)} %get-tuple-element.47), calls=%async_computation | async-start | bytes 3145728 | tf_op jit(solution)/shard_map/all_to_all | solution.py:182
  39.7 35.8 %copy-start = (bf16[16,32,1536]{2,1,0:T(8,128)(2,1)}, bf16[16,32,1536]{2,1,0:T(8,128)(2,1)S(1)}, u32[]{:S(2)}) copy-start(bf16[16,32,1536]{2,1,0:T(8,128)(2,1)S(1)} %all-to-all-done) | copy-start | bytes 4718596
  75.5 37.8 %all-to-all-start.3 = ((bf16[16,32,1536]{2,1,0:T(8,128)(2,1)}), bf16[16,32,1536]{2,1,0:T(8,128)(2,1)S(1)}, u32[]{:S(2)}, u32[]{:S(2)}) async-start(bf16[16,32,1536]{2,1,0:T(8,128)(2,1)} %get-tuple-element.46), calls=%async_computation.3 | async-start | bytes 3145728 | tf_op jit(solution)/shard_map/all_to_all | solution.py:182
  113.3 7.2 %copy-start.1 = (bf16[16,32,1536]{2,1,0:T(8,128)(2,1)}, bf16[16,32,1536]{2,1,0:T(8,128)(2,1)S(1)}, u32[]{:S(2)}) copy-start(bf16[16,32,1536]{2,1,0:T(8,128)(2,1)S(1)} %all-to-all-done.3) | copy-start | bytes 4718596
  113.3 39.7 %all-to-all-start.2 = ((bf16[16,32,1536]{2,1,0:T(8,128)(2,1)}), bf16[16,32,1536]{2,1,0:T(8,128)(2,1)S(1)}, u32[]{:S(2)}, u32[]{:S(2)}) async-start(bf16[16,32,1536]{2,1,0:T(8,128)(2,1)} %bitcast.127), calls=%async_computation.2 | async-start | bytes 3145728 | tf_op jit(solution)/shard_map/all_to_all | solution.py:188
  153.0 9.3 %copy-start.3 = (bf16[16,32,1536]{2,1,0:T(8,128)(2,1)}, bf16[16,32,1536]{2,1,0:T(8,128)(2,1)S(1)}, u32[]{:S(2)}) copy-start(bf16[16,32,1536]{2,1,0:T(8,128)(2,1)S(1)} %all-to-all-done.2) | copy-start | bytes 4718596
  153.0 29.2 %all-to-all-start.4 = ((bf16[16,32,1536]{2,1,0:T(8,128)(2,1)}), bf16[16,32,1536]{2,1,0:T(8,128)(2,1)S(1)}, u32[]{:S(2)}, u32[]{:S(2)}) async-start(bf16[16,32,1536]{2,1,0:T(8,128)(2,1)} %bitcast.126), calls=%async_computation.4 | async-start | bytes 3145728 | tf_op jit(solution)/shard_map/all_to_all | solution.py:188
  160.2 2.1 copy-start.9
  160.2 2.8 %copy-start.8 = (f32[2048,128]{1,0:T(8,128)S(1)}, f32[2048,128]{1,0:T(8,128)}, u32[]{:S(2)}) copy-start(f32[2048,128]{1,0:T(8,128)} %get-tuple-element.15) | copy-start | bytes 3145732
  162.3 1.4 copy-start.10
  163.0 1.4 copy-start.13
  182.2 1.1 copy-start.4
  183.3 34.4 %all-to-all-start.5 = ((bf16[128,32,256]{2,1,0:T(8,128)(2,1)}), bf16[128,32,256]{2,1,0:T(8,128)(2,1)S(1)}, u32[]{:S(2)}, u32[]{:S(2)}) async-start(bf16[128,32,256]{2,1,0:T(8,128)(2,1)} %bitcast.34), calls=%async_computation.5 | async-start | bytes 4194304 | tf_op jit(solution)/shard_map/all_to_all | solution.py:208
  188.2 2.4 %copy-start.5 = (bf16[16,32,1536]{2,1,0:T(8,128)(2,1)S(1)}, bf16[16,32,1536]{2,1,0:T(8,128)(2,1)}, u32[]{:S(2)}) copy-start(bf16[16,32,1536]{2,1,0:T(8,128)(2,1)} %copy-done.4) | copy-start | bytes 4718596
  191.5 2.1 copy-start.2

commit v13 on v12

--- a/solution.py
+++ b/solution.py
@@ -14,9 +14,9 @@
 
 
 def attend_kernel(owner_ref, mask_ref, q_ref, g_ref, ko_ref, vo_ref, *refs):
-    levels = (len(refs) - 5) // 2
+    levels = (len(refs) - 7) // 2
     ka_refs, va_refs = refs[:levels], refs[levels : 2 * levels]
-    back_ref, dka_ref, dva_ref, dko_acc, dvo_acc = refs[2 * levels :]
+    back_ref, dka_ref, dva_ref, dko_acc, dvo_acc, ka_all, va_all = refs[2 * levels :]
     leaf_i = pl.program_id(0)
     head_i = pl.program_id(1)
     row_i = pl.program_id(2)
@@ -40,8 +40,14 @@
     tn = (((0,), (0,)), ((), ()))
     q = q_ref[...]
     g = g_ref[...]
-    ka = jnp.concatenate([r[...] for r in ka_refs], axis=0)
-    va = jnp.concatenate([r[...] for r in va_refs], axis=0)
+    @pl.when((leaf_i == 0) & (head_i == 0) & (row_i == 0))
+    def _():
+        for level in range(levels):
+            ka_all[level * seg_len : (level + 1) * seg_len, :] = ka_refs[level][...]
+            va_all[level * seg_len : (level + 1) * seg_len, :] = va_refs[level][...]
+
+    ka = ka_all[...]
+    va = va_all[...]
     ko = ko_ref[...]
     vo = vo_ref[...]
     s_a = lax.dot_general(q, ka, nt, preferred_element_type=jnp.float32) * scale
@@ -112,7 +118,12 @@
             grid=grid,
             in_specs=[maskspec, qspec, gspec, kospec, vospec] + kaspecs + vaspecs,
             out_specs=[backspec, ancspec, ancspec],
-            scratch_shapes=[pltpu.VMEM((seg_len, HD), jnp.float32), pltpu.VMEM((seg_len, HD), jnp.float32)],
+            scratch_shapes=[
+                pltpu.VMEM((seg_len, HD), jnp.float32),
+                pltpu.VMEM((seg_len, HD), jnp.float32),
+                pltpu.VMEM((anc, HD), anc_blocks.dtype),
+                pltpu.VMEM((anc, HD), anc_blocks.dtype),
+            ],
         ),
         out_shape=[back_rows, anc_grad, anc_grad],
         compiler_params=pltpu.CompilerParams(dimension_semantics=("arbitrary", "arbitrary", "arbitrary")),

time: 222 us -> 222 us (level)
  transfers between devices with their start and end apart: 5 -> 5, of which waited for: 3 -> 3; matrix products, arithmetic and copies ran while one was open for 12% -> 12% of each run, Pallas kernels for 29% -> 30%
where the time goes in v13:
time: 222 us; the launch traced here: 221 us
  Pallas kernels  65.4 us (29%)
  waiting for transfers between devices  50.6 us (23%)
  blocking collectives  35.5 us (16%)
  local copies, waits for them, and re-layouts  31.8 us (14%)
  starting transfers between devices  31.3 us (14%)
  matrix products  3.52 us (2%)
    pallas_call x2, Pallas kernels, attend_all(): pl.pallas_call(attend_kernel, grid_spec=pltpu.PrefetchScalarGridSpec(num_...  65.4 us
    all_to_all x1, blocking collectives, on_device(): lax.all_to_all(anc_send, ('seg', 'leaf'), split_axis=0, concat_axis=0, ti...  35.5 us
    all_to_all x2, waiting for transfers between devices, on_device(): lax.all_to_all(packed[:, chunk], 'leaf', split_axis=0, concat_axis=0, til...  22.8 us
    all_to_all x2, starting transfers between devices, on_device(): lax.all_to_all(back, 'leaf', split_axis=0, concat_axis=0, tiled=True)  14.4 us
    all_to_all x1, waiting for transfers between devices, on_device(): lax.all_to_all(homeward, ('seg', 'leaf'), split_axis=0, concat_axis=0, ti...  14.1 us
    all_to_all x2, waiting for transfers between devices, on_device(): lax.all_to_all(back, 'leaf', split_axis=0, concat_axis=0, tiled=True)  13.7 us
    all_to_all x2, starting transfers between devices, on_device(): lax.all_to_all(packed[:, chunk], 'leaf', split_axis=0, concat_axis=0, til...  12 us
    unnamed x41, local copies, waits for them, and re-layouts  8.41 us
  transfers between devices with their start and end apart: 5, of which 3 were waited for; matrix products, arithmetic and copies ran while one was open for 12% of the time, Pallas kernels for 30%

profile of v13, /device:TPU:0, one launch (start us, length us, event | category | flops | bytes accessed | tf_op | source)
XLA Modules:
  0.0 221.2 jit_solution(16491033463417386942)
XLA Ops:
  0.6 1.1 copy.92
  1.8 1.0 copy.93
  3.3 0.9 copy-done.7
  5.0 1.8 slice_bitcast_fusion
  6.9 8.3 %all-to-all-start = ((bf16[16,32,1536]{2,1,0:T(8,128)(2,1)}), bf16[16,32,1536]{2,1,0:T(8,128)(2,1)S(1)}, u32[]{:S(2)}, u32[]{:S(2)}) async-start(bf16[16,32,1536]{2,1,0:T(8,128)(2,1)} %get-tuple-element.47), calls=%async_computation | async-start | bytes 3145728 | tf_op jit(solution)/shard_map/all_to_all | solution.py:193
  17.0 22.8 %all-to-all-done = bf16[16,32,1536]{2,1,0:T(8,128)(2,1)S(1)} async-done(((bf16[16,32,1536]{2,1,0:T(8,128)(2,1)}), bf16[16,32,1536]{2,1,0:T(8,128)(2,1)S(1)}, u32[]{:S(2)}, u32[]{:S(2)}) %all-to-all-start) | async-done | bytes 1572896 | tf_op jit(solution)/shard_map/all_to_all | solution.py:193
  40.0 35.5 %all_to_all.30 = bf16[128,32,256]{2,1,0:T(8,128)(2,1)} all-to-all(bf16[128,32,256]{2,1,0:T(8,128)(2,1)S(1)} %bitcast.119), channel_id=1, replica_groups=mesh['seg'=8,'leaf'=16] {'seg','leaf'}, dimensions={0} | all-to-all | bytes 4194304 | tf_op jit(solution)/shard_map/all_to_all | solution.py:178
  75.5 3.7 %all-to-all-start.3 = ((bf16[16,32,1536]{2,1,0:T(8,128)(2,1)}), bf16[16,32,1536]{2,1,0:T(8,128)(2,1)S(1)}, u32[]{:S(2)}, u32[]{:S(2)}) async-start(bf16[16,32,1536]{2,1,0:T(8,128)(2,1)} %get-tuple-element.46), calls=%async_computation.3 | async-start | bytes 3145728 | tf_op jit(solution)/shard_map/all_to_all | solution.py:193
  80.1 0.7 select_reduce_fusion.owner_ref
  80.8 32.7 %shard_map.127 = (bf16[1,512,1536]{2,1,0:T(8,128)(2,1)}, f32[2048,128]{1,0:T(8,128)}, f32[2048,128]{1,0:T(8,128)}) custom-call(s32[4]{0:T(128)} %select_reduce_fusion.owner_ref, f32[1,2048]{1,0:T(1,128)} %bitcast.140, bf16[1,512,1536]{2,1,0:T(8,128)(2,1)} %bitcast.111, bf16[1,512,1536]{2,1,0:T(8,128)(2,1)} %bitcast.112, bf16[1,512,1536]{2,1,0:T(8,128)(2,1)} %bitcast.113, ...), custom_call_target="tpu_custom_call" | custom-call | tf_op jit(solution)/shard_map/pallas_call | solution.py:114
  113.5 7.2 %all-to-all-start.2 = ((bf16[16,32,1536]{2,1,0:T(8,128)(2,1)}), bf16[16,32,1536]{2,1,0:T(8,128)(2,1)S(1)}, u32[]{:S(2)}, u32[]{:S(2)}) async-start(bf16[16,32,1536]{2,1,0:T(8,128)(2,1)} %bitcast.127), calls=%async_computation.2 | async-start | bytes 3145728 | tf_op jit(solution)/shard_map/all_to_all | solution.py:199
  120.7 32.7 %shard_map.128 = (bf16[1,512,1536]{2,1,0:T(8,128)(2,1)}, f32[2048,128]{1,0:T(8,128)}, f32[2048,128]{1,0:T(8,128)}) custom-call(s32[4]{0:T(128)} %select_reduce_fusion.owner_ref, f32[1,2048]{1,0:T(1,128)} %bitcast.141, bf16[1,512,1536]{2,1,0:T(8,128)(2,1)} %bitcast.115, bf16[1,512,1536]{2,1,0:T(8,128)(2,1)} %bitcast.116, bf16[1,512,1536]{2,1,0:T(8,128)(2,1)} %bitcast.117, ...), custom_call_target="tpu_custom_call" | custom-call | tf_op jit(solution)/shard_map/pallas_call | solution.py:114
  153.4 7.2 %all-to-all-start.4 = ((bf16[16,32,1536]{2,1,0:T(8,128)(2,1)}), bf16[16,32,1536]{2,1,0:T(8,128)(2,1)S(1)}, u32[]{:S(2)}, u32[]{:S(2)}) async-start(bf16[16,32,1536]{2,1,0:T(8,128)(2,1)} %bitcast.126), calls=%async_computation.4 | async-start | bytes 3145728 | tf_op jit(solution)/shard_map/all_to_all | solution.py:199
  160.7 2.0 copy.82
  164.1 0.7 copy.83
  164.8 2.3 %convolution_convert_fusion.1 = bf16[8,512,256]{2,0,1:T(8,128)(2,1)S(1)} fusion(f32[4,512,128]{2,0,1:T(4,128)S(1)} %copy.81, f32[4,512,128]{2,0,1:T(4,128)S(1)} %copy.80, f32[4,512,128]{2,0,1:T(4,128)S(1)} %copy.83, f32[4,512,128]{2,0,1:T(4,128)S(1)} %copy.82, s32[4]{0:T(128)S(1)} %copy-done.13, pred[4]{0:T(512)(128)(4,1)S(1)} %select_reduce_fusion.1), kind=kOutput, calls=%fused_computation.7 | convolution fusion | flops 11534400 | bytes 6291476 | tf_op jit(solution)/shard_map/ok,krc->orc/dot_general | solution.py:215
  167.1 1.8 copy.84
  168.9 13.7 %all-to-all-done.4 = bf16[16,32,1536]{2,1,0:T(8,128)(2,1)S(1)} async-done(((bf16[16,32,1536]{2,1,0:T(8,128)(2,1)}), bf16[16,32,1536]{2,1,0:T(8,128)(2,1)S(1)}, u32[]{:S(2)}, u32[]{:S(2)}) %all-to-all-start.4) | async-done | bytes 1572896 | tf_op jit(solution)/shard_map/all_to_all | solution.py:199
  182.6 1.1 copy-done.4
  183.7 4.9 %all-to-all-start.5 = ((bf16[128,32,256]{2,1,0:T(8,128)(2,1)}), bf16[128,32,256]{2,1,0:T(8,128)(2,1)S(1)}, u32[]{:S(2)}, u32[]{:S(2)}) async-start(bf16[128,32,256]{2,1,0:T(8,128)(2,1)} %bitcast.34), calls=%async_computation.5 | async-start | bytes 4194304 | tf_op jit(solution)/shard_map/all_to_all | solution.py:219
  188.6 2.4 %copy_dynamic-update-slice_fusion.1 = bf16[8,2,2,32,1536]{4,0,3,2,1:T(8,128)(2,1)S(1)} fusion(bf16[8,2,1,32,1536]{4,3,1,0,2:T(8,128)(2,1)} %bitcast.120), kind=kLoop, calls=%fused_computation.11 | loop fusion | bytes 3145728
  191.0 0.9 copy_dynamic-update-slice_fusion
  191.9 1.6 slice_bitcast_fusion.2
  194.0 3.2 %reshape.139 = bf16[4,32,5120]{2,1,0:T(8,128)(2,1)} reshape(bf16[2,2,32,8,640]{4,3,2,1,0:T(8,128)(2,1)} %get-tuple-element.44) | data formatting | bytes 2621440 | tf_op jit(solution)/shard_map/reshape | solution.py:205
  197.2 1.9 slice_bitcast_fusion.6
  199.1 1.8 reshape.141
  200.8 1.8 reshape.140
  202.6 1.4 reshape.138
  204.1 14.1 %all-to-all-done.5 = bf16[128,32,256]{2,1,0:T(8,128)(2,1)S(1)} async-done(((bf16[128,32,256]{2,1,0:T(8,128)(2,1)}), bf16[128,32,256]{2,1,0:T(8,128)(2,1)S(1)}, u32[]{:S(2)}, u32[]{:S(2)}) %all-to-all-start.5) | async-done | bytes 2097184 | tf_op jit(solution)/shard_map/all_to_all | solution.py:219
  218.7 0.7 fusion.3
  219.7 0.7 convert_element_type.57
  220.5 0.7 convert_element_type.55
  (63 shorter events, 6.9 us)
Async XLA Ops:
  0.6 2.2 %copy-start.6 = (bf16[4,32,5120]{2,1,0:T(8,128)(2,1)S(1)}, bf16[4,32,5120]{2,1,0:T(8,128)(2,1)}, u32[]{:S(2)}) copy-start(bf16[4,32,5120]{2,1,0:T(8,128)(2,1)} %param.8) | copy-start | bytes 3932164
  2.9 1.3 copy-start.7
  6.9 8.3 %copy-start.15 = (s32[32]{0:T(128)S(1)}, s32[32]{0:T(128)}, u32[]{:S(2)}) copy-start(s32[32]{0:T(128)} %param.15) | copy-start | bytes 388
  6.9 8.4 %copy-start.14 = (s32[32,4]{0,1:T(4,128)S(1)}, s32[32,4]{0,1:T(4,128)}, u32[]{:S(2)}) copy-start(s32[32,4]{0,1:T(4,128)} %param.14) | copy-start | bytes 1540
  6.9 8.5 %copy-start.11 = (bf16[2,32,1024]{2,1,0:T(8,128)(2,1)S(1)}, bf16[2,32,1024]{2,1,0:T(8,128)(2,1)}, u32[]{:S(2)}) copy-start(bf16[2,32,1024]{2,1,0:T(8,128)(2,1)} %param.11) | copy-start | bytes 393220
  6.9 8.7 %copy-start.12 = (bf16[2,32,1024]{2,1,0:T(8,128)(2,1)S(1)}, bf16[2,32,1024]{2,1,0:T(8,128)(2,1)}, u32[]{:S(2)}) copy-start(bf16[2,32,1024]{2,1,0:T(8,128)(2,1)} %param.12) | copy-start | bytes 393220
  6.9 32.8 %all-to-all-start = ((bf16[16,32,1536]{2,1,0:T(8,128)(2,1)}), bf16[16,32,1536]{2,1,0:T(8,128)(2,1)S(1)}, u32[]{:S(2)}, u32[]{:S(2)}) async-start(bf16[16,32,1536]{2,1,0:T(8,128)(2,1)} %get-tuple-element.47), calls=%async_computation | async-start | bytes 3145728 | tf_op jit(solution)/shard_map/all_to_all | solution.py:193
  39.7 35.8 %copy-start = (bf16[16,32,1536]{2,1,0:T(8,128)(2,1)}, bf16[16,32,1536]{2,1,0:T(8,128)(2,1)S(1)}, u32[]{:S(2)}) copy-start(bf16[16,32,1536]{2,1,0:T(8,128)(2,1)S(1)} %all-to-all-done) | copy-start | bytes 4718596
  75.5 38.0 %all-to-all-start.3 = ((bf16[16,32,1536]{2,1,0:T(8,128)(2,1)}), bf16[16,32,1536]{2,1,0:T(8,128)(2,1)S(1)}, u32[]{:S(2)}, u32[]{:S(2)}) async-start(bf16[16,32,1536]{2,1,0:T(8,128)(2,1)} %get-tuple-element.46), calls=%async_computation.3 | async-start | bytes 3145728 | tf_op jit(solution)/shard_map/all_to_all | solution.py:193
  113.5 7.2 %copy-start.1 = (bf16[16,32,1536]{2,1,0:T(8,128)(2,1)}, bf16[16,32,1536]{2,1,0:T(8,128)(2,1)S(1)}, u32[]{:S(2)}) copy-start(bf16[16,32,1536]{2,1,0:T(8,128)(2,1)S(1)} %all-to-all-done.3) | copy-start | bytes 4718596
  113.5 39.9 %all-to-all-start.2 = ((bf16[16,32,1536]{2,1,0:T(8,128)(2,1)}), bf16[16,32,1536]{2,1,0:T(8,128)(2,1)S(1)}, u32[]{:S(2)}, u32[]{:S(2)}) async-start(bf16[16,32,1536]{2,1,0:T(8,128)(2,1)} %bitcast.127), calls=%async_computation.2 | async-start | bytes 3145728 | tf_op jit(solution)/shard_map/all_to_all | solution.py:199
  153.4 9.3 %copy-start.3 = (bf16[16,32,1536]{2,1,0:T(8,128)(2,1)}, bf16[16,32,1536]{2,1,0:T(8,128)(2,1)S(1)}, u32[]{:S(2)}) copy-start(bf16[16,32,1536]{2,1,0:T(8,128)(2,1)S(1)} %all-to-all-done.2) | copy-start | bytes 4718596
  153.4 29.2 %all-to-all-start.4 = ((bf16[16,32,1536]{2,1,0:T(8,128)(2,1)}), bf16[16,32,1536]{2,1,0:T(8,128)(2,1)S(1)}, u32[]{:S(2)}, u32[]{:S(2)}) async-start(bf16[16,32,1536]{2,1,0:T(8,128)(2,1)} %bitcast.126), calls=%async_computation.4 | async-start | bytes 3145728 | tf_op jit(solution)/shard_map/all_to_all | solution.py:199
  160.6 2.1 copy-start.9
  160.6 2.8 %copy-start.8 = (f32[2048,128]{1,0:T(8,128)S(1)}, f32[2048,128]{1,0:T(8,128)}, u32[]{:S(2)}) copy-start(f32[2048,128]{1,0:T(8,128)} %get-tuple-element.15) | copy-start | bytes 3145732
  162.7 1.4 copy-start.10
  163.4 1.4 copy-start.13
  182.6 1.1 copy-start.4
  183.7 34.4 %all-to-all-start.5 = ((bf16[128,32,256]{2,1,0:T(8,128)(2,1)}), bf16[128,32,256]{2,1,0:T(8,128)(2,1)S(1)}, u32[]{:S(2)}, u32[]{:S(2)}) async-start(bf16[128,32,256]{2,1,0:T(8,128)(2,1)} %bitcast.34), calls=%async_computation.5 | async-start | bytes 4194304 | tf_op jit(solution)/shard_map/all_to_all | solution.py:219
  188.6 2.4 %copy-start.5 = (bf16[16,32,1536]{2,1,0:T(8,128)(2,1)S(1)}, bf16[16,32,1536]{2,1,0:T(8,128)(2,1)}, u32[]{:S(2)}) copy-start(bf16[16,32,1536]{2,1,0:T(8,128)(2,1)} %copy-done.4) | copy-start | bytes 4718596
  191.9 2.1 copy-start.2

commit v14 on v12

--- a/solution.py
+++ b/solution.py
@@ -46,7 +46,7 @@
     vo = vo_ref[...]
     s_a = lax.dot_general(q, ka, nt, preferred_element_type=jnp.float32) * scale
     s_o = lax.dot_general(q, ko, nt, preferred_element_type=jnp.float32) * scale
-    s_a = jnp.where(mask_ref[...] > 0.5, s_a, NEG_FILL)
+    s_a = s_a + mask_ref[...]
     rows = row_i * block_rows + lax.broadcasted_iota(jnp.int32, (block_rows, seg_len), 0)
     cols = lax.broadcasted_iota(jnp.int32, (block_rows, seg_len), 1)
     s_o = jnp.where(cols <= rows, s_o, NEG_FILL)
@@ -166,7 +166,7 @@
     ).reshape(seg_count * leaf_count, rows_here, 2 * HD)
     anc_arrived = lax.all_to_all(anc_send, ("seg", "leaf"), split_axis=0, concat_axis=0, tiled=True)
     anc_arrived = anc_arrived.reshape(seg_count, leaf_count * rows_here, 2 * HD)
-    anc_mask = jnp.repeat(my_alive, seg_len).astype(jnp.float32)[None, :]
+    anc_mask = jnp.where(jnp.repeat(my_alive, seg_len), 0.0, NEG_FILL).astype(jnp.float32)[None, :]
 
     def to_heads(x, width):
         shaped = x.reshape(pair_count, pair_leaves, rows_here, kv_heads, width)

time: 222 us -> 221 us (level)
  no operation moved by 1% of the time
where the time goes in v14:
time: 221 us; the launch traced here: 220 us
  Pallas kernels  64.3 us (29%)
  waiting for transfers between devices  50.6 us (23%)
  blocking collectives  35.5 us (16%)
  local copies, waits for them, and re-layouts  31.8 us (14%)
  starting transfers between devices  31.3 us (14%)
  matrix products  3.52 us (2%)
    pallas_call x2, Pallas kernels, attend_all(): pl.pallas_call(attend_kernel, grid_spec=pltpu.PrefetchScalarGridSpec(num_...  64.3 us
    all_to_all x1, blocking collectives, on_device(): lax.all_to_all(anc_send, ('seg', 'leaf'), split_axis=0, concat_axis=0, ti...  35.5 us
    all_to_all x2, waiting for transfers between devices, on_device(): lax.all_to_all(packed[:, chunk], 'leaf', split_axis=0, concat_axis=0, til...  22.8 us
    all_to_all x2, starting transfers between devices, on_device(): lax.all_to_all(back, 'leaf', split_axis=0, concat_axis=0, tiled=True)  14.4 us
    all_to_all x1, waiting for transfers between devices, on_device(): lax.all_to_all(homeward, ('seg', 'leaf'), split_axis=0, concat_axis=0, ti...  14.1 us
    all_to_all x2, waiting for transfers between devices, on_device(): lax.all_to_all(back, 'leaf', split_axis=0, concat_axis=0, tiled=True)  13.7 us
    all_to_all x2, starting transfers between devices, on_device(): lax.all_to_all(packed[:, chunk], 'leaf', split_axis=0, concat_axis=0, til...  12 us
    unnamed x41, local copies, waits for them, and re-layouts  8.41 us
  transfers between devices with their start and end apart: 5, of which 3 were waited for; matrix products, arithmetic and copies ran while one was open for 12% of the time, Pallas kernels for 29%

profile of v14, /device:TPU:0, one launch (start us, length us, event | category | flops | bytes accessed | tf_op | source)
XLA Modules:
  0.0 220.1 jit_solution(7101642162777474407)
XLA Ops:
  0.6 1.1 copy.92
  1.8 1.0 copy.93
  3.3 0.9 copy-done.7
  5.0 1.8 slice_bitcast_fusion
  6.9 8.3 %all-to-all-start = ((bf16[16,32,1536]{2,1,0:T(8,128)(2,1)}), bf16[16,32,1536]{2,1,0:T(8,128)(2,1)S(1)}, u32[]{:S(2)}, u32[]{:S(2)}) async-start(bf16[16,32,1536]{2,1,0:T(8,128)(2,1)} %get-tuple-element.47), calls=%async_computation | async-start | bytes 3145728 | tf_op jit(solution)/shard_map/all_to_all | solution.py:182
  17.0 22.8 %all-to-all-done = bf16[16,32,1536]{2,1,0:T(8,128)(2,1)S(1)} async-done(((bf16[16,32,1536]{2,1,0:T(8,128)(2,1)}), bf16[16,32,1536]{2,1,0:T(8,128)(2,1)S(1)}, u32[]{:S(2)}, u32[]{:S(2)}) %all-to-all-start) | async-done | bytes 1572896 | tf_op jit(solution)/shard_map/all_to_all | solution.py:182
  40.0 35.5 %all_to_all.30 = bf16[128,32,256]{2,1,0:T(8,128)(2,1)} all-to-all(bf16[128,32,256]{2,1,0:T(8,128)(2,1)S(1)} %bitcast.119), channel_id=1, replica_groups=mesh['seg'=8,'leaf'=16] {'seg','leaf'}, dimensions={0} | all-to-all | bytes 4194304 | tf_op jit(solution)/shard_map/all_to_all | solution.py:167
  75.5 3.7 %all-to-all-start.3 = ((bf16[16,32,1536]{2,1,0:T(8,128)(2,1)}), bf16[16,32,1536]{2,1,0:T(8,128)(2,1)S(1)}, u32[]{:S(2)}, u32[]{:S(2)}) async-start(bf16[16,32,1536]{2,1,0:T(8,128)(2,1)} %get-tuple-element.46), calls=%async_computation.3 | async-start | bytes 3145728 | tf_op jit(solution)/shard_map/all_to_all | solution.py:182
  80.1 0.7 select_reduce_fusion.owner_ref
  80.8 32.1 %shard_map.127 = (bf16[1,512,1536]{2,1,0:T(8,128)(2,1)}, f32[2048,128]{1,0:T(8,128)}, f32[2048,128]{1,0:T(8,128)}) custom-call(s32[4]{0:T(128)} %select_reduce_fusion.owner_ref, f32[1,2048]{1,0:T(1,128)} %bitcast.140, bf16[1,512,1536]{2,1,0:T(8,128)(2,1)} %bitcast.111, bf16[1,512,1536]{2,1,0:T(8,128)(2,1)} %bitcast.112, bf16[1,512,1536]{2,1,0:T(8,128)(2,1)} %bitcast.113, ...), custom_call_target="tpu_custom_call" | custom-call | tf_op jit(solution)/shard_map/pallas_call | solution.py:108
  112.9 7.2 %all-to-all-start.2 = ((bf16[16,32,1536]{2,1,0:T(8,128)(2,1)}), bf16[16,32,1536]{2,1,0:T(8,128)(2,1)S(1)}, u32[]{:S(2)}, u32[]{:S(2)}) async-start(bf16[16,32,1536]{2,1,0:T(8,128)(2,1)} %bitcast.127), calls=%async_computation.2 | async-start | bytes 3145728 | tf_op jit(solution)/shard_map/all_to_all | solution.py:188
  120.1 32.1 %shard_map.128 = (bf16[1,512,1536]{2,1,0:T(8,128)(2,1)}, f32[2048,128]{1,0:T(8,128)}, f32[2048,128]{1,0:T(8,128)}) custom-call(s32[4]{0:T(128)} %select_reduce_fusion.owner_ref, f32[1,2048]{1,0:T(1,128)} %bitcast.141, bf16[1,512,1536]{2,1,0:T(8,128)(2,1)} %bitcast.115, bf16[1,512,1536]{2,1,0:T(8,128)(2,1)} %bitcast.116, bf16[1,512,1536]{2,1,0:T(8,128)(2,1)} %bitcast.117, ...), custom_call_target="tpu_custom_call" | custom-call | tf_op jit(solution)/shard_map/pallas_call | solution.py:108
  152.3 7.2 %all-to-all-start.4 = ((bf16[16,32,1536]{2,1,0:T(8,128)(2,1)}), bf16[16,32,1536]{2,1,0:T(8,128)(2,1)S(1)}, u32[]{:S(2)}, u32[]{:S(2)}) async-start(bf16[16,32,1536]{2,1,0:T(8,128)(2,1)} %bitcast.126), calls=%async_computation.4 | async-start | bytes 3145728 | tf_op jit(solution)/shard_map/all_to_all | solution.py:188
  159.5 2.0 copy.82
  161.6 0.7 copy.80
  163.7 2.3 %convolution_convert_fusion.1 = bf16[8,512,256]{2,0,1:T(8,128)(2,1)S(1)} fusion(f32[4,512,128]{2,0,1:T(4,128)S(1)} %copy.81, f32[4,512,128]{2,0,1:T(4,128)S(1)} %copy.80, f32[4,512,128]{2,0,1:T(4,128)S(1)} %copy.83, f32[4,512,128]{2,0,1:T(4,128)S(1)} %copy.82, s32[4]{0:T(128)S(1)} %copy-done.13, pred[4]{0:T(512)(128)(4,1)S(1)} %select_reduce_fusion.1), kind=kOutput, calls=%fused_computation.7 | convolution fusion | flops 11534400 | bytes 6291476 | tf_op jit(solution)/shard_map/ok,krc->orc/dot_general | solution.py:204
  166.0 1.8 copy.84
  167.8 13.7 %all-to-all-done.4 = bf16[16,32,1536]{2,1,0:T(8,128)(2,1)S(1)} async-done(((bf16[16,32,1536]{2,1,0:T(8,128)(2,1)}), bf16[16,32,1536]{2,1,0:T(8,128)(2,1)S(1)}, u32[]{:S(2)}, u32[]{:S(2)}) %all-to-all-start.4) | async-done | bytes 1572896 | tf_op jit(solution)/shard_map/all_to_all | solution.py:188
  181.5 1.1 copy-done.4
  182.6 4.9 %all-to-all-start.5 = ((bf16[128,32,256]{2,1,0:T(8,128)(2,1)}), bf16[128,32,256]{2,1,0:T(8,128)(2,1)S(1)}, u32[]{:S(2)}, u32[]{:S(2)}) async-start(bf16[128,32,256]{2,1,0:T(8,128)(2,1)} %bitcast.34), calls=%async_computation.5 | async-start | bytes 4194304 | tf_op jit(solution)/shard_map/all_to_all | solution.py:208
  187.5 2.4 %copy_dynamic-update-slice_fusion.1 = bf16[8,2,2,32,1536]{4,0,3,2,1:T(8,128)(2,1)S(1)} fusion(bf16[8,2,1,32,1536]{4,3,1,0,2:T(8,128)(2,1)} %bitcast.120), kind=kLoop, calls=%fused_computation.11 | loop fusion | bytes 3145728
  189.9 0.9 copy_dynamic-update-slice_fusion
  190.8 1.6 slice_bitcast_fusion.2
  192.9 3.2 %reshape.141 = bf16[4,32,5120]{2,1,0:T(8,128)(2,1)} reshape(bf16[2,2,32,8,640]{4,3,2,1,0:T(8,128)(2,1)} %get-tuple-element.44) | data formatting | bytes 2621440 | tf_op jit(solution)/shard_map/reshape | solution.py:194
  196.1 1.9 slice_bitcast_fusion.6
  197.9 1.8 reshape.143
  199.7 1.8 reshape.142
  201.5 1.4 reshape.140
  202.9 14.1 %all-to-all-done.5 = bf16[128,32,256]{2,1,0:T(8,128)(2,1)S(1)} async-done(((bf16[128,32,256]{2,1,0:T(8,128)(2,1)}), bf16[128,32,256]{2,1,0:T(8,128)(2,1)S(1)}, u32[]{:S(2)}, u32[]{:S(2)}) %all-to-all-start.5) | async-done | bytes 2097184 | tf_op jit(solution)/shard_map/all_to_all | solution.py:208
  217.5 0.7 fusion.3
  218.6 0.7 convert_element_type.41
  219.4 0.7 convert_element_type.39
  (63 shorter events, 6.9 us)
Async XLA Ops:
  0.6 2.2 %copy-start.6 = (bf16[4,32,5120]{2,1,0:T(8,128)(2,1)S(1)}, bf16[4,32,5120]{2,1,0:T(8,128)(2,1)}, u32[]{:S(2)}) copy-start(bf16[4,32,5120]{2,1,0:T(8,128)(2,1)} %param.8) | copy-start | bytes 3932164
  2.9 1.3 copy-start.7
  6.9 8.3 %copy-start.15 = (s32[32]{0:T(128)S(1)}, s32[32]{0:T(128)}, u32[]{:S(2)}) copy-start(s32[32]{0:T(128)} %param.15) | copy-start | bytes 388
  6.9 8.4 %copy-start.14 = (s32[32,4]{0,1:T(4,128)S(1)}, s32[32,4]{0,1:T(4,128)}, u32[]{:S(2)}) copy-start(s32[32,4]{0,1:T(4,128)} %param.14) | copy-start | bytes 1540
  6.9 8.5 %copy-start.11 = (bf16[2,32,1024]{2,1,0:T(8,128)(2,1)S(1)}, bf16[2,32,1024]{2,1,0:T(8,128)(2,1)}, u32[]{:S(2)}) copy-start(bf16[2,32,1024]{2,1,0:T(8,128)(2,1)} %param.11) | copy-start | bytes 393220
  6.9 8.7 %copy-start.12 = (bf16[2,32,1024]{2,1,0:T(8,128)(2,1)S(1)}, bf16[2,32,1024]{2,1,0:T(8,128)(2,1)}, u32[]{:S(2)}) copy-start(bf16[2,32,1024]{2,1,0:T(8,128)(2,1)} %param.12) | copy-start | bytes 393220
  6.9 32.8 %all-to-all-start = ((bf16[16,32,1536]{2,1,0:T(8,128)(2,1)}), bf16[16,32,1536]{2,1,0:T(8,128)(2,1)S(1)}, u32[]{:S(2)}, u32[]{:S(2)}) async-start(bf16[16,32,1536]{2,1,0:T(8,128)(2,1)} %get-tuple-element.47), calls=%async_computation | async-start | bytes 3145728 | tf_op jit(solution)/shard_map/all_to_all | solution.py:182
  39.7 35.8 %copy-start = (bf16[16,32,1536]{2,1,0:T(8,128)(2,1)}, bf16[16,32,1536]{2,1,0:T(8,128)(2,1)S(1)}, u32[]{:S(2)}) copy-start(bf16[16,32,1536]{2,1,0:T(8,128)(2,1)S(1)} %all-to-all-done) | copy-start | bytes 4718596
  75.5 37.4 %all-to-all-start.3 = ((bf16[16,32,1536]{2,1,0:T(8,128)(2,1)}), bf16[16,32,1536]{2,1,0:T(8,128)(2,1)S(1)}, u32[]{:S(2)}, u32[]{:S(2)}) async-start(bf16[16,32,1536]{2,1,0:T(8,128)(2,1)} %get-tuple-element.46), calls=%async_computation.3 | async-start | bytes 3145728 | tf_op jit(solution)/shard_map/all_to_all | solution.py:182
  112.9 7.2 %copy-start.1 = (bf16[16,32,1536]{2,1,0:T(8,128)(2,1)}, bf16[16,32,1536]{2,1,0:T(8,128)(2,1)S(1)}, u32[]{:S(2)}) copy-start(bf16[16,32,1536]{2,1,0:T(8,128)(2,1)S(1)} %all-to-all-done.3) | copy-start | bytes 4718596
  112.9 39.3 %all-to-all-start.2 = ((bf16[16,32,1536]{2,1,0:T(8,128)(2,1)}), bf16[16,32,1536]{2,1,0:T(8,128)(2,1)S(1)}, u32[]{:S(2)}, u32[]{:S(2)}) async-start(bf16[16,32,1536]{2,1,0:T(8,128)(2,1)} %bitcast.127), calls=%async_computation.2 | async-start | bytes 3145728 | tf_op jit(solution)/shard_map/all_to_all | solution.py:188
  152.3 9.3 %copy-start.3 = (bf16[16,32,1536]{2,1,0:T(8,128)(2,1)}, bf16[16,32,1536]{2,1,0:T(8,128)(2,1)S(1)}, u32[]{:S(2)}) copy-start(bf16[16,32,1536]{2,1,0:T(8,128)(2,1)S(1)} %all-to-all-done.2) | copy-start | bytes 4718596
  152.3 29.2 %all-to-all-start.4 = ((bf16[16,32,1536]{2,1,0:T(8,128)(2,1)}), bf16[16,32,1536]{2,1,0:T(8,128)(2,1)S(1)}, u32[]{:S(2)}, u32[]{:S(2)}) async-start(bf16[16,32,1536]{2,1,0:T(8,128)(2,1)} %bitcast.126), calls=%async_computation.4 | async-start | bytes 3145728 | tf_op jit(solution)/shard_map/all_to_all | solution.py:188
  159.5 2.1 copy-start.9
  159.5 2.8 %copy-start.8 = (f32[2048,128]{1,0:T(8,128)S(1)}, f32[2048,128]{1,0:T(8,128)}, u32[]{:S(2)}) copy-start(f32[2048,128]{1,0:T(8,128)} %get-tuple-element.15) | copy-start | bytes 3145732
  161.6 1.4 copy-start.10
  162.3 1.4 copy-start.13
  181.5 1.1 copy-start.4
  182.6 34.4 %all-to-all-start.5 = ((bf16[128,32,256]{2,1,0:T(8,128)(2,1)}), bf16[128,32,256]{2,1,0:T(8,128)(2,1)S(1)}, u32[]{:S(2)}, u32[]{:S(2)}) async-start(bf16[128,32,256]{2,1,0:T(8,128)(2,1)} %bitcast.34), calls=%async_computation.5 | async-start | bytes 4194304 | tf_op jit(solution)/shard_map/all_to_all | solution.py:208
  187.5 2.4 %copy-start.5 = (bf16[16,32,1536]{2,1,0:T(8,128)(2,1)S(1)}, bf16[16,32,1536]{2,1,0:T(8,128)(2,1)}, u32[]{:S(2)}) copy-start(bf16[16,32,1536]{2,1,0:T(8,128)(2,1)} %copy-done.4) | copy-start | bytes 4718596
  190.8 2.1 copy-start.2

commit v15 on v14

--- a/solution.py
+++ b/solution.py
@@ -13,7 +13,7 @@
 NEG_FILL = -1e30
 
 
-def attend_kernel(owner_ref, mask_ref, q_ref, g_ref, ko_ref, vo_ref, *refs):
+def attend_kernel(owner_ref, mask_ref, causal_ref, q_ref, g_ref, ko_ref, vo_ref, *refs):
     levels = (len(refs) - 5) // 2
     ka_refs, va_refs = refs[:levels], refs[levels : 2 * levels]
     back_ref, dka_ref, dva_ref, dko_acc, dvo_acc = refs[2 * levels :]
@@ -47,9 +47,7 @@
     s_a = lax.dot_general(q, ka, nt, preferred_element_type=jnp.float32) * scale
     s_o = lax.dot_general(q, ko, nt, preferred_element_type=jnp.float32) * scale
     s_a = s_a + mask_ref[...]
-    rows = row_i * block_rows + lax.broadcasted_iota(jnp.int32, (block_rows, seg_len), 0)
-    cols = lax.broadcasted_iota(jnp.int32, (block_rows, seg_len), 1)
-    s_o = jnp.where(cols <= rows, s_o, NEG_FILL)
+    s_o = s_o + causal_ref[...]
     m = jnp.maximum(jnp.max(s_a, axis=1, keepdims=True), jnp.max(s_o, axis=1, keepdims=True))
     w_a = jnp.exp(s_a - m)
     w_o = jnp.exp(s_o - m)
@@ -95,6 +93,9 @@
     kospec = pl.BlockSpec((None, seg_len, HD), lambda l, h, r, own: (l, 0, 2 * heads))
     vospec = pl.BlockSpec((None, seg_len, HD), lambda l, h, r, own: (l, 0, 2 * heads + 1))
     maskspec = pl.BlockSpec((1, anc), lambda l, h, r, own: (0, 0))
+    causalspec = pl.BlockSpec((block_rows, seg_len), lambda l, h, r, own: (r, 0))
+    positions = lax.broadcasted_iota(jnp.int32, (seg_len, seg_len), 0) + anc_owner[0] * 0
+    causal = jnp.where(lax.broadcasted_iota(jnp.int32, (seg_len, seg_len), 1) <= positions, 0.0, NEG_FILL).astype(jnp.float32)
     ancspec = pl.BlockSpec((anc, HD), lambda l, h, r, own: (0, 0))
 
     def level_spec(level, column):
@@ -110,13 +111,13 @@
         grid_spec=pltpu.PrefetchScalarGridSpec(
             num_scalar_prefetch=1,
             grid=grid,
-            in_specs=[maskspec, qspec, gspec, kospec, vospec] + kaspecs + vaspecs,
+            in_specs=[maskspec, causalspec, qspec, gspec, kospec, vospec] + kaspecs + vaspecs,
             out_specs=[backspec, ancspec, ancspec],
             scratch_shapes=[pltpu.VMEM((seg_len, HD), jnp.float32), pltpu.VMEM((seg_len, HD), jnp.float32)],
         ),
         out_shape=[back_rows, anc_grad, anc_grad],
         compiler_params=pltpu.CompilerParams(dimension_semantics=("arbitrary", "arbitrary", "arbitrary")),
-    )(anc_owner, anc_mask, packed, packed, packed, packed, *([anc_blocks] * (2 * levels)))
+    )(anc_owner, anc_mask, causal, packed, packed, packed, packed, *([anc_blocks] * (2 * levels)))
 
 
 def on_device(queries, leaf_keys, leaf_values, inner_keys, inner_values, out_grad, ancestors, depths):

time: 221 us -> 223 us (level)
  no operation moved by 1% of the time
where the time goes in v15:
time: 223 us; the launch traced here: 222 us
  Pallas kernels  64.9 us (29%)
  waiting for transfers between devices  50.6 us (23%)
  blocking collectives  35.5 us (16%)
  local copies, waits for them, and re-layouts  31.8 us (14%)
  starting transfers between devices  31.3 us (14%)
  matrix products  3.52 us (2%)
  other arithmetic  3.1 us (1%)
    pallas_call x2, Pallas kernels, attend_all(): pl.pallas_call(attend_kernel, grid_spec=pltpu.PrefetchScalarGridSpec(num_...  64.9 us
    all_to_all x1, blocking collectives, on_device(): lax.all_to_all(anc_send, ('seg', 'leaf'), split_axis=0, concat_axis=0, ti...  35.5 us
    all_to_all x2, waiting for transfers between devices, on_device(): lax.all_to_all(packed[:, chunk], 'leaf', split_axis=0, concat_axis=0, til...  22.8 us
    all_to_all x2, starting transfers between devices, on_device(): lax.all_to_all(back, 'leaf', split_axis=0, concat_axis=0, tiled=True)  14.4 us
    all_to_all x1, waiting for transfers between devices, on_device(): lax.all_to_all(homeward, ('seg', 'leaf'), split_axis=0, concat_axis=0, ti...  14.1 us
    all_to_all x2, waiting for transfers between devices, on_device(): lax.all_to_all(back, 'leaf', split_axis=0, concat_axis=0, tiled=True)  13.7 us
    all_to_all x2, starting transfers between devices, on_device(): lax.all_to_all(packed[:, chunk], 'leaf', split_axis=0, concat_axis=0, til...  12 us
    unnamed x41, local copies, waits for them, and re-layouts  8.41 us
  transfers between devices with their start and end apart: 5, of which 3 were waited for; matrix products, arithmetic and copies ran while one was open for 12% of the time, Pallas kernels for 29%

profile of v15, /device:TPU:0, one launch (start us, length us, event | category | flops | bytes accessed | tf_op | source)
XLA Modules:
  0.0 221.8 jit_solution(4016248812702945400)
XLA Ops:
  0.6 1.1 copy.92
  1.8 1.0 copy.93
  3.3 0.9 copy-done.7
  5.0 1.8 slice_bitcast_fusion
  6.9 8.3 %all-to-all-start = ((bf16[16,32,1536]{2,1,0:T(8,128)(2,1)}), bf16[16,32,1536]{2,1,0:T(8,128)(2,1)S(1)}, u32[]{:S(2)}, u32[]{:S(2)}) async-start(bf16[16,32,1536]{2,1,0:T(8,128)(2,1)} %get-tuple-element.47), calls=%async_computation | async-start | bytes 3145728 | tf_op jit(solution)/shard_map/all_to_all | solution.py:183
  17.0 22.8 %all-to-all-done = bf16[16,32,1536]{2,1,0:T(8,128)(2,1)S(1)} async-done(((bf16[16,32,1536]{2,1,0:T(8,128)(2,1)}), bf16[16,32,1536]{2,1,0:T(8,128)(2,1)S(1)}, u32[]{:S(2)}, u32[]{:S(2)}) %all-to-all-start) | async-done | bytes 1572896 | tf_op jit(solution)/shard_map/all_to_all | solution.py:183
  40.0 35.5 %all_to_all.30 = bf16[128,32,256]{2,1,0:T(8,128)(2,1)} all-to-all(bf16[128,32,256]{2,1,0:T(8,128)(2,1)S(1)} %bitcast.119), channel_id=1, replica_groups=mesh['seg'=8,'leaf'=16] {'seg','leaf'}, dimensions={0} | all-to-all | bytes 4194304 | tf_op jit(solution)/shard_map/all_to_all | solution.py:168
  75.5 3.7 %all-to-all-start.3 = ((bf16[16,32,1536]{2,1,0:T(8,128)(2,1)}), bf16[16,32,1536]{2,1,0:T(8,128)(2,1)S(1)}, u32[]{:S(2)}, u32[]{:S(2)}) async-start(bf16[16,32,1536]{2,1,0:T(8,128)(2,1)} %get-tuple-element.46), calls=%async_computation.3 | async-start | bytes 3145728 | tf_op jit(solution)/shard_map/all_to_all | solution.py:183
  80.1 0.7 select_reduce_fusion.owner_ref
  80.8 1.1 fusion.7.causal_ref
  81.9 32.4 %shard_map.127 = (bf16[1,512,1536]{2,1,0:T(8,128)(2,1)}, f32[2048,128]{1,0:T(8,128)}, f32[2048,128]{1,0:T(8,128)}) custom-call(s32[4]{0:T(128)} %select_reduce_fusion.owner_ref, f32[1,2048]{1,0:T(1,128)} %bitcast.140, f32[512,512]{1,0:T(8,128)} %fusion.7.causal_ref, bf16[1,512,1536]{2,1,0:T(8,128)(2,1)} %bitcast.111, bf16[1,512,1536]{2,1,0:T(8,128)(2,1)} %bitcast.112, ...), custom_call_target="tpu_custom_call" | custom-call | tf_op jit(solution)/shard_map/pallas_call | solution.py:109
  114.3 7.2 %all-to-all-start.2 = ((bf16[16,32,1536]{2,1,0:T(8,128)(2,1)}), bf16[16,32,1536]{2,1,0:T(8,128)(2,1)S(1)}, u32[]{:S(2)}, u32[]{:S(2)}) async-start(bf16[16,32,1536]{2,1,0:T(8,128)(2,1)} %bitcast.127), calls=%async_computation.2 | async-start | bytes 3145728 | tf_op jit(solution)/shard_map/all_to_all | solution.py:189
  121.5 32.5 %shard_map.128 = (bf16[1,512,1536]{2,1,0:T(8,128)(2,1)}, f32[2048,128]{1,0:T(8,128)}, f32[2048,128]{1,0:T(8,128)}) custom-call(s32[4]{0:T(128)} %select_reduce_fusion.owner_ref, f32[1,2048]{1,0:T(1,128)} %bitcast.141, f32[512,512]{1,0:T(8,128)} %fusion.7.causal_ref, bf16[1,512,1536]{2,1,0:T(8,128)(2,1)} %bitcast.115, bf16[1,512,1536]{2,1,0:T(8,128)(2,1)} %bitcast.116, ...), custom_call_target="tpu_custom_call" | custom-call | tf_op jit(solution)/shard_map/pallas_call | solution.py:109
  154.0 7.2 %all-to-all-start.4 = ((bf16[16,32,1536]{2,1,0:T(8,128)(2,1)}), bf16[16,32,1536]{2,1,0:T(8,128)(2,1)S(1)}, u32[]{:S(2)}, u32[]{:S(2)}) async-start(bf16[16,32,1536]{2,1,0:T(8,128)(2,1)} %bitcast.126), calls=%async_computation.4 | async-start | bytes 3145728 | tf_op jit(solution)/shard_map/all_to_all | solution.py:189
  161.3 2.0 copy.82
  165.5 2.3 %convolution_convert_fusion.1 = bf16[8,512,256]{2,0,1:T(8,128)(2,1)S(1)} fusion(f32[4,512,128]{2,0,1:T(4,128)S(1)} %copy.81, f32[4,512,128]{2,0,1:T(4,128)S(1)} %copy.80, f32[4,512,128]{2,0,1:T(4,128)S(1)} %copy.83, f32[4,512,128]{2,0,1:T(4,128)S(1)} %copy.82, s32[4]{0:T(128)S(1)} %copy-done.13, pred[4]{0:T(512)(128)(4,1)S(1)} %select_reduce_fusion.1), kind=kOutput, calls=%fused_computation.7 | convolution fusion | flops 11534400 | bytes 6291476 | tf_op jit(solution)/shard_map/ok,krc->orc/dot_general | solution.py:205
  167.7 1.8 copy.84
  169.5 13.7 %all-to-all-done.4 = bf16[16,32,1536]{2,1,0:T(8,128)(2,1)S(1)} async-done(((bf16[16,32,1536]{2,1,0:T(8,128)(2,1)}), bf16[16,32,1536]{2,1,0:T(8,128)(2,1)S(1)}, u32[]{:S(2)}, u32[]{:S(2)}) %all-to-all-start.4) | async-done | bytes 1572896 | tf_op jit(solution)/shard_map/all_to_all | solution.py:189
  183.2 1.1 copy-done.4
  184.4 4.9 %all-to-all-start.5 = ((bf16[128,32,256]{2,1,0:T(8,128)(2,1)}), bf16[128,32,256]{2,1,0:T(8,128)(2,1)S(1)}, u32[]{:S(2)}, u32[]{:S(2)}) async-start(bf16[128,32,256]{2,1,0:T(8,128)(2,1)} %bitcast.34), calls=%async_computation.5 | async-start | bytes 4194304 | tf_op jit(solution)/shard_map/all_to_all | solution.py:209
  189.3 2.4 %copy_dynamic-update-slice_fusion.1 = bf16[8,2,2,32,1536]{4,0,3,2,1:T(8,128)(2,1)S(1)} fusion(bf16[8,2,1,32,1536]{4,3,1,0,2:T(8,128)(2,1)} %bitcast.120), kind=kLoop, calls=%fused_computation.11 | loop fusion | bytes 3145728
  191.7 0.9 copy_dynamic-update-slice_fusion
  192.5 1.6 slice_bitcast_fusion.2
  194.6 3.2 %reshape.141 = bf16[4,32,5120]{2,1,0:T(8,128)(2,1)} reshape(bf16[2,2,32,8,640]{4,3,2,1,0:T(8,128)(2,1)} %get-tuple-element.44) | data formatting | bytes 2621440 | tf_op jit(solution)/shard_map/reshape | solution.py:195
  197.8 1.9 slice_bitcast_fusion.6
  199.7 1.8 reshape.143
  201.5 1.8 reshape.142
  203.2 1.4 reshape.140
  204.7 14.1 %all-to-all-done.5 = bf16[128,32,256]{2,1,0:T(8,128)(2,1)S(1)} async-done(((bf16[128,32,256]{2,1,0:T(8,128)(2,1)}), bf16[128,32,256]{2,1,0:T(8,128)(2,1)S(1)}, u32[]{:S(2)}, u32[]{:S(2)}) %all-to-all-start.5) | async-done | bytes 2097184 | tf_op jit(solution)/shard_map/all_to_all | solution.py:209
  219.3 0.7 fusion.3
  220.3 0.7 convert_element_type.41
  221.1 0.7 convert_element_type.39
  (64 shorter events, 7.6 us)
Async XLA Ops:
  0.6 2.2 %copy-start.6 = (bf16[4,32,5120]{2,1,0:T(8,128)(2,1)S(1)}, bf16[4,32,5120]{2,1,0:T(8,128)(2,1)}, u32[]{:S(2)}) copy-start(bf16[4,32,5120]{2,1,0:T(8,128)(2,1)} %param.8) | copy-start | bytes 3932164
  2.9 1.3 copy-start.7
  6.9 8.3 %copy-start.15 = (s32[32]{0:T(128)S(1)}, s32[32]{0:T(128)}, u32[]{:S(2)}) copy-start(s32[32]{0:T(128)} %param.15) | copy-start | bytes 388
  6.9 8.4 %copy-start.14 = (s32[32,4]{0,1:T(4,128)S(1)}, s32[32,4]{0,1:T(4,128)}, u32[]{:S(2)}) copy-start(s32[32,4]{0,1:T(4,128)} %param.14) | copy-start | bytes 1540
  6.9 8.5 %copy-start.11 = (bf16[2,32,1024]{2,1,0:T(8,128)(2,1)S(1)}, bf16[2,32,1024]{2,1,0:T(8,128)(2,1)}, u32[]{:S(2)}) copy-start(bf16[2,32,1024]{2,1,0:T(8,128)(2,1)} %param.11) | copy-start | bytes 393220
  6.9 8.7 %copy-start.12 = (bf16[2,32,1024]{2,1,0:T(8,128)(2,1)S(1)}, bf16[2,32,1024]{2,1,0:T(8,128)(2,1)}, u32[]{:S(2)}) copy-start(bf16[2,32,1024]{2,1,0:T(8,128)(2,1)} %param.12) | copy-start | bytes 393220
  6.9 32.8 %all-to-all-start = ((bf16[16,32,1536]{2,1,0:T(8,128)(2,1)}), bf16[16,32,1536]{2,1,0:T(8,128)(2,1)S(1)}, u32[]{:S(2)}, u32[]{:S(2)}) async-start(bf16[16,32,1536]{2,1,0:T(8,128)(2,1)} %get-tuple-element.47), calls=%async_computation | async-start | bytes 3145728 | tf_op jit(solution)/shard_map/all_to_all | solution.py:183
  39.7 35.8 %copy-start = (bf16[16,32,1536]{2,1,0:T(8,128)(2,1)}, bf16[16,32,1536]{2,1,0:T(8,128)(2,1)S(1)}, u32[]{:S(2)}) copy-start(bf16[16,32,1536]{2,1,0:T(8,128)(2,1)S(1)} %all-to-all-done) | copy-start | bytes 4718596
  75.5 38.8 %all-to-all-start.3 = ((bf16[16,32,1536]{2,1,0:T(8,128)(2,1)}), bf16[16,32,1536]{2,1,0:T(8,128)(2,1)S(1)}, u32[]{:S(2)}, u32[]{:S(2)}) async-start(bf16[16,32,1536]{2,1,0:T(8,128)(2,1)} %get-tuple-element.46), calls=%async_computation.3 | async-start | bytes 3145728 | tf_op jit(solution)/shard_map/all_to_all | solution.py:183
  114.3 7.2 %copy-start.1 = (bf16[16,32,1536]{2,1,0:T(8,128)(2,1)}, bf16[16,32,1536]{2,1,0:T(8,128)(2,1)S(1)}, u32[]{:S(2)}) copy-start(bf16[16,32,1536]{2,1,0:T(8,128)(2,1)S(1)} %all-to-all-done.3) | copy-start | bytes 4718596
  114.3 39.7 %all-to-all-start.2 = ((bf16[16,32,1536]{2,1,0:T(8,128)(2,1)}), bf16[16,32,1536]{2,1,0:T(8,128)(2,1)S(1)}, u32[]{:S(2)}, u32[]{:S(2)}) async-start(bf16[16,32,1536]{2,1,0:T(8,128)(2,1)} %bitcast.127), calls=%async_computation.2 | async-start | bytes 3145728 | tf_op jit(solution)/shard_map/all_to_all | solution.py:189
  154.0 9.3 %copy-start.3 = (bf16[16,32,1536]{2,1,0:T(8,128)(2,1)}, bf16[16,32,1536]{2,1,0:T(8,128)(2,1)S(1)}, u32[]{:S(2)}) copy-start(bf16[16,32,1536]{2,1,0:T(8,128)(2,1)S(1)} %all-to-all-done.2) | copy-start | bytes 4718596
  154.0 29.2 %all-to-all-start.4 = ((bf16[16,32,1536]{2,1,0:T(8,128)(2,1)}), bf16[16,32,1536]{2,1,0:T(8,128)(2,1)S(1)}, u32[]{:S(2)}, u32[]{:S(2)}) async-start(bf16[16,32,1536]{2,1,0:T(8,128)(2,1)} %bitcast.126), calls=%async_computation.4 | async-start | bytes 3145728 | tf_op jit(solution)/shard_map/all_to_all | solution.py:189
  161.3 2.1 copy-start.9
  161.3 2.8 %copy-start.8 = (f32[2048,128]{1,0:T(8,128)S(1)}, f32[2048,128]{1,0:T(8,128)}, u32[]{:S(2)}) copy-start(f32[2048,128]{1,0:T(8,128)} %get-tuple-element.15) | copy-start | bytes 3145732
  163.3 1.4 copy-start.10
  164.1 1.4 copy-start.13
  183.2 1.1 copy-start.4
  184.4 34.4 %all-to-all-start.5 = ((bf16[128,32,256]{2,1,0:T(8,128)(2,1)}), bf16[128,32,256]{2,1,0:T(8,128)(2,1)S(1)}, u32[]{:S(2)}, u32[]{:S(2)}) async-start(bf16[128,32,256]{2,1,0:T(8,128)(2,1)} %bitcast.34), calls=%async_computation.5 | async-start | bytes 4194304 | tf_op jit(solution)/shard_map/all_to_all | solution.py:209
  189.2 2.4 %copy-start.5 = (bf16[16,32,1536]{2,1,0:T(8,128)(2,1)S(1)}, bf16[16,32,1536]{2,1,0:T(8,128)(2,1)}, u32[]{:S(2)}) copy-start(bf16[16,32,1536]{2,1,0:T(8,128)(2,1)} %copy-done.4) | copy-start | bytes 4718596
  192.5 2.1 copy-start.2
